TPU v7x, 256 devices: a whole 4x4x8 slice. The times are simulated.
256 devices in a mesh: cfg: 2 (over x_hi), seq: 32 (over x_lo, z, core), tp: 4 (over y).
Axes of the slice: x: 4 (x_hi: 2, x_lo: 2; x = x_hi * 2 + x_lo), y: 4, z: 8, core: 2. Of those that a mesh axis runs over, the one named last changes fastest.
Arguments:
- img_hidden: bfloat16 [2, 1024, 8, 1536], P('cfg', 'seq'), may hold values from -80 to 80
- txt_hidden: bfloat16 [2, 160, 8, 1536], P('cfg', 'seq'), may hold values from -6 to 6
- modulation: bfloat16 [2, 8, 10, 1536], P('cfg'), may hold values from -3 to 5
- text_lengths: int32 [2, 8], P('cfg'), may hold values from 1 to 160, as said below
- timestep_index: int32 [8], replicated, may hold values from 0 to 7
- sigmas: float32 [9], replicated, may hold values from 0 to 2, as said below
- latents: float32 [1024, 8, 64], P(('seq', 'tp'), None, 'cfg'), may hold values from -6 to 6
- w_qkv: bfloat16 [1536, 3, 1536], P(None, None, 'tp'), may hold values from -0.3125 to 0.3125
- w_kv_text: bfloat16 [1536, 2, 1536], P(None, None, 'tp'), may hold values from -0.3125 to 0.3125
- w_out: bfloat16 [1536, 1536], P('tp'), may hold values from -0.15625 to 0.15625
- w_up: bfloat16 [1536, 3072], P(None, 'tp'), may hold values from -0.15625 to 0.15625
- w_down: bfloat16 [3072, 1536], P('tp'), may hold values from -0.109375 to 0.109375
- w_final: bfloat16 [1536, 64], replicated, may hold values from -0.15625 to 0.15625
Outputs:
- velocity: float32 [1024, 8, 64], P(('seq', 'tp'), None, 'cfg')
- latent_next: float32 [1024, 8, 64], P(('seq', 'tp'), None, 'cfg')
Inputs may be any that keep to these rules, and one draw needn't show every extreme that they name: `text_lengths`: in every draw the conditional copy of some request fills all 160 text slots. `sigmas`: Falling; each step down lies between 0.5 / 8 and 1.5 / 8.
All inputs are finite; a program needn't handle non-finite values.
Results may differ from a plain program's by a relative error of at most 0.014.
The roundings to bfloat16 on the way count: a program that leaves them out, or rounds other values in their place, can miss the bound.
Values may be sent and summed in bfloat16 or wider, within the bound.
No kernel may reach another device: no remote copies, remote signals or barrier semaphores. Data moves between devices by JAX's collectives and lax.ppermute only.
A program may use at most 128 MiB of HBM per device.

v0:
```python
import math

import jax
import jax.numpy as jnp
from jax import lax
from jax.sharding import PartitionSpec as P

HEAD_DIM = 64


EPSILON = 1e-06
GUIDANCE = 7.0


def swapped(value, axis, apart):
    return lax.ppermute(value, axis, [(i, i ^ 1 << apart) for i in range(lax.axis_size(axis))])


def layer_norm(values):
    center = values - jnp.mean(values, -1, keepdims=True)
    return center * lax.rsqrt(jnp.mean(center * center, -1, keepdims=True) + EPSILON)


def modulate(values, shift_add, scale_mul):
    return (layer_norm(values) * (1.0 + scale_mul) + shift_add).astype(jnp.bfloat16)


def attend(queries, keys_in, values_in, key_valid):
    heads = queries.shape[2] // HEAD_DIM
    query_heads = queries.reshape(queries.shape[0], queries.shape[1], heads, HEAD_DIM)
    key_heads = keys_in.reshape(keys_in.shape[0], keys_in.shape[1], heads, HEAD_DIM)
    value_heads = values_in.reshape(values_in.shape[0], values_in.shape[1], heads, HEAD_DIM)
    scores = jnp.einsum(
        "qrhd,krhd->rhqk", query_heads, key_heads, preferred_element_type=jnp.float32
    ) * (1.0 / math.sqrt(HEAD_DIM))
    scores = jnp.where(key_valid[:, None, None, :], scores, -jnp.inf)
    row_max = jnp.max(scores, -1, keepdims=True)
    exp_scores = jnp.exp(scores - row_max)
    weights = (exp_scores / jnp.sum(exp_scores, -1, keepdims=True)).astype(jnp.bfloat16)
    result = jnp.einsum("rhqk,krhd->qrhd", weights, value_heads, preferred_element_type=jnp.float32)
    return result.astype(jnp.bfloat16).reshape(queries.shape)


def spread(image_part, text_part, members):
    joined = jnp.concatenate([image_part, text_part], 0).transpose(1, 0, 2)
    widened = jnp.broadcast_to(joined[:, None], (joined.shape[0], members) + joined.shape[1:])
    return widened.reshape(joined.shape[0] * members, joined.shape[1], joined.shape[2])


def shards(
    img_hidden,
    txt_hidden,
    modulation,
    text_lengths,
    timestep_index,
    sigmas,
    latents,
    w_qkv,
    w_kv_text,
    w_out,
    w_up,
    w_down,
    w_final,
):
    img_slice = img_hidden.shape[1]
    requests = img_hidden.shape[2]
    model_width = img_hidden.shape[3]
    txt_slice = txt_hidden.shape[1]
    features = w_out.shape[0]
    members = lax.axis_size("seq") // requests
    parties = lax.axis_size("tp")
    portion = img_slice // parties
    rows_all = img_slice * requests
    adaptive = modulation[0].astype(jnp.float32)
    resident = img_hidden[0].astype(jnp.float32)
    lengths_all = text_lengths[0]
    normed = modulate(resident, adaptive[:, 0], adaptive[:, 1]).reshape(rows_all, model_width)
    projected = jnp.dot(
        normed, w_qkv.reshape(model_width, 3 * features), preferred_element_type=jnp.float32
    ).astype(jnp.bfloat16)
    queries = projected[:, :features].reshape(img_slice, requests, features)
    keys_img = projected[:, features : 2 * features].reshape(img_slice, requests, features)
    vals_img = projected[:, 2 * features :].reshape(img_slice, requests, features)
    text_in = modulate(txt_hidden[0].astype(jnp.float32), adaptive[:, 6], adaptive[:, 7]).reshape(
        txt_slice * requests, model_width
    )
    text_kv = jnp.dot(
        text_in, w_kv_text.reshape(model_width, 2 * features), preferred_element_type=jnp.float32
    ).astype(jnp.bfloat16)
    keys_txt = text_kv[:, :features].reshape(txt_slice, requests, features)
    vals_txt = text_kv[:, features:].reshape(txt_slice, requests, features)
    key_span = img_slice + txt_slice
    within = jnp.arange(key_span)
    query_share = img_slice // members
    senders = requests * members
    query_send = (
        queries.reshape(members, query_share, requests, features)
        .transpose(2, 0, 1, 3)
        .reshape(senders, query_share, features)
    )
    key_send = spread(keys_img, keys_txt, members)
    value_send = spread(vals_img, vals_txt, members)
    query_got, key_got, value_got = (
        lax.all_to_all(query_send, "seq", split_axis=0, concat_axis=0, tiled=True),
        lax.all_to_all(key_send, "seq", split_axis=0, concat_axis=0, tiled=True),
        lax.all_to_all(value_send, "seq", split_axis=0, concat_axis=0, tiled=True),
    )
    my_request = lax.axis_index("seq") // members
    length_now = jnp.sum(jnp.where(jnp.arange(requests) == my_request, lengths_all, 0))
    text_slot = jnp.arange(senders)[:, None] * txt_slice + within[None, :] - img_slice
    key_valid = (within[None, :] < img_slice) | (text_slot < length_now)
    answer = attend(
        query_got.reshape(senders * query_share, 1, features),
        key_got.reshape(senders * key_span, 1, features),
        value_got.reshape(senders * key_span, 1, features),
        key_valid.reshape(1, senders * key_span),
    )
    answer_back = lax.all_to_all(
        answer.reshape(senders, query_share, features),
        "seq",
        split_axis=0,
        concat_axis=0,
        tiled=True,
    )
    attn_rows = (
        answer_back.reshape(requests, members, query_share, features)
        .transpose(1, 2, 0, 3)
        .reshape(rows_all, features)
    )
    tp_index = lax.axis_index("tp")
    attn_mixed = lax.psum(
        jnp.dot(attn_rows, w_out, preferred_element_type=jnp.float32).astype(jnp.bfloat16), "tp"
    ).astype(jnp.float32)
    after_attn = resident + adaptive[:, 2] * attn_mixed.reshape(img_slice, requests, model_width)
    mlp_in = modulate(after_attn, adaptive[:, 3], adaptive[:, 4]).reshape(rows_all, model_width)
    hidden = jax.nn.gelu(
        jnp.dot(mlp_in, w_up, preferred_element_type=jnp.float32), approximate=True
    ).astype(jnp.bfloat16)
    mlp_grown = lax.psum(
        jnp.dot(hidden, w_down, preferred_element_type=jnp.float32).astype(jnp.bfloat16), "tp"
    ).astype(jnp.float32)
    after_mlp = after_attn + adaptive[:, 5] * mlp_grown.reshape(img_slice, requests, model_width)
    rows_mine = lax.dynamic_slice_in_dim(after_mlp, tp_index * portion, portion, 0)
    head_in = modulate(rows_mine, adaptive[:, 8], adaptive[:, 9]).reshape(
        portion * requests, model_width
    )
    velocity_own = jnp.dot(head_in, w_final, preferred_element_type=jnp.float32).reshape(
        portion, requests, w_final.shape[1]
    )
    half_width = w_final.shape[1] // 2
    cfg_index = lax.axis_index("cfg")
    own_kept = lax.dynamic_slice_in_dim(velocity_own, cfg_index * half_width, half_width, 2)
    own_given = lax.dynamic_slice_in_dim(velocity_own, (1 - cfg_index) * half_width, half_width, 2)
    velocity_other = swapped(own_given, "cfg", 0)
    is_first = cfg_index == 0
    guided_cond = jnp.where(is_first, own_kept, velocity_other)
    guided_free = jnp.where(is_first, velocity_other, own_kept)
    velocity = guided_free + GUIDANCE * (guided_cond - guided_free)
    steps_all = jnp.arange(sigmas.shape[0], dtype=jnp.int32)
    sigma_now = jnp.sum(
        jnp.where(steps_all[None, :] == timestep_index[:, None], sigmas[None, :], 0.0), 1
    )
    sigma_after = jnp.sum(
        jnp.where(steps_all[None, :] == timestep_index[:, None] + 1, sigmas[None, :], 0.0), 1
    )
    latent_next = latents + (sigma_after - sigma_now)[None, :, None] * velocity
    return (velocity, latent_next)


def solution(mesh):
    return jax.shard_map(
        shards,
        mesh=mesh,
        in_specs=(
            P("cfg", "seq", None, None),
            P("cfg", "seq", None, None),
            P("cfg", None, None, None),
            P("cfg", None),
            P(),
            P(),
            P(("seq", "tp"), None, "cfg"),
            P(None, None, "tp"),
            P(None, None, "tp"),
            P("tp", None),
            P(None, "tp"),
            P("tp", None),
            P(),
        ),
        out_specs=(P(("seq", "tp"), None, "cfg"), P(("seq", "tp"), None, "cfg")),
        check_vma=False,
    )
```

profile of v0, /device:TPU:4, one launch (start us, length us, event | category | flops | bytes accessed | tf_op | source)
XLA Modules:
  0.0 261.1 jit_solution(15725999960782495820)
XLA Ops:
  7.2 0.0 copy-start
  7.2 1.1 bitcast_convert_fusion
  8.3 0.8 slice_bitcast_fusion.4
  9.1 0.0 copy-done.1
  9.1 0.2 convert_reduce_fusion
  9.3 0.3 fusion.14
  9.6 6.1 %copy.26 = bf16[1536,3,384]{0,2,1:T(8,128)(2,1)} copy(bf16[1536,3,384]{2,0,1:T(8,128)(2,1)} %param.20) | data formatting | bytes 7077888 | tf_op args[7]
  15.7 3.3 %convolution_convert_fusion.1 = bf16[256,1152]{1,0:T(8,128)(2,1)S(1)} fusion(bf16[1536,1152]{0,1:T(8,128)(2,1)} %bitcast.154, bf16[1,32,8,1536]{3,2,1,0:T(8,128)(2,1)S(1)} %copy-done.1, f32[8,1536]{1,0:T(8,128)S(1)} %get-tuple-element.18, f32[8,1536]{1,0:T(8,128)S(1)} %get-tuple-element.19, f32[32,8]{1,0:T(8,128)S(1)} %add_rsqrt_fusion.1, ...), kind=kOutput, calls=%fused_computation.10 | convolution fusion | flops 908623872 | bytes 5015552 | tf_op jit(solution)/shard_map/dot_general | solution.py:78
  19.0 0.0 copy-start.2
  19.0 0.7 slice_bitcast_fusion.1
  19.8 0.7 copy.28
  20.5 9.6 %all-to-all-start.1 = ((bf16[32,8,384]{2,1,0:T(8,128)(2,1)}), bf16[32,8,384]{2,1,0:T(8,128)(2,1)}, u32[]{:S(2)}, u32[]{:S(2)}) async-start(bf16[32,8,384]{2,1,0:T(8,128)(2,1)} %bitcast.158), calls=%async_computation.1 | async-start | bytes 393216 | tf_op jit(solution)/shard_map/all_to_all | solution.py:104
  30.1 0.1 convert_reduce_fusion.1
  30.2 0.2 fusion.74
  30.4 2.1 copy.35
  32.5 0.0 copy-start.3
  32.5 0.0 copy-done.8
  32.6 0.0 copy-done.9
  32.6 0.6 convolution_convert_fusion.3
  33.2 0.3 copy-done.3
  33.5 0.8 maximum_bitcast_fusion
  34.3 7.6 %all-to-all-done.1 = bf16[32,8,384]{2,1,0:T(8,128)(2,1)} async-done(((bf16[32,8,384]{2,1,0:T(8,128)(2,1)}), bf16[32,8,384]{2,1,0:T(8,128)(2,1)}, u32[]{:S(2)}, u32[]{:S(2)}) %all-to-all-start.1) | async-done | bytes 196640 | tf_op jit(solution)/shard_map/all_to_all | solution.py:104
  41.9 1.0 broadcast_in_dim.35
  42.9 4.6 %all-to-all-start.2 = ((bf16[32,37,384]{2,1,0:T(8,128)(2,1)}), bf16[32,37,384]{2,1,0:T(8,128)(2,1)}, u32[]{:S(2)}, u32[]{:S(2)}) async-start(bf16[32,37,384]{2,1,0:T(8,128)(2,1)} %bitcast.153), calls=%async_computation.2 | async-start | bytes 1966080 | tf_op jit(solution)/shard_map/all_to_all | solution.py:105
  47.5 0.0 copy-start.15
  47.6 1.0 copy.27
  48.5 26.2 %all-to-all-done.2 = bf16[32,37,384]{2,1,0:T(8,128)(2,1)} async-done(((bf16[32,37,384]{2,1,0:T(8,128)(2,1)}), bf16[32,37,384]{2,1,0:T(8,128)(2,1)}, u32[]{:S(2)}, u32[]{:S(2)}) %all-to-all-start.2) | async-done | bytes 909344 | tf_op jit(solution)/shard_map/all_to_all | solution.py:105
  74.7 1.1 broadcast_in_dim.32
  75.8 4.6 %all-to-all-start = ((bf16[32,37,384]{2,1,0:T(8,128)(2,1)}), bf16[32,37,384]{2,1,0:T(8,128)(2,1)}, u32[]{:S(2)}, u32[]{:S(2)}) async-start(bf16[32,37,384]{2,1,0:T(8,128)(2,1)} %bitcast.152), calls=%async_computation | async-start | bytes 1966080 | tf_op jit(solution)/shard_map/all_to_all | solution.py:106
  80.4 0.2 all-reduce.3.cloned.1.call-start
  80.7 0.6 fusion.103
  81.3 0.7 fusion.102
  82.0 0.1 or.17
  82.2 2.0 reshape.389
  84.2 4.0 %reshape.393 = bf16[1184,6,64]{2,1,0:T(8,128)(2,1)} reshape(bf16[32,37,384]{2,1,0:T(8,128)(2,1)} %all-to-all-done.2) | data formatting | bytes 1818624 | tf_op jit(solution)/shard_map/reshape.2
  88.2 4.2 %fusion.117 = f32[6,256]{1,0:T(8,128)S(1)} fusion(pred[1184]{0:T(1024)(128)(4,1)S(1)} %or.17, bf16[1184,6,64]{2,1,0:T(8,128)(2,1)} %reshape.393, bf16[256,6,64]{2,1,0:T(8,128)(2,1)} %reshape.389), kind=kOutput, calls=%fused_computation.142 | convolution fusion | flops 240059552 | bytes 1113248 | tf_op jit(solution)/shard_map/sub | solution.py:38
  92.4 15.1 %all-to-all-done = bf16[32,37,384]{2,1,0:T(8,128)(2,1)} async-done(((bf16[32,37,384]{2,1,0:T(8,128)(2,1)}), bf16[32,37,384]{2,1,0:T(8,128)(2,1)}, u32[]{:S(2)}, u32[]{:S(2)}) %all-to-all-start) | async-done | bytes 909344 | tf_op jit(solution)/shard_map/all_to_all | solution.py:106
  107.6 4.0 %reshape.387 = bf16[1184,6,64]{2,1,0:T(8,128)(2,1)} reshape(bf16[32,37,384]{2,1,0:T(8,128)(2,1)} %all-to-all-done) | data formatting | bytes 1818624 | tf_op jit(solution)/shard_map/reshape.6
  111.6 5.7 %fusion.28 = bf16[256,1,6,64]{0,3,2,1:T(8,128)(2,1)S(1)} fusion(f32[6,256]{1,0:T(8,128)S(1)} %fusion.117, bf16[1184,6,64]{2,1,0:T(8,128)(2,1)} %reshape.387, pred[1184]{0:T(1024)(128)(4,1)S(1)} %or.17, bf16[1184,6,64]{2,1,0:T(8,128)(2,1)} %reshape.393, bf16[256,6,64]{2,1,0:T(8,128)(2,1)} %reshape.389), kind=kOutput, calls=%fused_computation.39 | convolution fusion | flops 474761888 | bytes 2219168 | tf_op jit(solution)/shard_map/rhqk,krhd->qrhd/dot_general | solution.py:40
  117.4 1.1 copy.33
  118.4 1.4 reshape_reshape.10
  119.8 15.6 %all_to_all.20 = bf16[32,8,384]{2,1,0:T(8,128)(2,1)S(1)} all-to-all(bf16[32,8,384]{2,1,0:T(8,128)(2,1)S(1)} %reshape_reshape.10), channel_id=1, replica_groups=mesh['cfg'=2,'seq'=32,'tp'=4] {'seq'}, dimensions={0} | all-to-all | bytes 393216 | tf_op jit(solution)/shard_map/all_to_all | solution.py:118
  135.4 0.1 copy.34
  135.5 2.7 %convolution_convert_fusion.2 = bf16[256,1536]{1,0:T(8,128)(2,1)} fusion(bf16[256,384]{1,0:T(8,128)(2,1)S(1)} %bitcast.157, bf16[384,1536]{1,0:T(8,128)(2,1)} %param.22), kind=kOutput, calls=%fused_computation.11 | convolution fusion | flops 302383104 | bytes 2162688 | tf_op jit(solution)/shard_map/dot_general | solution.py:132
  138.2 0.0 all-reduce.3.cloned.1.call-update
  138.2 0.0 all-reduce.5.cloned.1.call-start
  138.3 46.2 %all-reduce.3.cloned.1.call-done = bf16[256,1536]{1,0:T(8,128)(2,1)} async-done(((bf16[256,1536]{1,0:T(8,128)(2,1)}), bf16[256,1536]{1,0:T(8,128)(2,1)}) %all-reduce.3.cloned.1.call-update) | async-done | bytes 786448 | tf_op jit(solution)/shard_map/psum | solution.py:131
  184.4 2.5 fusion.115
  187.0 0.1 div.53
  187.1 1.7 multiply_reduce_fusion
  188.8 0.1 rsqrt.38
  188.9 0.0 copy-start.13
  188.9 4.6 %fusion.6 = bf16[32,8,1536]{2,1,0:T(8,128)(2,1)} fusion(bf16[768,1536]{1,0:T(8,128)(2,1)S(1)} %copy-done, bf16[1536,768]{1,0:T(8,128)(2,1)} %param.23, bf16[256,1536]{1,0:T(8,128)(2,1)} %all-reduce.3.cloned.1.call-done, bf16[1,32,8,1536]{3,2,1,0:T(8,128)(2,1)S(1)} %copy-done.1, f32[8,1536]{1,0:T(8,128)S(1)} %copy-done.10, f32[8,1536]{1,0:T(8,128)S(1)} %copy-done.11, ...), kind=kOutput, calls=%fused_computation.12 | convolution fusion | flops 1213661184 | bytes 7227392 | tf_op jit(solution)/shard_map/dot_general | solution.py:140
  193.6 0.0 copy-start.12
  193.6 0.0 all-reduce.5.cloned.1.call-update
  193.6 50.5 %all-reduce.5.cloned.1.call-done = bf16[32,8,1536]{2,1,0:T(8,128)(2,1)} async-done(((bf16[32,8,1536]{2,1,0:T(8,128)(2,1)}), bf16[32,8,1536]{2,1,0:T(8,128)(2,1)}) %all-reduce.5.cloned.1.call-update) | async-done | bytes 786448 | tf_op jit(solution)/shard_map/psum | solution.py:139
  244.1 1.2 fusion.114
  245.3 1.3 multiply_reduce_fusion.1
  246.6 1.4 fusion.78
  248.0 0.1 constant_dynamic-slice_fusion
  248.1 0.6 collective-permute-start
  248.7 0.2 select_reduce_fusion
  248.9 4.6 %collective-permute-done = f32[8,8,32]{2,1,0:T(8,128)S(1)} collective-permute-done((f32[8,8,32]{2,1,0:T(8,128)S(1)}, f32[8,8,32]{2,1,0:T(8,128)S(1)}, u32[]{:S(2)}, u32[]{:S(2)}) %collective-permute-start) | collective-permute-done | bytes 8224 | tf_op jit(solution)/shard_map/ppermute | solution.py:16
  253.5 0.7 multiply_add_fusion
  (36 shorter events, 0.2 us)
Async XLA Ops:
  7.2 181.7 %copy-start = (bf16[768,1536]{1,0:T(8,128)(2,1)S(1)}, bf16[768,1536]{1,0:T(8,128)(2,1)}, u32[]{:S(2)}) copy-start(bf16[768,1536]{1,0:T(8,128)(2,1)} %param.24) | copy-start | bytes 7077892
  7.2 1.9 copy-start.1
  19.0 11.1 %copy-start.2 = (bf16[1,5,8,1536]{3,2,1,0:T(8,128)(2,1)S(1)}, bf16[1,5,8,1536]{3,2,1,0:T(8,128)(2,1)}, u32[]{:S(2)}) copy-start(bf16[1,5,8,1536]{3,2,1,0:T(8,128)(2,1)} %param.14) | copy-start | bytes 368644
  20.5 21.4 %all-to-all-start.1 = ((bf16[32,8,384]{2,1,0:T(8,128)(2,1)}), bf16[32,8,384]{2,1,0:T(8,128)(2,1)}, u32[]{:S(2)}, u32[]{:S(2)}) async-start(bf16[32,8,384]{2,1,0:T(8,128)(2,1)} %bitcast.158), calls=%async_computation.1 | async-start | bytes 393216 | tf_op jit(solution)/shard_map/all_to_all | solution.py:104
  30.4 2.2 copy-start.8
  30.4 2.2 copy-start.9
  32.5 0.9 copy-start.3
  42.9 31.8 %all-to-all-start.2 = ((bf16[32,37,384]{2,1,0:T(8,128)(2,1)}), bf16[32,37,384]{2,1,0:T(8,128)(2,1)}, u32[]{:S(2)}, u32[]{:S(2)}) async-start(bf16[32,37,384]{2,1,0:T(8,128)(2,1)} %bitcast.153), calls=%async_computation.2 | async-start | bytes 1966080 | tf_op jit(solution)/shard_map/all_to_all | solution.py:105
  47.5 33.1 %copy-start.15 = (s32[1,8]{1,0:T(1,128)S(1)}, s32[1,8]{1,0:T(1,128)}, u32[]{:S(2)}) copy-start(s32[1,8]{1,0:T(1,128)} %param.16) | copy-start | bytes 100
  75.8 31.8 %all-to-all-start = ((bf16[32,37,384]{2,1,0:T(8,128)(2,1)}), bf16[32,37,384]{2,1,0:T(8,128)(2,1)}, u32[]{:S(2)}, u32[]{:S(2)}) async-start(bf16[32,37,384]{2,1,0:T(8,128)(2,1)} %bitcast.152), calls=%async_computation | async-start | bytes 1966080 | tf_op jit(solution)/shard_map/all_to_all | solution.py:106
  80.4 104.0 %all-reduce.3.cloned.1.call-start = ((), (), s32[]{:S(2)}) async-start(), calls=%async_computation.4 | async-start | bytes 1572864 | tf_op jit(solution)/shard_map/psum | solution.py:131
  119.8 64.6 %copy-start.7 = (f32[8,1536]{1,0:T(8,128)S(1)}, f32[8,1536]{1,0:T(8,128)}, u32[]{:S(2)}) copy-start(f32[8,1536]{1,0:T(8,128)} %get-tuple-element.20) | copy-start | bytes 147460
  138.2 105.9 %all-reduce.5.cloned.1.call-start = ((), (), s32[]{:S(2)}) async-start(), calls=%async_computation.5 | async-start | bytes 1572864 | tf_op jit(solution)/shard_map/psum | solution.py:139
  184.4 4.5 %copy-start.10 = (f32[8,1536]{1,0:T(8,128)S(1)}, f32[8,1536]{1,0:T(8,128)}, u32[]{:S(2)}) copy-start(f32[8,1536]{1,0:T(8,128)} %get-tuple-element.14) | copy-start | bytes 147460
  184.4 4.5 %copy-start.11 = (f32[8,1536]{1,0:T(8,128)S(1)}, f32[8,1536]{1,0:T(8,128)}, u32[]{:S(2)}) copy-start(f32[8,1536]{1,0:T(8,128)} %get-tuple-element.15) | copy-start | bytes 147460
  188.9 4.7 %copy-start.13 = (s32[8]{0:T(128)S(1)}, s32[8]{0:T(128)}, u32[]{:S(2)}) copy-start(s32[8]{0:T(128)} %param.17) | copy-start | bytes 100
  193.5 53.1 %copy-start.4 = (bf16[1536,64]{0,1:T(8,128)(2,1)S(1)}, bf16[1536,64]{0,1:T(8,128)(2,1)}, u32[]{:S(2)}) copy-start(bf16[1536,64]{0,1:T(8,128)(2,1)} %param.25) | copy-start | bytes 589828
  193.5 53.1 %copy-start.5 = (f32[8,1536]{1,0:T(8,128)S(1)}, f32[8,1536]{1,0:T(8,128)}, u32[]{:S(2)}) copy-start(f32[8,1536]{1,0:T(8,128)} %get-tuple-element.12) | copy-start | bytes 147460
  193.5 53.1 %copy-start.6 = (f32[8,1536]{1,0:T(8,128)S(1)}, f32[8,1536]{1,0:T(8,128)}, u32[]{:S(2)}) copy-start(f32[8,1536]{1,0:T(8,128)} %get-tuple-element.13) | copy-start | bytes 147460
  193.5 55.1 %copy-start.14 = (f32[9]{0:T(128)S(1)}, f32[9]{0:T(128)}, u32[]{:S(2)}) copy-start(f32[9]{0:T(128)} %param.18) | copy-start | bytes 112
  193.6 60.0 %copy-start.12 = (f32[8,8,32]{2,1,0:T(8,128)S(1)}, f32[8,8,32]{2,1,0:T(8,128)}, u32[]{:S(2)}) copy-start(f32[8,8,32]{2,1,0:T(8,128)} %param.19) | copy-start | bytes 24580
  248.1 5.5 %collective-permute-start = (f32[8,8,32]{2,1,0:T(8,128)S(1)}, f32[8,8,32]{2,1,0:T(8,128)S(1)}, u32[]{:S(2)}, u32[]{:S(2)}) collective-permute-start(f32[8,8,32]{2,1,0:T(8,128)S(1)} %constant_dynamic-slice_fusion), channel_id=1, source_target_pairs={{0,128},{128,0},{1,129},{129,1},{2,130},{130,2},{3,131},{131,3},{4... | collective-permute-start | bytes 24584 | tf_op jit(solution)/shard_map/ppermute | solution.py:16
Sparse Core Ops, SparseCore 0:
  138.3 46.0 all-reduce.2
  193.7 50.3 all-reduce.4
where the time goes:
time: 262 us; the launch traced here: 261 us
  waiting for transfers between devices  150 us (57%)
  local copies, waits for them, and re-layouts  26.1 us (10%)
  matrix products  22.5 us (9%)
  starting transfers between devices  19.7 us (8%)
  blocking collectives  15.6 us (6%)
  between operations  14.4 us (5%)
  other arithmetic  12.6 us (5%)
    psum x1, waiting for transfers between devices, shards(): lax.psum(jnp.dot(hidden, w_down, preferred_element_type=jnp.float32).asty...  50.5 us
    psum x1, waiting for transfers between devices, shards(): lax.psum(jnp.dot(attn_rows, w_out, preferred_element_type=jnp.float32).as...  46.2 us
    all_to_all x1, waiting for transfers between devices, shards(): lax.all_to_all(key_send, 'seq', split_axis=0, concat_axis=0, tiled=True)  26.2 us
    all_to_all x1, blocking collectives, shards(): lax.all_to_all(answer.reshape(senders, query_share, features), 'seq', spl...  15.6 us
    all_to_all x1, waiting for transfers between devices, shards(): lax.all_to_all(value_send, 'seq', split_axis=0, concat_axis=0, tiled=True)  15.1 us
    another operation x3, local copies, waits for them, and re-layouts  10.1 us
    all_to_all x1, starting transfers between devices, shards(): lax.all_to_all(query_send, 'seq', split_axis=0, concat_axis=0, tiled=True)  9.6 us
    unnamed x34, local copies, waits for them, and re-layouts  8.6 us
  transfers between devices with their start and end apart: 6, of which 6 were waited for; matrix products, arithmetic and copies ran while one was open for 6% of the time, Pallas kernels for 0%

commit v1 on v0

--- a/solution.py
+++ b/solution.py
@@ -39,6 +39,12 @@
     weights = (exp_scores / jnp.sum(exp_scores, -1, keepdims=True)).astype(jnp.bfloat16)
     result = jnp.einsum("rhqk,krhd->qrhd", weights, value_heads, preferred_element_type=jnp.float32)
     return result.astype(jnp.bfloat16).reshape(queries.shape)
+
+
+def reduce_rows(partial, parties):
+    pieces = partial.reshape(parties, partial.shape[0] // parties, partial.shape[1])
+    got = lax.all_to_all(pieces, "tp", split_axis=0, concat_axis=0, tiled=True)
+    return jnp.sum(got.astype(jnp.float32), 0)
 
 
 def spread(image_part, text_part, members):
@@ -128,20 +134,19 @@
         .reshape(rows_all, features)
     )
     tp_index = lax.axis_index("tp")
-    attn_mixed = lax.psum(
-        jnp.dot(attn_rows, w_out, preferred_element_type=jnp.float32).astype(jnp.bfloat16), "tp"
-    ).astype(jnp.float32)
-    after_attn = resident + adaptive[:, 2] * attn_mixed.reshape(img_slice, requests, model_width)
-    mlp_in = modulate(after_attn, adaptive[:, 3], adaptive[:, 4]).reshape(rows_all, model_width)
+    resident_mine = lax.dynamic_slice_in_dim(resident, tp_index * portion, portion, 0)
+    attn_part = jnp.dot(attn_rows, w_out, preferred_element_type=jnp.float32).astype(jnp.bfloat16)
+    attn_mixed = reduce_rows(attn_part, parties).reshape(portion, requests, model_width)
+    after_attn = resident_mine + adaptive[:, 2] * attn_mixed
+    mlp_mine = modulate(after_attn, adaptive[:, 3], adaptive[:, 4])
+    mlp_in = lax.all_gather(mlp_mine, "tp", axis=0, tiled=True).reshape(rows_all, model_width)
     hidden = jax.nn.gelu(
         jnp.dot(mlp_in, w_up, preferred_element_type=jnp.float32), approximate=True
     ).astype(jnp.bfloat16)
-    mlp_grown = lax.psum(
-        jnp.dot(hidden, w_down, preferred_element_type=jnp.float32).astype(jnp.bfloat16), "tp"
-    ).astype(jnp.float32)
-    after_mlp = after_attn + adaptive[:, 5] * mlp_grown.reshape(img_slice, requests, model_width)
-    rows_mine = lax.dynamic_slice_in_dim(after_mlp, tp_index * portion, portion, 0)
-    head_in = modulate(rows_mine, adaptive[:, 8], adaptive[:, 9]).reshape(
+    mlp_part = jnp.dot(hidden, w_down, preferred_element_type=jnp.float32).astype(jnp.bfloat16)
+    mlp_grown = reduce_rows(mlp_part, parties).reshape(portion, requests, model_width)
+    after_mlp = after_attn + adaptive[:, 5] * mlp_grown
+    head_in = modulate(after_mlp, adaptive[:, 8], adaptive[:, 9]).reshape(
         portion * requests, model_width
     )
     velocity_own = jnp.dot(head_in, w_final, preferred_element_type=jnp.float32).reshape(

time: 262 us -> 193 us (0.74)
  waiting for transfers between devices: 150 us -> 72.7 us
  blocking collectives: 15.6 us -> 29.5 us
  between operations: 14.4 us -> 0.94 us
  starting transfers between devices: 19.7 us -> 28.9 us
    psum x2 -> x0, waiting for transfers between devices: 96.6 us -> none  [the longest x1 50.5 us: shards(): lax.psum(jnp.dot(hidden, w_down, preferred_element_type=jnp.float32).asty...]
    all_to_all x0 -> x2, waiting for transfers between devices: none -> 19.3 us  [reduce_rows(): got = lax.all_to_all(pieces, 'tp', split_axis=0, concat_axis=0, tiled=True)]
    all_gather x0 -> x1, blocking collectives: none -> 14.1 us  [shards(): lax.all_gather(mlp_mine, 'tp', axis=0, tiled=True)]
    all_to_all x0 -> x2, starting transfers between devices: none -> 8.91 us  [reduce_rows(): got = lax.all_to_all(pieces, 'tp', split_axis=0, concat_axis=0, tiled=True)]
  transfers between devices with their start and end apart: 6 -> 6, of which waited for: 6 -> 6; matrix products, arithmetic and copies ran while one was open for 6% -> 9% of each run, Pallas kernels for 0% -> 0%
where the time goes in v1:
time: 193 us; the launch traced here: 192 us
  waiting for transfers between devices  72.7 us (38%)
  blocking collectives  29.5 us (15%)
  starting transfers between devices  28.9 us (15%)
  local copies, waits for them, and re-layouts  25.9 us (13%)
  matrix products  21.4 us (11%)
  other arithmetic  12.6 us (7%)
    all_to_all x1, waiting for transfers between devices, shards(): lax.all_to_all(key_send, 'seq', split_axis=0, concat_axis=0, tiled=True)  26.2 us
    all_to_all x2, waiting for transfers between devices, reduce_rows(): got = lax.all_to_all(pieces, 'tp', split_axis=0, concat_axis=0, tiled=True)  19.3 us
    all_to_all x1, blocking collectives, shards(): lax.all_to_all(answer.reshape(senders, query_share, features), 'seq', spl...  15.4 us
    all_to_all x1, waiting for transfers between devices, shards(): lax.all_to_all(value_send, 'seq', split_axis=0, concat_axis=0, tiled=True)  15.2 us
    all_gather x1, blocking collectives, shards(): lax.all_gather(mlp_mine, 'tp', axis=0, tiled=True)  14.1 us
    another operation x3, local copies, waits for them, and re-layouts  10.1 us
    all_to_all x1, starting transfers between devices, shards(): lax.all_to_all(query_send, 'seq', split_axis=0, concat_axis=0, tiled=True)  9.6 us
    all_to_all x2, starting transfers between devices, reduce_rows(): got = lax.all_to_all(pieces, 'tp', split_axis=0, concat_axis=0, tiled=True)  8.91 us
  transfers between devices with their start and end apart: 6, of which 6 were waited for; matrix products, arithmetic and copies ran while one was open for 9% of the time, Pallas kernels for 0%

profile of v1, /device:TPU:4, one launch (start us, length us, event | category | flops | bytes accessed | tf_op | source)
XLA Modules:
  0.0 192.0 jit_solution(13063402290482550401)
XLA Ops:
  0.6 0.0 copy-start
  0.6 0.0 copy-start.1
  0.7 1.1 bitcast_convert_fusion
  1.8 0.7 fusion.79
  2.5 1.3 convert_reduce_fusion.2
  3.9 0.0 copy-done.1
  3.9 0.3 multiply_reduce_fusion
  4.2 6.1 %copy.35 = bf16[1536,3,384]{0,2,1:T(8,128)(2,1)} copy(bf16[1536,3,384]{2,0,1:T(8,128)(2,1)} %param.20) | data formatting | bytes 7077888 | tf_op args[7]
  10.3 3.3 %convolution_convert_fusion.1 = bf16[256,1152]{1,0:T(8,128)(2,1)S(1)} fusion(bf16[1536,1152]{0,1:T(8,128)(2,1)} %bitcast.124, bf16[1,32,8,1536]{3,2,1,0:T(8,128)(2,1)S(1)} %copy-done.1, f32[8,1536]{1,0:T(8,128)S(1)} %get-tuple-element.20, f32[8,1536]{1,0:T(8,128)S(1)} %get-tuple-element.21, f32[32,8]{1,0:T(8,128)S(1)} %add_rsqrt_fusion, ...), kind=kOutput, calls=%fused_computation.10 | convolution fusion | flops 908623872 | bytes 5015552 | tf_op jit(solution)/shard_map/dot_general | solution.py:84
  13.7 0.7 slice_bitcast_fusion.1
  14.4 0.7 copy.37
  15.1 9.6 %all-to-all-start.1 = ((bf16[32,8,384]{2,1,0:T(8,128)(2,1)}), bf16[32,8,384]{2,1,0:T(8,128)(2,1)}, u32[]{:S(2)}, u32[]{:S(2)}) async-start(bf16[32,8,384]{2,1,0:T(8,128)(2,1)} %bitcast.130), calls=%async_computation.1 | async-start | bytes 393216 | tf_op jit(solution)/shard_map/all_to_all | solution.py:110
  24.7 0.1 convert_reduce_fusion.3
  24.8 0.2 fusion.55
  25.0 2.1 %copy.44 = bf16[192,8,2,384]{3,1,2,0:T(8,128)(2,1)S(1)} copy(bf16[192,8,2,384]{3,2,1,0:T(2,128)(2,1)} %bitcast.126) | data formatting | bytes 4718592
  27.2 0.6 convolution_convert_fusion.3
  27.8 0.3 copy-done.3
  28.1 0.8 maximum_bitcast_fusion
  28.9 7.6 %all-to-all-done.1 = bf16[32,8,384]{2,1,0:T(8,128)(2,1)} async-done(((bf16[32,8,384]{2,1,0:T(8,128)(2,1)}), bf16[32,8,384]{2,1,0:T(8,128)(2,1)}, u32[]{:S(2)}, u32[]{:S(2)}) %all-to-all-start.1) | async-done | bytes 196640 | tf_op jit(solution)/shard_map/all_to_all | solution.py:110
  36.5 1.0 broadcast_in_dim.35
  37.5 4.8 %all-to-all-start.2 = ((bf16[32,37,384]{2,1,0:T(8,128)(2,1)}), bf16[32,37,384]{2,1,0:T(8,128)(2,1)}, u32[]{:S(2)}, u32[]{:S(2)}) async-start(bf16[32,37,384]{2,1,0:T(8,128)(2,1)} %bitcast.123), calls=%async_computation.2 | async-start | bytes 1966080 | tf_op jit(solution)/shard_map/all_to_all | solution.py:111
  42.3 1.0 copy.36
  43.3 26.2 %all-to-all-done.2 = bf16[32,37,384]{2,1,0:T(8,128)(2,1)} async-done(((bf16[32,37,384]{2,1,0:T(8,128)(2,1)}), bf16[32,37,384]{2,1,0:T(8,128)(2,1)}, u32[]{:S(2)}, u32[]{:S(2)}) %all-to-all-start.2) | async-done | bytes 909344 | tf_op jit(solution)/shard_map/all_to_all | solution.py:111
  69.5 1.1 broadcast_in_dim.32
  70.5 4.8 %all-to-all-start = ((bf16[32,37,384]{2,1,0:T(8,128)(2,1)}), bf16[32,37,384]{2,1,0:T(8,128)(2,1)}, u32[]{:S(2)}, u32[]{:S(2)}) async-start(bf16[32,37,384]{2,1,0:T(8,128)(2,1)} %bitcast.122), calls=%async_computation | async-start | bytes 1966080 | tf_op jit(solution)/shard_map/all_to_all | solution.py:112
  75.4 0.0 copy-done.15
  75.4 0.6 fusion.84
  76.0 0.7 fusion.83
  76.8 0.1 or.17
  76.9 2.0 %reshape.376 = bf16[256,6,64]{2,1,0:T(8,128)(2,1)} reshape(bf16[32,8,384]{2,1,0:T(8,128)(2,1)} %all-to-all-done.1) | data formatting | bytes 393216 | tf_op jit(solution)/shard_map/reshape.1
  78.9 4.0 %reshape.380 = bf16[1184,6,64]{2,1,0:T(8,128)(2,1)} reshape(bf16[32,37,384]{2,1,0:T(8,128)(2,1)} %all-to-all-done.2) | data formatting | bytes 1818624 | tf_op jit(solution)/shard_map/reshape.2
  82.9 4.2 %fusion.99 = f32[6,256]{1,0:T(8,128)S(1)} fusion(pred[1184]{0:T(1024)(128)(4,1)S(1)} %or.17, bf16[1184,6,64]{2,1,0:T(8,128)(2,1)} %reshape.380, bf16[256,6,64]{2,1,0:T(8,128)(2,1)} %reshape.376), kind=kOutput, calls=%fused_computation.127 | convolution fusion | flops 240059552 | bytes 1113248 | tf_op jit(solution)/shard_map/sub | solution.py:38
  87.2 15.2 %all-to-all-done = bf16[32,37,384]{2,1,0:T(8,128)(2,1)} async-done(((bf16[32,37,384]{2,1,0:T(8,128)(2,1)}), bf16[32,37,384]{2,1,0:T(8,128)(2,1)}, u32[]{:S(2)}, u32[]{:S(2)}) %all-to-all-start) | async-done | bytes 909344 | tf_op jit(solution)/shard_map/all_to_all | solution.py:112
  102.3 4.0 %reshape.374 = bf16[1184,6,64]{2,1,0:T(8,128)(2,1)} reshape(bf16[32,37,384]{2,1,0:T(8,128)(2,1)} %all-to-all-done) | data formatting | bytes 1818624 | tf_op jit(solution)/shard_map/reshape.6
  106.4 5.7 %fusion.12 = bf16[256,1,6,64]{0,3,2,1:T(8,128)(2,1)S(1)} fusion(f32[6,256]{1,0:T(8,128)S(1)} %fusion.99, bf16[1184,6,64]{2,1,0:T(8,128)(2,1)} %reshape.374, pred[1184]{0:T(1024)(128)(4,1)S(1)} %or.17, bf16[1184,6,64]{2,1,0:T(8,128)(2,1)} %reshape.380, bf16[256,6,64]{2,1,0:T(8,128)(2,1)} %reshape.376), kind=kOutput, calls=%fused_computation.23 | convolution fusion | flops 474761888 | bytes 2219168 | tf_op jit(solution)/shard_map/rhqk,krhd->qrhd/dot_general | solution.py:40
  112.1 1.1 copy.42
  113.2 1.4 reshape_reshape.10
  114.6 15.4 %all_to_all.30 = bf16[32,8,384]{2,1,0:T(8,128)(2,1)S(1)} all-to-all(bf16[32,8,384]{2,1,0:T(8,128)(2,1)S(1)} %reshape_reshape.10), channel_id=1, replica_groups=mesh['cfg'=2,'seq'=32,'tp'=4] {'seq'}, dimensions={0} | all-to-all | bytes 393216 | tf_op jit(solution)/shard_map/all_to_all | solution.py:124
  130.0 0.1 copy.43
  130.1 2.7 %convolution_convert_fusion.2 = bf16[256,1536]{1,0:T(8,128)(2,1)} fusion(bf16[256,384]{1,0:T(8,128)(2,1)S(1)} %bitcast.128, bf16[384,1536]{1,0:T(8,128)(2,1)} %param.22), kind=kOutput, calls=%fused_computation.11 | convolution fusion | flops 302383104 | bytes 2162688 | tf_op jit(solution)/shard_map/dot_general | solution.py:138
  132.8 4.6 %all-to-all-start.4 = ((bf16[4,64,1536]{2,1,0:T(8,128)(2,1)}), bf16[4,64,1536]{2,1,0:T(8,128)(2,1)}, u32[]{:S(2)}, u32[]{:S(2)}) async-start(bf16[4,64,1536]{2,1,0:T(8,128)(2,1)} %bitcast.125), calls=%async_computation.4 | async-start | bytes 1572864 | tf_op jit(solution)/shard_map/all_to_all | solution.py:46
  137.4 1.3 convert_element_type.100
  138.8 9.8 %all-to-all-done.4 = bf16[4,64,1536]{2,1,0:T(8,128)(2,1)} async-done(((bf16[4,64,1536]{2,1,0:T(8,128)(2,1)}), bf16[4,64,1536]{2,1,0:T(8,128)(2,1)}, u32[]{:S(2)}, u32[]{:S(2)}) %all-to-all-start.4) | async-done | bytes 786464 | tf_op jit(solution)/shard_map/all_to_all | solution.py:46
  148.6 1.3 convert_reduce_fusion.1
  149.9 0.0 copy-done.4
  149.9 1.1 fusion.97
  151.0 0.2 multiply_reduce_fusion.2
  151.2 0.0 copy-done.8
  151.2 0.1 add_convert_fusion.2
  151.4 14.1 %all_gather.3 = bf16[32,8,1536]{2,1,0:T(8,128)(2,1)} all-gather(bf16[8,8,1536]{2,1,0:T(8,128)(2,1)S(1)} %add_convert_fusion.2), channel_id=1, replica_groups=mesh['cfg'=2,'seq'=32,'tp'=4] {'tp'}, dimensions={0}, use_global_device_ids=true | all-gather | bytes 983040 | tf_op jit(solution)/shard_map/all_gather | solution.py:142
  165.4 4.5 %convolution_convert_fusion = bf16[256,1536]{1,0:T(8,128)(2,1)} fusion(bf16[768,1536]{1,0:T(8,128)(2,1)S(1)} %copy-done, bf16[1536,768]{1,0:T(8,128)(2,1)} %param.23, bf16[32,8,1536]{2,1,0:T(8,128)(2,1)} %all_gather.3), kind=kOutput, calls=%fused_computation.9 | convolution fusion | flops 1210122240 | bytes 6291456 | tf_op jit(solution)/shard_map/dot_general | solution.py:146
  170.0 0.0 copy-start.12
  170.0 4.3 %all-to-all-start.5 = ((bf16[4,64,1536]{2,1,0:T(8,128)(2,1)}), bf16[4,64,1536]{2,1,0:T(8,128)(2,1)}, u32[]{:S(2)}, u32[]{:S(2)}) async-start(bf16[4,64,1536]{2,1,0:T(8,128)(2,1)} %bitcast.129), calls=%async_computation.5 | async-start | bytes 1572864 | tf_op jit(solution)/shard_map/all_to_all | solution.py:46
  174.4 9.5 %all-to-all-done.5 = bf16[4,64,1536]{2,1,0:T(8,128)(2,1)} async-done(((bf16[4,64,1536]{2,1,0:T(8,128)(2,1)}), bf16[4,64,1536]{2,1,0:T(8,128)(2,1)}, u32[]{:S(2)}, u32[]{:S(2)}) %all-to-all-start.5) | async-done | bytes 786464 | tf_op jit(solution)/shard_map/all_to_all | solution.py:46
  183.9 1.3 convert_reduce_fusion
  185.2 0.1 fusion.95
  185.3 0.2 multiply_reduce_fusion.1
  185.5 0.0 copy-done.6
  185.5 0.3 fusion.59
  185.8 0.1 constant_dynamic-slice_fusion
  185.9 0.8 collective-permute-start
  186.7 0.2 select_reduce_fusion
  186.9 4.4 %collective-permute-done = f32[8,8,32]{2,1,0:T(8,128)S(1)} collective-permute-done((f32[8,8,32]{2,1,0:T(8,128)S(1)}, f32[8,8,32]{2,1,0:T(8,128)S(1)}, u32[]{:S(2)}, u32[]{:S(2)}) %collective-permute-start) | collective-permute-done | bytes 8224 | tf_op jit(solution)/shard_map/ppermute | solution.py:16
  191.3 0.7 multiply_add_fusion
  (37 shorter events, 0.2 us)
Async XLA Ops:
  0.6 164.8 %copy-start = (bf16[768,1536]{1,0:T(8,128)(2,1)S(1)}, bf16[768,1536]{1,0:T(8,128)(2,1)}, u32[]{:S(2)}) copy-start(bf16[768,1536]{1,0:T(8,128)(2,1)} %param.24) | copy-start | bytes 7077892
  0.6 3.2 %copy-start.1 = (bf16[1,32,8,1536]{3,2,1,0:T(8,128)(2,1)S(1)}, bf16[1,32,8,1536]{3,2,1,0:T(8,128)(2,1)}, u32[]{:S(2)}) copy-start(bf16[1,32,8,1536]{3,2,1,0:T(8,128)(2,1)} %param.13) | copy-start | bytes 2359300
  10.3 14.4 %copy-start.2 = (bf16[1,5,8,1536]{3,2,1,0:T(8,128)(2,1)S(1)}, bf16[1,5,8,1536]{3,2,1,0:T(8,128)(2,1)}, u32[]{:S(2)}) copy-start(bf16[1,5,8,1536]{3,2,1,0:T(8,128)(2,1)} %param.14) | copy-start | bytes 368644
  15.1 21.4 %all-to-all-start.1 = ((bf16[32,8,384]{2,1,0:T(8,128)(2,1)}), bf16[32,8,384]{2,1,0:T(8,128)(2,1)}, u32[]{:S(2)}, u32[]{:S(2)}) async-start(bf16[32,8,384]{2,1,0:T(8,128)(2,1)} %bitcast.130), calls=%async_computation.1 | async-start | bytes 393216 | tf_op jit(solution)/shard_map/all_to_all | solution.py:110
  25.0 2.2 %copy-start.10 = (f32[8,1536]{1,0:T(8,128)S(1)}, f32[8,1536]{1,0:T(8,128)}, u32[]{:S(2)}) copy-start(f32[8,1536]{1,0:T(8,128)} %get-tuple-element.18) | copy-start | bytes 147460
  25.0 2.2 %copy-start.11 = (f32[8,1536]{1,0:T(8,128)S(1)}, f32[8,1536]{1,0:T(8,128)}, u32[]{:S(2)}) copy-start(f32[8,1536]{1,0:T(8,128)} %get-tuple-element.19) | copy-start | bytes 147460
  27.2 0.9 copy-start.3
  37.5 37.9 %copy-start.15 = (s32[1,8]{1,0:T(1,128)S(1)}, s32[1,8]{1,0:T(1,128)}, u32[]{:S(2)}) copy-start(s32[1,8]{1,0:T(1,128)} %param.16) | copy-start | bytes 100
  37.5 31.9 %all-to-all-start.2 = ((bf16[32,37,384]{2,1,0:T(8,128)(2,1)}), bf16[32,37,384]{2,1,0:T(8,128)(2,1)}, u32[]{:S(2)}, u32[]{:S(2)}) async-start(bf16[32,37,384]{2,1,0:T(8,128)(2,1)} %bitcast.123), calls=%async_computation.2 | async-start | bytes 1966080 | tf_op jit(solution)/shard_map/all_to_all | solution.py:111
  70.5 31.8 %all-to-all-start = ((bf16[32,37,384]{2,1,0:T(8,128)(2,1)}), bf16[32,37,384]{2,1,0:T(8,128)(2,1)}, u32[]{:S(2)}, u32[]{:S(2)}) async-start(bf16[32,37,384]{2,1,0:T(8,128)(2,1)} %bitcast.122), calls=%async_computation | async-start | bytes 1966080 | tf_op jit(solution)/shard_map/all_to_all | solution.py:112
  132.8 17.0 %copy-start.4 = (f32[8,1536]{1,0:T(8,128)S(1)}, f32[8,1536]{1,0:T(8,128)}, u32[]{:S(2)}) copy-start(f32[8,1536]{1,0:T(8,128)} %get-tuple-element.22) | copy-start | bytes 147460
  132.8 15.7 %all-to-all-start.4 = ((bf16[4,64,1536]{2,1,0:T(8,128)(2,1)}), bf16[4,64,1536]{2,1,0:T(8,128)(2,1)}, u32[]{:S(2)}, u32[]{:S(2)}) async-start(bf16[4,64,1536]{2,1,0:T(8,128)(2,1)} %bitcast.125), calls=%async_computation.4 | async-start | bytes 1572864 | tf_op jit(solution)/shard_map/all_to_all | solution.py:46
  137.4 13.8 %copy-start.8 = (f32[8,1536]{1,0:T(8,128)S(1)}, f32[8,1536]{1,0:T(8,128)}, u32[]{:S(2)}) copy-start(f32[8,1536]{1,0:T(8,128)} %get-tuple-element.15) | copy-start | bytes 147460
  137.4 13.8 %copy-start.9 = (f32[8,1536]{1,0:T(8,128)S(1)}, f32[8,1536]{1,0:T(8,128)}, u32[]{:S(2)}) copy-start(f32[8,1536]{1,0:T(8,128)} %get-tuple-element.16) | copy-start | bytes 147460
  165.4 8.9 %copy-start.13 = (s32[8]{0:T(128)S(1)}, s32[8]{0:T(128)}, u32[]{:S(2)}) copy-start(s32[8]{0:T(128)} %param.17) | copy-start | bytes 100
  170.0 15.5 %copy-start.5 = (bf16[1536,64]{0,1:T(8,128)(2,1)S(1)}, bf16[1536,64]{0,1:T(8,128)(2,1)}, u32[]{:S(2)}) copy-start(bf16[1536,64]{0,1:T(8,128)(2,1)} %param.25) | copy-start | bytes 589828
  170.0 15.5 %copy-start.6 = (f32[8,1536]{1,0:T(8,128)S(1)}, f32[8,1536]{1,0:T(8,128)}, u32[]{:S(2)}) copy-start(f32[8,1536]{1,0:T(8,128)} %get-tuple-element.13) | copy-start | bytes 147460
  170.0 15.5 %copy-start.7 = (f32[8,1536]{1,0:T(8,128)S(1)}, f32[8,1536]{1,0:T(8,128)}, u32[]{:S(2)}) copy-start(f32[8,1536]{1,0:T(8,128)} %get-tuple-element.14) | copy-start | bytes 147460
  170.0 16.7 %copy-start.14 = (f32[9]{0:T(128)S(1)}, f32[9]{0:T(128)}, u32[]{:S(2)}) copy-start(f32[9]{0:T(128)} %param.18) | copy-start | bytes 112
  170.0 21.3 %copy-start.12 = (f32[8,8,32]{2,1,0:T(8,128)S(1)}, f32[8,8,32]{2,1,0:T(8,128)}, u32[]{:S(2)}) copy-start(f32[8,8,32]{2,1,0:T(8,128)} %param.19) | copy-start | bytes 24580
  170.0 13.9 %all-to-all-start.5 = ((bf16[4,64,1536]{2,1,0:T(8,128)(2,1)}), bf16[4,64,1536]{2,1,0:T(8,128)(2,1)}, u32[]{:S(2)}, u32[]{:S(2)}) async-start(bf16[4,64,1536]{2,1,0:T(8,128)(2,1)} %bitcast.129), calls=%async_computation.5 | async-start | bytes 1572864 | tf_op jit(solution)/shard_map/all_to_all | solution.py:46
  185.9 5.5 %collective-permute-start = (f32[8,8,32]{2,1,0:T(8,128)S(1)}, f32[8,8,32]{2,1,0:T(8,128)S(1)}, u32[]{:S(2)}, u32[]{:S(2)}) collective-permute-start(f32[8,8,32]{2,1,0:T(8,128)S(1)} %constant_dynamic-slice_fusion), channel_id=1, source_target_pairs={{0,128},{128,0},{1,129},{129,1},{2,130},{130,2},{3,131},{131,3},{4... | collective-permute-start | bytes 24584 | tf_op jit(solution)/shard_map/ppermute | solution.py:16

commit v2 on v1

--- a/solution.py
+++ b/solution.py
@@ -97,40 +97,46 @@
     vals_txt = text_kv[:, features:].reshape(txt_slice, requests, features)
     key_span = img_slice + txt_slice
     within = jnp.arange(key_span)
-    query_share = img_slice // members
     senders = requests * members
+    halves = members // 2
+    query_share = img_slice // halves
+    head_share = features // 2
     query_send = (
-        queries.reshape(members, query_share, requests, features)
-        .transpose(2, 0, 1, 3)
-        .reshape(senders, query_share, features)
-    )
-    key_send = spread(keys_img, keys_txt, members)
-    value_send = spread(vals_img, vals_txt, members)
-    query_got, key_got, value_got = (
-        lax.all_to_all(query_send, "seq", split_axis=0, concat_axis=0, tiled=True),
-        lax.all_to_all(key_send, "seq", split_axis=0, concat_axis=0, tiled=True),
-        lax.all_to_all(value_send, "seq", split_axis=0, concat_axis=0, tiled=True),
-    )
+        queries.reshape(halves, query_share, requests, 2, head_share)
+        .transpose(2, 0, 3, 1, 4)
+        .reshape(senders, query_share, head_share)
+    )
+    joined_k = jnp.concatenate([keys_img, keys_txt], 0).reshape(key_span, requests, 2, head_share)
+    joined_v = jnp.concatenate([vals_img, vals_txt], 0).reshape(key_span, requests, 2, head_share)
+    both = jnp.concatenate([joined_k, joined_v], 0).transpose(1, 2, 0, 3)
+    kv_send = jnp.broadcast_to(
+        both[:, None], (requests, halves, 2, 2 * key_span, head_share)
+    ).reshape(senders, 2 * key_span, head_share)
+    payload = jnp.concatenate([query_send, kv_send], 1)
+    got = lax.all_to_all(payload, "seq", split_axis=0, concat_axis=0, tiled=True)
+    query_got = got[:, :query_share]
+    key_got = got[:, query_share : query_share + key_span]
+    value_got = got[:, query_share + key_span :]
     my_request = lax.axis_index("seq") // members
     length_now = jnp.sum(jnp.where(jnp.arange(requests) == my_request, lengths_all, 0))
     text_slot = jnp.arange(senders)[:, None] * txt_slice + within[None, :] - img_slice
     key_valid = (within[None, :] < img_slice) | (text_slot < length_now)
     answer = attend(
-        query_got.reshape(senders * query_share, 1, features),
-        key_got.reshape(senders * key_span, 1, features),
-        value_got.reshape(senders * key_span, 1, features),
+        query_got.reshape(senders * query_share, 1, head_share),
+        key_got.reshape(senders * key_span, 1, head_share),
+        value_got.reshape(senders * key_span, 1, head_share),
         key_valid.reshape(1, senders * key_span),
     )
     answer_back = lax.all_to_all(
-        answer.reshape(senders, query_share, features),
+        answer.reshape(senders, query_share, head_share),
         "seq",
         split_axis=0,
         concat_axis=0,
         tiled=True,
     )
     attn_rows = (
-        answer_back.reshape(requests, members, query_share, features)
-        .transpose(1, 2, 0, 3)
+        answer_back.reshape(requests, halves, 2, query_share, head_share)
+        .transpose(1, 3, 0, 2, 4)
         .reshape(rows_all, features)
     )
     tp_index = lax.axis_index("tp")

time: 193 us -> 179 us (0.927)
  waiting for transfers between devices: 72.7 us -> 60.5 us
  starting transfers between devices: 28.9 us -> 18.7 us
  local copies, waits for them, and re-layouts: 25.9 us -> 34.2 us
    all_to_all x3 -> x1, waiting for transfers between devices: 49 us -> 36.8 us  [shards(): lax.all_to_all(payload, 'seq', split_axis=0, concat_axis=0, tiled=True)]
    all_to_all x3 -> x1, starting transfers between devices: 19.2 us -> 9.91 us  [shards(): lax.all_to_all(payload, 'seq', split_axis=0, concat_axis=0, tiled=True)]
    concatenate x0 -> x4, local copies, waits for them, and re-layouts: none -> 5.1 us  [the longest x2 3.27 us: shards(): jnp.concatenate([keys_img, keys_txt], 0)]
    slice x0 -> x4, local copies, waits for them, and re-layouts: none -> 5.07 us  [the longest x1 2.66 us: shards(): value_got = got[:, query_share + key_span:]]
    all_to_all x1, blocking collectives: 15.4 us -> 17.5 us  [shards(): lax.all_to_all(answer.reshape(senders, query_share, head_share), 'seq', s...]
    another operation x5 -> x6, local copies, waits for them, and re-layouts: 12.2 us -> 10.4 us
    unnamed x34 -> x26, local copies, waits for them, and re-layouts: 8.59 us -> 8.49 us
  transfers between devices with their start and end apart: 6 -> 4, of which waited for: 6 -> 4; matrix products, arithmetic and copies ran while one was open for 9% -> 2% of each run, Pallas kernels for 0% -> 0%
where the time goes in v2:
time: 179 us; the launch traced here: 178 us
  waiting for transfers between devices  60.5 us (34%)
  local copies, waits for them, and re-layouts  34.2 us (19%)
  blocking collectives  30.8 us (17%)
  matrix products  20 us (11%)
  starting transfers between devices  18.7 us (10%)
  other arithmetic  12.6 us (7%)
    all_to_all x1, waiting for transfers between devices, shards(): lax.all_to_all(payload, 'seq', split_axis=0, concat_axis=0, tiled=True)  36.8 us
    all_to_all x2, waiting for transfers between devices, reduce_rows(): got = lax.all_to_all(pieces, 'tp', split_axis=0, concat_axis=0, tiled=True)  19.3 us
    all_to_all x1, blocking collectives, shards(): lax.all_to_all(answer.reshape(senders, query_share, head_share), 'seq', s...  17.5 us
    all_gather x1, blocking collectives, shards(): lax.all_gather(mlp_mine, 'tp', axis=0, tiled=True)  13.3 us
    all_to_all x1, starting transfers between devices, shards(): lax.all_to_all(payload, 'seq', split_axis=0, concat_axis=0, tiled=True)  9.91 us
    unnamed x26, local copies, waits for them, and re-layouts  8.49 us
    all_to_all x2, starting transfers between devices, reduce_rows(): got = lax.all_to_all(pieces, 'tp', split_axis=0, concat_axis=0, tiled=True)  7.95 us
    another operation x3, local copies, waits for them, and re-layouts  7.73 us
  transfers between devices with their start and end apart: 4, of which 4 were waited for; matrix products, arithmetic and copies ran while one was open for 2% of the time, Pallas kernels for 0%

profile of v2, /device:TPU:4, one launch (start us, length us, event | category | flops | bytes accessed | tf_op | source)
XLA Modules:
  0.0 177.7 jit_solution(765277360057450457)
XLA Ops:
  0.6 0.0 copy-start
  0.7 2.3 %copy.40 = bf16[192,8,2,384]{3,1,2,0:T(8,128)(2,1)S(1)} copy(bf16[192,8,2,384]{3,2,1,0:T(2,128)(2,1)} %bitcast.113) | data formatting | bytes 4718592
  3.0 0.7 fusion.73
  3.7 0.1 convert_reduce_fusion.3
  3.8 0.2 fusion.49
  4.0 0.6 convolution_convert_fusion.3
  4.6 0.6 fusion.95
  5.2 0.7 concatenate.22
  5.9 6.1 %copy.32 = bf16[1536,3,384]{0,2,1:T(8,128)(2,1)} copy(bf16[1536,3,384]{2,0,1:T(8,128)(2,1)} %param.20) | data formatting | bytes 7077888 | tf_op args[7]
  12.1 0.2 convert_reduce_fusion.2
  12.2 0.3 multiply_reduce_fusion
  12.6 3.3 %convolution_convert_fusion.1 = bf16[256,1152]{1,0:T(8,128)(2,1)S(1)} fusion(bf16[1536,1152]{0,1:T(8,128)(2,1)} %bitcast.111, bf16[1,32,8,1536]{3,2,1,0:T(8,128)(2,1)S(1)} %copy-done.1, f32[8,1536]{1,0:T(8,128)S(1)} %get-tuple-element.22, f32[8,1536]{1,0:T(8,128)S(1)} %get-tuple-element.23, f32[32,8]{1,0:T(8,128)S(1)} %add_rsqrt_fusion, ...), kind=kOutput, calls=%fused_computation.10 | convolution fusion | flops 908623872 | bytes 5015552 | tf_op jit(solution)/shard_map/dot_general | solution.py:84
  15.9 0.8 fusion.94
  16.7 1.1 concatenate.21
  17.9 1.5 concatenate.20
  19.3 1.8 %concatenate.19 = bf16[32,8,2,192]{3,2,1,0:T(2,128)(2,1)} reshape(bf16[256,384]{1,0:T(8,128)(2,1)} %get-tuple-element.14) | data formatting | bytes 393216 | tf_op jit(solution)/shard_map/concatenate | solution.py:109
  21.1 2.0 %maximum_bitcast_fusion = bf16[8,2,74,192]{3,1,0,2:T(2,128)(2,1)S(1)} fusion(bf16[5,8,2,192]{3,2,1,0:T(2,128)(2,1)} %concatenate.22, bf16[32,8,2,192]{3,2,1,0:T(2,128)(2,1)S(1)} %concatenate.21, bf16[5,8,2,192]{3,2,1,0:T(2,128)(2,1)} %concatenate.20, bf16[32,8,2,192]{3,2,1,0:T(2,128)(2,1)} %concatenate.19), kind=kLoop, calls=%fused_computation.43 | loop fusion | flops 681984 | bytes 909312 | tf_op jit(solution)/shard_map/transpose | solution.py:111
  23.1 1.0 copy.34
  24.1 1.1 reshape_reshape.4
  25.2 0.1 copy.33
  25.3 1.2 broadcast_in_dim.30
  26.5 1.5 pad_maximum_fusion
  28.0 9.9 %all-to-all-start = ((bf16[32,90,192]{2,1,0:T(8,128)(2,1)}), bf16[32,90,192]{2,1,0:T(8,128)(2,1)}, u32[]{:S(2)}, u32[]{:S(2)}) async-start(bf16[32,90,192]{2,1,0:T(8,128)(2,1)} %pad_maximum_fusion), calls=%async_computation | async-start | bytes 3145728 | tf_op jit(solution)/shard_map/all_to_all | solution.py:116
  38.0 0.6 fusion.78
  38.6 0.7 fusion.77
  39.3 0.7 or.17
  40.0 36.8 %all-to-all-done = bf16[32,90,192]{2,1,0:T(8,128)(2,1)} async-done(((bf16[32,90,192]{2,1,0:T(8,128)(2,1)}), bf16[32,90,192]{2,1,0:T(8,128)(2,1)}, u32[]{:S(2)}, u32[]{:S(2)}) %all-to-all-start) | async-done | bytes 1105952 | tf_op jit(solution)/shard_map/all_to_all | solution.py:116
  76.9 2.7 %fusion.93 = (bf16[32,37,192]{2,1,0:T(8,128)(2,1)}, bf16[32,37,192]{2,1,0:T(8,128)(2,1)}) fusion(bf16[32,90,192]{2,1,0:T(8,128)(2,1)} %all-to-all-done), kind=kLoop, calls=%fused_computation.126 | loop fusion | bytes 1818624 | tf_op jit(solution)/shard_map/slice | solution.py:119
  79.5 3.4 %reshape.373 = bf16[1184,3,64]{2,1,0:T(4,128)(2,1)} reshape(bf16[32,37,192]{2,1,0:T(8,128)(2,1)} %get-tuple-element.11) | data formatting | bytes 909312 | tf_op jit(solution)/shard_map/reshape.2
  82.9 1.0 slice.83
  83.9 0.9 reshape.372
  84.8 3.4 %reshape.371 = bf16[1184,3,64]{2,1,0:T(4,128)(2,1)} reshape(bf16[32,37,192]{2,1,0:T(8,128)(2,1)} %get-tuple-element.10) | data formatting | bytes 909312 | tf_op jit(solution)/shard_map/reshape.6
  88.2 0.0 copy-done.8
  88.2 3.8 %fusion.96 = f32[3,512]{1,0:T(4,128)S(1)} fusion(pred[1184]{0:T(1024)(128)(4,1)S(1)} %copy-done.8, bf16[1184,3,64]{2,1,0:T(4,128)(2,1)} %reshape.373, bf16[512,3,64]{2,1,0:T(4,128)(2,1)} %reshape.372), kind=kOutput, calls=%fused_computation.129 | convolution fusion | flops 240059552 | bytes 658592 | tf_op jit(solution)/shard_map/sub | solution.py:38
  92.1 4.9 %fusion.9 = bf16[512,1,3,64]{0,3,2,1:T(8,128)(2,1)S(1)} fusion(f32[3,512]{1,0:T(4,128)S(1)} %fusion.96, bf16[1184,3,64]{2,1,0:T(4,128)(2,1)} %reshape.371, pred[1184]{0:T(1024)(128)(4,1)S(1)} %copy-done.8, bf16[1184,3,64]{2,1,0:T(4,128)(2,1)} %reshape.373, bf16[512,3,64]{2,1,0:T(4,128)(2,1)} %reshape.372), kind=kOutput, calls=%fused_computation.22 | convolution fusion | flops 474761888 | bytes 1309856 | tf_op jit(solution)/shard_map/rhqk,krhd->qrhd/dot_general | solution.py:40
  97.0 1.1 copy.38
  98.0 1.5 reshape_reshape.10
  99.5 17.5 %all_to_all.20 = bf16[32,16,192]{2,1,0:T(8,128)(2,1)S(1)} all-to-all(bf16[32,16,192]{2,1,0:T(8,128)(2,1)S(1)} %reshape_reshape.10), channel_id=1, replica_groups=mesh['cfg'=2,'seq'=32,'tp'=4] {'seq'}, dimensions={0} | all-to-all | bytes 393216 | tf_op jit(solution)/shard_map/all_to_all | solution.py:130
  117.0 0.2 copy.68
  117.2 0.8 reshape.375
  118.1 2.8 %convolution_convert_fusion.2 = bf16[256,1536]{1,0:T(8,128)(2,1)} fusion(bf16[256,384]{1,0:T(8,128)(2,1)} %reshape.375, bf16[384,1536]{1,0:T(8,128)(2,1)} %param.22), kind=kOutput, calls=%fused_computation.11 | convolution fusion | flops 302383104 | bytes 2162688 | tf_op jit(solution)/shard_map/dot_general | solution.py:144
  120.9 4.5 %all-to-all-start.2 = ((bf16[4,64,1536]{2,1,0:T(8,128)(2,1)}), bf16[4,64,1536]{2,1,0:T(8,128)(2,1)}, u32[]{:S(2)}, u32[]{:S(2)}) async-start(bf16[4,64,1536]{2,1,0:T(8,128)(2,1)} %bitcast.112), calls=%async_computation.2 | async-start | bytes 1572864 | tf_op jit(solution)/shard_map/all_to_all | solution.py:46
  125.4 1.3 convert_element_type.100
  126.7 9.9 %all-to-all-done.2 = bf16[4,64,1536]{2,1,0:T(8,128)(2,1)} async-done(((bf16[4,64,1536]{2,1,0:T(8,128)(2,1)}), bf16[4,64,1536]{2,1,0:T(8,128)(2,1)}, u32[]{:S(2)}, u32[]{:S(2)}) %all-to-all-start.2) | async-done | bytes 786464 | tf_op jit(solution)/shard_map/all_to_all | solution.py:46
  136.6 1.3 convert_reduce_fusion.1
  137.9 1.1 fusion.91
  139.0 0.2 multiply_reduce_fusion.2
  139.2 0.1 add_convert_fusion.2
  139.4 13.3 %all_gather.3 = bf16[32,8,1536]{2,1,0:T(8,128)(2,1)S(1)} all-gather(bf16[8,8,1536]{2,1,0:T(8,128)(2,1)S(1)} %add_convert_fusion.2), channel_id=1, replica_groups=mesh['cfg'=2,'seq'=32,'tp'=4] {'tp'}, dimensions={0}, use_global_device_ids=true | all-gather | bytes 983040 | tf_op jit(solution)/shard_map/all_gather | solution.py:148
  152.7 0.0 copy-done
  152.7 4.3 %convolution_convert_fusion = bf16[256,1536]{1,0:T(8,128)(2,1)} fusion(bf16[768,1536]{1,0:T(8,128)(2,1)S(1)} %copy-done, bf16[1536,768]{1,0:T(8,128)(2,1)} %param.23, bf16[32,8,1536]{2,1,0:T(8,128)(2,1)S(1)} %all_gather.3), kind=kOutput, calls=%fused_computation.9 | convolution fusion | flops 1210122240 | bytes 6291456 | tf_op jit(solution)/shard_map/dot_general | solution.py:152
  157.0 3.5 %all-to-all-start.3 = ((bf16[4,64,1536]{2,1,0:T(8,128)(2,1)}), bf16[4,64,1536]{2,1,0:T(8,128)(2,1)S(1)}, u32[]{:S(2)}, u32[]{:S(2)}) async-start(bf16[4,64,1536]{2,1,0:T(8,128)(2,1)} %bitcast.117), calls=%async_computation.3 | async-start | bytes 1572864 | tf_op jit(solution)/shard_map/all_to_all | solution.py:46
  160.5 0.0 copy-start.10
  160.5 9.4 %all-to-all-done.3 = bf16[4,64,1536]{2,1,0:T(8,128)(2,1)S(1)} async-done(((bf16[4,64,1536]{2,1,0:T(8,128)(2,1)}), bf16[4,64,1536]{2,1,0:T(8,128)(2,1)S(1)}, u32[]{:S(2)}, u32[]{:S(2)}) %all-to-all-start.3) | async-done | bytes 786464 | tf_op jit(solution)/shard_map/all_to_all | solution.py:46
  170.0 0.1 convert_reduce_fusion
  170.1 0.0 copy-start.7
  170.1 0.9 fusion.89
  171.0 0.2 multiply_reduce_fusion.1
  171.2 0.3 fusion.53
  171.5 0.1 constant_dynamic-slice_fusion
  171.6 0.8 collective-permute-start
  172.4 0.2 select_reduce_fusion
  172.7 4.4 %collective-permute-done = f32[8,8,32]{2,1,0:T(8,128)S(1)} collective-permute-done((f32[8,8,32]{2,1,0:T(8,128)S(1)}, f32[8,8,32]{2,1,0:T(8,128)S(1)}, u32[]{:S(2)}, u32[]{:S(2)}) %collective-permute-start) | collective-permute-done | bytes 8224 | tf_op jit(solution)/shard_map/ppermute | solution.py:16
  177.0 0.7 multiply_add_fusion
  (32 shorter events, 0.1 us)
Async XLA Ops:
  0.6 152.1 %copy-start = (bf16[768,1536]{1,0:T(8,128)(2,1)S(1)}, bf16[768,1536]{1,0:T(8,128)(2,1)}, u32[]{:S(2)}) copy-start(bf16[768,1536]{1,0:T(8,128)(2,1)} %param.24) | copy-start | bytes 7077892
  0.6 2.3 %copy-start.3 = (bf16[1,8,10,1536]{3,1,2,0:T(8,128)(2,1)S(1)}, bf16[1,8,10,1536]{3,1,2,0:T(8,128)(2,1)}, u32[]{:S(2)}) copy-start(bf16[1,8,10,1536]{3,1,2,0:T(8,128)(2,1)} %param.15) | copy-start | bytes 737284
  0.7 3.0 %copy-start.2 = (bf16[1,5,8,1536]{3,2,1,0:T(8,128)(2,1)S(1)}, bf16[1,5,8,1536]{3,2,1,0:T(8,128)(2,1)}, u32[]{:S(2)}) copy-start(bf16[1,5,8,1536]{3,2,1,0:T(8,128)(2,1)} %param.14) | copy-start | bytes 368644
  5.9 6.2 %copy-start.1 = (bf16[1,32,8,1536]{3,2,1,0:T(8,128)(2,1)S(1)}, bf16[1,32,8,1536]{3,2,1,0:T(8,128)(2,1)}, u32[]{:S(2)}) copy-start(bf16[1,32,8,1536]{3,2,1,0:T(8,128)(2,1)} %param.13) | copy-start | bytes 2359300
  28.0 10.0 %copy-start.11 = (s32[1,8]{1,0:T(1,128)S(1)}, s32[1,8]{1,0:T(1,128)}, u32[]{:S(2)}) copy-start(s32[1,8]{1,0:T(1,128)} %param.16) | copy-start | bytes 100
  28.0 48.9 %all-to-all-start = ((bf16[32,90,192]{2,1,0:T(8,128)(2,1)}), bf16[32,90,192]{2,1,0:T(8,128)(2,1)}, u32[]{:S(2)}, u32[]{:S(2)}) async-start(bf16[32,90,192]{2,1,0:T(8,128)(2,1)} %pad_maximum_fusion), calls=%async_computation | async-start | bytes 3145728 | tf_op jit(solution)/shard_map/all_to_all | solution.py:116
  84.8 3.4 %copy-start.8 = (pred[1184]{0:T(1024)(128)(4,1)S(1)}, pred[1184]{0:T(1024)(128)(4,1)}, u32[]{:S(2)}) copy-start(pred[1184]{0:T(1024)(128)(4,1)} %or.17) | copy-start | bytes 3556
  120.9 15.7 %all-to-all-start.2 = ((bf16[4,64,1536]{2,1,0:T(8,128)(2,1)}), bf16[4,64,1536]{2,1,0:T(8,128)(2,1)}, u32[]{:S(2)}, u32[]{:S(2)}) async-start(bf16[4,64,1536]{2,1,0:T(8,128)(2,1)} %bitcast.112), calls=%async_computation.2 | async-start | bytes 1572864 | tf_op jit(solution)/shard_map/all_to_all | solution.py:46
  152.7 7.8 %copy-start.9 = (s32[8]{0:T(128)S(1)}, s32[8]{0:T(128)}, u32[]{:S(2)}) copy-start(s32[8]{0:T(128)} %param.17) | copy-start | bytes 100
  157.0 13.0 %all-to-all-start.3 = ((bf16[4,64,1536]{2,1,0:T(8,128)(2,1)}), bf16[4,64,1536]{2,1,0:T(8,128)(2,1)S(1)}, u32[]{:S(2)}, u32[]{:S(2)}) async-start(bf16[4,64,1536]{2,1,0:T(8,128)(2,1)} %bitcast.117), calls=%async_computation.3 | async-start | bytes 1572864 | tf_op jit(solution)/shard_map/all_to_all | solution.py:46
  160.5 11.9 %copy-start.10 = (f32[9]{0:T(128)S(1)}, f32[9]{0:T(128)}, u32[]{:S(2)}) copy-start(f32[9]{0:T(128)} %param.18) | copy-start | bytes 112
  169.9 1.3 copy-start.4
  170.0 1.3 copy-start.5
  170.0 1.3 copy-start.6
  170.1 7.0 %copy-start.7 = (f32[8,8,32]{2,1,0:T(8,128)S(1)}, f32[8,8,32]{2,1,0:T(8,128)}, u32[]{:S(2)}) copy-start(f32[8,8,32]{2,1,0:T(8,128)} %param.19) | copy-start | bytes 24580
  171.6 5.5 %collective-permute-start = (f32[8,8,32]{2,1,0:T(8,128)S(1)}, f32[8,8,32]{2,1,0:T(8,128)S(1)}, u32[]{:S(2)}, u32[]{:S(2)}) collective-permute-start(f32[8,8,32]{2,1,0:T(8,128)S(1)} %constant_dynamic-slice_fusion), channel_id=1, source_target_pairs={{0,128},{128,0},{1,129},{129,1},{2,130},{130,2},{3,131},{131,3},{4... | collective-permute-start | bytes 24584 | tf_op jit(solution)/shard_map/ppermute | solution.py:16

commit v3 on v2

--- a/solution.py
+++ b/solution.py
@@ -25,20 +25,31 @@
     return (layer_norm(values) * (1.0 + scale_mul) + shift_add).astype(jnp.bfloat16)
 
 
-def attend(queries, keys_in, values_in, key_valid):
-    heads = queries.shape[2] // HEAD_DIM
-    query_heads = queries.reshape(queries.shape[0], queries.shape[1], heads, HEAD_DIM)
-    key_heads = keys_in.reshape(keys_in.shape[0], keys_in.shape[1], heads, HEAD_DIM)
-    value_heads = values_in.reshape(values_in.shape[0], values_in.shape[1], heads, HEAD_DIM)
-    scores = jnp.einsum(
-        "qrhd,krhd->rhqk", query_heads, key_heads, preferred_element_type=jnp.float32
-    ) * (1.0 / math.sqrt(HEAD_DIM))
-    scores = jnp.where(key_valid[:, None, None, :], scores, -jnp.inf)
-    row_max = jnp.max(scores, -1, keepdims=True)
-    exp_scores = jnp.exp(scores - row_max)
-    weights = (exp_scores / jnp.sum(exp_scores, -1, keepdims=True)).astype(jnp.bfloat16)
-    result = jnp.einsum("rhqk,krhd->qrhd", weights, value_heads, preferred_element_type=jnp.float32)
-    return result.astype(jnp.bfloat16).reshape(queries.shape)
+def attend(queries, keys_img, values_img, keys_txt, values_txt, text_valid):
+    width = queries.shape[1]
+    heads = width // HEAD_DIM
+    chosen = (jnp.arange(width)[None, :] // HEAD_DIM) == jnp.arange(heads)[:, None]
+    query_heads = jnp.where(chosen[:, None, :], queries[None], 0).astype(queries.dtype)
+    scale = 1.0 / math.sqrt(HEAD_DIM)
+    scores_img = (
+        jnp.einsum("hqf,kf->hqk", query_heads, keys_img, preferred_element_type=jnp.float32) * scale
+    )
+    scores_txt = (
+        jnp.einsum("hqf,kf->hqk", query_heads, keys_txt, preferred_element_type=jnp.float32) * scale
+    )
+    scores_txt = jnp.where(text_valid[None, None, :], scores_txt, -jnp.inf)
+    row_max = jnp.maximum(
+        jnp.max(scores_img, -1, keepdims=True), jnp.max(scores_txt, -1, keepdims=True)
+    )
+    exp_img = jnp.exp(scores_img - row_max)
+    exp_txt = jnp.exp(scores_txt - row_max)
+    total = jnp.sum(exp_img, -1, keepdims=True) + jnp.sum(exp_txt, -1, keepdims=True)
+    weights_img = (exp_img / total).astype(jnp.bfloat16)
+    weights_txt = (exp_txt / total).astype(jnp.bfloat16)
+    mixed = jnp.einsum(
+        "hqk,kf->hqf", weights_img, values_img, preferred_element_type=jnp.float32
+    ) + jnp.einsum("hqk,kf->hqf", weights_txt, values_txt, preferred_element_type=jnp.float32)
+    return jnp.sum(jnp.where(chosen[:, None, :], mixed, 0.0), 0).astype(jnp.bfloat16)
 
 
 def reduce_rows(partial, parties):
@@ -81,20 +92,20 @@
     resident = img_hidden[0].astype(jnp.float32)
     lengths_all = text_lengths[0]
     normed = modulate(resident, adaptive[:, 0], adaptive[:, 1]).reshape(rows_all, model_width)
-    projected = jnp.dot(
-        normed, w_qkv.reshape(model_width, 3 * features), preferred_element_type=jnp.float32
+    projected = jnp.einsum(
+        "nd,dkf->knf", normed, w_qkv, preferred_element_type=jnp.float32
     ).astype(jnp.bfloat16)
-    queries = projected[:, :features].reshape(img_slice, requests, features)
-    keys_img = projected[:, features : 2 * features].reshape(img_slice, requests, features)
-    vals_img = projected[:, 2 * features :].reshape(img_slice, requests, features)
+    queries = projected[0].reshape(img_slice, requests, features)
+    keys_img = projected[1].reshape(img_slice, requests, features)
+    vals_img = projected[2].reshape(img_slice, requests, features)
     text_in = modulate(txt_hidden[0].astype(jnp.float32), adaptive[:, 6], adaptive[:, 7]).reshape(
         txt_slice * requests, model_width
     )
-    text_kv = jnp.dot(
-        text_in, w_kv_text.reshape(model_width, 2 * features), preferred_element_type=jnp.float32
+    text_kv = jnp.einsum(
+        "nd,dkf->knf", text_in, w_kv_text, preferred_element_type=jnp.float32
     ).astype(jnp.bfloat16)
-    keys_txt = text_kv[:, :features].reshape(txt_slice, requests, features)
-    vals_txt = text_kv[:, features:].reshape(txt_slice, requests, features)
+    keys_txt = text_kv[0].reshape(txt_slice, requests, features)
+    vals_txt = text_kv[1].reshape(txt_slice, requests, features)
     key_span = img_slice + txt_slice
     within = jnp.arange(key_span)
     senders = requests * members
@@ -106,27 +117,33 @@
         .transpose(2, 0, 3, 1, 4)
         .reshape(senders, query_share, head_share)
     )
-    joined_k = jnp.concatenate([keys_img, keys_txt], 0).reshape(key_span, requests, 2, head_share)
-    joined_v = jnp.concatenate([vals_img, vals_txt], 0).reshape(key_span, requests, 2, head_share)
-    both = jnp.concatenate([joined_k, joined_v], 0).transpose(1, 2, 0, 3)
+    def by_head_half(values, rows):
+        return values.reshape(rows, requests, 2, head_share).transpose(1, 2, 0, 3)
+
+    both = jnp.concatenate(
+        [
+            by_head_half(keys_img, img_slice),
+            by_head_half(vals_img, img_slice),
+            by_head_half(keys_txt, txt_slice),
+            by_head_half(vals_txt, txt_slice),
+        ],
+        2,
+    )
     kv_send = jnp.broadcast_to(
         both[:, None], (requests, halves, 2, 2 * key_span, head_share)
     ).reshape(senders, 2 * key_span, head_share)
     payload = jnp.concatenate([query_send, kv_send], 1)
     got = lax.all_to_all(payload, "seq", split_axis=0, concat_axis=0, tiled=True)
-    query_got = got[:, :query_share]
-    key_got = got[:, query_share : query_share + key_span]
-    value_got = got[:, query_share + key_span :]
+    cut = [query_share, img_slice, img_slice, txt_slice, txt_slice]
+    edges = [sum(cut[:i]) for i in range(len(cut) + 1)]
+    query_got, key_img_got, val_img_got, key_txt_got, val_txt_got = [
+        got[:, edges[i] : edges[i + 1]].reshape(senders * cut[i], head_share)
+        for i in range(len(cut))
+    ]
     my_request = lax.axis_index("seq") // members
     length_now = jnp.sum(jnp.where(jnp.arange(requests) == my_request, lengths_all, 0))
-    text_slot = jnp.arange(senders)[:, None] * txt_slice + within[None, :] - img_slice
-    key_valid = (within[None, :] < img_slice) | (text_slot < length_now)
-    answer = attend(
-        query_got.reshape(senders * query_share, 1, head_share),
-        key_got.reshape(senders * key_span, 1, head_share),
-        value_got.reshape(senders * key_span, 1, head_share),
-        key_valid.reshape(1, senders * key_span),
-    )
+    text_valid = jnp.arange(senders * txt_slice) < length_now
+    answer = attend(query_got, key_img_got, val_img_got, key_txt_got, val_txt_got, text_valid)
     answer_back = lax.all_to_all(
         answer.reshape(senders, query_share, head_share),
         "seq",

time: 179 us -> 194 us (1.084)
  other arithmetic: 12.6 us -> 27.1 us
    unnamed x26 -> x42, local copies, waits for them, and re-layouts: 8.49 us -> 2.42 us
    concatenate x4 -> x1, local copies, waits for them, and re-layouts: 5.1 us -> 1.02 us  [shards(): jnp.concatenate([by_head_half(keys_img, img_slice), by_head_half(vals_img...]
    dot_general x3 -> x6, matrix products: 8.78 us -> 12.6 us  [the longest x1 4.15 us: attend(): jnp.einsum('hqk,kf->hqf', weights_img, values_img, preferred_element_type...]
    sub x1 -> x0, matrix products: 3.83 us -> none  [attend(): exp_scores = jnp.exp(scores - row_max)]
    reduce_sum x4, other arithmetic: 0.91 us -> 4.13 us  [layer_norm(): jnp.mean(center * center, -1, keepdims=True) + EPSILON]
    reshape x1 -> x2, local copies, waits for them, and re-layouts: 0.2 us -> 3.2 us  [shards(): got[:, edges[i]:edges[i + 1]].reshape(senders * cut[i], head_share)]
    another operation x4, local copies, waits for them, and re-layouts: 9.23 us -> 6.57 us  [by_head_half(): return values.reshape(rows, requests, 2, head_share).transpose(1, 2, 0, 3)]
    reduce_sum x4, other arithmetic: 2.34 us -> 4.76 us  [layer_norm(): center = values - jnp.mean(values, -1, keepdims=True)]
  transfers between devices with their start and end apart: 4 -> 4, of which waited for: 4 -> 4; matrix products, arithmetic and copies ran while one was open for 2% -> 3% of each run, Pallas kernels for 0% -> 0%
where the time goes in v3:
time: 194 us; the launch traced here: 193 us
  waiting for transfers between devices  59.6 us (31%)
  local copies, waits for them, and re-layouts  33.1 us (17%)
  blocking collectives  31.9 us (16%)
  other arithmetic  27.1 us (14%)
  matrix products  21 us (11%)
  starting transfers between devices  19.3 us (10%)
    all_to_all x1, waiting for transfers between devices, shards(): lax.all_to_all(payload, 'seq', split_axis=0, concat_axis=0, tiled=True)  37.8 us
    all_to_all x2, waiting for transfers between devices, reduce_rows(): got = lax.all_to_all(pieces, 'tp', split_axis=0, concat_axis=0, tiled=True)  18.3 us
    all_to_all x1, blocking collectives, shards(): lax.all_to_all(answer.reshape(senders, query_share, head_share), 'seq', s...  17.7 us
    all_gather x1, blocking collectives, shards(): lax.all_gather(mlp_mine, 'tp', axis=0, tiled=True)  14.2 us
    all_to_all x1, starting transfers between devices, shards(): lax.all_to_all(payload, 'seq', split_axis=0, concat_axis=0, tiled=True)  9.73 us
    all_to_all x2, starting transfers between devices, reduce_rows(): got = lax.all_to_all(pieces, 'tp', split_axis=0, concat_axis=0, tiled=True)  8.79 us
    another operation x4, local copies, waits for them, and re-layouts, by_head_half(): return values.reshape(rows, requests, 2, head_share).transpose(1, 2, 0, 3)  6.57 us
    slice x3, local copies, waits for them, and re-layouts, shards(): got[:, edges[i]:edges[i + 1]].reshape(senders * cut[i], head_share)  5.43 us
  transfers between devices with their start and end apart: 4, of which 4 were waited for; matrix products, arithmetic and copies ran while one was open for 3% of the time, Pallas kernels for 0%

profile of v3, /device:TPU:4, one launch (start us, length us, event | category | flops | bytes accessed | tf_op | source)
XLA Modules:
  0.0 192.9 jit_solution(10036567538214968848)
XLA Ops:
  0.6 1.5 convert_reduce_fusion.2
  2.1 2.1 %fusion.6 = f32[32,8]{1,0:T(8,128)} fusion(bf16[1,32,8,1536]{3,2,1,0:T(8,128)(2,1)} %param.13, f32[32,8]{1,0:T(8,128)S(1)} %broadcast_multiply_fusion), kind=kLoop, calls=%fused_computation.15 | loop fusion | flops 1572608 | bytes 788480 | tf_op jit(solution)/shard_map/reduce_sum | solution.py:21
  4.2 0.7 div.65
  4.9 1.0 convert_reduce_fusion.3
  5.9 1.7 fusion.63
  7.5 0.6 div.68
  8.2 1.0 bitcast_convert_fusion
  9.1 0.8 fusion.76
  9.9 0.7 add_rsqrt_fusion
  10.7 0.7 rsqrt.39
  11.3 2.4 %fusion.11 = bf16[3,256,384]{2,1,0:T(8,128)(2,1)S(1)} fusion(bf16[1536,3,384]{2,0,1:T(8,128)(2,1)S(1)} %copy-done, bf16[1,32,8,1536]{3,2,1,0:T(8,128)(2,1)} %param.13, f32[8,1536]{1,0:T(8,128)} %get-tuple-element.24, f32[8,1536]{1,0:T(8,128)} %get-tuple-element.25, f32[256]{0:T(256)} %rsqrt.39, f32[256]{0:T(256)} %div.65), kind=kOutput, calls=%fused_computation.26 | convolution fusion | flops 908623872 | bytes 5015552 | tf_op jit(solution)/shard_map/nd,dkf->knf/dot_general | solution.py:95
  13.8 0.8 fusion.94
  14.6 1.8 reshape_reshape_squeeze.16
  16.4 1.8 reshape_reshape_squeeze.17
  18.3 2.4 %fusion.15 = bf16[2,40,384]{2,1,0:T(8,128)(2,1)S(1)} fusion(bf16[1536,2,384]{2,1,0:T(2,128)(2,1)} %param.21, bf16[1,5,8,1536]{3,2,1,0:T(8,128)(2,1)} %param.14, f32[8,1536]{1,0:T(8,128)} %get-tuple-element.22, f32[8,1536]{1,0:T(8,128)} %get-tuple-element.23, f32[40]{0:T(128)S(1)} %rsqrt.41, f32[40]{0:T(128)S(1)} %copy-done.19), kind=kOutput, calls=%fused_computation.30 | convolution fusion | flops 94771200 | bytes 2642240 | tf_op jit(solution)/shard_map/nd,dkf->knf/dot_general | solution.py:104
  20.7 0.6 fusion.95
  21.3 1.5 reshape_reshape_squeeze.18
  22.8 1.5 reshape_reshape_squeeze.19
  24.2 2.0 %pad_maximum_fusion.1 = bf16[8,2,74,192]{3,1,0,2:T(2,128)(2,1)S(1)} fusion(bf16[8,2,5,192]{3,1,0,2:T(2,128)(2,1)} %bitcast.162, bf16[8,2,5,192]{3,1,0,2:T(2,128)(2,1)} %bitcast.161, bf16[8,2,32,192]{3,1,0,2:T(2,128)(2,1)} %bitcast.154, bf16[8,2,32,192]{3,1,0,2:T(2,128)(2,1)} %bitcast.153), kind=kLoop, calls=%fused_computation.52 | loop fusion | flops 681984 | bytes 909312 | tf_op jit(solution)/shard_map/concatenate | solution.py:123
  26.3 1.0 copy.50
  27.3 1.8 reshape_reshape_squeeze.15
  29.1 1.0 copy.48
  30.2 1.2 broadcast_in_dim.69
  31.4 1.5 pad_maximum_fusion
  32.8 9.7 %all-to-all-start = ((bf16[32,90,192]{2,1,0:T(8,128)(2,1)}), bf16[32,90,192]{2,1,0:T(8,128)(2,1)}, u32[]{:S(2)}, u32[]{:S(2)}) async-start(bf16[32,90,192]{2,1,0:T(8,128)(2,1)} %pad_maximum_fusion), calls=%async_computation | async-start | bytes 3145728 | tf_op jit(solution)/shard_map/all_to_all | solution.py:136
  42.6 0.6 fusion.80
  43.2 0.6 iota_compare_fusion.3
  43.9 37.8 %all-to-all-done = bf16[32,90,192]{2,1,0:T(8,128)(2,1)} async-done(((bf16[32,90,192]{2,1,0:T(8,128)(2,1)}), bf16[32,90,192]{2,1,0:T(8,128)(2,1)}, u32[]{:S(2)}, u32[]{:S(2)}) %all-to-all-start) | async-done | bytes 1105952 | tf_op jit(solution)/shard_map/all_to_all | solution.py:136
  81.7 1.7 slice.90
  83.4 1.8 copy.51
  85.1 1.7 fusion.92
  86.8 1.6 reshape.275
  88.4 2.1 %fusion.93 = (bf16[32,32,192]{2,1,0:T(8,128)(2,1)S(1)}, bf16[32,32,192]{2,1,0:T(8,128)(2,1)}) fusion(bf16[32,90,192]{2,1,0:T(8,128)(2,1)} %all-to-all-done), kind=kLoop, calls=%fused_computation.144 | loop fusion | bytes 1572864 | tf_op jit(solution)/shard_map/slice | solution.py:140
  90.5 2.3 %multiply_reduce_fusion = (f32[3,512]{1,0:T(4,128)S(1)}, f32[3,512,1024]{2,1,0:T(8,128)S(1)}) fusion(bf16[1024,192,1]{1,0,2:T(8,128)(2,1)S(1)} %bitcast.152, pred[3,192]{1,0:T(4,128)(4,1)S(1)} %iota_compare_fusion.2, bf16[512,192]{0,1:T(8,128)(2,1)} %copy.51), kind=kOutput, calls=%fused_computation.2 | convolution fusion | flops 607418880 | bytes 6888000 | tf_op jit(solution)/shard_map/hqf,kf->hqk/dot_general | solution.py:35
  93.2 1.2 copy-done.3
  94.6 1.9 fusion
  96.5 1.6 reshape.277
  98.1 0.7 add.195
  98.8 4.2 %fusion.1 = f32[3,512,192]{1,2,0:T(8,128)S(1)} fusion(bf16[1024,192,1]{1,0,2:T(8,128)(2,1)} %bitcast.160, f32[3,512,1024]{2,1,0:T(8,128)} %copy-done.1, f32[3,512]{1,0:T(4,128)S(1)} %add.195, f32[3,512]{1,0:T(4,128)S(1)} %max.8), kind=kOutput, calls=%fused_computation.4 | convolution fusion | flops 610271232 | bytes 7876608 | tf_op jit(solution)/shard_map/hqk,kf->hqf/dot_general | solution.py:49
  103.0 1.1 fusion.10
  104.0 1.8 copy.54
  105.8 17.7 %all_to_all.20 = bf16[32,16,192]{2,1,0:T(8,128)(2,1)S(1)} all-to-all(bf16[32,16,192]{2,1,0:T(8,128)(2,1)} %bitcast.156), channel_id=1, replica_groups=mesh['cfg'=2,'seq'=32,'tp'=4] {'seq'}, dimensions={0} | all-to-all | bytes 393216 | tf_op jit(solution)/shard_map/all_to_all | solution.py:147
  123.5 0.9 copy.55
  124.4 1.8 reshape.263
  126.2 2.8 %convolution_convert_fusion.1 = bf16[256,1536]{1,0:T(8,128)(2,1)} fusion(bf16[256,384]{1,0:T(8,128)(2,1)} %reshape.263, bf16[384,1536]{1,0:T(8,128)(2,1)} %param.22), kind=kOutput, calls=%fused_computation.6 | convolution fusion | flops 302383104 | bytes 2162688 | tf_op jit(solution)/shard_map/dot_general | solution.py:161
  129.1 4.5 %all-to-all-start.2 = ((bf16[4,64,1536]{2,1,0:T(8,128)(2,1)}), bf16[4,64,1536]{2,1,0:T(8,128)(2,1)}, u32[]{:S(2)}, u32[]{:S(2)}) async-start(bf16[4,64,1536]{2,1,0:T(8,128)(2,1)} %bitcast.151), calls=%async_computation.2 | async-start | bytes 1572864 | tf_op jit(solution)/shard_map/all_to_all | solution.py:57
  133.5 2.5 %convert_element_type.86 = f32[1,32,8,1536]{3,2,1,0:T(8,128)} convert(bf16[1,32,8,1536]{3,2,1,0:T(8,128)(2,1)} %param.13) | non-fusion elementwise | flops 393216 | bytes 2359296 | tf_op jit(solution)/shard_map/convert_element_type | solution.py:92
  136.0 8.8 %all-to-all-done.2 = bf16[4,64,1536]{2,1,0:T(8,128)(2,1)} async-done(((bf16[4,64,1536]{2,1,0:T(8,128)(2,1)}), bf16[4,64,1536]{2,1,0:T(8,128)(2,1)}, u32[]{:S(2)}, u32[]{:S(2)}) %all-to-all-start.2) | async-done | bytes 786464 | tf_op jit(solution)/shard_map/all_to_all | solution.py:57
  144.8 1.3 convert_reduce_fusion.1
  146.1 1.2 fusion.90
  147.4 0.5 copy-done.2
  148.1 14.2 %all_gather.3 = bf16[32,8,1536]{2,1,0:T(8,128)(2,1)} all-gather(bf16[8,8,1536]{2,1,0:T(8,128)(2,1)S(1)} %add_convert_fusion.1), channel_id=1, replica_groups=mesh['cfg'=2,'seq'=32,'tp'=4] {'tp'}, dimensions={0}, use_global_device_ids=true | all-gather | bytes 983040 | tf_op jit(solution)/shard_map/all_gather | solution.py:165
  162.3 5.2 %convolution_convert_fusion = bf16[256,1536]{1,0:T(8,128)(2,1)} fusion(bf16[768,1536]{1,0:T(8,128)(2,1)} %param.24, bf16[1536,768]{1,0:T(8,128)(2,1)} %param.23, bf16[32,8,1536]{2,1,0:T(8,128)(2,1)} %all_gather.3), kind=kOutput, calls=%fused_computation.5 | convolution fusion | flops 1210122240 | bytes 6291456 | tf_op jit(solution)/shard_map/dot_general | solution.py:169
  167.6 4.3 %all-to-all-start.3 = ((bf16[4,64,1536]{2,1,0:T(8,128)(2,1)}), bf16[4,64,1536]{2,1,0:T(8,128)(2,1)}, u32[]{:S(2)}, u32[]{:S(2)}) async-start(bf16[4,64,1536]{2,1,0:T(8,128)(2,1)} %bitcast.159), calls=%async_computation.3 | async-start | bytes 1572864 | tf_op jit(solution)/shard_map/all_to_all | solution.py:57
  171.9 9.5 %all-to-all-done.3 = bf16[4,64,1536]{2,1,0:T(8,128)(2,1)} async-done(((bf16[4,64,1536]{2,1,0:T(8,128)(2,1)}), bf16[4,64,1536]{2,1,0:T(8,128)(2,1)}, u32[]{:S(2)}, u32[]{:S(2)}) %all-to-all-start.3) | async-done | bytes 786464 | tf_op jit(solution)/shard_map/all_to_all | solution.py:57
  181.5 1.3 convert_reduce_fusion
  182.8 1.1 fusion.88
  184.4 0.6 copy-done.6
  185.0 0.7 constant_dynamic-slice_fusion
  185.7 0.8 collective-permute-start
  186.5 0.7 select_reduce_fusion
  187.2 0.7 sub.103
  187.9 3.6 %collective-permute-done = f32[8,8,32]{2,1,0:T(8,128)} collective-permute-done((f32[8,8,32]{2,1,0:T(8,128)}, f32[8,8,32]{2,1,0:T(8,128)}, u32[]{:S(2)}, u32[]{:S(2)}) %collective-permute-start) | collective-permute-done | bytes 8224 | tf_op jit(solution)/shard_map/ppermute | solution.py:16
  191.4 1.5 multiply_add_fusion
  (57 shorter events, 1.5 us)
Async XLA Ops:
  0.6 10.7 %copy-start = (bf16[1536,3,384]{2,0,1:T(8,128)(2,1)S(1)}, bf16[1536,3,384]{2,0,1:T(8,128)(2,1)}, u32[]{:S(2)}) copy-start(bf16[1536,3,384]{2,0,1:T(8,128)(2,1)} %param.20) | copy-start | bytes 10616836
  11.3 6.9 %copy-start.14 = (f32[5,8]{1,0:T(8,128)S(1)}, f32[5,8]{1,0:T(8,128)}, u32[]{:S(2)}) copy-start(f32[5,8]{1,0:T(8,128)} %fusion.63) | copy-start | bytes 484
  11.3 7.0 %copy-start.19 = (f32[40]{0:T(128)S(1)}, f32[40]{0:T(128)}, u32[]{:S(2)}) copy-start(f32[40]{0:T(128)} %div.68) | copy-start | bytes 484
  32.8 9.8 %copy-start.20 = (s32[1,8]{1,0:T(1,128)S(1)}, s32[1,8]{1,0:T(1,128)}, u32[]{:S(2)}) copy-start(s32[1,8]{1,0:T(1,128)} %param.16) | copy-start | bytes 100
  32.8 48.9 %all-to-all-start = ((bf16[32,90,192]{2,1,0:T(8,128)(2,1)}), bf16[32,90,192]{2,1,0:T(8,128)(2,1)}, u32[]{:S(2)}, u32[]{:S(2)}) async-start(bf16[32,90,192]{2,1,0:T(8,128)(2,1)} %pad_maximum_fusion), calls=%async_computation | async-start | bytes 3145728 | tf_op jit(solution)/shard_map/all_to_all | solution.py:136
  43.9 48.8 %copy-start.15 = (pred[3,192]{1,0:T(4,128)(4,1)}, pred[3,192]{1,0:T(4,128)(4,1)S(1)}, u32[]{:S(2)}) copy-start(pred[3,192]{1,0:T(4,128)(4,1)S(1)} %iota_compare_fusion.2) | copy-start | bytes 1732
  90.5 2.3 %copy-start.5 = (bf16[512,192]{0,1:T(8,128)(2,1)S(1)}, bf16[512,192]{0,1:T(8,128)(2,1)}, u32[]{:S(2)}) copy-start(bf16[512,192]{0,1:T(8,128)(2,1)} %copy.51) | copy-start | bytes 589828
  90.5 2.3 %copy-start.12 = (bf16[160,192,1]{1,0,2:T(8,128)(2,1)S(1)}, bf16[160,192,1]{1,0,2:T(8,128)(2,1)}, u32[]{:S(2)}) copy-start(bf16[160,192,1]{1,0,2:T(8,128)(2,1)} %reshape.275) | copy-start | bytes 184324
  92.8 3.7 %copy-start.1 = (f32[3,512,1024]{2,1,0:T(8,128)}, f32[3,512,1024]{2,1,0:T(8,128)S(1)}, u32[]{:S(2)}) copy-start(f32[3,512,1024]{2,1,0:T(8,128)S(1)} %get-tuple-element.30) | copy-start | bytes 18874372
  93.2 1.2 copy-start.3
  98.8 4.2 %copy-start.4 = (f32[3,512,160]{1,2,0:T(8,128)S(1)}, f32[3,512,160]{1,2,0:T(8,128)}, u32[]{:S(2)}) copy-start(f32[3,512,160]{1,2,0:T(8,128)} %copy-done.3) | copy-start | bytes 2949124
  98.8 4.2 %copy-start.13 = (bf16[160,192,1]{1,0,2:T(8,128)(2,1)S(1)}, bf16[160,192,1]{1,0,2:T(8,128)(2,1)}, u32[]{:S(2)}) copy-start(bf16[160,192,1]{1,0,2:T(8,128)(2,1)} %reshape.277) | copy-start | bytes 184324
  98.8 4.2 %copy-start.16 = (pred[3,192]{1,0:T(4,128)(4,1)S(1)}, pred[3,192]{1,0:T(4,128)(4,1)}, u32[]{:S(2)}) copy-start(pred[3,192]{1,0:T(4,128)(4,1)} %copy-done.15) | copy-start | bytes 1732
  129.1 15.7 %all-to-all-start.2 = ((bf16[4,64,1536]{2,1,0:T(8,128)(2,1)}), bf16[4,64,1536]{2,1,0:T(8,128)(2,1)}, u32[]{:S(2)}, u32[]{:S(2)}) async-start(bf16[4,64,1536]{2,1,0:T(8,128)(2,1)} %bitcast.151), calls=%async_computation.2 | async-start | bytes 1572864 | tf_op jit(solution)/shard_map/all_to_all | solution.py:57
  144.8 3.2 %copy-start.10 = (f32[8,1536]{1,0:T(8,128)S(1)}, f32[8,1536]{1,0:T(8,128)}, u32[]{:S(2)}) copy-start(f32[8,1536]{1,0:T(8,128)} %get-tuple-element.19) | copy-start | bytes 147460
  144.8 3.2 %copy-start.11 = (f32[8,1536]{1,0:T(8,128)S(1)}, f32[8,1536]{1,0:T(8,128)}, u32[]{:S(2)}) copy-start(f32[8,1536]{1,0:T(8,128)} %get-tuple-element.20) | copy-start | bytes 147460
  147.2 0.7 copy-start.2
  162.3 9.6 %copy-start.17 = (s32[8]{0:T(128)S(1)}, s32[8]{0:T(128)}, u32[]{:S(2)}) copy-start(s32[8]{0:T(128)} %param.17) | copy-start | bytes 100
  167.6 18.9 %copy-start.18 = (f32[9]{0:T(128)S(1)}, f32[9]{0:T(128)}, u32[]{:S(2)}) copy-start(f32[9]{0:T(128)} %param.18) | copy-start | bytes 112
  167.6 13.9 %all-to-all-start.3 = ((bf16[4,64,1536]{2,1,0:T(8,128)(2,1)}), bf16[4,64,1536]{2,1,0:T(8,128)(2,1)}, u32[]{:S(2)}, u32[]{:S(2)}) async-start(bf16[4,64,1536]{2,1,0:T(8,128)(2,1)} %bitcast.159), calls=%async_computation.3 | async-start | bytes 1572864 | tf_op jit(solution)/shard_map/all_to_all | solution.py:57
  181.5 2.7 %copy-start.7 = (bf16[1536,64]{0,1:T(8,128)(2,1)S(1)}, bf16[1536,64]{0,1:T(8,128)(2,1)}, u32[]{:S(2)}) copy-start(bf16[1536,64]{0,1:T(8,128)(2,1)} %param.25) | copy-start | bytes 589828
  181.5 2.7 %copy-start.8 = (f32[8,1536]{1,0:T(8,128)S(1)}, f32[8,1536]{1,0:T(8,128)}, u32[]{:S(2)}) copy-start(f32[8,1536]{1,0:T(8,128)} %get-tuple-element.17) | copy-start | bytes 147460
  181.5 2.7 %copy-start.9 = (f32[8,1536]{1,0:T(8,128)S(1)}, f32[8,1536]{1,0:T(8,128)}, u32[]{:S(2)}) copy-start(f32[8,1536]{1,0:T(8,128)} %get-tuple-element.18) | copy-start | bytes 147460
  184.4 0.6 copy-start.6
  185.7 5.7 %collective-permute-start = (f32[8,8,32]{2,1,0:T(8,128)}, f32[8,8,32]{2,1,0:T(8,128)}, u32[]{:S(2)}, u32[]{:S(2)}) collective-permute-start(f32[8,8,32]{2,1,0:T(8,128)} %constant_dynamic-slice_fusion), channel_id=1, source_target_pairs={{0,128},{128,0},{1,129},{129,1},{2,130},{130,2},{3,131},{131,3},{4... | collective-permute-start | bytes 24584 | tf_op jit(solution)/shard_map/ppermute | solution.py:16

commit v4 on v2

--- a/solution.py
+++ b/solution.py
@@ -103,20 +103,24 @@
     head_share = features // 2
     query_send = (
         queries.reshape(halves, query_share, requests, 2, head_share)
-        .transpose(2, 0, 3, 1, 4)
+        .transpose(2, 3, 0, 1, 4)
         .reshape(senders, query_share, head_share)
     )
     joined_k = jnp.concatenate([keys_img, keys_txt], 0).reshape(key_span, requests, 2, head_share)
     joined_v = jnp.concatenate([vals_img, vals_txt], 0).reshape(key_span, requests, 2, head_share)
-    both = jnp.concatenate([joined_k, joined_v], 0).transpose(1, 2, 0, 3)
-    kv_send = jnp.broadcast_to(
-        both[:, None], (requests, halves, 2, 2 * key_span, head_share)
-    ).reshape(senders, 2 * key_span, head_share)
+    kv_send = (
+        jnp.stack([joined_k, joined_v], 3)
+        .transpose(1, 2, 3, 0, 4)
+        .reshape(senders, key_span, head_share)
+    )
     payload = jnp.concatenate([query_send, kv_send], 1)
     got = lax.all_to_all(payload, "seq", split_axis=0, concat_axis=0, tiled=True)
     query_got = got[:, :query_share]
-    key_got = got[:, query_share : query_share + key_span]
-    value_got = got[:, query_share + key_span :]
+    kv_mine = got[:, query_share:]
+    kv_other = swapped(kv_mine, "seq", 0)
+    first_core = lax.axis_index("seq") % 2 == 0
+    key_got = jnp.where(first_core, kv_mine, kv_other)
+    value_got = jnp.where(first_core, kv_other, kv_mine)
     my_request = lax.axis_index("seq") // members
     length_now = jnp.sum(jnp.where(jnp.arange(requests) == my_request, lengths_all, 0))
     text_slot = jnp.arange(senders)[:, None] * txt_slice + within[None, :] - img_slice
@@ -135,8 +139,8 @@
         tiled=True,
     )
     attn_rows = (
-        answer_back.reshape(requests, halves, 2, query_share, head_share)
-        .transpose(1, 3, 0, 2, 4)
+        answer_back.reshape(requests, 2, halves, query_share, head_share)
+        .transpose(2, 3, 0, 1, 4)
         .reshape(rows_all, features)
     )
     tp_index = lax.axis_index("tp")

time: 179 us -> 171 us (0.955)
  waiting for transfers between devices: 60.5 us -> 23.8 us
  blocking collectives: 30.8 us -> 66 us
  starting transfers between devices: 18.7 us -> 9.48 us
  other arithmetic: 12.6 us -> 18 us
  local copies, waits for them, and re-layouts: 34.2 us -> 31.3 us
    all_to_all x1 -> x0, waiting for transfers between devices: 36.8 us -> none  [shards(): lax.all_to_all(payload, 'seq', split_axis=0, concat_axis=0, tiled=True)]
    all_to_all x0 -> x1, blocking collectives: none -> 35.2 us  [shards(): lax.all_to_all(payload, 'seq', split_axis=0, concat_axis=0, tiled=True)]
    all_to_all x1 -> x0, starting transfers between devices: 9.91 us -> none  [shards(): lax.all_to_all(payload, 'seq', split_axis=0, concat_axis=0, tiled=True)]
    reshape x2 -> x4, local copies, waits for them, and re-layouts: 1.04 us -> 3.83 us  [the longest x1 2.64 us: shards(): kv_send = jnp.stack([joined_k, joined_v], 3).transpose(1, 2, 3, 0, 4).res...]
    select_n x0 -> x1, other arithmetic: none -> 2.74 us  [shards(): value_got = jnp.where(first_core, kv_other, kv_mine)]
    unnamed x26 -> x34, local copies, waits for them, and re-layouts: 8.49 us -> 9.23 us
    ppermute x1 -> x2, waiting for transfers between devices: 4.38 us -> 4.41 us  [swapped(): lax.ppermute(value, axis, [(i, i ^ 1 << apart) for i in range(lax.axis_si...]
  transfers between devices with their start and end apart: 4 -> 4, of which waited for: 4 -> 3; matrix products, arithmetic and copies ran while one was open for 2% -> 2% of each run, Pallas kernels for 0% -> 0%
where the time goes in v4:
time: 171 us; the launch traced here: 170 us
  blocking collectives  66 us (39%)
  local copies, waits for them, and re-layouts  31.3 us (18%)
  waiting for transfers between devices  23.8 us (14%)
  matrix products  20.3 us (12%)
  other arithmetic  18 us (11%)
  starting transfers between devices  9.48 us (6%)
    all_to_all x1, blocking collectives, shards(): lax.all_to_all(payload, 'seq', split_axis=0, concat_axis=0, tiled=True)  35.2 us
    all_to_all x2, waiting for transfers between devices, reduce_rows(): got = lax.all_to_all(pieces, 'tp', split_axis=0, concat_axis=0, tiled=True)  19.3 us
    all_to_all x1, blocking collectives, shards(): lax.all_to_all(answer.reshape(senders, query_share, head_share), 'seq', s...  16.8 us
    all_gather x1, blocking collectives, shards(): lax.all_gather(mlp_mine, 'tp', axis=0, tiled=True)  14.1 us
    unnamed x34, local copies, waits for them, and re-layouts  9.23 us
    all_to_all x2, starting transfers between devices, reduce_rows(): got = lax.all_to_all(pieces, 'tp', split_axis=0, concat_axis=0, tiled=True)  8.66 us
    another operation x3, local copies, waits for them, and re-layouts  7.79 us
    dot_general x1, matrix products, attend(): jnp.einsum('rhqk,krhd->qrhd', weights, value_heads, preferred_element_typ...  4.9 us
  transfers between devices with their start and end apart: 4, of which 3 were waited for; matrix products, arithmetic and copies ran while one was open for 2% of the time, Pallas kernels for 0%

profile of v4, /device:TPU:4, one launch (start us, length us, event | category | flops | bytes accessed | tf_op | source)
XLA Modules:
  0.0 169.8 jit_solution(160840511749150728)
XLA Ops:
  0.6 0.0 copy-start
  0.7 1.1 bitcast_convert_fusion
  1.8 0.7 fusion.73
  2.5 0.2 convert_reduce_fusion.2
  2.7 0.3 multiply_reduce_fusion
  3.1 6.1 %copy.59 = bf16[1536,3,384]{0,2,1:T(8,128)(2,1)} copy(bf16[1536,3,384]{2,0,1:T(8,128)(2,1)} %param.20) | data formatting | bytes 7077888 | tf_op args[7]
  9.2 3.3 %convolution_convert_fusion.1 = bf16[256,1152]{1,0:T(8,128)(2,1)S(1)} fusion(bf16[1536,1152]{0,1:T(8,128)(2,1)} %bitcast.111, bf16[1,32,8,1536]{3,2,1,0:T(8,128)(2,1)S(1)} %copy-done.1, f32[8,1536]{1,0:T(8,128)S(1)} %get-tuple-element.22, f32[8,1536]{1,0:T(8,128)S(1)} %get-tuple-element.23, f32[32,8]{1,0:T(8,128)S(1)} %add_rsqrt_fusion, ...), kind=kOutput, calls=%fused_computation.10 | convolution fusion | flops 908623872 | bytes 5015552 | tf_op jit(solution)/shard_map/dot_general | solution.py:84
  12.5 0.0 copy-start.3
  12.5 0.8 fusion.93
  13.3 2.8 %concatenate.26 = bf16[32,8,2,1,192]{4,3,2,1,0:T(2,128)(2,1)} reshape(bf16[256,384]{1,0:T(8,128)(2,1)} %get-tuple-element.14) | data formatting | bytes 393216 | tf_op jit(solution)/shard_map/concatenate | solution.py:109
  16.1 1.1 concatenate.28
  17.2 0.1 convert_reduce_fusion.3
  17.3 0.2 fusion.49
  17.5 2.1 %copy.75 = bf16[192,8,2,384]{3,1,2,0:T(8,128)(2,1)S(1)} copy(bf16[192,8,2,384]{3,2,1,0:T(2,128)(2,1)} %bitcast.113) | data formatting | bytes 4718592
  19.7 0.6 convolution_convert_fusion.3
  20.3 0.1 concatenate.27
  20.4 0.1 concatenate.29
  20.5 3.4 %maximum_bitcast_fusion = bf16[8,2,2,37,192]{4,2,1,0,3:T(2,128)(2,1)} fusion(bf16[5,8,2,1,192]{4,3,2,1,0:T(2,128)(2,1)S(1)} %concatenate.29, bf16[32,8,2,1,192]{4,3,2,1,0:T(2,128)(2,1)} %concatenate.28, bf16[5,8,2,1,192]{4,3,2,1,0:T(2,128)(2,1)S(1)} %concatenate.27, bf16[32,8,2,1,192]{4,3,2,1,0:T(2,128)(2,1)} %concatenate.26), kind=kLoop, calls=%fused_computation.45 | loop fusion | flops 1818624 | bytes 909312 | tf_op jit(solution)/shard_map/transpose | solution.py:113
  23.9 2.6 %reshape.367 = bf16[32,37,192]{2,0,1:T(8,128)(2,1)} reshape(bf16[8,2,2,37,192]{4,2,1,0,3:T(2,128)(2,1)} %maximum_bitcast_fusion) | data formatting | bytes 909312 | tf_op jit(solution)/shard_map/reshape | solution.py:114
  26.5 1.1 reshape_reshape.4
  27.6 0.1 copy.60
  27.7 0.1 copy.65
  27.8 1.2 pad_maximum_fusion
  29.0 0.5 copy.66
  29.5 0.0 copy-start.15
  29.5 35.2 %all_to_all.20 = bf16[32,53,192]{2,1,0:T(8,128)(2,1)S(1)} all-to-all(bf16[32,53,192]{2,1,0:T(8,128)(2,1)S(1)} %copy.66), channel_id=1, replica_groups=mesh['cfg'=2,'seq'=32,'tp'=4] {'seq'}, dimensions={0} | all-to-all | bytes 1302528 | tf_op jit(solution)/shard_map/all_to_all | solution.py:117
  64.7 0.9 copy-done.2
  65.7 1.0 copy.67
  66.7 0.6 fusion.78
  67.3 0.7 fusion.77
  68.0 0.1 or.17
  68.2 1.0 reshape.369
  69.1 2.7 %broadcast_select_fusion.1 = (bf16[32,37,192]{2,1,0:T(8,128)(2,1)}, bf16[32,37,192]{2,1,0:T(8,128)(2,1)}) fusion(pred[]{:T(512)S(6)} %eq.41, bf16[32,37,192]{2,0,1:T(8,128)(2,1)} %collective-permute-done, bf16[32,53,192]{2,1,0:T(8,128)(2,1)} %copy-done.2), kind=kLoop, calls=%fused_computation.41 | loop fusion | flops 454656 | bytes 1818625 | tf_op jit(solution)/shard_map/jit(_where)/select_n | solution.py:123
  71.9 3.4 %reshape.370 = bf16[1184,3,64]{2,1,0:T(4,128)(2,1)} reshape(bf16[32,37,192]{2,1,0:T(8,128)(2,1)} %get-tuple-element.11) | data formatting | bytes 909312 | tf_op jit(solution)/shard_map/reshape.2
  75.3 3.4 %reshape.368 = bf16[1184,3,64]{2,1,0:T(4,128)(2,1)} reshape(bf16[32,37,192]{2,1,0:T(8,128)(2,1)} %get-tuple-element.10) | data formatting | bytes 909312 | tf_op jit(solution)/shard_map/reshape.6
  78.7 3.9 %fusion.95 = f32[3,512]{1,0:T(4,128)S(1)} fusion(pred[1184]{0:T(1024)(128)(4,1)S(1)} %or.17, bf16[1184,3,64]{2,1,0:T(4,128)(2,1)} %reshape.370, bf16[512,3,64]{2,1,0:T(4,128)(2,1)} %reshape.369), kind=kOutput, calls=%fused_computation.130 | convolution fusion | flops 240059552 | bytes 658592 | tf_op jit(solution)/shard_map/sub | solution.py:38
  82.6 4.9 %fusion.9 = bf16[512,1,3,64]{0,3,2,1:T(8,128)(2,1)S(1)} fusion(f32[3,512]{1,0:T(4,128)S(1)} %fusion.95, bf16[1184,3,64]{2,1,0:T(4,128)(2,1)} %reshape.368, pred[1184]{0:T(1024)(128)(4,1)S(1)} %or.17, bf16[1184,3,64]{2,1,0:T(4,128)(2,1)} %reshape.370, bf16[512,3,64]{2,1,0:T(4,128)(2,1)} %reshape.369), kind=kOutput, calls=%fused_computation.21 | convolution fusion | flops 474761888 | bytes 1309856 | tf_op jit(solution)/shard_map/rhqk,krhd->qrhd/dot_general | solution.py:40
  87.5 1.1 copy.73
  88.5 1.5 reshape_reshape.10
  90.0 16.8 %all_to_all.21 = bf16[32,16,192]{2,1,0:T(8,128)(2,1)S(1)} all-to-all(bf16[32,16,192]{2,1,0:T(8,128)(2,1)S(1)} %reshape_reshape.10), channel_id=1, replica_groups=mesh['cfg'=2,'seq'=32,'tp'=4] {'seq'}, dimensions={0} | all-to-all | bytes 393216 | tf_op jit(solution)/shard_map/all_to_all | solution.py:134
  106.8 0.3 copy.105
  107.1 0.8 reshape.372
  108.0 2.8 %convolution_convert_fusion.2 = bf16[256,1536]{1,0:T(8,128)(2,1)} fusion(bf16[256,384]{1,0:T(8,128)(2,1)} %reshape.372, bf16[384,1536]{1,0:T(8,128)(2,1)} %param.22), kind=kOutput, calls=%fused_computation.11 | convolution fusion | flops 302383104 | bytes 2162688 | tf_op jit(solution)/shard_map/dot_general | solution.py:148
  110.8 4.5 %all-to-all-start.2 = ((bf16[4,64,1536]{2,1,0:T(8,128)(2,1)}), bf16[4,64,1536]{2,1,0:T(8,128)(2,1)}, u32[]{:S(2)}, u32[]{:S(2)}) async-start(bf16[4,64,1536]{2,1,0:T(8,128)(2,1)} %bitcast.112), calls=%async_computation.2 | async-start | bytes 1572864 | tf_op jit(solution)/shard_map/all_to_all | solution.py:46
  115.3 1.3 convert_element_type.100
  116.6 9.9 %all-to-all-done.2 = bf16[4,64,1536]{2,1,0:T(8,128)(2,1)} async-done(((bf16[4,64,1536]{2,1,0:T(8,128)(2,1)}), bf16[4,64,1536]{2,1,0:T(8,128)(2,1)}, u32[]{:S(2)}, u32[]{:S(2)}) %all-to-all-start.2) | async-done | bytes 786464 | tf_op jit(solution)/shard_map/all_to_all | solution.py:46
  126.5 1.3 convert_reduce_fusion.1
  127.8 1.1 fusion.91
  128.9 0.2 multiply_reduce_fusion.2
  129.1 0.1 add_convert_fusion.2
  129.3 14.1 %all_gather.3 = bf16[32,8,1536]{2,1,0:T(8,128)(2,1)} all-gather(bf16[8,8,1536]{2,1,0:T(8,128)(2,1)S(1)} %add_convert_fusion.2), channel_id=1, replica_groups=mesh['cfg'=2,'seq'=32,'tp'=4] {'tp'}, dimensions={0}, use_global_device_ids=true | all-gather | bytes 983040 | tf_op jit(solution)/shard_map/all_gather | solution.py:152
  143.3 4.5 %convolution_convert_fusion = bf16[256,1536]{1,0:T(8,128)(2,1)} fusion(bf16[768,1536]{1,0:T(8,128)(2,1)S(1)} %copy-done, bf16[1536,768]{1,0:T(8,128)(2,1)} %param.23, bf16[32,8,1536]{2,1,0:T(8,128)(2,1)} %all_gather.3), kind=kOutput, calls=%fused_computation.9 | convolution fusion | flops 1210122240 | bytes 6291456 | tf_op jit(solution)/shard_map/dot_general | solution.py:156
  147.9 4.2 %all-to-all-start.3 = ((bf16[4,64,1536]{2,1,0:T(8,128)(2,1)}), bf16[4,64,1536]{2,1,0:T(8,128)(2,1)}, u32[]{:S(2)}, u32[]{:S(2)}) async-start(bf16[4,64,1536]{2,1,0:T(8,128)(2,1)} %bitcast.117), calls=%async_computation.3 | async-start | bytes 1572864 | tf_op jit(solution)/shard_map/all_to_all | solution.py:46
  152.1 0.0 copy-start.14
  152.2 9.5 %all-to-all-done.3 = bf16[4,64,1536]{2,1,0:T(8,128)(2,1)} async-done(((bf16[4,64,1536]{2,1,0:T(8,128)(2,1)}), bf16[4,64,1536]{2,1,0:T(8,128)(2,1)}, u32[]{:S(2)}, u32[]{:S(2)}) %all-to-all-start.3) | async-done | bytes 786464 | tf_op jit(solution)/shard_map/all_to_all | solution.py:46
  161.6 1.3 convert_reduce_fusion
  162.9 0.1 fusion.89
  163.0 0.2 multiply_reduce_fusion.1
  163.3 0.3 fusion.53
  163.5 0.1 constant_dynamic-slice_fusion
  163.6 0.8 collective-permute-start.1
  164.4 0.2 select_reduce_fusion
  164.7 4.4 %collective-permute-done.1 = f32[8,8,32]{2,1,0:T(8,128)S(1)} collective-permute-done((f32[8,8,32]{2,1,0:T(8,128)S(1)}, f32[8,8,32]{2,1,0:T(8,128)S(1)}, u32[]{:S(2)}, u32[]{:S(2)}) %collective-permute-start.1) | collective-permute-done | bytes 8224 | tf_op jit(solution)/shard_map/ppermute | solution.py:16
  169.1 0.7 multiply_add_fusion
  (45 shorter events, 0.2 us)
Async XLA Ops:
  0.6 142.7 %copy-start = (bf16[768,1536]{1,0:T(8,128)(2,1)S(1)}, bf16[768,1536]{1,0:T(8,128)(2,1)}, u32[]{:S(2)}) copy-start(bf16[768,1536]{1,0:T(8,128)(2,1)} %param.24) | copy-start | bytes 7077892
  0.6 1.9 %copy-start.1 = (bf16[1,32,8,1536]{3,2,1,0:T(8,128)(2,1)S(1)}, bf16[1,32,8,1536]{3,2,1,0:T(8,128)(2,1)}, u32[]{:S(2)}) copy-start(bf16[1,32,8,1536]{3,2,1,0:T(8,128)(2,1)} %param.13) | copy-start | bytes 2359300
  12.5 4.7 %copy-start.3 = (bf16[1,5,8,1536]{3,2,1,0:T(8,128)(2,1)S(1)}, bf16[1,5,8,1536]{3,2,1,0:T(8,128)(2,1)}, u32[]{:S(2)}) copy-start(bf16[1,5,8,1536]{3,2,1,0:T(8,128)(2,1)} %param.14) | copy-start | bytes 368644
  17.5 2.2 %copy-start.10 = (f32[8,1536]{1,0:T(8,128)S(1)}, f32[8,1536]{1,0:T(8,128)}, u32[]{:S(2)}) copy-start(f32[8,1536]{1,0:T(8,128)} %get-tuple-element.20) | copy-start | bytes 147460
  17.5 2.2 %copy-start.11 = (f32[8,1536]{1,0:T(8,128)S(1)}, f32[8,1536]{1,0:T(8,128)}, u32[]{:S(2)}) copy-start(f32[8,1536]{1,0:T(8,128)} %get-tuple-element.21) | copy-start | bytes 147460
  29.5 37.2 %copy-start.15 = (s32[1,8]{1,0:T(1,128)S(1)}, s32[1,8]{1,0:T(1,128)}, u32[]{:S(2)}) copy-start(s32[1,8]{1,0:T(1,128)} %param.16) | copy-start | bytes 100
  64.7 0.9 copy-start.2
  65.7 2.5 %slice-start = ((bf16[32,53,192]{2,1,0:T(8,128)(2,1)}), bf16[32,16,192]{2,1,0:T(8,128)(2,1)S(1)}, s32[]{:S(2)}) async-start(bf16[32,53,192]{2,1,0:T(8,128)(2,1)} %copy-done.2), calls=%async_computation.4 | async-start | bytes 524288 | tf_op jit(solution)/shard_map/slice | solution.py:118
  66.7 2.5 %collective-permute-start = (bf16[32,37,192]{2,0,1:T(8,128)(2,1)}, bf16[32,37,192]{2,0,1:T(8,128)(2,1)}, u32[]{:S(2)}, u32[]{:S(2)}) collective-permute-start(bf16[32,37,192]{2,0,1:T(8,128)(2,1)} %copy.67), channel_id=1, source_target_pairs={{0,4},{4,0},{8,12},{12,8},{16,20},{20,16},{24,28},{28,24},{32,36},... | collective-permute-start | bytes 1363976 | tf_op jit(solution)/shard_map/ppermute | solution.py:16
  110.8 15.7 %all-to-all-start.2 = ((bf16[4,64,1536]{2,1,0:T(8,128)(2,1)}), bf16[4,64,1536]{2,1,0:T(8,128)(2,1)}, u32[]{:S(2)}, u32[]{:S(2)}) async-start(bf16[4,64,1536]{2,1,0:T(8,128)(2,1)} %bitcast.112), calls=%async_computation.2 | async-start | bytes 1572864 | tf_op jit(solution)/shard_map/all_to_all | solution.py:46
  115.3 12.5 %copy-start.4 = (f32[8,1536]{1,0:T(8,128)S(1)}, f32[8,1536]{1,0:T(8,128)}, u32[]{:S(2)}) copy-start(f32[8,1536]{1,0:T(8,128)} %get-tuple-element.24) | copy-start | bytes 147460
  116.6 12.5 %copy-start.8 = (f32[8,1536]{1,0:T(8,128)S(1)}, f32[8,1536]{1,0:T(8,128)}, u32[]{:S(2)}) copy-start(f32[8,1536]{1,0:T(8,128)} %get-tuple-element.17) | copy-start | bytes 147460
  116.6 12.5 %copy-start.9 = (f32[8,1536]{1,0:T(8,128)S(1)}, f32[8,1536]{1,0:T(8,128)}, u32[]{:S(2)}) copy-start(f32[8,1536]{1,0:T(8,128)} %get-tuple-element.18) | copy-start | bytes 147460
  143.3 8.8 %copy-start.13 = (s32[8]{0:T(128)S(1)}, s32[8]{0:T(128)}, u32[]{:S(2)}) copy-start(s32[8]{0:T(128)} %param.17) | copy-start | bytes 100
  147.9 13.7 %all-to-all-start.3 = ((bf16[4,64,1536]{2,1,0:T(8,128)(2,1)}), bf16[4,64,1536]{2,1,0:T(8,128)(2,1)}, u32[]{:S(2)}, u32[]{:S(2)}) async-start(bf16[4,64,1536]{2,1,0:T(8,128)(2,1)} %bitcast.117), calls=%async_computation.3 | async-start | bytes 1572864 | tf_op jit(solution)/shard_map/all_to_all | solution.py:46
  152.1 11.2 %copy-start.5 = (bf16[1536,64]{0,1:T(8,128)(2,1)S(1)}, bf16[1536,64]{0,1:T(8,128)(2,1)}, u32[]{:S(2)}) copy-start(bf16[1536,64]{0,1:T(8,128)(2,1)} %param.25) | copy-start | bytes 589828
  152.1 11.2 %copy-start.6 = (f32[8,1536]{1,0:T(8,128)S(1)}, f32[8,1536]{1,0:T(8,128)}, u32[]{:S(2)}) copy-start(f32[8,1536]{1,0:T(8,128)} %get-tuple-element.15) | copy-start | bytes 147460
  152.1 11.2 %copy-start.7 = (f32[8,1536]{1,0:T(8,128)S(1)}, f32[8,1536]{1,0:T(8,128)}, u32[]{:S(2)}) copy-start(f32[8,1536]{1,0:T(8,128)} %get-tuple-element.16) | copy-start | bytes 147460
  152.1 12.3 %copy-start.14 = (f32[9]{0:T(128)S(1)}, f32[9]{0:T(128)}, u32[]{:S(2)}) copy-start(f32[9]{0:T(128)} %param.18) | copy-start | bytes 112
  152.2 16.9 %copy-start.12 = (f32[8,8,32]{2,1,0:T(8,128)S(1)}, f32[8,8,32]{2,1,0:T(8,128)}, u32[]{:S(2)}) copy-start(f32[8,8,32]{2,1,0:T(8,128)} %param.19) | copy-start | bytes 24580
  163.6 5.5 %collective-permute-start.1 = (f32[8,8,32]{2,1,0:T(8,128)S(1)}, f32[8,8,32]{2,1,0:T(8,128)S(1)}, u32[]{:S(2)}, u32[]{:S(2)}) collective-permute-start(f32[8,8,32]{2,1,0:T(8,128)S(1)} %constant_dynamic-slice_fusion), channel_id=1, source_target_pairs={{0,128},{128,0},{1,129},{129,1},{2,130},{130,2},{3,131},{131,3},{4... | collective-permute-start | bytes 24584 | tf_op jit(solution)/shard_map/ppermute | solution.py:16

commit v5 on v4

--- a/solution.py
+++ b/solution.py
@@ -3,6 +3,7 @@
 import jax
 import jax.numpy as jnp
 from jax import lax
+from jax.experimental import pallas as pl
 from jax.sharding import PartitionSpec as P
 
 HEAD_DIM = 64
@@ -25,32 +26,40 @@
     return (layer_norm(values) * (1.0 + scale_mul) + shift_add).astype(jnp.bfloat16)
 
 
-def attend(queries, keys_in, values_in, key_valid):
-    heads = queries.shape[2] // HEAD_DIM
-    query_heads = queries.reshape(queries.shape[0], queries.shape[1], heads, HEAD_DIM)
-    key_heads = keys_in.reshape(keys_in.shape[0], keys_in.shape[1], heads, HEAD_DIM)
-    value_heads = values_in.reshape(values_in.shape[0], values_in.shape[1], heads, HEAD_DIM)
-    scores = jnp.einsum(
-        "qrhd,krhd->rhqk", query_heads, key_heads, preferred_element_type=jnp.float32
-    ) * (1.0 / math.sqrt(HEAD_DIM))
-    scores = jnp.where(key_valid[:, None, None, :], scores, -jnp.inf)
-    row_max = jnp.max(scores, -1, keepdims=True)
-    exp_scores = jnp.exp(scores - row_max)
-    weights = (exp_scores / jnp.sum(exp_scores, -1, keepdims=True)).astype(jnp.bfloat16)
-    result = jnp.einsum("rhqk,krhd->qrhd", weights, value_heads, preferred_element_type=jnp.float32)
-    return result.astype(jnp.bfloat16).reshape(queries.shape)
+def attention_kernel(q_ref, k_ref, v_ref, valid_ref, o_ref):
+    queries = q_ref[...]
+    keys = k_ref[...]
+    values = v_ref[...]
+    valid = valid_ref[...] > 0.5
+    width = queries.shape[1]
+    lane_head = lax.broadcasted_iota(jnp.int32, (1, width), 1) // HEAD_DIM
+    result = jnp.zeros(o_ref.shape, jnp.float32)
+    for head in range(width // HEAD_DIM):
+        chosen = lane_head == head
+        query_head = jnp.where(chosen, queries, jnp.zeros_like(queries))
+        scores = lax.dot_general(
+            query_head, keys, (((1,), (1,)), ((), ())), preferred_element_type=jnp.float32
+        ) * (1.0 / math.sqrt(HEAD_DIM))
+        scores = jnp.where(valid, scores, -jnp.inf)
+        row_max = jnp.max(scores, axis=1, keepdims=True)
+        exp_scores = jnp.exp(scores - row_max)
+        total = jnp.sum(exp_scores, axis=1, keepdims=True)
+        weights = (exp_scores / total).astype(jnp.bfloat16)
+        mixed = jnp.dot(weights, values, preferred_element_type=jnp.float32)
+        result = jnp.where(chosen, mixed, result)
+    o_ref[...] = result.astype(o_ref.dtype)
+
+def attend_kernel(queries, keys, values, valid):
+    return pl.pallas_call(
+        attention_kernel,
+        out_shape=jax.ShapeDtypeStruct(queries.shape, jnp.bfloat16),
+    )(queries, keys, values, valid)
 
 
 def reduce_rows(partial, parties):
     pieces = partial.reshape(parties, partial.shape[0] // parties, partial.shape[1])
     got = lax.all_to_all(pieces, "tp", split_axis=0, concat_axis=0, tiled=True)
     return jnp.sum(got.astype(jnp.float32), 0)
-
-
-def spread(image_part, text_part, members):
-    joined = jnp.concatenate([image_part, text_part], 0).transpose(1, 0, 2)
-    widened = jnp.broadcast_to(joined[:, None], (joined.shape[0], members) + joined.shape[1:])
-    return widened.reshape(joined.shape[0] * members, joined.shape[1], joined.shape[2])
 
 
 def shards(
@@ -96,7 +105,6 @@
     keys_txt = text_kv[:, :features].reshape(txt_slice, requests, features)
     vals_txt = text_kv[:, features:].reshape(txt_slice, requests, features)
     key_span = img_slice + txt_slice
-    within = jnp.arange(key_span)
     senders = requests * members
     halves = members // 2
     query_share = img_slice // halves
@@ -123,13 +131,21 @@
     value_got = jnp.where(first_core, kv_other, kv_mine)
     my_request = lax.axis_index("seq") // members
     length_now = jnp.sum(jnp.where(jnp.arange(requests) == my_request, lengths_all, 0))
-    text_slot = jnp.arange(senders)[:, None] * txt_slice + within[None, :] - img_slice
-    key_valid = (within[None, :] < img_slice) | (text_slot < length_now)
-    answer = attend(
-        query_got.reshape(senders * query_share, 1, head_share),
-        key_got.reshape(senders * key_span, 1, head_share),
-        value_got.reshape(senders * key_span, 1, head_share),
-        key_valid.reshape(1, senders * key_span),
+    padded_span = -(-key_span // 8) * 8
+    slot = jnp.arange(padded_span)
+    text_slot = jnp.arange(senders)[:, None] * txt_slice + slot[None, :] - img_slice
+    key_valid = (slot[None, :] < img_slice) | ((slot[None, :] < key_span) & (text_slot < length_now))
+
+    def padded(block):
+        return jnp.pad(block, ((0, 0), (0, padded_span - key_span), (0, 0))).reshape(
+            senders * padded_span, head_share
+        )
+
+    answer = attend_kernel(
+        query_got.reshape(senders * query_share, head_share),
+        padded(key_got),
+        padded(value_got),
+        key_valid.astype(jnp.float32).reshape(1, senders * padded_span),
     )
     answer_back = lax.all_to_all(
         answer.reshape(senders, query_share, head_share),

time: 171 us -> 157 us (0.918)
  matrix products: 20.3 us -> 11.3 us
  local copies, waits for them, and re-layouts: 31.3 us -> 24.9 us
  Pallas kernels: 0 us -> 6.18 us
  other arithmetic: 18 us -> 14.1 us
    another operation x4 -> x0, local copies, waits for them, and re-layouts: 9.29 us -> none
    pallas_call x0 -> x1, Pallas kernels: none -> 6.18 us  [attend_kernel(): pl.pallas_call(attention_kernel, out_shape=jax.ShapeDtypeStruct(queries.s...]
    dot_general x1 -> x0, matrix products: 4.9 us -> none  [attend(): jnp.einsum('rhqk,krhd->qrhd', weights, value_heads, preferred_element_typ...]
    sub x1 -> x0, matrix products: 3.85 us -> none  [attend(): exp_scores = jnp.exp(scores - row_max)]
    reshape x3 -> x0, local copies, waits for them, and re-layouts: 3 us -> none  [the longest x1 2.64 us: shards(): kv_send = jnp.stack([joined_k, joined_v], 3).transpose(1, 2, 3, 0, 4).res...]
    pad x0 -> x2, local copies, waits for them, and re-layouts: none -> 1.92 us  [padded(): jnp.pad(block, ((0, 0), (0, padded_span - key_span), (0, 0)))]
    unnamed x34 -> x26, local copies, waits for them, and re-layouts: 9.23 us -> 9.61 us
  transfers between devices with their start and end apart: 4 -> 4, of which waited for: 3 -> 3; matrix products, arithmetic and copies ran while one was open for 2% -> 3% of each run, Pallas kernels for 0% -> 0%
where the time goes in v5:
time: 157 us; the launch traced here: 156 us
  blocking collectives  65.5 us (42%)
  local copies, waits for them, and re-layouts  24.9 us (16%)
  waiting for transfers between devices  23.9 us (15%)
  other arithmetic  14.1 us (9%)
  matrix products  11.3 us (7%)
  starting transfers between devices  8.92 us (6%)
  Pallas kernels  6.18 us (4%)
    all_to_all x1, blocking collectives, shards(): lax.all_to_all(payload, 'seq', split_axis=0, concat_axis=0, tiled=True)  35.2 us
    all_to_all x2, waiting for transfers between devices, reduce_rows(): got = lax.all_to_all(pieces, 'tp', split_axis=0, concat_axis=0, tiled=True)  19.5 us
    all_to_all x1, blocking collectives, shards(): lax.all_to_all(answer.reshape(senders, query_share, head_share), 'seq', s...  17 us
    all_gather x1, blocking collectives, shards(): lax.all_gather(mlp_mine, 'tp', axis=0, tiled=True)  13.3 us
    unnamed x26, local copies, waits for them, and re-layouts  9.61 us
    all_to_all x2, starting transfers between devices, reduce_rows(): got = lax.all_to_all(pieces, 'tp', split_axis=0, concat_axis=0, tiled=True)  8.09 us
    pallas_call x1, Pallas kernels, attend_kernel(): pl.pallas_call(attention_kernel, out_shape=jax.ShapeDtypeStruct(queries.s...  6.18 us
    ppermute x2, waiting for transfers between devices, swapped(): lax.ppermute(value, axis, [(i, i ^ 1 << apart) for i in range(lax.axis_si...  4.39 us
  transfers between devices with their start and end apart: 4, of which 3 were waited for; matrix products, arithmetic and copies ran while one was open for 3% of the time, Pallas kernels for 0%

profile of v5, /device:TPU:4, one launch (start us, length us, event | category | flops | bytes accessed | tf_op | source)
XLA Modules:
  0.0 155.7 jit_solution(8656383568428471954)
XLA Ops:
  0.6 0.0 copy-start
  0.7 2.3 %copy.45 = bf16[192,8,2,384]{3,1,2,0:T(8,128)(2,1)S(1)} copy(bf16[192,8,2,384]{3,2,1,0:T(2,128)(2,1)} %bitcast.111) | data formatting | bytes 4718592
  3.0 0.0 copy-start.3
  3.0 0.7 fusion.45
  3.7 0.2 copy-done.3
  3.9 0.1 convert_reduce_fusion.3
  4.0 0.2 fusion.29
  4.2 0.6 convolution_convert_fusion.3
  4.8 0.6 fusion.62
  5.4 0.7 concatenate.23
  6.1 6.1 %copy.38 = bf16[1536,3,384]{0,2,1:T(8,128)(2,1)} copy(bf16[1536,3,384]{2,0,1:T(8,128)(2,1)} %param.20) | data formatting | bytes 7077888 | tf_op args[7]
  12.2 0.0 copy-done.1
  12.2 0.2 convert_reduce_fusion.2
  12.4 0.3 multiply_reduce_fusion
  12.8 3.3 %convolution_convert_fusion.1 = bf16[256,1152]{1,0:T(8,128)(2,1)S(1)} fusion(bf16[1536,1152]{0,1:T(8,128)(2,1)} %bitcast.106, bf16[1,32,8,1536]{3,2,1,0:T(8,128)(2,1)S(1)} %copy-done.1, f32[8,1536]{1,0:T(8,128)S(1)} %get-tuple-element.22, f32[8,1536]{1,0:T(8,128)S(1)} %get-tuple-element.23, f32[32,8]{1,0:T(8,128)S(1)} %add_rsqrt_fusion, ...), kind=kOutput, calls=%fused_computation.1 | convolution fusion | flops 908623872 | bytes 5015552 | tf_op jit(solution)/shard_map/dot_general | solution.py:93
  16.1 0.8 fusion.61
  16.9 1.1 concatenate.22
  18.0 1.5 concatenate.20
  19.5 1.8 %concatenate.19 = bf16[32,8,2,1,192]{4,2,1,0,3:T(2,128)(2,1)} reshape(bf16[256,384]{1,0:T(8,128)(2,1)} %get-tuple-element.14) | data formatting | bytes 393216 | tf_op jit(solution)/shard_map/concatenate | solution.py:117
  21.3 2.0 %maximum_bitcast_fusion = bf16[8,2,2,37,192]{4,1,0,3,2:T(2,128)(2,1)S(1)} fusion(bf16[5,8,2,1,192]{4,2,1,0,3:T(2,128)(2,1)} %concatenate.23, bf16[32,8,2,1,192]{4,2,1,0,3:T(2,128)(2,1)S(1)} %concatenate.22, bf16[5,8,2,1,192]{4,2,1,0,3:T(2,128)(2,1)} %concatenate.20, bf16[32,8,2,1,192]{4,2,1,0,3:T(2,128)(2,1)} %concatenate.19), kind=kLoop, calls=%fused_computation.29 | loop fusion | flops 681984 | bytes 909312 | tf_op jit(solution)/shard_map/transpose | solution.py:121
  23.4 1.0 copy.40
  24.4 1.1 reshape_reshape.3
  25.5 0.1 copy.39
  25.6 1.2 pad_maximum_fusion
  26.9 35.2 %all_to_all.20 = bf16[32,53,192]{2,1,0:T(8,128)(2,1)S(1)} all-to-all(bf16[32,53,192]{2,1,0:T(8,128)(2,1)S(1)} %pad_maximum_fusion), channel_id=1, replica_groups=mesh['cfg'=2,'seq'=32,'tp'=4] {'seq'}, dimensions={0} | all-to-all | bytes 1302528 | tf_op jit(solution)/shard_map/all_to_all | solution.py:125
  62.0 0.9 copy-done.2
  63.0 1.0 copy.41
  64.0 0.0 collective-permute-start
  64.0 0.0 copy-done.11
  64.0 0.6 fusion.52
  64.6 0.7 fusion.51
  65.4 0.7 reshape.396.valid_ref
  66.1 1.7 %slice.78 = bf16[32,16,192]{2,1,0:T(8,128)(2,1)} slice(bf16[32,53,192]{2,1,0:T(8,128)(2,1)} %copy-done.2), slice={[0:32], [0:16], [0:192]} | slice | bytes 393216 | tf_op jit(solution)/shard_map/slice | solution.py:126
  67.8 0.0 collective-permute-done
  67.8 1.7 %broadcast_select_fusion = (bf16[32,37,192]{2,1,0:T(8,128)(2,1)S(1)}, bf16[32,37,192]{2,1,0:T(8,128)(2,1)S(1)}) fusion(pred[]{:T(512)S(6)} %eq.41, bf16[32,37,192]{2,0,1:T(8,128)(2,1)} %collective-permute-done, bf16[32,53,192]{2,1,0:T(8,128)(2,1)} %copy-done.2), kind=kLoop, calls=%fused_computation.27 | loop fusion | flops 454656 | bytes 1818625 | tf_op jit(solution)/shard_map/jit(_where)/select_n | solution.py:131
  69.4 1.0 pad.7
  70.4 1.0 pad.8
  71.3 6.2 %shard_map.140 = bf16[512,192]{1,0:T(8,128)(2,1)} custom-call(bf16[512,192]{1,0:T(8,128)(2,1)} %bitcast.112, bf16[1280,192]{1,0:T(8,128)(2,1)} %bitcast.108, bf16[1280,192]{1,0:T(8,128)(2,1)} %bitcast.110, f32[1,1280]{1,0:T(1,128)} %reshape.396.valid_ref), custom_call_target="tpu_custom_call" | custom-call | tf_op jit(solution)/shard_map/pallas_call | solution.py:53
  77.5 17.0 %all_to_all.21 = bf16[32,16,192]{2,1,0:T(8,128)(2,1)S(1)} all-to-all(bf16[32,16,192]{2,1,0:T(8,128)(2,1)} %bitcast.113), channel_id=1, replica_groups=mesh['cfg'=2,'seq'=32,'tp'=4] {'seq'}, dimensions={0} | all-to-all | bytes 393216 | tf_op jit(solution)/shard_map/all_to_all | solution.py:150
  94.5 0.3 copy.44
  94.8 0.8 reshape.388
  95.6 2.8 %convolution_convert_fusion.2 = bf16[256,1536]{1,0:T(8,128)(2,1)} fusion(bf16[256,384]{1,0:T(8,128)(2,1)} %reshape.388, bf16[384,1536]{1,0:T(8,128)(2,1)} %param.22), kind=kOutput, calls=%fused_computation.2 | convolution fusion | flops 302383104 | bytes 2162688 | tf_op jit(solution)/shard_map/dot_general | solution.py:164
  98.5 4.5 %all-to-all-start.2 = ((bf16[4,64,1536]{2,1,0:T(8,128)(2,1)}), bf16[4,64,1536]{2,1,0:T(8,128)(2,1)}, u32[]{:S(2)}, u32[]{:S(2)}) async-start(bf16[4,64,1536]{2,1,0:T(8,128)(2,1)} %bitcast.107), calls=%async_computation.2 | async-start | bytes 1572864 | tf_op jit(solution)/shard_map/all_to_all | solution.py:61
  103.0 1.3 convert_element_type.100
  104.3 10.1 %all-to-all-done.2 = bf16[4,64,1536]{2,1,0:T(8,128)(2,1)} async-done(((bf16[4,64,1536]{2,1,0:T(8,128)(2,1)}), bf16[4,64,1536]{2,1,0:T(8,128)(2,1)}, u32[]{:S(2)}, u32[]{:S(2)}) %all-to-all-start.2) | async-done | bytes 786464 | tf_op jit(solution)/shard_map/all_to_all | solution.py:61
  114.4 1.3 convert_reduce_fusion.1
  115.7 1.1 fusion.59
  116.8 0.2 multiply_reduce_fusion.2
  117.0 0.1 add_convert_fusion.2
  117.2 13.3 %all_gather.3 = bf16[32,8,1536]{2,1,0:T(8,128)(2,1)S(1)} all-gather(bf16[8,8,1536]{2,1,0:T(8,128)(2,1)S(1)} %add_convert_fusion.2), channel_id=1, replica_groups=mesh['cfg'=2,'seq'=32,'tp'=4] {'tp'}, dimensions={0}, use_global_device_ids=true | all-gather | bytes 983040 | tf_op jit(solution)/shard_map/all_gather | solution.py:168
  130.5 4.3 %convolution_convert_fusion = bf16[256,1536]{1,0:T(8,128)(2,1)} fusion(bf16[768,1536]{1,0:T(8,128)(2,1)S(1)} %copy-done, bf16[1536,768]{1,0:T(8,128)(2,1)} %param.23, bf16[32,8,1536]{2,1,0:T(8,128)(2,1)S(1)} %all_gather.3), kind=kOutput, calls=%fused_computation | convolution fusion | flops 1210122240 | bytes 6291456 | tf_op jit(solution)/shard_map/dot_general | solution.py:172
  134.8 3.6 %all-to-all-start.3 = ((bf16[4,64,1536]{2,1,0:T(8,128)(2,1)}), bf16[4,64,1536]{2,1,0:T(8,128)(2,1)S(1)}, u32[]{:S(2)}, u32[]{:S(2)}) async-start(bf16[4,64,1536]{2,1,0:T(8,128)(2,1)} %bitcast.117), calls=%async_computation.3 | async-start | bytes 1572864 | tf_op jit(solution)/shard_map/all_to_all | solution.py:61
  138.5 0.0 copy-start.10
  138.5 9.4 %all-to-all-done.3 = bf16[4,64,1536]{2,1,0:T(8,128)(2,1)S(1)} async-done(((bf16[4,64,1536]{2,1,0:T(8,128)(2,1)}), bf16[4,64,1536]{2,1,0:T(8,128)(2,1)S(1)}, u32[]{:S(2)}, u32[]{:S(2)}) %all-to-all-start.3) | async-done | bytes 786464 | tf_op jit(solution)/shard_map/all_to_all | solution.py:61
  147.9 0.1 convert_reduce_fusion
  148.0 0.0 copy-start.8
  148.0 0.9 fusion.57
  149.0 0.2 multiply_reduce_fusion.1
  149.2 0.3 fusion.33
  149.4 0.1 constant_dynamic-slice_fusion
  149.5 0.8 collective-permute-start.1
  150.3 0.2 select_reduce_fusion
  150.6 4.4 %collective-permute-done.1 = f32[8,8,32]{2,1,0:T(8,128)S(1)} collective-permute-done((f32[8,8,32]{2,1,0:T(8,128)S(1)}, f32[8,8,32]{2,1,0:T(8,128)S(1)}, u32[]{:S(2)}, u32[]{:S(2)}) %collective-permute-start.1) | collective-permute-done | bytes 8224 | tf_op jit(solution)/shard_map/ppermute | solution.py:17
  155.0 0.7 multiply_add_fusion
  (30 shorter events, 0.2 us)
Async XLA Ops:
  0.6 129.9 %copy-start = (bf16[768,1536]{1,0:T(8,128)(2,1)S(1)}, bf16[768,1536]{1,0:T(8,128)(2,1)}, u32[]{:S(2)}) copy-start(bf16[768,1536]{1,0:T(8,128)(2,1)} %param.24) | copy-start | bytes 7077892
  0.6 2.3 %copy-start.4 = (bf16[1,8,10,1536]{3,1,2,0:T(8,128)(2,1)S(1)}, bf16[1,8,10,1536]{3,1,2,0:T(8,128)(2,1)}, u32[]{:S(2)}) copy-start(bf16[1,8,10,1536]{3,1,2,0:T(8,128)(2,1)} %param.15) | copy-start | bytes 737284
  3.0 0.9 copy-start.3
  6.1 6.2 %copy-start.1 = (bf16[1,32,8,1536]{3,2,1,0:T(8,128)(2,1)S(1)}, bf16[1,32,8,1536]{3,2,1,0:T(8,128)(2,1)}, u32[]{:S(2)}) copy-start(bf16[1,32,8,1536]{3,2,1,0:T(8,128)(2,1)} %param.13) | copy-start | bytes 2359300
  62.0 0.9 copy-start.2
  63.0 1.0 copy-start.11
  64.0 3.8 %collective-permute-start = (bf16[32,37,192]{2,0,1:T(8,128)(2,1)}, bf16[32,37,192]{2,0,1:T(8,128)(2,1)}, u32[]{:S(2)}, u32[]{:S(2)}) collective-permute-start(bf16[32,37,192]{2,0,1:T(8,128)(2,1)} %copy.41), channel_id=1, source_target_pairs={{0,4},{4,0},{8,12},{12,8},{16,20},{20,16},{24,28},{28,24},{32,36},... | collective-permute-start | bytes 1363976 | tf_op jit(solution)/shard_map/ppermute | solution.py:17
  98.5 15.9 %all-to-all-start.2 = ((bf16[4,64,1536]{2,1,0:T(8,128)(2,1)}), bf16[4,64,1536]{2,1,0:T(8,128)(2,1)}, u32[]{:S(2)}, u32[]{:S(2)}) async-start(bf16[4,64,1536]{2,1,0:T(8,128)(2,1)} %bitcast.107), calls=%async_computation.2 | async-start | bytes 1572864 | tf_op jit(solution)/shard_map/all_to_all | solution.py:61
  134.8 3.6 %copy-start.9 = (s32[8]{0:T(128)S(1)}, s32[8]{0:T(128)}, u32[]{:S(2)}) copy-start(s32[8]{0:T(128)} %param.17) | copy-start | bytes 100
  134.8 13.1 %all-to-all-start.3 = ((bf16[4,64,1536]{2,1,0:T(8,128)(2,1)}), bf16[4,64,1536]{2,1,0:T(8,128)(2,1)S(1)}, u32[]{:S(2)}, u32[]{:S(2)}) async-start(bf16[4,64,1536]{2,1,0:T(8,128)(2,1)} %bitcast.117), calls=%async_computation.3 | async-start | bytes 1572864 | tf_op jit(solution)/shard_map/all_to_all | solution.py:61
  138.5 11.9 %copy-start.10 = (f32[9]{0:T(128)S(1)}, f32[9]{0:T(128)}, u32[]{:S(2)}) copy-start(f32[9]{0:T(128)} %param.18) | copy-start | bytes 112
  147.9 1.3 copy-start.5
  147.9 1.3 copy-start.6
  147.9 1.3 copy-start.7
  148.0 7.0 %copy-start.8 = (f32[8,8,32]{2,1,0:T(8,128)S(1)}, f32[8,8,32]{2,1,0:T(8,128)}, u32[]{:S(2)}) copy-start(f32[8,8,32]{2,1,0:T(8,128)} %param.19) | copy-start | bytes 24580
  149.5 5.5 %collective-permute-start.1 = (f32[8,8,32]{2,1,0:T(8,128)S(1)}, f32[8,8,32]{2,1,0:T(8,128)S(1)}, u32[]{:S(2)}, u32[]{:S(2)}) collective-permute-start(f32[8,8,32]{2,1,0:T(8,128)S(1)} %constant_dynamic-slice_fusion), channel_id=1, source_target_pairs={{0,128},{128,0},{1,129},{129,1},{2,130},{130,2},{3,131},{131,3},{4... | collective-permute-start | bytes 24584 | tf_op jit(solution)/shard_map/ppermute | solution.py:17

commit v6 on v5

--- a/solution.py
+++ b/solution.py
@@ -56,10 +56,31 @@
     )(queries, keys, values, valid)
 
 
+def shifted(value, axis, step):
+    size = lax.axis_size(axis)
+    return lax.ppermute(value, axis, [(i, (i + step) % size) for i in range(size)])
+
+
 def reduce_rows(partial, parties):
     pieces = partial.reshape(parties, partial.shape[0] // parties, partial.shape[1])
-    got = lax.all_to_all(pieces, "tp", split_axis=0, concat_axis=0, tiled=True)
-    return jnp.sum(got.astype(jnp.float32), 0)
+    me = lax.axis_index("tp")
+    total = lax.dynamic_index_in_dim(pieces, me, 0, False).astype(jnp.float32)
+    for step in range(1, parties):
+        sent = lax.dynamic_index_in_dim(pieces, (me + step) % parties, 0, False)
+        total = total + shifted(sent, "tp", step).astype(jnp.float32)
+    return total
+
+
+def gather_blocks(block, parties):
+    return jnp.stack([block] + [shifted(block, "tp", step) for step in range(1, parties)], 0)
+
+
+def return_blocks(partial, parties):
+    pieces = partial.reshape(parties, partial.shape[0] // parties, partial.shape[1])
+    total = pieces[0].astype(jnp.float32)
+    for step in range(1, parties):
+        total = total + shifted(pieces[step], "tp", -step).astype(jnp.float32)
+    return total
 
 
 def shards(
@@ -165,12 +186,12 @@
     attn_mixed = reduce_rows(attn_part, parties).reshape(portion, requests, model_width)
     after_attn = resident_mine + adaptive[:, 2] * attn_mixed
     mlp_mine = modulate(after_attn, adaptive[:, 3], adaptive[:, 4])
-    mlp_in = lax.all_gather(mlp_mine, "tp", axis=0, tiled=True).reshape(rows_all, model_width)
+    mlp_in = gather_blocks(mlp_mine, parties).reshape(rows_all, model_width)
     hidden = jax.nn.gelu(
         jnp.dot(mlp_in, w_up, preferred_element_type=jnp.float32), approximate=True
     ).astype(jnp.bfloat16)
     mlp_part = jnp.dot(hidden, w_down, preferred_element_type=jnp.float32).astype(jnp.bfloat16)
-    mlp_grown = reduce_rows(mlp_part, parties).reshape(portion, requests, model_width)
+    mlp_grown = return_blocks(mlp_part, parties).reshape(portion, requests, model_width)
     after_mlp = after_attn + adaptive[:, 5] * mlp_grown
     head_in = modulate(after_mlp, adaptive[:, 8], adaptive[:, 9]).reshape(
         portion * requests, model_width

time: 157 us -> 158 us (level)
  blocking collectives: 65.5 us -> 35.2 us
  waiting for transfers between devices: 23.9 us -> 45.3 us
  starting transfers between devices: 8.92 us -> 15.1 us
  local copies, waits for them, and re-layouts: 24.9 us -> 29.5 us
    ppermute x0 -> x9, waiting for transfers between devices: none -> 28 us  [shifted(): lax.ppermute(value, axis, [(i, (i + step) % size) for i in range(size)])]
    all_to_all x1 -> x0, blocking collectives: 17 us -> none  [shards(): lax.all_to_all(answer.reshape(senders, query_share, head_share), 'seq', s...]
    all_gather x1 -> x0, blocking collectives: 13.3 us -> none  [shards(): lax.all_gather(mlp_mine, 'tp', axis=0, tiled=True)]
    ppermute x0 -> x9, starting transfers between devices: none -> 10.2 us  [shifted(): lax.ppermute(value, axis, [(i, (i + step) % size) for i in range(size)])]
    all_to_all x2 -> x1, waiting for transfers between devices: 19.5 us -> 12.9 us  [shards(): lax.all_to_all(answer.reshape(senders, query_share, head_share), 'seq', s...]
    all_to_all x2 -> x1, starting transfers between devices: 8.09 us -> 4.05 us  [shards(): lax.all_to_all(answer.reshape(senders, query_share, head_share), 'seq', s...]
    unnamed x26 -> x32, local copies, waits for them, and re-layouts: 9.61 us -> 11.3 us
  transfers between devices with their start and end apart: 4 -> 12, of which waited for: 3 -> 10; matrix products, arithmetic and copies ran while one was open for 3% -> 3% of each run, Pallas kernels for 0% -> 0%
where the time goes in v6:
time: 158 us; the launch traced here: 157 us
  waiting for transfers between devices  45.3 us (29%)
  blocking collectives  35.2 us (22%)
  local copies, waits for them, and re-layouts  29.5 us (19%)
  starting transfers between devices  15.1 us (10%)
  other arithmetic  14.5 us (9%)
  matrix products  10.6 us (7%)
  Pallas kernels  6.16 us (4%)
    all_to_all x1, blocking collectives, shards(): lax.all_to_all(payload, 'seq', split_axis=0, concat_axis=0, tiled=True)  35.2 us
    ppermute x9, waiting for transfers between devices, shifted(): lax.ppermute(value, axis, [(i, (i + step) % size) for i in range(size)])  28 us
    all_to_all x1, waiting for transfers between devices, shards(): lax.all_to_all(answer.reshape(senders, query_share, head_share), 'seq', s...  12.9 us
    unnamed x32, local copies, waits for them, and re-layouts  11.3 us
    ppermute x9, starting transfers between devices, shifted(): lax.ppermute(value, axis, [(i, (i + step) % size) for i in range(size)])  10.2 us
    pallas_call x1, Pallas kernels, attend_kernel(): pl.pallas_call(attention_kernel, out_shape=jax.ShapeDtypeStruct(queries.s...  6.16 us
    dot_general x1, matrix products, shards(): jnp.dot(hidden, w_down, preferred_element_type=jnp.float32)  4.56 us
    ppermute x2, waiting for transfers between devices, swapped(): lax.ppermute(value, axis, [(i, i ^ 1 << apart) for i in range(lax.axis_si...  4.4 us
  transfers between devices with their start and end apart: 12, of which 10 were waited for; matrix products, arithmetic and copies ran while one was open for 3% of the time, Pallas kernels for 0%

profile of v6, /device:TPU:4, one launch (start us, length us, event | category | flops | bytes accessed | tf_op | source)
XLA Modules:
  0.0 157.2 jit_solution(3327382527774897944)
XLA Ops:
  0.7 2.3 %copy.45 = bf16[192,8,2,384]{3,1,2,0:T(8,128)(2,1)S(1)} copy(bf16[192,8,2,384]{3,2,1,0:T(2,128)(2,1)} %bitcast.123) | data formatting | bytes 4718592
  3.0 0.7 fusion.44
  4.2 0.6 convolution_convert_fusion.3
  4.8 0.6 fusion.62
  5.4 0.7 concatenate.23
  6.1 6.2 %copy.38 = bf16[1536,3,384]{0,2,1:T(8,128)(2,1)} copy(bf16[1536,3,384]{2,0,1:T(8,128)(2,1)} %param.20) | data formatting | bytes 7077888 | tf_op args[7]
  12.5 0.3 multiply_reduce_fusion
  12.8 3.3 %convolution_convert_fusion.1 = bf16[256,1152]{1,0:T(8,128)(2,1)S(1)} fusion(bf16[1536,1152]{0,1:T(8,128)(2,1)} %bitcast.117, bf16[1,32,8,1536]{3,2,1,0:T(8,128)(2,1)S(1)} %copy-done.1, f32[8,1536]{1,0:T(8,128)S(1)} %get-tuple-element.28, f32[8,1536]{1,0:T(8,128)S(1)} %get-tuple-element.29, f32[32,8]{1,0:T(8,128)S(1)} %add_rsqrt_fusion, ...), kind=kOutput, calls=%fused_computation.1 | convolution fusion | flops 908623872 | bytes 5015552 | tf_op jit(solution)/shard_map/dot_general | solution.py:114
  16.1 0.8 fusion.61
  17.0 1.1 concatenate.22
  18.1 1.5 concatenate.20
  19.6 1.8 %concatenate.19 = bf16[32,8,2,1,192]{4,2,1,0,3:T(2,128)(2,1)} reshape(bf16[256,384]{1,0:T(8,128)(2,1)} %get-tuple-element.20) | data formatting | bytes 393216 | tf_op jit(solution)/shard_map/concatenate | solution.py:138
  21.4 2.0 %maximum_bitcast_fusion = bf16[8,2,2,37,192]{4,1,0,3,2:T(2,128)(2,1)S(1)} fusion(bf16[5,8,2,1,192]{4,2,1,0,3:T(2,128)(2,1)} %concatenate.23, bf16[32,8,2,1,192]{4,2,1,0,3:T(2,128)(2,1)S(1)} %concatenate.22, bf16[5,8,2,1,192]{4,2,1,0,3:T(2,128)(2,1)} %concatenate.20, bf16[32,8,2,1,192]{4,2,1,0,3:T(2,128)(2,1)} %concatenate.19), kind=kLoop, calls=%fused_computation.26 | loop fusion | flops 681984 | bytes 909312 | tf_op jit(solution)/shard_map/transpose | solution.py:142
  23.4 1.0 copy.40
  24.5 1.1 reshape_reshape.3
  25.7 1.2 pad_maximum_fusion
  26.9 35.2 %all_to_all.10 = bf16[32,53,192]{2,1,0:T(8,128)(2,1)S(1)} all-to-all(bf16[32,53,192]{2,1,0:T(8,128)(2,1)S(1)} %pad_maximum_fusion), channel_id=1, replica_groups=mesh['cfg'=2,'seq'=32,'tp'=4] {'seq'}, dimensions={0} | all-to-all | bytes 1302528 | tf_op jit(solution)/shard_map/all_to_all | solution.py:146
  62.1 1.0 copy-done.2
  63.1 1.0 copy.41
  64.1 0.6 fusion.51
  64.7 0.7 fusion.50
  65.4 0.7 reshape.404.valid_ref
  66.1 1.7 %slice.98 = bf16[32,16,192]{2,1,0:T(8,128)(2,1)} slice(bf16[32,53,192]{2,1,0:T(8,128)(2,1)} %copy-done.2), slice={[0:32], [0:16], [0:192]} | slice | bytes 393216 | tf_op jit(solution)/shard_map/slice | solution.py:147
  67.8 1.7 %broadcast_select_fusion = (bf16[32,37,192]{2,1,0:T(8,128)(2,1)S(1)}, bf16[32,37,192]{2,1,0:T(8,128)(2,1)S(1)}) fusion(pred[]{:T(512)S(6)} %eq.44, bf16[32,37,192]{2,0,1:T(8,128)(2,1)} %collective-permute-done, bf16[32,53,192]{2,1,0:T(8,128)(2,1)} %copy-done.2), kind=kLoop, calls=%fused_computation.24 | loop fusion | flops 454656 | bytes 1818625 | tf_op jit(solution)/shard_map/jit(_where)/select_n | solution.py:152
  69.5 1.0 pad.7
  70.4 1.0 pad.8
  71.4 6.2 %shard_map.140 = bf16[512,192]{1,0:T(8,128)(2,1)} custom-call(bf16[512,192]{1,0:T(8,128)(2,1)} %bitcast.125, bf16[1280,192]{1,0:T(8,128)(2,1)} %bitcast.120, bf16[1280,192]{1,0:T(8,128)(2,1)} %bitcast.122, f32[1,1280]{1,0:T(1,128)} %reshape.404.valid_ref), custom_call_target="tpu_custom_call" | custom-call | tf_op jit(solution)/shard_map/pallas_call | solution.py:53
  77.6 4.1 %all-to-all-start.1 = ((bf16[32,16,192]{2,1,0:T(8,128)(2,1)}), bf16[32,16,192]{2,1,0:T(8,128)(2,1)S(1)}, u32[]{:S(2)}, u32[]{:S(2)}) async-start(bf16[32,16,192]{2,1,0:T(8,128)(2,1)} %bitcast.124), calls=%async_computation.1 | async-start | bytes 524288 | tf_op jit(solution)/shard_map/all_to_all | solution.py:171
  81.7 12.9 %all-to-all-done.1 = bf16[32,16,192]{2,1,0:T(8,128)(2,1)S(1)} async-done(((bf16[32,16,192]{2,1,0:T(8,128)(2,1)}), bf16[32,16,192]{2,1,0:T(8,128)(2,1)S(1)}, u32[]{:S(2)}, u32[]{:S(2)}) %all-to-all-start.1) | async-done | bytes 196640 | tf_op jit(solution)/shard_map/all_to_all | solution.py:171
  94.6 0.7 copy-done.5
  95.3 1.2 copy.44
  96.5 0.8 reshape.396
  97.3 1.9 %convolution_convert_fusion.2 = bf16[256,1536]{1,0:T(8,128)(2,1)S(1)} fusion(bf16[256,384]{1,0:T(8,128)(2,1)} %reshape.396, bf16[384,1536]{1,0:T(8,128)(2,1)} %param.22), kind=kOutput, calls=%fused_computation.2 | convolution fusion | flops 302383104 | bytes 2162688 | tf_op jit(solution)/shard_map/dot_general | solution.py:185
  99.3 0.9 copy-done.3
  100.2 0.8 dynamic-slice_bitcast_fusion.2
  101.0 3.0 %collective-permute-start.3 = (bf16[64,1536]{1,0:T(8,128)(2,1)}, bf16[64,1536]{1,0:T(8,128)(2,1)}, u32[]{:S(2)}, u32[]{:S(2)}) collective-permute-start(bf16[64,1536]{1,0:T(8,128)(2,1)} %get-tuple-element.16), channel_id=1, source_target_pairs={{0,3},{1,0},{2,1},{3,2},{4,7},{5,4},{6,5},{7,6},{8,11},{9,8},{10,9... | collective-permute-start | bytes 589832 | tf_op jit(solution)/shard_map/ppermute | solution.py:61
  104.0 0.6 collective-permute-start.2
  104.6 1.0 collective-permute-start.1
  105.6 1.3 convert_element_type.121
  107.0 4.8 %collective-permute-done.3 = bf16[64,1536]{1,0:T(8,128)(2,1)} collective-permute-done((bf16[64,1536]{1,0:T(8,128)(2,1)}, bf16[64,1536]{1,0:T(8,128)(2,1)}, u32[]{:S(2)}, u32[]{:S(2)}) %collective-permute-start.3) | collective-permute-done | bytes 196640 | tf_op jit(solution)/shard_map/ppermute | solution.py:61
  111.8 1.6 %collective-permute-done.2 = bf16[64,1536]{1,0:T(8,128)(2,1)} collective-permute-done((bf16[64,1536]{1,0:T(8,128)(2,1)}, bf16[64,1536]{1,0:T(8,128)(2,1)}, u32[]{:S(2)}, u32[]{:S(2)}) %collective-permute-start.2) | collective-permute-done | bytes 196640 | tf_op jit(solution)/shard_map/ppermute | solution.py:61
  113.4 1.9 %collective-permute-done.1 = bf16[64,1536]{1,0:T(8,128)(2,1)} collective-permute-done((bf16[64,1536]{1,0:T(8,128)(2,1)S(1)}, bf16[64,1536]{1,0:T(8,128)(2,1)}, u32[]{:S(2)}, u32[]{:S(2)}) %collective-permute-start.1) | collective-permute-done | bytes 196640 | tf_op jit(solution)/shard_map/ppermute | solution.py:61
  115.3 1.6 fusion.58
  116.9 0.2 multiply_reduce_fusion.2
  117.2 0.8 collective-permute-start.6
  118.1 0.6 collective-permute-start.5
  118.7 0.9 collective-permute-start.4
  119.7 5.4 %collective-permute-done.6 = bf16[8,8,1536]{2,1,0:T(8,128)(2,1)S(1)} collective-permute-done((bf16[8,8,1536]{2,1,0:T(8,128)(2,1)S(1)}, bf16[8,8,1536]{2,1,0:T(8,128)(2,1)S(1)}, u32[]{:S(2)}, u32[]{:S(2)}) %collective-permute-start.6) | collective-permute-done | bytes 196640 | tf_op jit(solution)/shard_map/ppermute | solution.py:61
  125.1 2.3 %collective-permute-done.5 = bf16[8,8,1536]{2,1,0:T(8,128)(2,1)S(1)} collective-permute-done((bf16[8,8,1536]{2,1,0:T(8,128)(2,1)S(1)}, bf16[8,8,1536]{2,1,0:T(8,128)(2,1)S(1)}, u32[]{:S(2)}, u32[]{:S(2)}) %collective-permute-start.5) | collective-permute-done | bytes 196640 | tf_op jit(solution)/shard_map/ppermute | solution.py:61
  127.4 2.2 %collective-permute-done.4 = bf16[8,8,1536]{2,1,0:T(8,128)(2,1)S(1)} collective-permute-done((bf16[8,8,1536]{2,1,0:T(8,128)(2,1)S(1)}, bf16[8,8,1536]{2,1,0:T(8,128)(2,1)S(1)}, u32[]{:S(2)}, u32[]{:S(2)}) %collective-permute-start.4) | collective-permute-done | bytes 196640 | tf_op jit(solution)/shard_map/ppermute | solution.py:61
  129.6 1.0 pad_maximum_fusion.1
  130.6 4.6 %convolution_convert_fusion = bf16[256,1536]{1,0:T(8,128)(2,1)} fusion(bf16[768,1536]{1,0:T(8,128)(2,1)S(1)} %copy-done, bf16[256,1536]{1,0:T(8,128)(2,1)} %bitcast.129, bf16[1536,768]{1,0:T(8,128)(2,1)} %param.23), kind=kOutput, calls=%fused_computation | convolution fusion | flops 1210122240 | bytes 6291456 | tf_op jit(solution)/shard_map/dot_general | solution.py:193
  135.2 1.2 fusion.60
  136.5 2.5 %collective-permute-start.8 = (bf16[64,1536]{1,0:T(8,128)(2,1)S(1)}, bf16[64,1536]{1,0:T(8,128)(2,1)S(1)}, u32[]{:S(2)}, u32[]{:S(2)}) collective-permute-start(bf16[64,1536]{1,0:T(8,128)(2,1)S(1)} %get-tuple-element.14), channel_id=1, source_target_pairs={{0,2},{1,3},{2,0},{3,1},{4,6},{5,7},{6,4},{7,5},{8,10},{9,11},{10,... | collective-permute-start | bytes 589832 | tf_op jit(solution)/shard_map/ppermute | solution.py:61
  139.0 0.7 collective-permute-start.7
  139.7 9.0 %collective-permute-done.9 = bf16[64,1536]{1,0:T(8,128)(2,1)S(1)} collective-permute-done((bf16[64,1536]{1,0:T(8,128)(2,1)S(1)}, bf16[64,1536]{1,0:T(8,128)(2,1)S(1)}, u32[]{:S(2)}, u32[]{:S(2)}) %collective-permute-start.9) | collective-permute-done | bytes 196640 | tf_op jit(solution)/shard_map/ppermute | solution.py:61
  148.7 0.6 collective-permute-done.7
  149.3 1.1 fusion.56
  150.5 0.2 multiply_reduce_fusion.1
  150.7 0.3 fusion.32
  151.1 0.8 collective-permute-start.10
  151.9 0.2 select_reduce_fusion
  152.1 4.4 %collective-permute-done.10 = f32[8,8,32]{2,1,0:T(8,128)S(1)} collective-permute-done((f32[8,8,32]{2,1,0:T(8,128)S(1)}, f32[8,8,32]{2,1,0:T(8,128)S(1)}, u32[]{:S(2)}, u32[]{:S(2)}) %collective-permute-start.10) | collective-permute-done | bytes 8224 | tf_op jit(solution)/shard_map/ppermute | solution.py:17
  156.5 0.7 multiply_add_fusion
  (52 shorter events, 1.4 us)
Async XLA Ops:
  0.6 130.0 %copy-start = (bf16[768,1536]{1,0:T(8,128)(2,1)S(1)}, bf16[768,1536]{1,0:T(8,128)(2,1)}, u32[]{:S(2)}) copy-start(bf16[768,1536]{1,0:T(8,128)(2,1)} %param.24) | copy-start | bytes 7077892
  0.6 2.3 %copy-start.6 = (bf16[1,8,10,1536]{3,1,2,0:T(8,128)(2,1)S(1)}, bf16[1,8,10,1536]{3,1,2,0:T(8,128)(2,1)}, u32[]{:S(2)}) copy-start(bf16[1,8,10,1536]{3,1,2,0:T(8,128)(2,1)} %param.15) | copy-start | bytes 737284
  3.0 0.9 copy-start.4
  6.1 6.2 %copy-start.1 = (bf16[1,32,8,1536]{3,2,1,0:T(8,128)(2,1)S(1)}, bf16[1,32,8,1536]{3,2,1,0:T(8,128)(2,1)}, u32[]{:S(2)}) copy-start(bf16[1,32,8,1536]{3,2,1,0:T(8,128)(2,1)} %param.13) | copy-start | bytes 2359300
  62.1 1.0 copy-start.2
  63.1 1.0 copy-start.14
  64.1 3.7 %collective-permute-start = (bf16[32,37,192]{2,0,1:T(8,128)(2,1)}, bf16[32,37,192]{2,0,1:T(8,128)(2,1)}, u32[]{:S(2)}, u32[]{:S(2)}) collective-permute-start(bf16[32,37,192]{2,0,1:T(8,128)(2,1)} %copy.41), channel_id=1, source_target_pairs={{0,4},{4,0},{8,12},{12,8},{16,20},{20,16},{24,28},{28,24},{32,36},... | collective-permute-start | bytes 1363976 | tf_op jit(solution)/shard_map/ppermute | solution.py:17
  77.6 17.0 %all-to-all-start.1 = ((bf16[32,16,192]{2,1,0:T(8,128)(2,1)}), bf16[32,16,192]{2,1,0:T(8,128)(2,1)S(1)}, u32[]{:S(2)}, u32[]{:S(2)}) async-start(bf16[32,16,192]{2,1,0:T(8,128)(2,1)} %bitcast.124), calls=%async_computation.1 | async-start | bytes 524288 | tf_op jit(solution)/shard_map/all_to_all | solution.py:171
  94.6 0.7 copy-start.5
  99.3 0.9 copy-start.3
  100.2 15.2 %copy-start.7 = (f32[8,1536]{1,0:T(8,128)S(1)}, f32[8,1536]{1,0:T(8,128)}, u32[]{:S(2)}) copy-start(f32[8,1536]{1,0:T(8,128)} %get-tuple-element.30) | copy-start | bytes 147460
  101.0 10.8 %collective-permute-start.3 = (bf16[64,1536]{1,0:T(8,128)(2,1)}, bf16[64,1536]{1,0:T(8,128)(2,1)}, u32[]{:S(2)}, u32[]{:S(2)}) collective-permute-start(bf16[64,1536]{1,0:T(8,128)(2,1)} %get-tuple-element.16), channel_id=1, source_target_pairs={{0,3},{1,0},{2,1},{3,2},{4,7},{5,4},{6,5},{7,6},{8,11},{9,8},{10,9... | collective-permute-start | bytes 589832 | tf_op jit(solution)/shard_map/ppermute | solution.py:61
  104.0 9.4 %collective-permute-start.2 = (bf16[64,1536]{1,0:T(8,128)(2,1)}, bf16[64,1536]{1,0:T(8,128)(2,1)}, u32[]{:S(2)}, u32[]{:S(2)}) collective-permute-start(bf16[64,1536]{1,0:T(8,128)(2,1)} %get-tuple-element.17), channel_id=1, source_target_pairs={{0,2},{1,3},{2,0},{3,1},{4,6},{5,7},{6,4},{7,5},{8,10},{9,11},{10,... | collective-permute-start | bytes 589832 | tf_op jit(solution)/shard_map/ppermute | solution.py:61
  104.6 10.7 %collective-permute-start.1 = (bf16[64,1536]{1,0:T(8,128)(2,1)S(1)}, bf16[64,1536]{1,0:T(8,128)(2,1)}, u32[]{:S(2)}, u32[]{:S(2)}) collective-permute-start(bf16[64,1536]{1,0:T(8,128)(2,1)S(1)} %get-tuple-element.15), channel_id=1, source_target_pairs={{0,1},{1,2},{2,3},{3,0},{4,5},{5,6},{6,7},{7,4},{8,9},{9,10},{10,1... | collective-permute-start | bytes 589832 | tf_op jit(solution)/shard_map/ppermute | solution.py:61
  117.2 7.8 %collective-permute-start.6 = (bf16[8,8,1536]{2,1,0:T(8,128)(2,1)S(1)}, bf16[8,8,1536]{2,1,0:T(8,128)(2,1)S(1)}, u32[]{:S(2)}, u32[]{:S(2)}) collective-permute-start(bf16[8,8,1536]{2,1,0:T(8,128)(2,1)S(1)} %add_convert_fusion.2), channel_id=1, source_target_pairs={{0,3},{1,0},{2,1},{3,2},{4,7},{5,4},{6,5},{7,6},{8,11},{9,8},{10,9... | collective-permute-start | bytes 589832 | tf_op jit(solution)/shard_map/ppermute | solution.py:61
  118.1 9.3 %collective-permute-start.5 = (bf16[8,8,1536]{2,1,0:T(8,128)(2,1)S(1)}, bf16[8,8,1536]{2,1,0:T(8,128)(2,1)S(1)}, u32[]{:S(2)}, u32[]{:S(2)}) collective-permute-start(bf16[8,8,1536]{2,1,0:T(8,128)(2,1)S(1)} %add_convert_fusion.2), channel_id=1, source_target_pairs={{0,2},{1,3},{2,0},{3,1},{4,6},{5,7},{6,4},{7,5},{8,10},{9,11},{10,... | collective-permute-start | bytes 589832 | tf_op jit(solution)/shard_map/ppermute | solution.py:61
  118.7 10.9 %collective-permute-start.4 = (bf16[8,8,1536]{2,1,0:T(8,128)(2,1)S(1)}, bf16[8,8,1536]{2,1,0:T(8,128)(2,1)S(1)}, u32[]{:S(2)}, u32[]{:S(2)}) collective-permute-start(bf16[8,8,1536]{2,1,0:T(8,128)(2,1)S(1)} %add_convert_fusion.2), channel_id=1, source_target_pairs={{0,1},{1,2},{2,3},{3,0},{4,5},{5,6},{6,7},{7,4},{8,9},{9,10},{10,1... | collective-permute-start | bytes 589832 | tf_op jit(solution)/shard_map/ppermute | solution.py:61
  130.6 9.1 %copy-start.12 = (s32[8]{0:T(128)S(1)}, s32[8]{0:T(128)}, u32[]{:S(2)}) copy-start(s32[8]{0:T(128)} %param.17) | copy-start | bytes 100
  135.2 15.5 %copy-start.8 = (bf16[1536,64]{0,1:T(8,128)(2,1)S(1)}, bf16[1536,64]{0,1:T(8,128)(2,1)}, u32[]{:S(2)}) copy-start(bf16[1536,64]{0,1:T(8,128)(2,1)} %param.25) | copy-start | bytes 589828
  135.2 15.5 %copy-start.9 = (f32[8,1536]{1,0:T(8,128)S(1)}, f32[8,1536]{1,0:T(8,128)}, u32[]{:S(2)}) copy-start(f32[8,1536]{1,0:T(8,128)} %get-tuple-element.21) | copy-start | bytes 147460
  135.2 15.5 %copy-start.10 = (f32[8,1536]{1,0:T(8,128)S(1)}, f32[8,1536]{1,0:T(8,128)}, u32[]{:S(2)}) copy-start(f32[8,1536]{1,0:T(8,128)} %get-tuple-element.22) | copy-start | bytes 147460
  136.4 15.5 %copy-start.13 = (f32[9]{0:T(128)S(1)}, f32[9]{0:T(128)}, u32[]{:S(2)}) copy-start(f32[9]{0:T(128)} %param.18) | copy-start | bytes 112
  136.4 20.1 %copy-start.11 = (f32[8,8,32]{2,1,0:T(8,128)S(1)}, f32[8,8,32]{2,1,0:T(8,128)}, u32[]{:S(2)}) copy-start(f32[8,8,32]{2,1,0:T(8,128)} %param.19) | copy-start | bytes 24580
  136.4 12.3 %collective-permute-start.9 = (bf16[64,1536]{1,0:T(8,128)(2,1)S(1)}, bf16[64,1536]{1,0:T(8,128)(2,1)S(1)}, u32[]{:S(2)}, u32[]{:S(2)}) collective-permute-start(bf16[64,1536]{1,0:T(8,128)(2,1)S(1)} %get-tuple-element.13), channel_id=1, source_target_pairs={{0,1},{1,2},{2,3},{3,0},{4,5},{5,6},{6,7},{7,4},{8,9},{9,10},{10,1... | collective-permute-start | bytes 589832 | tf_op jit(solution)/shard_map/ppermute | solution.py:61
  136.5 12.2 %collective-permute-start.8 = (bf16[64,1536]{1,0:T(8,128)(2,1)S(1)}, bf16[64,1536]{1,0:T(8,128)(2,1)S(1)}, u32[]{:S(2)}, u32[]{:S(2)}) collective-permute-start(bf16[64,1536]{1,0:T(8,128)(2,1)S(1)} %get-tuple-element.14), channel_id=1, source_target_pairs={{0,2},{1,3},{2,0},{3,1},{4,6},{5,7},{6,4},{7,5},{8,10},{9,11},{10,... | collective-permute-start | bytes 589832 | tf_op jit(solution)/shard_map/ppermute | solution.py:61
  139.0 10.3 %collective-permute-start.7 = (bf16[64,1536]{1,0:T(8,128)(2,1)S(1)}, bf16[64,1536]{1,0:T(8,128)(2,1)S(1)}, u32[]{:S(2)}, u32[]{:S(2)}) collective-permute-start(bf16[64,1536]{1,0:T(8,128)(2,1)S(1)} %get-tuple-element.12), channel_id=1, source_target_pairs={{0,3},{1,0},{2,1},{3,2},{4,7},{5,4},{6,5},{7,6},{8,11},{9,8},{10,9... | collective-permute-start | bytes 589832 | tf_op jit(solution)/shard_map/ppermute | solution.py:61
  151.1 5.5 %collective-permute-start.10 = (f32[8,8,32]{2,1,0:T(8,128)S(1)}, f32[8,8,32]{2,1,0:T(8,128)S(1)}, u32[]{:S(2)}, u32[]{:S(2)}) collective-permute-start(f32[8,8,32]{2,1,0:T(8,128)S(1)} %constant_dynamic-slice_fusion), channel_id=1, source_target_pairs={{0,128},{128,0},{1,129},{129,1},{2,130},{130,2},{3,131},{131,3},{4... | collective-permute-start | bytes 24584 | tf_op jit(solution)/shard_map/ppermute | solution.py:17

commit v7 on v5

--- a/solution.py
+++ b/solution.py
@@ -90,20 +90,20 @@
     resident = img_hidden[0].astype(jnp.float32)
     lengths_all = text_lengths[0]
     normed = modulate(resident, adaptive[:, 0], adaptive[:, 1]).reshape(rows_all, model_width)
-    projected = jnp.dot(
-        normed, w_qkv.reshape(model_width, 3 * features), preferred_element_type=jnp.float32
+    projected = jnp.einsum(
+        "nd,dkf->knf", normed, w_qkv, preferred_element_type=jnp.float32
     ).astype(jnp.bfloat16)
-    queries = projected[:, :features].reshape(img_slice, requests, features)
-    keys_img = projected[:, features : 2 * features].reshape(img_slice, requests, features)
-    vals_img = projected[:, 2 * features :].reshape(img_slice, requests, features)
+    queries = projected[0].reshape(img_slice, requests, features)
+    keys_img = projected[1].reshape(img_slice, requests, features)
+    vals_img = projected[2].reshape(img_slice, requests, features)
     text_in = modulate(txt_hidden[0].astype(jnp.float32), adaptive[:, 6], adaptive[:, 7]).reshape(
         txt_slice * requests, model_width
     )
-    text_kv = jnp.dot(
-        text_in, w_kv_text.reshape(model_width, 2 * features), preferred_element_type=jnp.float32
+    text_kv = jnp.einsum(
+        "nd,dkf->knf", text_in, w_kv_text, preferred_element_type=jnp.float32
     ).astype(jnp.bfloat16)
-    keys_txt = text_kv[:, :features].reshape(txt_slice, requests, features)
-    vals_txt = text_kv[:, features:].reshape(txt_slice, requests, features)
+    keys_txt = text_kv[0].reshape(txt_slice, requests, features)
+    vals_txt = text_kv[1].reshape(txt_slice, requests, features)
     key_span = img_slice + txt_slice
     senders = requests * members
     halves = members // 2

time: 157 us -> 173 us (1.10)
  other arithmetic: 14.1 us -> 27 us
  matrix products: 11.3 us -> 13.1 us
    unnamed x26 -> x32, local copies, waits for them, and re-layouts: 9.61 us -> 2.7 us
    reduce_sum x4, other arithmetic: 0.91 us -> 4.14 us  [layer_norm(): jnp.mean(center * center, -1, keepdims=True) + EPSILON]
    reduce_sum x4, other arithmetic: 2.34 us -> 4.77 us  [layer_norm(): center = values - jnp.mean(values, -1, keepdims=True)]
    div x0 -> x2, local copies, waits for them, and re-layouts: none -> 1.96 us  [layer_norm(): center = values - jnp.mean(values, -1, keepdims=True)]
  transfers between devices with their start and end apart: 4 -> 4, of which waited for: 3 -> 3; matrix products, arithmetic and copies ran while one was open for 3% -> 5% of each run, Pallas kernels for 0% -> 0%
where the time goes in v7:
time: 173 us; the launch traced here: 171 us
  blocking collectives  66.3 us (38%)
  other arithmetic  27 us (16%)
  local copies, waits for them, and re-layouts  26.3 us (15%)
  waiting for transfers between devices  22.2 us (13%)
  matrix products  13.1 us (8%)
  starting transfers between devices  9.59 us (6%)
  Pallas kernels  6.18 us (4%)
    all_to_all x1, blocking collectives, shards(): lax.all_to_all(payload, 'seq', split_axis=0, concat_axis=0, tiled=True)  35.2 us
    all_to_all x2, waiting for transfers between devices, reduce_rows(): got = lax.all_to_all(pieces, 'tp', split_axis=0, concat_axis=0, tiled=True)  18.6 us
    all_to_all x1, blocking collectives, shards(): lax.all_to_all(answer.reshape(senders, query_share, head_share), 'seq', s...  17 us
    all_gather x1, blocking collectives, shards(): lax.all_gather(mlp_mine, 'tp', axis=0, tiled=True)  14.1 us
    all_to_all x2, starting transfers between devices, reduce_rows(): got = lax.all_to_all(pieces, 'tp', split_axis=0, concat_axis=0, tiled=True)  8.79 us
    pallas_call x1, Pallas kernels, attend_kernel(): pl.pallas_call(attention_kernel, out_shape=jax.ShapeDtypeStruct(queries.s...  6.18 us
    dot_general x1, matrix products, shards(): jnp.dot(hidden, w_down, preferred_element_type=jnp.float32)  5.23 us
    reduce_sum x4, other arithmetic, layer_norm(): center = values - jnp.mean(values, -1, keepdims=True)  4.77 us
  transfers between devices with their start and end apart: 4, of which 3 were waited for; matrix products, arithmetic and copies ran while one was open for 5% of the time, Pallas kernels for 0%

profile of v7, /device:TPU:4, one launch (start us, length us, event | category | flops | bytes accessed | tf_op | source)
XLA Modules:
  0.0 171.4 jit_solution(930299360487540290)
XLA Ops:
  0.6 1.5 convert_reduce_fusion.2
  2.1 2.1 %fusion.4 = f32[32,8]{1,0:T(8,128)} fusion(bf16[1,32,8,1536]{3,2,1,0:T(8,128)(2,1)} %param.13, f32[32,8]{1,0:T(8,128)S(1)} %broadcast_multiply_fusion), kind=kLoop, calls=%fused_computation.9 | loop fusion | flops 1572608 | bytes 788480 | tf_op jit(solution)/shard_map/reduce_sum | solution.py:22
  4.2 0.7 div.37
  4.9 1.0 convert_reduce_fusion.3
  5.9 0.6 copy-done.10
  6.5 1.7 fusion.46
  8.2 1.3 div.40
  9.5 1.0 bitcast_convert_fusion
  10.4 0.8 fusion.59
  11.2 0.6 add_rsqrt_fusion
  11.8 0.8 rsqrt.39
  12.7 2.4 %fusion.6 = bf16[3,256,384]{2,1,0:T(8,128)(2,1)S(1)} fusion(bf16[1536,3,384]{2,0,1:T(8,128)(2,1)S(1)} %copy-done, bf16[1,32,8,1536]{3,2,1,0:T(8,128)(2,1)} %param.13, f32[8,1536]{1,0:T(8,128)} %get-tuple-element.22, f32[8,1536]{1,0:T(8,128)} %get-tuple-element.23, f32[256]{0:T(256)S(1)} %rsqrt.39, f32[256]{0:T(256)} %div.37), kind=kOutput, calls=%fused_computation.15 | convolution fusion | flops 908623872 | bytes 5015552 | tf_op jit(solution)/shard_map/nd,dkf->knf/dot_general | solution.py:93
  15.1 0.8 fusion.75
  15.9 1.8 %concatenate.19 = bf16[32,8,2,1,192]{4,2,1,0,3:T(2,128)(2,1)} reshape(bf16[1,256,384]{2,1,0:T(8,128)(2,1)} %get-tuple-element.14) | data formatting | bytes 393216 | tf_op jit(solution)/shard_map/concatenate | solution.py:117
  17.7 1.8 %concatenate.22 = bf16[32,8,2,1,192]{4,2,1,0,3:T(2,128)(2,1)} reshape(bf16[1,256,384]{2,1,0:T(8,128)(2,1)} %get-tuple-element.13) | data formatting | bytes 393216 | tf_op jit(solution)/shard_map/concatenate | solution.py:118
  19.6 0.1 rsqrt.41
  19.7 2.4 %fusion.10 = bf16[2,40,384]{2,1,0:T(8,128)(2,1)S(1)} fusion(bf16[1536,2,384]{2,1,0:T(2,128)(2,1)} %param.21, bf16[1,5,8,1536]{3,2,1,0:T(8,128)(2,1)} %param.14, f32[8,1536]{1,0:T(8,128)} %get-tuple-element.20, f32[8,1536]{1,0:T(8,128)} %get-tuple-element.21, f32[40]{0:T(128)S(1)} %rsqrt.41, f32[40]{0:T(128)S(1)} %copy-done.14), kind=kOutput, calls=%fused_computation.19 | convolution fusion | flops 94771200 | bytes 2642240 | tf_op jit(solution)/shard_map/nd,dkf->knf/dot_general | solution.py:102
  22.0 0.6 fusion.76
  22.7 1.5 concatenate.20
  24.1 1.5 concatenate.23
  25.6 2.1 %maximum_bitcast_fusion = bf16[8,2,2,37,192]{4,1,0,3,2:T(2,128)(2,1)S(1)} fusion(bf16[5,8,2,1,192]{4,2,1,0,3:T(2,128)(2,1)} %concatenate.23, bf16[32,8,2,1,192]{4,2,1,0,3:T(2,128)(2,1)} %concatenate.22, bf16[5,8,2,1,192]{4,2,1,0,3:T(2,128)(2,1)} %concatenate.20, bf16[32,8,2,1,192]{4,2,1,0,3:T(2,128)(2,1)} %concatenate.19), kind=kLoop, calls=%fused_computation.38 | loop fusion | flops 681984 | bytes 909312 | tf_op jit(solution)/shard_map/transpose | solution.py:121
  27.7 1.0 copy.41
  28.8 1.8 %reshape_reshape_squeeze.3 = bf16[2,16,8,2,192]{4,3,2,1,0:T(2,128)(2,1)} reshape(bf16[1,256,384]{2,1,0:T(8,128)(2,1)} %get-tuple-element.12) | data formatting | bytes 393216 | tf_op jit(solution)/shard_map/reshape;reshape;squeeze | solution.py:113
  30.6 1.0 copy.39
  31.6 1.2 pad_maximum_fusion
  32.9 35.2 %all_to_all.20 = bf16[32,53,192]{2,1,0:T(8,128)(2,1)S(1)} all-to-all(bf16[32,53,192]{2,1,0:T(8,128)(2,1)S(1)} %pad_maximum_fusion), channel_id=1, replica_groups=mesh['cfg'=2,'seq'=32,'tp'=4] {'seq'}, dimensions={0} | all-to-all | bytes 1302528 | tf_op jit(solution)/shard_map/all_to_all | solution.py:125
  68.0 0.9 copy-done.1
  69.0 1.0 copy.42
  70.0 0.5 iota_multiply_fusion
  70.5 0.6 fusion.66
  71.1 1.4 fusion.65
  72.5 0.7 reshape.282.valid_ref
  73.2 1.7 slice.78
  74.9 1.7 broadcast_select_fusion
  76.6 1.0 pad.7
  77.5 1.0 pad.8
  78.5 6.2 %shard_map.140 = bf16[512,192]{1,0:T(8,128)(2,1)} custom-call(bf16[512,192]{1,0:T(8,128)(2,1)} %bitcast.143, bf16[1280,192]{1,0:T(8,128)(2,1)} %bitcast.140, bf16[1280,192]{1,0:T(8,128)(2,1)} %bitcast.142, f32[1,1280]{1,0:T(1,128)} %reshape.282.valid_ref), custom_call_target="tpu_custom_call" | custom-call | tf_op jit(solution)/shard_map/pallas_call | solution.py:53
  84.7 17.0 %all_to_all.21 = bf16[32,16,192]{2,1,0:T(8,128)(2,1)S(1)} all-to-all(bf16[32,16,192]{2,1,0:T(8,128)(2,1)} %bitcast.144), channel_id=1, replica_groups=mesh['cfg'=2,'seq'=32,'tp'=4] {'seq'}, dimensions={0} | all-to-all | bytes 393216 | tf_op jit(solution)/shard_map/all_to_all | solution.py:150
  101.7 1.0 copy.45
  102.6 1.8 %reshape.272 = bf16[256,384]{1,0:T(8,128)(2,1)} reshape(bf16[2,16,8,2,192]{4,3,2,1,0:T(2,128)(2,1)} %copy.45) | data formatting | bytes 393216 | tf_op jit(solution)/shard_map/reshape | solution.py:160
  104.5 2.8 %convolution_convert_fusion.1 = bf16[256,1536]{1,0:T(8,128)(2,1)} fusion(bf16[256,384]{1,0:T(8,128)(2,1)} %reshape.272, bf16[384,1536]{1,0:T(8,128)(2,1)} %param.22), kind=kOutput, calls=%fused_computation.1 | convolution fusion | flops 302383104 | bytes 2162688 | tf_op jit(solution)/shard_map/dot_general | solution.py:164
  107.3 4.5 %all-to-all-start.2 = ((bf16[4,64,1536]{2,1,0:T(8,128)(2,1)}), bf16[4,64,1536]{2,1,0:T(8,128)(2,1)}, u32[]{:S(2)}, u32[]{:S(2)}) async-start(bf16[4,64,1536]{2,1,0:T(8,128)(2,1)} %bitcast.139), calls=%async_computation.2 | async-start | bytes 1572864 | tf_op jit(solution)/shard_map/all_to_all | solution.py:61
  111.8 2.5 %convert_element_type.84 = f32[1,32,8,1536]{3,2,1,0:T(8,128)} convert(bf16[1,32,8,1536]{3,2,1,0:T(8,128)(2,1)} %param.13) | non-fusion elementwise | flops 393216 | bytes 2359296 | tf_op jit(solution)/shard_map/convert_element_type | solution.py:90
  114.2 9.1 %all-to-all-done.2 = bf16[4,64,1536]{2,1,0:T(8,128)(2,1)} async-done(((bf16[4,64,1536]{2,1,0:T(8,128)(2,1)}), bf16[4,64,1536]{2,1,0:T(8,128)(2,1)}, u32[]{:S(2)}, u32[]{:S(2)}) %all-to-all-start.2) | async-done | bytes 786464 | tf_op jit(solution)/shard_map/all_to_all | solution.py:61
  123.3 1.3 convert_reduce_fusion.1
  124.6 1.2 fusion.73
  125.8 0.2 multiply_reduce_fusion.1
  126.0 0.5 copy-done.2
  126.5 0.1 add_convert_fusion.1
  126.7 14.1 %all_gather.3 = bf16[32,8,1536]{2,1,0:T(8,128)(2,1)} all-gather(bf16[8,8,1536]{2,1,0:T(8,128)(2,1)S(1)} %add_convert_fusion.1), channel_id=1, replica_groups=mesh['cfg'=2,'seq'=32,'tp'=4] {'tp'}, dimensions={0}, use_global_device_ids=true | all-gather | bytes 983040 | tf_op jit(solution)/shard_map/all_gather | solution.py:168
  140.8 5.2 %convolution_convert_fusion = bf16[256,1536]{1,0:T(8,128)(2,1)} fusion(bf16[768,1536]{1,0:T(8,128)(2,1)} %param.24, bf16[1536,768]{1,0:T(8,128)(2,1)} %param.23, bf16[32,8,1536]{2,1,0:T(8,128)(2,1)} %all_gather.3), kind=kOutput, calls=%fused_computation | convolution fusion | flops 1210122240 | bytes 6291456 | tf_op jit(solution)/shard_map/dot_general | solution.py:172
  146.0 4.3 %all-to-all-start.3 = ((bf16[4,64,1536]{2,1,0:T(8,128)(2,1)}), bf16[4,64,1536]{2,1,0:T(8,128)(2,1)}, u32[]{:S(2)}, u32[]{:S(2)}) async-start(bf16[4,64,1536]{2,1,0:T(8,128)(2,1)} %bitcast.148), calls=%async_computation.3 | async-start | bytes 1572864 | tf_op jit(solution)/shard_map/all_to_all | solution.py:61
  150.4 9.5 %all-to-all-done.3 = bf16[4,64,1536]{2,1,0:T(8,128)(2,1)} async-done(((bf16[4,64,1536]{2,1,0:T(8,128)(2,1)}), bf16[4,64,1536]{2,1,0:T(8,128)(2,1)}, u32[]{:S(2)}, u32[]{:S(2)}) %all-to-all-start.3) | async-done | bytes 786464 | tf_op jit(solution)/shard_map/all_to_all | solution.py:61
  159.9 1.3 convert_reduce_fusion
  161.2 1.1 fusion.71
  162.4 0.2 multiply_reduce_fusion
  162.6 0.3 fusion.47
  162.9 0.6 copy-done.3
  163.5 0.7 constant_dynamic-slice_fusion
  164.2 0.8 collective-permute-start.1
  165.0 0.7 select_reduce_fusion
  165.6 0.7 sub.79
  166.3 3.6 %collective-permute-done.1 = f32[8,8,32]{2,1,0:T(8,128)} collective-permute-done((f32[8,8,32]{2,1,0:T(8,128)}, f32[8,8,32]{2,1,0:T(8,128)}, u32[]{:S(2)}, u32[]{:S(2)}) %collective-permute-start.1) | collective-permute-done | bytes 8224 | tf_op jit(solution)/shard_map/ppermute | solution.py:17
  169.9 1.5 multiply_add_fusion
  (40 shorter events, 0.2 us)
Async XLA Ops:
  0.6 12.0 %copy-start = (bf16[1536,3,384]{2,0,1:T(8,128)(2,1)S(1)}, bf16[1536,3,384]{2,0,1:T(8,128)(2,1)}, u32[]{:S(2)}) copy-start(bf16[1536,3,384]{2,0,1:T(8,128)(2,1)} %param.20) | copy-start | bytes 10616836
  4.9 6.4 %copy-start.9 = (f32[32,8]{1,0:T(8,128)S(1)}, f32[32,8]{1,0:T(8,128)}, u32[]{:S(2)}) copy-start(f32[32,8]{1,0:T(8,128)} %fusion.4) | copy-start | bytes 3076
  5.9 0.6 copy-start.10
  15.1 4.5 %copy-start.11 = (f32[5,8]{1,0:T(8,128)S(1)}, f32[5,8]{1,0:T(8,128)}, u32[]{:S(2)}) copy-start(f32[5,8]{1,0:T(8,128)} %fusion.46) | copy-start | bytes 484
  15.1 4.6 %copy-start.14 = (f32[40]{0:T(128)S(1)}, f32[40]{0:T(128)}, u32[]{:S(2)}) copy-start(f32[40]{0:T(128)} %div.40) | copy-start | bytes 484
  68.0 0.9 copy-start.1
  69.0 1.5 copy-start.15
  70.0 4.9 %collective-permute-start = (bf16[32,37,192]{2,0,1:T(8,128)(2,1)}, bf16[32,37,192]{2,0,1:T(8,128)(2,1)}, u32[]{:S(2)}, u32[]{:S(2)}) collective-permute-start(bf16[32,37,192]{2,0,1:T(8,128)(2,1)} %copy.42), channel_id=1, source_target_pairs={{0,4},{4,0},{8,12},{12,8},{16,20},{20,16},{24,28},{28,24},{32,36},... | collective-permute-start | bytes 1363976 | tf_op jit(solution)/shard_map/ppermute | solution.py:17
  107.3 16.0 %all-to-all-start.2 = ((bf16[4,64,1536]{2,1,0:T(8,128)(2,1)}), bf16[4,64,1536]{2,1,0:T(8,128)(2,1)}, u32[]{:S(2)}, u32[]{:S(2)}) async-start(bf16[4,64,1536]{2,1,0:T(8,128)(2,1)} %bitcast.139), calls=%async_computation.2 | async-start | bytes 1572864 | tf_op jit(solution)/shard_map/all_to_all | solution.py:61
  123.3 3.2 %copy-start.7 = (f32[8,1536]{1,0:T(8,128)S(1)}, f32[8,1536]{1,0:T(8,128)}, u32[]{:S(2)}) copy-start(f32[8,1536]{1,0:T(8,128)} %get-tuple-element.17) | copy-start | bytes 147460
  123.3 3.2 %copy-start.8 = (f32[8,1536]{1,0:T(8,128)S(1)}, f32[8,1536]{1,0:T(8,128)}, u32[]{:S(2)}) copy-start(f32[8,1536]{1,0:T(8,128)} %get-tuple-element.18) | copy-start | bytes 147460
  125.8 0.7 copy-start.2
  146.0 4.3 %copy-start.12 = (s32[8]{0:T(128)S(1)}, s32[8]{0:T(128)}, u32[]{:S(2)}) copy-start(s32[8]{0:T(128)} %param.17) | copy-start | bytes 100
  146.0 13.9 %all-to-all-start.3 = ((bf16[4,64,1536]{2,1,0:T(8,128)(2,1)}), bf16[4,64,1536]{2,1,0:T(8,128)(2,1)}, u32[]{:S(2)}, u32[]{:S(2)}) async-start(bf16[4,64,1536]{2,1,0:T(8,128)(2,1)} %bitcast.148), calls=%async_computation.3 | async-start | bytes 1572864 | tf_op jit(solution)/shard_map/all_to_all | solution.py:61
  150.4 14.6 %copy-start.13 = (f32[9]{0:T(128)S(1)}, f32[9]{0:T(128)}, u32[]{:S(2)}) copy-start(f32[9]{0:T(128)} %param.18) | copy-start | bytes 112
  159.9 2.7 %copy-start.4 = (bf16[1536,64]{0,1:T(8,128)(2,1)S(1)}, bf16[1536,64]{0,1:T(8,128)(2,1)}, u32[]{:S(2)}) copy-start(bf16[1536,64]{0,1:T(8,128)(2,1)} %param.25) | copy-start | bytes 589828
  159.9 2.7 %copy-start.5 = (f32[8,1536]{1,0:T(8,128)S(1)}, f32[8,1536]{1,0:T(8,128)}, u32[]{:S(2)}) copy-start(f32[8,1536]{1,0:T(8,128)} %get-tuple-element.15) | copy-start | bytes 147460
  159.9 2.7 %copy-start.6 = (f32[8,1536]{1,0:T(8,128)S(1)}, f32[8,1536]{1,0:T(8,128)}, u32[]{:S(2)}) copy-start(f32[8,1536]{1,0:T(8,128)} %get-tuple-element.16) | copy-start | bytes 147460
  162.9 0.6 copy-start.3
  164.2 5.7 %collective-permute-start.1 = (f32[8,8,32]{2,1,0:T(8,128)}, f32[8,8,32]{2,1,0:T(8,128)}, u32[]{:S(2)}, u32[]{:S(2)}) collective-permute-start(f32[8,8,32]{2,1,0:T(8,128)} %constant_dynamic-slice_fusion), channel_id=1, source_target_pairs={{0,128},{128,0},{1,129},{129,1},{2,130},{130,2},{3,131},{131,3},{4... | collective-permute-start | bytes 24584 | tf_op jit(solution)/shard_map/ppermute | solution.py:17

commit v8 on v5

--- a/solution.py
+++ b/solution.py
@@ -90,12 +90,12 @@
     resident = img_hidden[0].astype(jnp.float32)
     lengths_all = text_lengths[0]
     normed = modulate(resident, adaptive[:, 0], adaptive[:, 1]).reshape(rows_all, model_width)
-    projected = jnp.dot(
-        normed, w_qkv.reshape(model_width, 3 * features), preferred_element_type=jnp.float32
-    ).astype(jnp.bfloat16)
-    queries = projected[:, :features].reshape(img_slice, requests, features)
-    keys_img = projected[:, features : 2 * features].reshape(img_slice, requests, features)
-    vals_img = projected[:, 2 * features :].reshape(img_slice, requests, features)
+    queries, keys_img, vals_img = [
+        jnp.dot(normed, w_qkv[:, part], preferred_element_type=jnp.float32)
+        .astype(jnp.bfloat16)
+        .reshape(img_slice, requests, features)
+        for part in range(3)
+    ]
     text_in = modulate(txt_hidden[0].astype(jnp.float32), adaptive[:, 6], adaptive[:, 7]).reshape(
         txt_slice * requests, model_width
     )

time: 157 us -> 154 us (0.981)
  local copies, waits for them, and re-layouts: 24.9 us -> 16.8 us
  matrix products: 11.3 us -> 13.6 us
    unnamed x26 -> x29, local copies, waits for them, and re-layouts: 9.61 us -> 2.31 us
    dot_general x1 -> x3, matrix products: 3.29 us -> 5.37 us  [shards(): jnp.dot(normed, w_qkv[:, part], preferred_element_type=jnp.float32)]
where the time goes in v8:
time: 154 us; the launch traced here: 153 us
  blocking collectives  66.2 us (43%)
  waiting for transfers between devices  24 us (16%)
  local copies, waits for them, and re-layouts  16.8 us (11%)
  other arithmetic  15.6 us (10%)
  matrix products  13.6 us (9%)
  starting transfers between devices  9.61 us (6%)
  Pallas kernels  6.18 us (4%)
    all_to_all x1, blocking collectives, shards(): lax.all_to_all(payload, 'seq', split_axis=0, concat_axis=0, tiled=True)  35.2 us
    all_to_all x2, waiting for transfers between devices, reduce_rows(): got = lax.all_to_all(pieces, 'tp', split_axis=0, concat_axis=0, tiled=True)  19.6 us
    all_to_all x1, blocking collectives, shards(): lax.all_to_all(answer.reshape(senders, query_share, head_share), 'seq', s...  17 us
    all_gather x1, blocking collectives, shards(): lax.all_gather(mlp_mine, 'tp', axis=0, tiled=True)  14.1 us
    all_to_all x2, starting transfers between devices, reduce_rows(): got = lax.all_to_all(pieces, 'tp', split_axis=0, concat_axis=0, tiled=True)  8.78 us
    pallas_call x1, Pallas kernels, attend_kernel(): pl.pallas_call(attention_kernel, out_shape=jax.ShapeDtypeStruct(queries.s...  6.18 us
    dot_general x3, matrix products, shards(): jnp.dot(normed, w_qkv[:, part], preferred_element_type=jnp.float32)  5.37 us
    dot_general x1, matrix products, shards(): jnp.dot(hidden, w_down, preferred_element_type=jnp.float32)  4.54 us
  transfers between devices with their start and end apart: 4, of which 3 were waited for; matrix products, arithmetic and copies ran while one was open for 3% of the time, Pallas kernels for 0%

profile of v8, /device:TPU:4, one launch (start us, length us, event | category | flops | bytes accessed | tf_op | source)
XLA Modules:
  0.0 152.8 jit_solution(12519634712183028183)
XLA Ops:
  0.6 0.0 copy-start
  0.7 1.1 bitcast_convert_fusion
  1.8 0.7 fusion.58
  2.5 0.2 convert_reduce_fusion.2
  2.7 0.3 multiply_reduce_fusion
  3.0 0.0 copy-start.12
  3.0 2.7 %fusion.15 = bf16[256,384]{1,0:T(8,128)(2,1)} fusion(bf16[1536,3,384]{2,0,1:T(8,128)(2,1)} %param.20, bf16[1,32,8,1536]{3,2,1,0:T(8,128)(2,1)S(1)} %copy-done.1, f32[8,1536]{1,0:T(8,128)S(1)} %get-tuple-element.19, f32[8,1536]{1,0:T(8,128)S(1)} %get-tuple-element.20, f32[32,8]{1,0:T(8,128)S(1)} %add_rsqrt_fusion, f32[32,8]{1,0:T(8,128)S(1)} %broadcast_multiply_fusion), kind=kOutput, calls=%fused_computation.20 | convolution fusion | flops 304447488 | bytes 2263040 | tf_op jit(solution)/shard_map/dot_general | solution.py:94
  5.8 1.3 fusion.12
  7.1 1.3 fusion.9
  8.4 0.4 copy-done.3
  8.8 0.5 copy.40
  9.3 0.4 copy-done.4
  9.7 0.1 convert_reduce_fusion.3
  9.8 0.2 fusion.42
  10.0 0.6 convolution_convert_fusion.2
  10.6 0.6 fusion.77
  11.2 0.7 concatenate.23
  11.9 1.1 concatenate.22
  13.1 1.5 concatenate.20
  14.5 1.8 %concatenate.19 = bf16[32,8,2,1,192]{4,2,1,0,3:T(2,128)(2,1)} reshape(bf16[256,384]{1,0:T(8,128)(2,1)} %fusion.12) | data formatting | bytes 393216 | tf_op jit(solution)/shard_map/concatenate | solution.py:117
  16.3 2.0 %maximum_bitcast_fusion = bf16[8,2,2,37,192]{4,1,0,3,2:T(2,128)(2,1)S(1)} fusion(bf16[5,8,2,1,192]{4,2,1,0,3:T(2,128)(2,1)} %concatenate.23, bf16[32,8,2,1,192]{4,2,1,0,3:T(2,128)(2,1)S(1)} %concatenate.22, bf16[5,8,2,1,192]{4,2,1,0,3:T(2,128)(2,1)} %concatenate.20, bf16[32,8,2,1,192]{4,2,1,0,3:T(2,128)(2,1)} %concatenate.19), kind=kLoop, calls=%fused_computation.36 | loop fusion | flops 681984 | bytes 909312 | tf_op jit(solution)/shard_map/transpose | solution.py:121
  18.4 1.0 copy.35
  19.4 1.1 reshape_reshape.3
  20.6 0.1 copy.34
  20.6 1.2 pad_maximum_fusion
  21.9 35.2 %all_to_all.20 = bf16[32,53,192]{2,1,0:T(8,128)(2,1)S(1)} all-to-all(bf16[32,53,192]{2,1,0:T(8,128)(2,1)S(1)} %pad_maximum_fusion), channel_id=1, replica_groups=mesh['cfg'=2,'seq'=32,'tp'=4] {'seq'}, dimensions={0} | all-to-all | bytes 1302528 | tf_op jit(solution)/shard_map/all_to_all | solution.py:125
  57.1 0.9 copy-done.2
  58.0 1.0 copy.36
  59.0 0.0 collective-permute-start
  59.0 0.6 fusion.65
  59.6 0.7 fusion.64
  60.4 0.7 reshape.488.valid_ref
  61.1 1.7 %slice.75 = bf16[32,16,192]{2,1,0:T(8,128)(2,1)} slice(bf16[32,53,192]{2,1,0:T(8,128)(2,1)} %copy-done.2), slice={[0:32], [0:16], [0:192]} | slice | bytes 393216 | tf_op jit(solution)/shard_map/slice | solution.py:126
  62.8 1.7 %broadcast_select_fusion = (bf16[32,37,192]{2,1,0:T(8,128)(2,1)S(1)}, bf16[32,37,192]{2,1,0:T(8,128)(2,1)S(1)}) fusion(pred[]{:T(512)S(6)} %eq.41, bf16[32,37,192]{2,0,1:T(8,128)(2,1)} %collective-permute-done, bf16[32,53,192]{2,1,0:T(8,128)(2,1)} %copy-done.2), kind=kLoop, calls=%fused_computation.34 | loop fusion | flops 454656 | bytes 1818625 | tf_op jit(solution)/shard_map/jit(_where)/select_n | solution.py:131
  64.4 1.0 pad.7
  65.4 1.0 pad.8
  66.4 6.2 %shard_map.140 = bf16[512,192]{1,0:T(8,128)(2,1)} custom-call(bf16[512,192]{1,0:T(8,128)(2,1)} %bitcast.128, bf16[1280,192]{1,0:T(8,128)(2,1)} %bitcast.124, bf16[1280,192]{1,0:T(8,128)(2,1)} %bitcast.126, f32[1,1280]{1,0:T(1,128)} %reshape.488.valid_ref), custom_call_target="tpu_custom_call" | custom-call | tf_op jit(solution)/shard_map/pallas_call | solution.py:53
  72.5 17.0 %all_to_all.21 = bf16[32,16,192]{2,1,0:T(8,128)(2,1)S(1)} all-to-all(bf16[32,16,192]{2,1,0:T(8,128)(2,1)} %bitcast.129), channel_id=1, replica_groups=mesh['cfg'=2,'seq'=32,'tp'=4] {'seq'}, dimensions={0} | all-to-all | bytes 393216 | tf_op jit(solution)/shard_map/all_to_all | solution.py:150
  89.5 0.3 copy.39
  89.8 0.8 reshape.480
  90.7 2.8 %convolution_convert_fusion.1 = bf16[256,1536]{1,0:T(8,128)(2,1)} fusion(bf16[256,384]{1,0:T(8,128)(2,1)} %reshape.480, bf16[384,1536]{1,0:T(8,128)(2,1)} %param.22), kind=kOutput, calls=%fused_computation.1 | convolution fusion | flops 302383104 | bytes 2162688 | tf_op jit(solution)/shard_map/dot_general | solution.py:164
  93.5 4.5 %all-to-all-start.2 = ((bf16[4,64,1536]{2,1,0:T(8,128)(2,1)}), bf16[4,64,1536]{2,1,0:T(8,128)(2,1)}, u32[]{:S(2)}, u32[]{:S(2)}) async-start(bf16[4,64,1536]{2,1,0:T(8,128)(2,1)} %bitcast.123), calls=%async_computation.2 | async-start | bytes 1572864 | tf_op jit(solution)/shard_map/all_to_all | solution.py:61
  98.0 1.3 convert_element_type.122
  99.3 10.1 %all-to-all-done.2 = bf16[4,64,1536]{2,1,0:T(8,128)(2,1)} async-done(((bf16[4,64,1536]{2,1,0:T(8,128)(2,1)}), bf16[4,64,1536]{2,1,0:T(8,128)(2,1)}, u32[]{:S(2)}, u32[]{:S(2)}) %all-to-all-start.2) | async-done | bytes 786464 | tf_op jit(solution)/shard_map/all_to_all | solution.py:61
  109.4 1.3 convert_reduce_fusion.1
  110.7 1.1 fusion.75
  111.9 0.2 multiply_reduce_fusion.2
  112.1 0.1 add_convert_fusion.2
  112.2 14.1 %all_gather.3 = bf16[32,8,1536]{2,1,0:T(8,128)(2,1)} all-gather(bf16[8,8,1536]{2,1,0:T(8,128)(2,1)S(1)} %add_convert_fusion.2), channel_id=1, replica_groups=mesh['cfg'=2,'seq'=32,'tp'=4] {'tp'}, dimensions={0}, use_global_device_ids=true | all-gather | bytes 983040 | tf_op jit(solution)/shard_map/all_gather | solution.py:168
  126.3 4.5 %convolution_convert_fusion = bf16[256,1536]{1,0:T(8,128)(2,1)} fusion(bf16[768,1536]{1,0:T(8,128)(2,1)S(1)} %copy-done, bf16[1536,768]{1,0:T(8,128)(2,1)} %param.23, bf16[32,8,1536]{2,1,0:T(8,128)(2,1)} %all_gather.3), kind=kOutput, calls=%fused_computation | convolution fusion | flops 1210122240 | bytes 6291456 | tf_op jit(solution)/shard_map/dot_general | solution.py:172
  130.8 4.3 %all-to-all-start.3 = ((bf16[4,64,1536]{2,1,0:T(8,128)(2,1)}), bf16[4,64,1536]{2,1,0:T(8,128)(2,1)}, u32[]{:S(2)}, u32[]{:S(2)}) async-start(bf16[4,64,1536]{2,1,0:T(8,128)(2,1)} %bitcast.133), calls=%async_computation.3 | async-start | bytes 1572864 | tf_op jit(solution)/shard_map/all_to_all | solution.py:61
  135.1 0.0 copy-start.5
  135.2 0.0 copy-start.11
  135.2 0.0 copy-start.9
  135.2 9.5 %all-to-all-done.3 = bf16[4,64,1536]{2,1,0:T(8,128)(2,1)} async-done(((bf16[4,64,1536]{2,1,0:T(8,128)(2,1)}), bf16[4,64,1536]{2,1,0:T(8,128)(2,1)}, u32[]{:S(2)}, u32[]{:S(2)}) %all-to-all-start.3) | async-done | bytes 786464 | tf_op jit(solution)/shard_map/all_to_all | solution.py:61
  144.7 1.3 convert_reduce_fusion
  146.0 0.1 fusion.73
  146.1 0.2 multiply_reduce_fusion.1
  146.3 0.3 fusion.46
  146.6 0.1 constant_dynamic-slice_fusion
  146.7 0.8 collective-permute-start.1
  147.5 0.2 select_reduce_fusion
  147.7 4.4 %collective-permute-done.1 = f32[8,8,32]{2,1,0:T(8,128)S(1)} collective-permute-done((f32[8,8,32]{2,1,0:T(8,128)S(1)}, f32[8,8,32]{2,1,0:T(8,128)S(1)}, u32[]{:S(2)}, u32[]{:S(2)}) %collective-permute-start.1) | collective-permute-done | bytes 8224 | tf_op jit(solution)/shard_map/ppermute | solution.py:17
  152.1 0.7 multiply_add_fusion
  (34 shorter events, 0.2 us)
Async XLA Ops:
  0.6 125.6 %copy-start = (bf16[768,1536]{1,0:T(8,128)(2,1)S(1)}, bf16[768,1536]{1,0:T(8,128)(2,1)}, u32[]{:S(2)}) copy-start(bf16[768,1536]{1,0:T(8,128)(2,1)} %param.24) | copy-start | bytes 7077892
  0.6 1.8 %copy-start.1 = (bf16[1,32,8,1536]{3,2,1,0:T(8,128)(2,1)S(1)}, bf16[1,32,8,1536]{3,2,1,0:T(8,128)(2,1)}, u32[]{:S(2)}) copy-start(bf16[1,32,8,1536]{3,2,1,0:T(8,128)(2,1)} %param.13) | copy-start | bytes 2359300
  3.0 2.8 %copy-start.12 = (bf16[1536,3,384]{2,0,1:T(8,128)(2,1)S(1)}, bf16[1536,3,384]{2,0,1:T(8,128)(2,1)}, u32[]{:S(2)}) copy-start(bf16[1536,3,384]{2,0,1:T(8,128)(2,1)} %param.20) | copy-start | bytes 10616836
  7.1 1.7 %copy-start.3 = (bf16[1536,2,384]{2,1,0:T(2,128)(2,1)S(1)}, bf16[1536,2,384]{2,1,0:T(2,128)(2,1)}, u32[]{:S(2)}) copy-start(bf16[1536,2,384]{2,1,0:T(2,128)(2,1)} %param.21) | copy-start | bytes 7077892
  8.8 0.9 copy-start.4
  57.0 0.9 copy-start.2
  58.0 1.0 copy-start.13
  59.0 3.8 %collective-permute-start = (bf16[32,37,192]{2,0,1:T(8,128)(2,1)}, bf16[32,37,192]{2,0,1:T(8,128)(2,1)}, u32[]{:S(2)}, u32[]{:S(2)}) collective-permute-start(bf16[32,37,192]{2,0,1:T(8,128)(2,1)} %copy.36), channel_id=1, source_target_pairs={{0,4},{4,0},{8,12},{12,8},{16,20},{20,16},{24,28},{28,24},{32,36},... | collective-permute-start | bytes 1363976 | tf_op jit(solution)/shard_map/ppermute | solution.py:17
  93.5 15.9 %all-to-all-start.2 = ((bf16[4,64,1536]{2,1,0:T(8,128)(2,1)}), bf16[4,64,1536]{2,1,0:T(8,128)(2,1)}, u32[]{:S(2)}, u32[]{:S(2)}) async-start(bf16[4,64,1536]{2,1,0:T(8,128)(2,1)} %bitcast.123), calls=%async_computation.2 | async-start | bytes 1572864 | tf_op jit(solution)/shard_map/all_to_all | solution.py:61
  99.3 12.8 %copy-start.7 = (f32[8,1536]{1,0:T(8,128)S(1)}, f32[8,1536]{1,0:T(8,128)}, u32[]{:S(2)}) copy-start(f32[8,1536]{1,0:T(8,128)} %get-tuple-element.14) | copy-start | bytes 147460
  99.3 12.8 %copy-start.8 = (f32[8,1536]{1,0:T(8,128)S(1)}, f32[8,1536]{1,0:T(8,128)}, u32[]{:S(2)}) copy-start(f32[8,1536]{1,0:T(8,128)} %get-tuple-element.15) | copy-start | bytes 147460
  130.8 4.4 %copy-start.10 = (s32[8]{0:T(128)S(1)}, s32[8]{0:T(128)}, u32[]{:S(2)}) copy-start(s32[8]{0:T(128)} %param.17) | copy-start | bytes 100
  130.8 13.9 %all-to-all-start.3 = ((bf16[4,64,1536]{2,1,0:T(8,128)(2,1)}), bf16[4,64,1536]{2,1,0:T(8,128)(2,1)}, u32[]{:S(2)}, u32[]{:S(2)}) async-start(bf16[4,64,1536]{2,1,0:T(8,128)(2,1)} %bitcast.133), calls=%async_computation.3 | async-start | bytes 1572864 | tf_op jit(solution)/shard_map/all_to_all | solution.py:61
  135.1 11.2 %copy-start.5 = (bf16[1536,64]{0,1:T(8,128)(2,1)S(1)}, bf16[1536,64]{0,1:T(8,128)(2,1)}, u32[]{:S(2)}) copy-start(bf16[1536,64]{0,1:T(8,128)(2,1)} %param.25) | copy-start | bytes 589828
  135.1 11.2 %copy-start.6 = (f32[8,1536]{1,0:T(8,128)S(1)}, f32[8,1536]{1,0:T(8,128)}, u32[]{:S(2)}) copy-start(f32[8,1536]{1,0:T(8,128)} %get-tuple-element.13) | copy-start | bytes 147460
  135.2 12.3 %copy-start.11 = (f32[9]{0:T(128)S(1)}, f32[9]{0:T(128)}, u32[]{:S(2)}) copy-start(f32[9]{0:T(128)} %param.18) | copy-start | bytes 112
  135.2 16.9 %copy-start.9 = (f32[8,8,32]{2,1,0:T(8,128)S(1)}, f32[8,8,32]{2,1,0:T(8,128)}, u32[]{:S(2)}) copy-start(f32[8,8,32]{2,1,0:T(8,128)} %param.19) | copy-start | bytes 24580
  146.7 5.5 %collective-permute-start.1 = (f32[8,8,32]{2,1,0:T(8,128)S(1)}, f32[8,8,32]{2,1,0:T(8,128)S(1)}, u32[]{:S(2)}, u32[]{:S(2)}) collective-permute-start(f32[8,8,32]{2,1,0:T(8,128)S(1)} %constant_dynamic-slice_fusion), channel_id=1, source_target_pairs={{0,128},{128,0},{1,129},{129,1},{2,130},{130,2},{3,131},{131,3},{4... | collective-permute-start | bytes 24584 | tf_op jit(solution)/shard_map/ppermute | solution.py:17

commit v9 on v8

--- a/solution.py
+++ b/solution.py
@@ -4,6 +4,7 @@
 import jax.numpy as jnp
 from jax import lax
 from jax.experimental import pallas as pl
+from jax.experimental.pallas import tpu as pltpu
 from jax.sharding import PartitionSpec as P
 
 HEAD_DIM = 64
@@ -26,7 +27,7 @@
     return (layer_norm(values) * (1.0 + scale_mul) + shift_add).astype(jnp.bfloat16)
 
 
-def attention_kernel(q_ref, k_ref, v_ref, valid_ref, o_ref):
+def attention_body(q_ref, k_ref, v_ref, valid_ref, o_ref):
     queries = q_ref[...]
     keys = k_ref[...]
     values = v_ref[...]
@@ -49,11 +50,27 @@
         result = jnp.where(chosen, mixed, result)
     o_ref[...] = result.astype(o_ref.dtype)
 
-def attend_kernel(queries, keys, values, valid):
+
+def attention_kernel(order_ref, q_ref, mine_ref, other_ref, valid_ref, o_ref):
+    keys_first = order_ref[0] == 0
+
+    @pl.when(keys_first)
+    def _():
+        attention_body(q_ref, mine_ref, other_ref, valid_ref, o_ref)
+
+    @pl.when(jnp.logical_not(keys_first))
+    def _():
+        attention_body(q_ref, other_ref, mine_ref, valid_ref, o_ref)
+
+
+def attend_kernel(order, queries, kv_mine, kv_other, valid):
+    whole = pl.BlockSpec(memory_space=pltpu.VMEM)
     return pl.pallas_call(
         attention_kernel,
         out_shape=jax.ShapeDtypeStruct(queries.shape, jnp.bfloat16),
-    )(queries, keys, values, valid)
+        in_specs=[pl.BlockSpec(memory_space=pltpu.SMEM), whole, whole, whole, whole],
+        out_specs=whole,
+    )(order, queries, kv_mine, kv_other, valid)
 
 
 def reduce_rows(partial, parties):
@@ -99,11 +116,12 @@
     text_in = modulate(txt_hidden[0].astype(jnp.float32), adaptive[:, 6], adaptive[:, 7]).reshape(
         txt_slice * requests, model_width
     )
-    text_kv = jnp.dot(
-        text_in, w_kv_text.reshape(model_width, 2 * features), preferred_element_type=jnp.float32
-    ).astype(jnp.bfloat16)
-    keys_txt = text_kv[:, :features].reshape(txt_slice, requests, features)
-    vals_txt = text_kv[:, features:].reshape(txt_slice, requests, features)
+    keys_txt, vals_txt = [
+        jnp.dot(text_in, w_kv_text[:, part], preferred_element_type=jnp.float32)
+        .astype(jnp.bfloat16)
+        .reshape(txt_slice, requests, features)
+        for part in range(2)
+    ]
     key_span = img_slice + txt_slice
     senders = requests * members
     halves = members // 2
@@ -126,9 +144,6 @@
     query_got = got[:, :query_share]
     kv_mine = got[:, query_share:]
     kv_other = swapped(kv_mine, "seq", 0)
-    first_core = lax.axis_index("seq") % 2 == 0
-    key_got = jnp.where(first_core, kv_mine, kv_other)
-    value_got = jnp.where(first_core, kv_other, kv_mine)
     my_request = lax.axis_index("seq") // members
     length_now = jnp.sum(jnp.where(jnp.arange(requests) == my_request, lengths_all, 0))
     padded_span = -(-key_span // 8) * 8
@@ -142,9 +157,10 @@
         )
 
     answer = attend_kernel(
+        (lax.axis_index("seq") % 2).reshape(1).astype(jnp.int32),
         query_got.reshape(senders * query_share, head_share),
-        padded(key_got),
-        padded(value_got),
+        padded(kv_mine),
+        padded(kv_other),
         key_valid.astype(jnp.float32).reshape(1, senders * padded_span),
     )
     answer_back = lax.all_to_all(

time: 154 us -> 160 us (1.039)
  local copies, waits for them, and re-layouts: 16.8 us -> 21.4 us
  matrix products: 13.6 us -> 16.1 us
    slice x1, local copies, waits for them, and re-layouts: 0.62 us -> 4.32 us  [shards(): w_kv_text[:, part]]
    dot_general x1 -> x2, matrix products: 0.58 us -> 3.07 us  [shards(): jnp.dot(text_in, w_kv_text[:, part], preferred_element_type=jnp.float32)]
    select_n x1 -> x0, other arithmetic: 1.66 us -> none  [shards(): value_got = jnp.where(first_core, kv_other, kv_mine)]
  transfers between devices with their start and end apart: 4 -> 4, of which waited for: 3 -> 3; matrix products, arithmetic and copies ran while one was open for 3% -> 5% of each run, Pallas kernels for 0% -> 0%
where the time goes in v9:
time: 160 us; the launch traced here: 159 us
  blocking collectives  66.2 us (41%)
  waiting for transfers between devices  24 us (15%)
  local copies, waits for them, and re-layouts  21.4 us (13%)
  matrix products  16.1 us (10%)
  other arithmetic  14 us (9%)
  starting transfers between devices  9.62 us (6%)
  Pallas kernels  6.34 us (4%)
    all_to_all x1, blocking collectives, shards(): lax.all_to_all(payload, 'seq', split_axis=0, concat_axis=0, tiled=True)  35.2 us
    all_to_all x2, waiting for transfers between devices, reduce_rows(): got = lax.all_to_all(pieces, 'tp', split_axis=0, concat_axis=0, tiled=True)  19.6 us
    all_to_all x1, blocking collectives, shards(): lax.all_to_all(answer.reshape(senders, query_share, head_share), 'seq', s...  17 us
    all_gather x1, blocking collectives, shards(): lax.all_gather(mlp_mine, 'tp', axis=0, tiled=True)  14.1 us
    all_to_all x2, starting transfers between devices, reduce_rows(): got = lax.all_to_all(pieces, 'tp', split_axis=0, concat_axis=0, tiled=True)  8.79 us
    pallas_call x1, Pallas kernels, attend_kernel(): pl.pallas_call(attention_kernel, out_shape=jax.ShapeDtypeStruct(queries.s...  6.34 us
    dot_general x3, matrix products, shards(): jnp.dot(normed, w_qkv[:, part], preferred_element_type=jnp.float32)  5.39 us
    dot_general x1, matrix products, shards(): jnp.dot(hidden, w_down, preferred_element_type=jnp.float32)  4.54 us
  transfers between devices with their start and end apart: 4, of which 3 were waited for; matrix products, arithmetic and copies ran while one was open for 5% of the time, Pallas kernels for 0%

profile of v9, /device:TPU:4, one launch (start us, length us, event | category | flops | bytes accessed | tf_op | source)
XLA Modules:
  0.0 158.6 jit_solution(12763716271992344822)
XLA Ops:
  0.6 0.0 copy-start
  0.7 1.1 bitcast_convert_fusion
  1.8 0.7 fusion.57
  2.5 0.2 convert_reduce_fusion.2
  2.7 0.3 multiply_reduce_fusion
  3.1 0.0 copy-start.18
  3.1 2.7 %fusion.17 = bf16[256,384]{1,0:T(8,128)(2,1)} fusion(bf16[1536,3,384]{2,0,1:T(8,128)(2,1)} %param.20, bf16[1,32,8,1536]{3,2,1,0:T(8,128)(2,1)S(1)} %copy-done.2, f32[8,1536]{1,0:T(8,128)S(1)} %get-tuple-element.19, f32[8,1536]{1,0:T(8,128)S(1)} %get-tuple-element.20, f32[32,8]{1,0:T(8,128)S(1)} %add_rsqrt_fusion, f32[32,8]{1,0:T(8,128)S(1)} %broadcast_multiply_fusion), kind=kOutput, calls=%fused_computation.24 | convolution fusion | flops 304447488 | bytes 2263040 | tf_op jit(solution)/shard_map/dot_general | solution.py:111
  5.8 1.3 fusion.14
  7.2 1.3 fusion.11
  8.5 0.4 copy-done.1
  8.9 4.3 %fusion.78 = (bf16[1536,1,384]{2,1,0:T(2,128)(2,1)}, bf16[1536,1,384]{2,1,0:T(2,128)(2,1)S(1)}) fusion(bf16[1536,2,384]{2,1,0:T(2,128)(2,1)S(1)} %copy-done.1), kind=kLoop, calls=%fused_computation.114 | loop fusion | bytes 4718592 | tf_op jit(solution)/shard_map/slice | solution.py:120
  13.2 0.1 convert_reduce_fusion.3
  13.3 0.2 fusion.46
  13.5 0.4 fusion.21
  13.9 0.7 concatenate.23
  14.6 1.1 concatenate.22
  15.8 2.7 %fusion.20 = bf16[40,384]{1,0:T(8,128)(2,1)} fusion(bf16[1536,1,384]{2,1,0:T(2,128)(2,1)} %get-tuple-element.10, bf16[1,5,8,1536]{3,2,1,0:T(8,128)(2,1)S(1)} %copy-done.5, f32[8,1536]{1,0:T(8,128)} %copy-done.13, f32[8,1536]{1,0:T(8,128)} %copy-done.14, f32[5,8]{1,0:T(8,128)S(1)} %add_rsqrt_fusion.3, f32[5,8]{1,0:T(8,128)S(1)} %broadcast_multiply_fusion.3), kind=kOutput, calls=%fused_computation.25 | convolution fusion | flops 47569920 | bytes 1431872 | tf_op jit(solution)/shard_map/dot_general | solution.py:120
  18.5 0.8 concatenate.20
  19.3 1.8 %concatenate.19 = bf16[32,8,2,1,192]{4,2,1,0,3:T(2,128)(2,1)} reshape(bf16[256,384]{1,0:T(8,128)(2,1)} %fusion.14) | data formatting | bytes 393216 | tf_op jit(solution)/shard_map/concatenate | solution.py:135
  21.1 2.0 %maximum_bitcast_fusion = bf16[8,2,2,37,192]{4,1,0,3,2:T(2,128)(2,1)S(1)} fusion(bf16[5,8,2,1,192]{4,2,1,0,3:T(2,128)(2,1)} %concatenate.23, bf16[32,8,2,1,192]{4,2,1,0,3:T(2,128)(2,1)S(1)} %concatenate.22, bf16[5,8,2,1,192]{4,2,1,0,3:T(2,128)(2,1)S(1)} %concatenate.20, bf16[32,8,2,1,192]{4,2,1,0,3:T(2,128)(2,1)} %concatenate.19), kind=kLoop, calls=%fused_computation.39 | loop fusion | flops 681984 | bytes 909312 | tf_op jit(solution)/shard_map/transpose | solution.py:139
  23.2 1.0 copy.44
  24.2 1.1 reshape_reshape.3
  25.3 0.1 copy.41
  25.4 1.2 pad_maximum_fusion
  26.7 35.2 %all_to_all.20 = bf16[32,53,192]{2,1,0:T(8,128)(2,1)S(1)} all-to-all(bf16[32,53,192]{2,1,0:T(8,128)(2,1)S(1)} %pad_maximum_fusion), channel_id=1, replica_groups=mesh['cfg'=2,'seq'=32,'tp'=4] {'seq'}, dimensions={0} | all-to-all | bytes 1302528 | tf_op jit(solution)/shard_map/all_to_all | solution.py:143
  61.9 0.9 copy-done.3
  62.8 1.0 copy.45
  63.7 0.0 collective-permute-start
  63.8 0.6 fusion.66
  64.4 0.7 fusion.63
  65.2 0.7 reshape.536.valid_ref
  65.8 2.1 %pad.7 = bf16[32,40,192]{2,1,0:T(8,128)(2,1)} pad(bf16[32,37,192]{2,1,0:T(8,128)(2,1)} %copy-done.3, bf16[]{:T(256)} %constant.79.clone.1), padding=0_0x0_3x0_0 | pad | bytes 946178 | tf_op jit(solution)/shard_map/jit(_pad)/pad | solution.py:155
  67.9 1.7 %slice.73 = bf16[32,16,192]{2,1,0:T(8,128)(2,1)} slice(bf16[32,53,192]{2,1,0:T(8,128)(2,1)} %copy-done.4), slice={[0:32], [0:16], [0:192]} | slice | bytes 393216 | tf_op jit(solution)/shard_map/slice | solution.py:144
  69.6 0.0 collective-permute-done
  69.6 1.4 copy.50
  71.0 1.0 pad.8.clone
  71.9 6.3 %shard_map.140 = bf16[512,192]{1,0:T(8,128)(2,1)} custom-call(s32[1]{0:T(128)} %bitcast.3.order_ref, bf16[512,192]{1,0:T(8,128)(2,1)} %bitcast.139, bf16[1280,192]{1,0:T(8,128)(2,1)} %bitcast.134, bf16[1280,192]{1,0:T(8,128)(2,1)} %bitcast.135, f32[1,1280]{1,0:T(1,128)} %reshape.536.valid_ref), custom_call_target="tpu_custom_call" | custom-call | tf_op jit(solution)/shard_map/pallas_call | solution.py:68
  78.3 17.0 %all_to_all.21 = bf16[32,16,192]{2,1,0:T(8,128)(2,1)S(1)} all-to-all(bf16[32,16,192]{2,1,0:T(8,128)(2,1)} %bitcast.140), channel_id=1, replica_groups=mesh['cfg'=2,'seq'=32,'tp'=4] {'seq'}, dimensions={0} | all-to-all | bytes 393216 | tf_op jit(solution)/shard_map/all_to_all | solution.py:166
  95.3 0.3 copy.47
  95.6 0.8 reshape.528
  96.4 2.8 %convolution_convert_fusion.1 = bf16[256,1536]{1,0:T(8,128)(2,1)} fusion(bf16[256,384]{1,0:T(8,128)(2,1)} %reshape.528, bf16[384,1536]{1,0:T(8,128)(2,1)} %param.22), kind=kOutput, calls=%fused_computation.1 | convolution fusion | flops 302383104 | bytes 2162688 | tf_op jit(solution)/shard_map/dot_general | solution.py:180
  99.3 4.5 %all-to-all-start.2 = ((bf16[4,64,1536]{2,1,0:T(8,128)(2,1)}), bf16[4,64,1536]{2,1,0:T(8,128)(2,1)}, u32[]{:S(2)}, u32[]{:S(2)}) async-start(bf16[4,64,1536]{2,1,0:T(8,128)(2,1)} %bitcast.132), calls=%async_computation.2 | async-start | bytes 1572864 | tf_op jit(solution)/shard_map/all_to_all | solution.py:78
  103.7 1.3 convert_element_type.133
  105.1 10.1 %all-to-all-done.2 = bf16[4,64,1536]{2,1,0:T(8,128)(2,1)} async-done(((bf16[4,64,1536]{2,1,0:T(8,128)(2,1)}), bf16[4,64,1536]{2,1,0:T(8,128)(2,1)}, u32[]{:S(2)}, u32[]{:S(2)}) %all-to-all-start.2) | async-done | bytes 786464 | tf_op jit(solution)/shard_map/all_to_all | solution.py:78
  115.2 1.3 convert_reduce_fusion.1
  116.5 1.1 fusion.76
  117.6 0.2 multiply_reduce_fusion.2
  117.8 0.1 add_convert_fusion.2
  118.0 14.1 %all_gather.3 = bf16[32,8,1536]{2,1,0:T(8,128)(2,1)} all-gather(bf16[8,8,1536]{2,1,0:T(8,128)(2,1)S(1)} %add_convert_fusion.2), channel_id=1, replica_groups=mesh['cfg'=2,'seq'=32,'tp'=4] {'tp'}, dimensions={0}, use_global_device_ids=true | all-gather | bytes 983040 | tf_op jit(solution)/shard_map/all_gather | solution.py:184
  132.0 4.5 %convolution_convert_fusion = bf16[256,1536]{1,0:T(8,128)(2,1)} fusion(bf16[768,1536]{1,0:T(8,128)(2,1)S(1)} %copy-done, bf16[1536,768]{1,0:T(8,128)(2,1)} %param.23, bf16[32,8,1536]{2,1,0:T(8,128)(2,1)} %all_gather.3), kind=kOutput, calls=%fused_computation | convolution fusion | flops 1210122240 | bytes 6291456 | tf_op jit(solution)/shard_map/dot_general | solution.py:188
  136.6 4.3 %all-to-all-start.3 = ((bf16[4,64,1536]{2,1,0:T(8,128)(2,1)}), bf16[4,64,1536]{2,1,0:T(8,128)(2,1)}, u32[]{:S(2)}, u32[]{:S(2)}) async-start(bf16[4,64,1536]{2,1,0:T(8,128)(2,1)} %bitcast.141), calls=%async_computation.3 | async-start | bytes 1572864 | tf_op jit(solution)/shard_map/all_to_all | solution.py:78
  140.9 0.0 copy-start.8
  141.0 0.0 copy-start.17
  141.0 0.0 copy-start.15
  141.0 9.5 %all-to-all-done.3 = bf16[4,64,1536]{2,1,0:T(8,128)(2,1)} async-done(((bf16[4,64,1536]{2,1,0:T(8,128)(2,1)}), bf16[4,64,1536]{2,1,0:T(8,128)(2,1)}, u32[]{:S(2)}, u32[]{:S(2)}) %all-to-all-start.3) | async-done | bytes 786464 | tf_op jit(solution)/shard_map/all_to_all | solution.py:78
  150.4 1.3 convert_reduce_fusion
  151.7 0.1 fusion.74
  151.9 0.2 multiply_reduce_fusion.1
  152.1 0.3 fusion.50
  152.4 0.1 constant_dynamic-slice_fusion
  152.4 0.8 collective-permute-start.1
  153.3 0.2 select_reduce_fusion
  153.5 4.4 %collective-permute-done.1 = f32[8,8,32]{2,1,0:T(8,128)S(1)} collective-permute-done((f32[8,8,32]{2,1,0:T(8,128)S(1)}, f32[8,8,32]{2,1,0:T(8,128)S(1)}, u32[]{:S(2)}, u32[]{:S(2)}) %collective-permute-start.1) | collective-permute-done | bytes 8224 | tf_op jit(solution)/shard_map/ppermute | solution.py:18
  157.9 0.7 multiply_add_fusion
  (46 shorter events, 0.2 us)
Async XLA Ops:
  0.6 131.4 %copy-start = (bf16[768,1536]{1,0:T(8,128)(2,1)S(1)}, bf16[768,1536]{1,0:T(8,128)(2,1)}, u32[]{:S(2)}) copy-start(bf16[768,1536]{1,0:T(8,128)(2,1)} %param.24) | copy-start | bytes 7077892
  0.6 1.9 %copy-start.2 = (bf16[1,32,8,1536]{3,2,1,0:T(8,128)(2,1)S(1)}, bf16[1,32,8,1536]{3,2,1,0:T(8,128)(2,1)}, u32[]{:S(2)}) copy-start(bf16[1,32,8,1536]{3,2,1,0:T(8,128)(2,1)} %param.13) | copy-start | bytes 2359300
  2.5 11.0 %copy-start.13 = (f32[8,1536]{1,0:T(8,128)}, f32[8,1536]{1,0:T(8,128)S(1)}, u32[]{:S(2)}) copy-start(f32[8,1536]{1,0:T(8,128)S(1)} %get-tuple-element.17) | copy-start | bytes 147460
  2.5 11.0 %copy-start.14 = (f32[8,1536]{1,0:T(8,128)}, f32[8,1536]{1,0:T(8,128)S(1)}, u32[]{:S(2)}) copy-start(f32[8,1536]{1,0:T(8,128)S(1)} %get-tuple-element.18) | copy-start | bytes 147460
  3.1 2.7 %copy-start.18 = (bf16[1536,3,384]{2,0,1:T(8,128)(2,1)S(1)}, bf16[1536,3,384]{2,0,1:T(8,128)(2,1)}, u32[]{:S(2)}) copy-start(bf16[1536,3,384]{2,0,1:T(8,128)(2,1)} %param.20) | copy-start | bytes 10616836
  7.2 1.7 %copy-start.1 = (bf16[1536,2,384]{2,1,0:T(2,128)(2,1)S(1)}, bf16[1536,2,384]{2,1,0:T(2,128)(2,1)}, u32[]{:S(2)}) copy-start(bf16[1536,2,384]{2,1,0:T(2,128)(2,1)} %param.21) | copy-start | bytes 7077892
  8.9 4.3 %copy-start.5 = (bf16[1,5,8,1536]{3,2,1,0:T(8,128)(2,1)S(1)}, bf16[1,5,8,1536]{3,2,1,0:T(8,128)(2,1)}, u32[]{:S(2)}) copy-start(bf16[1,5,8,1536]{3,2,1,0:T(8,128)(2,1)} %param.14) | copy-start | bytes 368644
  61.8 1.9 %copy-start.4 = (bf16[32,53,192]{2,1,0:T(8,128)(2,1)}, bf16[32,53,192]{2,1,0:T(8,128)(2,1)S(1)}, u32[]{:S(2)}) copy-start(bf16[32,53,192]{2,1,0:T(8,128)(2,1)S(1)} %all_to_all.20) | copy-start | bytes 1953796
  61.8 2.0 %copy-start.19 = (s32[1,8]{1,0:T(1,128)S(1)}, s32[1,8]{1,0:T(1,128)}, u32[]{:S(2)}) copy-start(s32[1,8]{1,0:T(1,128)} %param.16) | copy-start | bytes 100
  61.9 0.9 copy-start.3
  63.7 5.8 %collective-permute-start = (bf16[32,37,192]{2,0,1:T(8,128)(2,1)}, bf16[32,37,192]{2,0,1:T(8,128)(2,1)}, u32[]{:S(2)}, u32[]{:S(2)}) collective-permute-start(bf16[32,37,192]{2,0,1:T(8,128)(2,1)} %copy.45), channel_id=1, source_target_pairs={{0,4},{4,0},{8,12},{12,8},{16,20},{20,16},{24,28},{28,24},{32,36},... | collective-permute-start | bytes 1363976 | tf_op jit(solution)/shard_map/ppermute | solution.py:18
  99.3 15.9 %all-to-all-start.2 = ((bf16[4,64,1536]{2,1,0:T(8,128)(2,1)}), bf16[4,64,1536]{2,1,0:T(8,128)(2,1)}, u32[]{:S(2)}, u32[]{:S(2)}) async-start(bf16[4,64,1536]{2,1,0:T(8,128)(2,1)} %bitcast.132), calls=%async_computation.2 | async-start | bytes 1572864 | tf_op jit(solution)/shard_map/all_to_all | solution.py:78
  103.7 12.8 %copy-start.7 = (f32[8,1536]{1,0:T(8,128)S(1)}, f32[8,1536]{1,0:T(8,128)}, u32[]{:S(2)}) copy-start(f32[8,1536]{1,0:T(8,128)} %get-tuple-element.21) | copy-start | bytes 147460
  105.1 12.8 %copy-start.11 = (f32[8,1536]{1,0:T(8,128)S(1)}, f32[8,1536]{1,0:T(8,128)}, u32[]{:S(2)}) copy-start(f32[8,1536]{1,0:T(8,128)} %get-tuple-element.14) | copy-start | bytes 147460
  105.1 12.8 %copy-start.12 = (f32[8,1536]{1,0:T(8,128)S(1)}, f32[8,1536]{1,0:T(8,128)}, u32[]{:S(2)}) copy-start(f32[8,1536]{1,0:T(8,128)} %get-tuple-element.15) | copy-start | bytes 147460
  136.6 4.4 %copy-start.16 = (s32[8]{0:T(128)S(1)}, s32[8]{0:T(128)}, u32[]{:S(2)}) copy-start(s32[8]{0:T(128)} %param.17) | copy-start | bytes 100
  136.6 15.2 %copy-start.6 = (f32[8,1536]{1,0:T(8,128)S(1)}, f32[8,1536]{1,0:T(8,128)}, u32[]{:S(2)}) copy-start(f32[8,1536]{1,0:T(8,128)} %get-tuple-element.16) | copy-start | bytes 147460
  136.6 13.9 %all-to-all-start.3 = ((bf16[4,64,1536]{2,1,0:T(8,128)(2,1)}), bf16[4,64,1536]{2,1,0:T(8,128)(2,1)}, u32[]{:S(2)}, u32[]{:S(2)}) async-start(bf16[4,64,1536]{2,1,0:T(8,128)(2,1)} %bitcast.141), calls=%async_computation.3 | async-start | bytes 1572864 | tf_op jit(solution)/shard_map/all_to_all | solution.py:78
  140.9 11.2 %copy-start.8 = (bf16[1536,64]{0,1:T(8,128)(2,1)S(1)}, bf16[1536,64]{0,1:T(8,128)(2,1)}, u32[]{:S(2)}) copy-start(bf16[1536,64]{0,1:T(8,128)(2,1)} %param.25) | copy-start | bytes 589828
  140.9 11.2 %copy-start.9 = (f32[8,1536]{1,0:T(8,128)S(1)}, f32[8,1536]{1,0:T(8,128)}, u32[]{:S(2)}) copy-start(f32[8,1536]{1,0:T(8,128)} %get-tuple-element.12) | copy-start | bytes 147460
  140.9 11.2 %copy-start.10 = (f32[8,1536]{1,0:T(8,128)S(1)}, f32[8,1536]{1,0:T(8,128)}, u32[]{:S(2)}) copy-start(f32[8,1536]{1,0:T(8,128)} %get-tuple-element.13) | copy-start | bytes 147460
  141.0 12.3 %copy-start.17 = (f32[9]{0:T(128)S(1)}, f32[9]{0:T(128)}, u32[]{:S(2)}) copy-start(f32[9]{0:T(128)} %param.18) | copy-start | bytes 112
  141.0 16.9 %copy-start.15 = (f32[8,8,32]{2,1,0:T(8,128)S(1)}, f32[8,8,32]{2,1,0:T(8,128)}, u32[]{:S(2)}) copy-start(f32[8,8,32]{2,1,0:T(8,128)} %param.19) | copy-start | bytes 24580
  152.4 5.5 %collective-permute-start.1 = (f32[8,8,32]{2,1,0:T(8,128)S(1)}, f32[8,8,32]{2,1,0:T(8,128)S(1)}, u32[]{:S(2)}, u32[]{:S(2)}) collective-permute-start(f32[8,8,32]{2,1,0:T(8,128)S(1)} %constant_dynamic-slice_fusion), channel_id=1, source_target_pairs={{0,128},{128,0},{1,129},{129,1},{2,130},{130,2},{3,131},{131,3},{4... | collective-permute-start | bytes 24584 | tf_op jit(solution)/shard_map/ppermute | solution.py:18

commit v10 on v8

--- a/solution.py
+++ b/solution.py
@@ -26,34 +26,50 @@
     return (layer_norm(values) * (1.0 + scale_mul) + shift_add).astype(jnp.bfloat16)
 
 
-def attention_kernel(q_ref, k_ref, v_ref, valid_ref, o_ref):
+def attention_kernel(q_ref, ki_ref, vi_ref, kt_ref, vt_ref, valid_ref, o_ref):
     queries = q_ref[...]
-    keys = k_ref[...]
-    values = v_ref[...]
+    keys_img = ki_ref[...]
+    values_img = vi_ref[...]
+    keys_txt = kt_ref[...]
+    values_txt = vt_ref[...]
     valid = valid_ref[...] > 0.5
     width = queries.shape[1]
     lane_head = lax.broadcasted_iota(jnp.int32, (1, width), 1) // HEAD_DIM
+    contract = (((1,), (1,)), ((), ()))
+    scale = 1.0 / math.sqrt(HEAD_DIM)
     result = jnp.zeros(o_ref.shape, jnp.float32)
     for head in range(width // HEAD_DIM):
         chosen = lane_head == head
         query_head = jnp.where(chosen, queries, jnp.zeros_like(queries))
-        scores = lax.dot_general(
-            query_head, keys, (((1,), (1,)), ((), ())), preferred_element_type=jnp.float32
-        ) * (1.0 / math.sqrt(HEAD_DIM))
-        scores = jnp.where(valid, scores, -jnp.inf)
-        row_max = jnp.max(scores, axis=1, keepdims=True)
-        exp_scores = jnp.exp(scores - row_max)
-        total = jnp.sum(exp_scores, axis=1, keepdims=True)
-        weights = (exp_scores / total).astype(jnp.bfloat16)
-        mixed = jnp.dot(weights, values, preferred_element_type=jnp.float32)
+        scores_img = (
+            lax.dot_general(query_head, keys_img, contract, preferred_element_type=jnp.float32)
+            * scale
+        )
+        scores_txt = (
+            lax.dot_general(query_head, keys_txt, contract, preferred_element_type=jnp.float32)
+            * scale
+        )
+        scores_txt = jnp.where(valid, scores_txt, -jnp.inf)
+        row_max = jnp.maximum(
+            jnp.max(scores_img, axis=1, keepdims=True), jnp.max(scores_txt, axis=1, keepdims=True)
+        )
+        exp_img = jnp.exp(scores_img - row_max)
+        exp_txt = jnp.exp(scores_txt - row_max)
+        total = jnp.sum(exp_img, axis=1, keepdims=True) + jnp.sum(exp_txt, axis=1, keepdims=True)
+        weights_img = (exp_img / total).astype(jnp.bfloat16)
+        weights_txt = (exp_txt / total).astype(jnp.bfloat16)
+        mixed = jnp.dot(weights_img, values_img, preferred_element_type=jnp.float32) + jnp.dot(
+            weights_txt, values_txt, preferred_element_type=jnp.float32
+        )
         result = jnp.where(chosen, mixed, result)
     o_ref[...] = result.astype(o_ref.dtype)
 
-def attend_kernel(queries, keys, values, valid):
+
+def attend_kernel(queries, keys_img, values_img, keys_txt, values_txt, valid):
     return pl.pallas_call(
         attention_kernel,
         out_shape=jax.ShapeDtypeStruct(queries.shape, jnp.bfloat16),
-    )(queries, keys, values, valid)
+    )(queries, keys_img, values_img, keys_txt, values_txt, valid)
 
 
 def reduce_rows(partial, parties):
@@ -131,21 +147,25 @@
     value_got = jnp.where(first_core, kv_other, kv_mine)
     my_request = lax.axis_index("seq") // members
     length_now = jnp.sum(jnp.where(jnp.arange(requests) == my_request, lengths_all, 0))
-    padded_span = -(-key_span // 8) * 8
-    slot = jnp.arange(padded_span)
-    text_slot = jnp.arange(senders)[:, None] * txt_slice + slot[None, :] - img_slice
-    key_valid = (slot[None, :] < img_slice) | ((slot[None, :] < key_span) & (text_slot < length_now))
-
-    def padded(block):
-        return jnp.pad(block, ((0, 0), (0, padded_span - key_span), (0, 0))).reshape(
-            senders * padded_span, head_share
+    text_rows = senders * txt_slice
+    text_span = -(-text_rows // 128) * 128
+    text_valid = jnp.arange(text_span) < jnp.minimum(length_now, text_rows)
+
+    def image_part(block):
+        return block[:, :img_slice].reshape(senders * img_slice, head_share)
+
+    def text_part(block):
+        return jnp.pad(
+            block[:, img_slice:].reshape(text_rows, head_share), ((0, text_span - text_rows), (0, 0))
         )
 
     answer = attend_kernel(
         query_got.reshape(senders * query_share, head_share),
-        padded(key_got),
-        padded(value_got),
-        key_valid.astype(jnp.float32).reshape(1, senders * padded_span),
+        image_part(key_got),
+        image_part(value_got),
+        text_part(key_got),
+        text_part(value_got),
+        text_valid.astype(jnp.float32).reshape(1, text_span),
     )
     answer_back = lax.all_to_all(
         answer.reshape(senders, query_share, head_share),

time: 154 us -> 153 us (level)
    slice x0 -> x4, local copies, waits for them, and re-layouts: none -> 1.75 us  [the longest x2 1.74 us: image_part(): return block[:, :img_slice].reshape(senders * img_slice, head_share)]
where the time goes in v10:
time: 153 us
  blocking collectives  66.2 us (43%)
  waiting for transfers between devices  24 us (16%)
  local copies, waits for them, and re-layouts  16.2 us (11%)
  other arithmetic  15.4 us (10%)
  matrix products  13.6 us (9%)
  starting transfers between devices  9.63 us (6%)
  Pallas kernels  6 us (4%)
  between operations  1.54 us (1%)
    all_to_all x1, blocking collectives, shards(): lax.all_to_all(payload, 'seq', split_axis=0, concat_axis=0, tiled=True)  35.2 us
    all_to_all x2, waiting for transfers between devices, reduce_rows(): got = lax.all_to_all(pieces, 'tp', split_axis=0, concat_axis=0, tiled=True)  19.6 us
    all_to_all x1, blocking collectives, shards(): lax.all_to_all(answer.reshape(senders, query_share, head_share), 'seq', s...  17 us
    all_gather x1, blocking collectives, shards(): lax.all_gather(mlp_mine, 'tp', axis=0, tiled=True)  14.1 us
    all_to_all x2, starting transfers between devices, reduce_rows(): got = lax.all_to_all(pieces, 'tp', split_axis=0, concat_axis=0, tiled=True)  8.79 us
    pallas_call x1, Pallas kernels, attend_kernel(): pl.pallas_call(attention_kernel, out_shape=jax.ShapeDtypeStruct(queries.s...  6 us
    dot_general x3, matrix products, shards(): jnp.dot(normed, w_qkv[:, part], preferred_element_type=jnp.float32)  5.36 us
    dot_general x1, matrix products, shards(): jnp.dot(hidden, w_down, preferred_element_type=jnp.float32)  4.54 us
  transfers between devices with their start and end apart: 4, of which 3 were waited for; matrix products, arithmetic and copies ran while one was open for 3% of the time, Pallas kernels for 0%

profile of v10, /device:TPU:4, one launch (start us, length us, event | category | flops | bytes accessed | tf_op | source)
XLA Modules:
  0.0 152.5 jit_solution(2253803777155293004)
XLA Ops:
  0.6 0.0 copy-start
  0.7 1.1 bitcast_convert_fusion
  1.8 0.7 fusion.58
  2.5 0.2 convert_reduce_fusion.2
  2.7 0.3 multiply_reduce_fusion
  3.1 0.0 copy-start.14
  3.1 2.7 %fusion.15 = bf16[256,384]{1,0:T(8,128)(2,1)} fusion(bf16[1536,3,384]{2,0,1:T(8,128)(2,1)} %param.20, bf16[1,32,8,1536]{3,2,1,0:T(8,128)(2,1)S(1)} %copy-done.1, f32[8,1536]{1,0:T(8,128)S(1)} %get-tuple-element.19, f32[8,1536]{1,0:T(8,128)S(1)} %get-tuple-element.20, f32[32,8]{1,0:T(8,128)S(1)} %add_rsqrt_fusion, f32[32,8]{1,0:T(8,128)S(1)} %broadcast_multiply_fusion), kind=kOutput, calls=%fused_computation.20 | convolution fusion | flops 304447488 | bytes 2263040 | tf_op jit(solution)/shard_map/dot_general | solution.py:110
  5.8 1.3 fusion.12
  7.1 1.3 fusion.9
  8.4 0.4 copy-done.3
  8.9 0.5 copy.42
  9.4 0.4 copy-done.4
  9.8 0.1 convert_reduce_fusion.3
  9.9 0.2 fusion.42
  10.1 0.6 convolution_convert_fusion.2
  10.7 0.6 fusion.74
  11.3 0.1 concatenate.23
  11.4 1.1 concatenate.22
  12.5 0.8 concatenate.20
  13.3 1.8 %concatenate.19 = bf16[32,8,2,1,192]{4,2,1,0,3:T(2,128)(2,1)} reshape(bf16[256,384]{1,0:T(8,128)(2,1)} %fusion.12) | data formatting | bytes 393216 | tf_op jit(solution)/shard_map/concatenate | solution.py:133
  15.2 2.0 %maximum_bitcast_fusion = bf16[8,2,2,37,192]{4,1,0,3,2:T(2,128)(2,1)S(1)} fusion(bf16[5,8,2,1,192]{4,2,1,0,3:T(2,128)(2,1)S(1)} %concatenate.23, bf16[32,8,2,1,192]{4,2,1,0,3:T(2,128)(2,1)S(1)} %concatenate.22, bf16[5,8,2,1,192]{4,2,1,0,3:T(2,128)(2,1)S(1)} %concatenate.20, bf16[32,8,2,1,192]{4,2,1,0,3:T(2,128)(2,1)} %concatenate.19), kind=kLoop, calls=%fused_computation.36 | loop fusion | flops 681984 | bytes 909312 | tf_op jit(solution)/shard_map/transpose | solution.py:137
  17.2 1.0 copy.37
  18.2 1.1 reshape_reshape.3
  19.3 0.1 copy.36
  19.4 1.2 pad_maximum_fusion
  20.7 35.2 %all_to_all.20 = bf16[32,53,192]{2,1,0:T(8,128)(2,1)S(1)} all-to-all(bf16[32,53,192]{2,1,0:T(8,128)(2,1)S(1)} %pad_maximum_fusion), channel_id=1, replica_groups=mesh['cfg'=2,'seq'=32,'tp'=4] {'seq'}, dimensions={0} | all-to-all | bytes 1302528 | tf_op jit(solution)/shard_map/all_to_all | solution.py:141
  55.8 0.9 copy-done.2
  56.8 1.0 copy.38
  57.8 0.6 fusion.62
  59.1 0.6 compare_convert_fusion.valid_ref
  59.6 1.7 %slice.91 = bf16[32,16,192]{2,1,0:T(8,128)(2,1)} slice(bf16[32,53,192]{2,1,0:T(8,128)(2,1)} %copy-done.2), slice={[0:32], [0:16], [0:192]} | slice | bytes 393216 | tf_op jit(solution)/shard_map/slice | solution.py:142
  61.3 1.7 %broadcast_select_fusion = (bf16[32,37,192]{2,1,0:T(8,128)(2,1)S(1)}, bf16[32,37,192]{2,1,0:T(8,128)(2,1)S(1)}) fusion(pred[]{:T(512)S(6)} %eq.41, bf16[32,37,192]{2,0,1:T(8,128)(2,1)} %collective-permute-done, bf16[32,53,192]{2,1,0:T(8,128)(2,1)} %copy-done.2), kind=kLoop, calls=%fused_computation.34 | loop fusion | flops 454656 | bytes 1818625 | tf_op jit(solution)/shard_map/jit(_where)/select_n | solution.py:147
  63.0 0.9 slice.93
  63.9 0.9 slice.94
  64.8 0.1 reshape.419
  64.8 0.1 reshape.420
  64.9 0.7 pad.7.kt_ref
  65.5 0.7 pad.8.vt_ref
  66.2 6.0 %shard_map.140 = bf16[512,192]{1,0:T(8,128)(2,1)} custom-call(bf16[512,192]{1,0:T(8,128)(2,1)} %bitcast.128, bf16[1024,192]{1,0:T(8,128)(2,1)} %bitcast.126, bf16[1024,192]{1,0:T(8,128)(2,1)} %bitcast.127, bf16[256,192]{1,0:T(8,128)(2,1)} %pad.7.kt_ref, bf16[256,192]{1,0:T(8,128)(2,1)} %pad.8.vt_ref, f32[1,256]{1,0:T(1,128)} %compare_convert_fusion.valid_ref), custom_call_target="tpu_custom_call" | custom-call | tf_op jit(solution)/shard_map/pallas_call | solution.py:69
  72.2 17.0 %all_to_all.21 = bf16[32,16,192]{2,1,0:T(8,128)(2,1)S(1)} all-to-all(bf16[32,16,192]{2,1,0:T(8,128)(2,1)} %bitcast.129), channel_id=1, replica_groups=mesh['cfg'=2,'seq'=32,'tp'=4] {'seq'}, dimensions={0} | all-to-all | bytes 393216 | tf_op jit(solution)/shard_map/all_to_all | solution.py:170
  89.2 0.3 copy.41
  89.5 0.8 reshape.423
  90.3 2.8 %convolution_convert_fusion.1 = bf16[256,1536]{1,0:T(8,128)(2,1)} fusion(bf16[256,384]{1,0:T(8,128)(2,1)} %reshape.423, bf16[384,1536]{1,0:T(8,128)(2,1)} %param.22), kind=kOutput, calls=%fused_computation.1 | convolution fusion | flops 302383104 | bytes 2162688 | tf_op jit(solution)/shard_map/dot_general | solution.py:184
  93.2 4.5 %all-to-all-start.2 = ((bf16[4,64,1536]{2,1,0:T(8,128)(2,1)}), bf16[4,64,1536]{2,1,0:T(8,128)(2,1)}, u32[]{:S(2)}, u32[]{:S(2)}) async-start(bf16[4,64,1536]{2,1,0:T(8,128)(2,1)} %bitcast.123), calls=%async_computation.2 | async-start | bytes 1572864 | tf_op jit(solution)/shard_map/all_to_all | solution.py:77
  97.7 1.3 convert_element_type.122
  99.0 10.1 %all-to-all-done.2 = bf16[4,64,1536]{2,1,0:T(8,128)(2,1)} async-done(((bf16[4,64,1536]{2,1,0:T(8,128)(2,1)}), bf16[4,64,1536]{2,1,0:T(8,128)(2,1)}, u32[]{:S(2)}, u32[]{:S(2)}) %all-to-all-start.2) | async-done | bytes 786464 | tf_op jit(solution)/shard_map/all_to_all | solution.py:77
  109.1 1.3 convert_reduce_fusion.1
  110.4 1.1 fusion.72
  111.6 0.2 multiply_reduce_fusion.2
  111.8 0.1 add_convert_fusion.2
  111.9 14.1 %all_gather.3 = bf16[32,8,1536]{2,1,0:T(8,128)(2,1)} all-gather(bf16[8,8,1536]{2,1,0:T(8,128)(2,1)S(1)} %add_convert_fusion.2), channel_id=1, replica_groups=mesh['cfg'=2,'seq'=32,'tp'=4] {'tp'}, dimensions={0}, use_global_device_ids=true | all-gather | bytes 983040 | tf_op jit(solution)/shard_map/all_gather | solution.py:188
  126.0 4.5 %convolution_convert_fusion = bf16[256,1536]{1,0:T(8,128)(2,1)} fusion(bf16[768,1536]{1,0:T(8,128)(2,1)S(1)} %copy-done, bf16[1536,768]{1,0:T(8,128)(2,1)} %param.23, bf16[32,8,1536]{2,1,0:T(8,128)(2,1)} %all_gather.3), kind=kOutput, calls=%fused_computation | convolution fusion | flops 1210122240 | bytes 6291456 | tf_op jit(solution)/shard_map/dot_general | solution.py:192
  130.5 4.3 %all-to-all-start.3 = ((bf16[4,64,1536]{2,1,0:T(8,128)(2,1)}), bf16[4,64,1536]{2,1,0:T(8,128)(2,1)}, u32[]{:S(2)}, u32[]{:S(2)}) async-start(bf16[4,64,1536]{2,1,0:T(8,128)(2,1)} %bitcast.133), calls=%async_computation.3 | async-start | bytes 1572864 | tf_op jit(solution)/shard_map/all_to_all | solution.py:77
  134.8 0.0 copy-start.6
  134.9 9.5 %all-to-all-done.3 = bf16[4,64,1536]{2,1,0:T(8,128)(2,1)} async-done(((bf16[4,64,1536]{2,1,0:T(8,128)(2,1)}), bf16[4,64,1536]{2,1,0:T(8,128)(2,1)}, u32[]{:S(2)}, u32[]{:S(2)}) %all-to-all-start.3) | async-done | bytes 786464 | tf_op jit(solution)/shard_map/all_to_all | solution.py:77
  144.4 1.3 convert_reduce_fusion
  145.7 0.1 fusion.70
  145.8 0.2 multiply_reduce_fusion.1
  146.0 0.3 fusion.46
  146.3 0.1 constant_dynamic-slice_fusion
  146.4 0.8 collective-permute-start.1
  147.2 0.2 select_reduce_fusion
  147.4 4.4 %collective-permute-done.1 = f32[8,8,32]{2,1,0:T(8,128)S(1)} collective-permute-done((f32[8,8,32]{2,1,0:T(8,128)S(1)}, f32[8,8,32]{2,1,0:T(8,128)S(1)}, u32[]{:S(2)}, u32[]{:S(2)}) %collective-permute-start.1) | collective-permute-done | bytes 8224 | tf_op jit(solution)/shard_map/ppermute | solution.py:17
  151.8 0.7 multiply_add_fusion
  (41 shorter events, 0.2 us)
Async XLA Ops:
  0.6 125.3 %copy-start = (bf16[768,1536]{1,0:T(8,128)(2,1)S(1)}, bf16[768,1536]{1,0:T(8,128)(2,1)}, u32[]{:S(2)}) copy-start(bf16[768,1536]{1,0:T(8,128)(2,1)} %param.24) | copy-start | bytes 7077892
  0.6 1.9 %copy-start.1 = (bf16[1,32,8,1536]{3,2,1,0:T(8,128)(2,1)S(1)}, bf16[1,32,8,1536]{3,2,1,0:T(8,128)(2,1)}, u32[]{:S(2)}) copy-start(bf16[1,32,8,1536]{3,2,1,0:T(8,128)(2,1)} %param.13) | copy-start | bytes 2359300
  3.1 2.8 %copy-start.14 = (bf16[1536,3,384]{2,0,1:T(8,128)(2,1)S(1)}, bf16[1536,3,384]{2,0,1:T(8,128)(2,1)}, u32[]{:S(2)}) copy-start(bf16[1536,3,384]{2,0,1:T(8,128)(2,1)} %param.20) | copy-start | bytes 10616836
  7.1 1.7 %copy-start.3 = (bf16[1536,2,384]{2,1,0:T(2,128)(2,1)S(1)}, bf16[1536,2,384]{2,1,0:T(2,128)(2,1)}, u32[]{:S(2)}) copy-start(bf16[1536,2,384]{2,1,0:T(2,128)(2,1)} %param.21) | copy-start | bytes 7077892
  8.9 0.9 copy-start.4
  55.8 0.9 copy-start.2
  56.8 1.0 copy-start.15
  57.8 3.6 %collective-permute-start = (bf16[32,37,192]{2,0,1:T(8,128)(2,1)}, bf16[32,37,192]{2,0,1:T(8,128)(2,1)}, u32[]{:S(2)}, u32[]{:S(2)}) collective-permute-start(bf16[32,37,192]{2,0,1:T(8,128)(2,1)} %copy.38), channel_id=1, source_target_pairs={{0,4},{4,0},{8,12},{12,8},{16,20},{20,16},{24,28},{28,24},{32,36},... | collective-permute-start | bytes 1363976 | tf_op jit(solution)/shard_map/ppermute | solution.py:17
  93.2 15.9 %all-to-all-start.2 = ((bf16[4,64,1536]{2,1,0:T(8,128)(2,1)}), bf16[4,64,1536]{2,1,0:T(8,128)(2,1)}, u32[]{:S(2)}, u32[]{:S(2)}) async-start(bf16[4,64,1536]{2,1,0:T(8,128)(2,1)} %bitcast.123), calls=%async_computation.2 | async-start | bytes 1572864 | tf_op jit(solution)/shard_map/all_to_all | solution.py:77
  97.7 12.8 %copy-start.5 = (f32[8,1536]{1,0:T(8,128)S(1)}, f32[8,1536]{1,0:T(8,128)}, u32[]{:S(2)}) copy-start(f32[8,1536]{1,0:T(8,128)} %get-tuple-element.21) | copy-start | bytes 147460
  99.0 12.8 %copy-start.9 = (f32[8,1536]{1,0:T(8,128)S(1)}, f32[8,1536]{1,0:T(8,128)}, u32[]{:S(2)}) copy-start(f32[8,1536]{1,0:T(8,128)} %get-tuple-element.14) | copy-start | bytes 147460
  99.0 12.8 %copy-start.10 = (f32[8,1536]{1,0:T(8,128)S(1)}, f32[8,1536]{1,0:T(8,128)}, u32[]{:S(2)}) copy-start(f32[8,1536]{1,0:T(8,128)} %get-tuple-element.15) | copy-start | bytes 147460
  130.5 4.4 %copy-start.12 = (s32[8]{0:T(128)S(1)}, s32[8]{0:T(128)}, u32[]{:S(2)}) copy-start(s32[8]{0:T(128)} %param.17) | copy-start | bytes 100
  130.5 13.9 %all-to-all-start.3 = ((bf16[4,64,1536]{2,1,0:T(8,128)(2,1)}), bf16[4,64,1536]{2,1,0:T(8,128)(2,1)}, u32[]{:S(2)}, u32[]{:S(2)}) async-start(bf16[4,64,1536]{2,1,0:T(8,128)(2,1)} %bitcast.133), calls=%async_computation.3 | async-start | bytes 1572864 | tf_op jit(solution)/shard_map/all_to_all | solution.py:77
  134.8 11.2 %copy-start.6 = (bf16[1536,64]{0,1:T(8,128)(2,1)S(1)}, bf16[1536,64]{0,1:T(8,128)(2,1)}, u32[]{:S(2)}) copy-start(bf16[1536,64]{0,1:T(8,128)(2,1)} %param.25) | copy-start | bytes 589828
  134.8 11.2 %copy-start.7 = (f32[8,1536]{1,0:T(8,128)S(1)}, f32[8,1536]{1,0:T(8,128)}, u32[]{:S(2)}) copy-start(f32[8,1536]{1,0:T(8,128)} %get-tuple-element.12) | copy-start | bytes 147460
  134.8 11.2 %copy-start.8 = (f32[8,1536]{1,0:T(8,128)S(1)}, f32[8,1536]{1,0:T(8,128)}, u32[]{:S(2)}) copy-start(f32[8,1536]{1,0:T(8,128)} %get-tuple-element.13) | copy-start | bytes 147460
  134.9 12.3 %copy-start.13 = (f32[9]{0:T(128)S(1)}, f32[9]{0:T(128)}, u32[]{:S(2)}) copy-start(f32[9]{0:T(128)} %param.18) | copy-start | bytes 112
  134.9 16.9 %copy-start.11 = (f32[8,8,32]{2,1,0:T(8,128)S(1)}, f32[8,8,32]{2,1,0:T(8,128)}, u32[]{:S(2)}) copy-start(f32[8,8,32]{2,1,0:T(8,128)} %param.19) | copy-start | bytes 24580
  146.4 5.5 %collective-permute-start.1 = (f32[8,8,32]{2,1,0:T(8,128)S(1)}, f32[8,8,32]{2,1,0:T(8,128)S(1)}, u32[]{:S(2)}, u32[]{:S(2)}) collective-permute-start(f32[8,8,32]{2,1,0:T(8,128)S(1)} %constant_dynamic-slice_fusion), channel_id=1, source_target_pairs={{0,128},{128,0},{1,129},{129,1},{2,130},{130,2},{3,131},{131,3},{4... | collective-permute-start | bytes 24584 | tf_op jit(solution)/shard_map/ppermute | solution.py:17

commit v11 on v10

--- a/solution.py
+++ b/solution.py
@@ -137,8 +137,16 @@
         .transpose(1, 2, 3, 0, 4)
         .reshape(senders, key_span, head_share)
     )
-    payload = jnp.concatenate([query_send, kv_send], 1)
-    got = lax.all_to_all(payload, "seq", split_axis=0, concat_axis=0, tiled=True)
+    rows_sent = query_share + key_span
+    rows_padded = -(-rows_sent // 8) * 8
+    payload = jnp.concatenate(
+        [query_send, kv_send, jnp.zeros((senders, rows_padded - rows_sent, head_share), kv_send.dtype)],
+        1,
+    )
+    dense = payload.reshape(senders, rows_padded * head_share // 128, 128)
+    got = lax.all_to_all(dense, "seq", split_axis=0, concat_axis=0, tiled=True).reshape(
+        senders, rows_padded, head_share
+    )[:, :rows_sent]
     query_got = got[:, :query_share]
     kv_mine = got[:, query_share:]
     kv_other = swapped(kv_mine, "seq", 0)

time: 153 us -> 159 us (1.039)
  local copies, waits for them, and re-layouts: 16.2 us -> 24.8 us
  blocking collectives: 66.2 us -> 62.7 us
    reshape x0 -> x4, local copies, waits for them, and re-layouts: none -> 8.15 us  [the longest x1 3.01 us: shards(): dense = payload.reshape(senders, rows_padded * head_share // 128, 128)]
    all_to_all x1, blocking collectives: 35.2 us -> 31.6 us  [shards(): lax.all_to_all(dense, 'seq', split_axis=0, concat_axis=0, tiled=True)]
where the time goes in v11:
time: 159 us; the launch traced here: 158 us
  blocking collectives  62.7 us (39%)
  local copies, waits for them, and re-layouts  24.8 us (16%)
  waiting for transfers between devices  24 us (15%)
  other arithmetic  16.8 us (11%)
  matrix products  12.9 us (8%)
  starting transfers between devices  9.63 us (6%)
  Pallas kernels  6 us (4%)
    all_to_all x1, blocking collectives, shards(): lax.all_to_all(dense, 'seq', split_axis=0, concat_axis=0, tiled=True)  31.6 us
    all_to_all x2, waiting for transfers between devices, reduce_rows(): got = lax.all_to_all(pieces, 'tp', split_axis=0, concat_axis=0, tiled=True)  19.6 us
    all_to_all x1, blocking collectives, shards(): lax.all_to_all(answer.reshape(senders, query_share, head_share), 'seq', s...  17 us
    all_gather x1, blocking collectives, shards(): lax.all_gather(mlp_mine, 'tp', axis=0, tiled=True)  14.1 us
    all_to_all x2, starting transfers between devices, reduce_rows(): got = lax.all_to_all(pieces, 'tp', split_axis=0, concat_axis=0, tiled=True)  8.79 us
    pallas_call x1, Pallas kernels, attend_kernel(): pl.pallas_call(attention_kernel, out_shape=jax.ShapeDtypeStruct(queries.s...  6 us
    dot_general x3, matrix products, shards(): jnp.dot(normed, w_qkv[:, part], preferred_element_type=jnp.float32)  4.7 us
    dot_general x1, matrix products, shards(): jnp.dot(hidden, w_down, preferred_element_type=jnp.float32)  4.54 us
  transfers between devices with their start and end apart: 4, of which 3 were waited for; matrix products, arithmetic and copies ran while one was open for 3% of the time, Pallas kernels for 0%

profile of v11, /device:TPU:4, one launch (start us, length us, event | category | flops | bytes accessed | tf_op | source)
XLA Modules:
  0.0 158.3 jit_solution(14237608904699253418)
XLA Ops:
  0.7 1.1 bitcast_convert_fusion
  1.8 0.7 fusion.58
  2.5 0.2 convert_reduce_fusion.2
  2.7 0.3 multiply_reduce_fusion
  3.1 2.1 %fusion.15 = bf16[256,384]{1,0:T(8,128)(2,1)S(1)} fusion(bf16[1536,3,384]{2,0,1:T(8,128)(2,1)} %param.20, bf16[1,32,8,1536]{3,2,1,0:T(8,128)(2,1)S(1)} %copy-done.1, f32[8,1536]{1,0:T(8,128)S(1)} %get-tuple-element.19, f32[8,1536]{1,0:T(8,128)S(1)} %get-tuple-element.20, f32[32,8]{1,0:T(8,128)S(1)} %add_rsqrt_fusion, f32[32,8]{1,0:T(8,128)S(1)} %broadcast_multiply_fusion), kind=kOutput, calls=%fused_computation.20 | convolution fusion | flops 304447488 | bytes 2263040 | tf_op jit(solution)/shard_map/dot_general | solution.py:110
  5.1 0.3 copy-done.13
  5.4 1.3 fusion.12
  6.7 1.3 fusion.9
  8.1 0.4 copy-done.2
  8.5 0.5 copy.52
  9.0 0.4 copy-done.3
  9.4 0.1 convert_reduce_fusion.3
  9.5 0.2 fusion.42
  9.7 0.6 convolution_convert_fusion.2
  10.3 0.1 concatenate.29
  10.4 1.1 concatenate.28
  11.5 0.1 concatenate.27
  11.6 2.8 %concatenate.26 = bf16[32,8,2,1,192]{4,3,2,1,0:T(2,128)(2,1)} reshape(bf16[256,384]{1,0:T(8,128)(2,1)} %fusion.12) | data formatting | bytes 393216 | tf_op jit(solution)/shard_map/concatenate | solution.py:133
  14.4 3.4 %maximum_bitcast_fusion = bf16[8,2,2,37,192]{4,2,1,0,3:T(2,128)(2,1)} fusion(bf16[5,8,2,1,192]{4,3,2,1,0:T(2,128)(2,1)S(1)} %concatenate.29, bf16[32,8,2,1,192]{4,3,2,1,0:T(2,128)(2,1)} %concatenate.28, bf16[5,8,2,1,192]{4,3,2,1,0:T(2,128)(2,1)S(1)} %concatenate.27, bf16[32,8,2,1,192]{4,3,2,1,0:T(2,128)(2,1)} %concatenate.26), kind=kLoop, calls=%fused_computation.36 | loop fusion | flops 1818624 | bytes 909312 | tf_op jit(solution)/shard_map/transpose | solution.py:137
  17.7 2.6 %reshape.421 = bf16[32,37,192]{2,0,1:T(8,128)(2,1)} reshape(bf16[8,2,2,37,192]{4,2,1,0,3:T(2,128)(2,1)} %maximum_bitcast_fusion) | data formatting | bytes 909312 | tf_op jit(solution)/shard_map/reshape | solution.py:138
  20.4 1.1 reshape_reshape.3
  21.5 0.1 copy.41
  21.6 0.1 copy.46
  21.7 0.1 pad.11.clone
  21.8 1.3 maximum_maximum_fusion
  23.0 1.4 copy.47
  24.5 3.0 %reshape.422 = bf16[32,84,128]{2,1,0:T(8,128)(2,1)} reshape(bf16[32,56,192]{2,1,0:T(8,128)(2,1)} %copy.47) | data formatting | bytes 1376256 | tf_op jit(solution)/shard_map/reshape | solution.py:146
  27.5 31.6 %all_to_all.20 = bf16[32,84,128]{2,1,0:T(8,128)(2,1)} all-to-all(bf16[32,84,128]{2,1,0:T(8,128)(2,1)} %reshape.422), channel_id=1, replica_groups=mesh['cfg'=2,'seq'=32,'tp'=4] {'seq'}, dimensions={0} | all-to-all | bytes 1376256 | tf_op jit(solution)/shard_map/all_to_all | solution.py:147
  59.1 2.4 %reshape.423 = bf16[32,56,192]{2,1,0:T(8,128)(2,1)} reshape(bf16[32,84,128]{2,1,0:T(8,128)(2,1)} %all_to_all.20) | data formatting | bytes 1376256 | tf_op jit(solution)/shard_map/reshape | solution.py:147
  61.5 1.1 slice-done
  62.6 1.0 copy.48
  63.6 0.6 fusion.62
  64.9 0.6 compare_convert_fusion.valid_ref
  65.4 1.7 %slice.94 = bf16[32,16,192]{2,1,0:T(8,128)(2,1)} slice(bf16[32,56,192]{2,1,0:T(8,128)(2,1)} %reshape.423), slice={[0:32], [0:16], [0:192]} | slice | bytes 393216 | tf_op jit(solution)/shard_map/slice | solution.py:150
  67.1 1.7 %broadcast_select_fusion = (bf16[32,37,192]{2,1,0:T(8,128)(2,1)S(1)}, bf16[32,37,192]{2,1,0:T(8,128)(2,1)S(1)}) fusion(pred[]{:T(512)S(6)} %eq.41, bf16[32,37,192]{2,0,1:T(8,128)(2,1)} %collective-permute-done, bf16[32,56,192]{2,1,0:T(8,128)(2,1)} %reshape.423), kind=kLoop, calls=%fused_computation.34 | loop fusion | flops 454656 | bytes 1818625 | tf_op jit(solution)/shard_map/jit(_where)/select_n | solution.py:155
  68.8 0.9 slice.96
  69.7 0.9 slice.97
  70.6 0.7 pad.7.kt_ref
  71.3 0.7 pad.8.vt_ref
  72.0 6.0 %shard_map.140 = bf16[512,192]{1,0:T(8,128)(2,1)} custom-call(bf16[512,192]{1,0:T(8,128)(2,1)} %bitcast.129, bf16[1024,192]{1,0:T(8,128)(2,1)} %bitcast.127, bf16[1024,192]{1,0:T(8,128)(2,1)} %bitcast.128, bf16[256,192]{1,0:T(8,128)(2,1)} %pad.7.kt_ref, bf16[256,192]{1,0:T(8,128)(2,1)} %pad.8.vt_ref, f32[1,256]{1,0:T(1,128)} %compare_convert_fusion.valid_ref), custom_call_target="tpu_custom_call" | custom-call | tf_op jit(solution)/shard_map/pallas_call | solution.py:69
  78.0 17.0 %all_to_all.21 = bf16[32,16,192]{2,1,0:T(8,128)(2,1)S(1)} all-to-all(bf16[32,16,192]{2,1,0:T(8,128)(2,1)} %bitcast.130), channel_id=1, replica_groups=mesh['cfg'=2,'seq'=32,'tp'=4] {'seq'}, dimensions={0} | all-to-all | bytes 393216 | tf_op jit(solution)/shard_map/all_to_all | solution.py:178
  95.0 0.3 copy.51
  95.3 0.8 reshape.431
  96.1 2.8 %convolution_convert_fusion.1 = bf16[256,1536]{1,0:T(8,128)(2,1)} fusion(bf16[256,384]{1,0:T(8,128)(2,1)} %reshape.431, bf16[384,1536]{1,0:T(8,128)(2,1)} %param.22), kind=kOutput, calls=%fused_computation.1 | convolution fusion | flops 302383104 | bytes 2162688 | tf_op jit(solution)/shard_map/dot_general | solution.py:192
  99.0 4.5 %all-to-all-start.2 = ((bf16[4,64,1536]{2,1,0:T(8,128)(2,1)}), bf16[4,64,1536]{2,1,0:T(8,128)(2,1)}, u32[]{:S(2)}, u32[]{:S(2)}) async-start(bf16[4,64,1536]{2,1,0:T(8,128)(2,1)} %bitcast.125), calls=%async_computation.2 | async-start | bytes 1572864 | tf_op jit(solution)/shard_map/all_to_all | solution.py:77
  103.5 1.3 convert_element_type.122
  104.8 10.1 %all-to-all-done.2 = bf16[4,64,1536]{2,1,0:T(8,128)(2,1)} async-done(((bf16[4,64,1536]{2,1,0:T(8,128)(2,1)}), bf16[4,64,1536]{2,1,0:T(8,128)(2,1)}, u32[]{:S(2)}, u32[]{:S(2)}) %all-to-all-start.2) | async-done | bytes 786464 | tf_op jit(solution)/shard_map/all_to_all | solution.py:77
  114.9 1.3 convert_reduce_fusion.1
  116.2 1.1 fusion.72
  117.4 0.2 multiply_reduce_fusion.2
  117.6 0.1 add_convert_fusion.2
  117.7 14.1 %all_gather.3 = bf16[32,8,1536]{2,1,0:T(8,128)(2,1)} all-gather(bf16[8,8,1536]{2,1,0:T(8,128)(2,1)S(1)} %add_convert_fusion.2), channel_id=1, replica_groups=mesh['cfg'=2,'seq'=32,'tp'=4] {'tp'}, dimensions={0}, use_global_device_ids=true | all-gather | bytes 983040 | tf_op jit(solution)/shard_map/all_gather | solution.py:196
  131.8 4.5 %convolution_convert_fusion = bf16[256,1536]{1,0:T(8,128)(2,1)} fusion(bf16[768,1536]{1,0:T(8,128)(2,1)S(1)} %copy-done, bf16[1536,768]{1,0:T(8,128)(2,1)} %param.23, bf16[32,8,1536]{2,1,0:T(8,128)(2,1)} %all_gather.3), kind=kOutput, calls=%fused_computation | convolution fusion | flops 1210122240 | bytes 6291456 | tf_op jit(solution)/shard_map/dot_general | solution.py:200
  136.3 4.3 %all-to-all-start.3 = ((bf16[4,64,1536]{2,1,0:T(8,128)(2,1)}), bf16[4,64,1536]{2,1,0:T(8,128)(2,1)}, u32[]{:S(2)}, u32[]{:S(2)}) async-start(bf16[4,64,1536]{2,1,0:T(8,128)(2,1)} %bitcast.133), calls=%async_computation.3 | async-start | bytes 1572864 | tf_op jit(solution)/shard_map/all_to_all | solution.py:77
  140.7 9.5 %all-to-all-done.3 = bf16[4,64,1536]{2,1,0:T(8,128)(2,1)} async-done(((bf16[4,64,1536]{2,1,0:T(8,128)(2,1)}), bf16[4,64,1536]{2,1,0:T(8,128)(2,1)}, u32[]{:S(2)}, u32[]{:S(2)}) %all-to-all-start.3) | async-done | bytes 786464 | tf_op jit(solution)/shard_map/all_to_all | solution.py:77
  150.2 1.3 convert_reduce_fusion
  151.5 0.1 fusion.70
  151.6 0.2 multiply_reduce_fusion.1
  151.8 0.3 fusion.46
  152.1 0.1 constant_dynamic-slice_fusion
  152.2 0.8 collective-permute-start.1
  153.0 0.2 select_reduce_fusion
  153.2 4.4 %collective-permute-done.1 = f32[8,8,32]{2,1,0:T(8,128)S(1)} collective-permute-done((f32[8,8,32]{2,1,0:T(8,128)S(1)}, f32[8,8,32]{2,1,0:T(8,128)S(1)}, u32[]{:S(2)}, u32[]{:S(2)}) %collective-permute-start.1) | collective-permute-done | bytes 8224 | tf_op jit(solution)/shard_map/ppermute | solution.py:17
  157.6 0.7 multiply_add_fusion
  (46 shorter events, 0.3 us)
Async XLA Ops:
  0.6 131.1 %copy-start = (bf16[768,1536]{1,0:T(8,128)(2,1)S(1)}, bf16[768,1536]{1,0:T(8,128)(2,1)}, u32[]{:S(2)}) copy-start(bf16[768,1536]{1,0:T(8,128)(2,1)} %param.24) | copy-start | bytes 7077892
  0.6 1.9 %copy-start.1 = (bf16[1,32,8,1536]{3,2,1,0:T(8,128)(2,1)S(1)}, bf16[1,32,8,1536]{3,2,1,0:T(8,128)(2,1)}, u32[]{:S(2)}) copy-start(bf16[1,32,8,1536]{3,2,1,0:T(8,128)(2,1)} %param.13) | copy-start | bytes 2359300
  3.1 2.4 %copy-start.13 = (bf16[1536,3,384]{2,0,1:T(8,128)(2,1)S(1)}, bf16[1536,3,384]{2,0,1:T(8,128)(2,1)}, u32[]{:S(2)}) copy-start(bf16[1536,3,384]{2,0,1:T(8,128)(2,1)} %param.20) | copy-start | bytes 10616836
  6.7 1.7 %copy-start.2 = (bf16[1536,2,384]{2,1,0:T(2,128)(2,1)S(1)}, bf16[1536,2,384]{2,1,0:T(2,128)(2,1)}, u32[]{:S(2)}) copy-start(bf16[1536,2,384]{2,1,0:T(2,128)(2,1)} %param.21) | copy-start | bytes 7077892
  8.5 0.9 copy-start.3
  61.5 1.1 slice-start
  61.5 2.1 %copy-start.14 = (s32[1,8]{1,0:T(1,128)S(1)}, s32[1,8]{1,0:T(1,128)}, u32[]{:S(2)}) copy-start(s32[1,8]{1,0:T(1,128)} %param.16) | copy-start | bytes 100
  63.6 3.6 %collective-permute-start = (bf16[32,37,192]{2,0,1:T(8,128)(2,1)}, bf16[32,37,192]{2,0,1:T(8,128)(2,1)}, u32[]{:S(2)}, u32[]{:S(2)}) collective-permute-start(bf16[32,37,192]{2,0,1:T(8,128)(2,1)} %copy.48), channel_id=1, source_target_pairs={{0,4},{4,0},{8,12},{12,8},{16,20},{20,16},{24,28},{28,24},{32,36},... | collective-permute-start | bytes 1363976 | tf_op jit(solution)/shard_map/ppermute | solution.py:17
  99.0 15.9 %all-to-all-start.2 = ((bf16[4,64,1536]{2,1,0:T(8,128)(2,1)}), bf16[4,64,1536]{2,1,0:T(8,128)(2,1)}, u32[]{:S(2)}, u32[]{:S(2)}) async-start(bf16[4,64,1536]{2,1,0:T(8,128)(2,1)} %bitcast.125), calls=%async_computation.2 | async-start | bytes 1572864 | tf_op jit(solution)/shard_map/all_to_all | solution.py:77
  103.4 12.8 %copy-start.4 = (f32[8,1536]{1,0:T(8,128)S(1)}, f32[8,1536]{1,0:T(8,128)}, u32[]{:S(2)}) copy-start(f32[8,1536]{1,0:T(8,128)} %get-tuple-element.21) | copy-start | bytes 147460
  104.8 12.8 %copy-start.8 = (f32[8,1536]{1,0:T(8,128)S(1)}, f32[8,1536]{1,0:T(8,128)}, u32[]{:S(2)}) copy-start(f32[8,1536]{1,0:T(8,128)} %get-tuple-element.14) | copy-start | bytes 147460
  104.8 12.8 %copy-start.9 = (f32[8,1536]{1,0:T(8,128)S(1)}, f32[8,1536]{1,0:T(8,128)}, u32[]{:S(2)}) copy-start(f32[8,1536]{1,0:T(8,128)} %get-tuple-element.15) | copy-start | bytes 147460
  136.3 4.4 %copy-start.11 = (s32[8]{0:T(128)S(1)}, s32[8]{0:T(128)}, u32[]{:S(2)}) copy-start(s32[8]{0:T(128)} %param.17) | copy-start | bytes 100
  136.3 13.9 %all-to-all-start.3 = ((bf16[4,64,1536]{2,1,0:T(8,128)(2,1)}), bf16[4,64,1536]{2,1,0:T(8,128)(2,1)}, u32[]{:S(2)}, u32[]{:S(2)}) async-start(bf16[4,64,1536]{2,1,0:T(8,128)(2,1)} %bitcast.133), calls=%async_computation.3 | async-start | bytes 1572864 | tf_op jit(solution)/shard_map/all_to_all | solution.py:77
  140.6 11.2 %copy-start.5 = (bf16[1536,64]{0,1:T(8,128)(2,1)S(1)}, bf16[1536,64]{0,1:T(8,128)(2,1)}, u32[]{:S(2)}) copy-start(bf16[1536,64]{0,1:T(8,128)(2,1)} %param.25) | copy-start | bytes 589828
  140.6 11.2 %copy-start.6 = (f32[8,1536]{1,0:T(8,128)S(1)}, f32[8,1536]{1,0:T(8,128)}, u32[]{:S(2)}) copy-start(f32[8,1536]{1,0:T(8,128)} %get-tuple-element.12) | copy-start | bytes 147460
  140.6 11.2 %copy-start.7 = (f32[8,1536]{1,0:T(8,128)S(1)}, f32[8,1536]{1,0:T(8,128)}, u32[]{:S(2)}) copy-start(f32[8,1536]{1,0:T(8,128)} %get-tuple-element.13) | copy-start | bytes 147460
  140.7 12.3 %copy-start.12 = (f32[9]{0:T(128)S(1)}, f32[9]{0:T(128)}, u32[]{:S(2)}) copy-start(f32[9]{0:T(128)} %param.18) | copy-start | bytes 112
  140.7 16.9 %copy-start.10 = (f32[8,8,32]{2,1,0:T(8,128)S(1)}, f32[8,8,32]{2,1,0:T(8,128)}, u32[]{:S(2)}) copy-start(f32[8,8,32]{2,1,0:T(8,128)} %param.19) | copy-start | bytes 24580
  152.2 5.5 %collective-permute-start.1 = (f32[8,8,32]{2,1,0:T(8,128)S(1)}, f32[8,8,32]{2,1,0:T(8,128)S(1)}, u32[]{:S(2)}, u32[]{:S(2)}) collective-permute-start(f32[8,8,32]{2,1,0:T(8,128)S(1)} %constant_dynamic-slice_fusion), channel_id=1, source_target_pairs={{0,128},{128,0},{1,129},{129,1},{2,130},{130,2},{3,131},{131,3},{4... | collective-permute-start | bytes 24584 | tf_op jit(solution)/shard_map/ppermute | solution.py:17

commit v12 on v10

--- a/solution.py
+++ b/solution.py
@@ -70,6 +70,11 @@
         attention_kernel,
         out_shape=jax.ShapeDtypeStruct(queries.shape, jnp.bfloat16),
     )(queries, keys_img, values_img, keys_txt, values_txt, valid)
+
+
+def shifted(value, axis, step):
+    size = lax.axis_size(axis)
+    return lax.ppermute(value, axis, [(i, (i + step) % size) for i in range(size)])
 
 
 def reduce_rows(partial, parties):
@@ -185,12 +190,22 @@
     attn_mixed = reduce_rows(attn_part, parties).reshape(portion, requests, model_width)
     after_attn = resident_mine + adaptive[:, 2] * attn_mixed
     mlp_mine = modulate(after_attn, adaptive[:, 3], adaptive[:, 4])
-    mlp_in = lax.all_gather(mlp_mine, "tp", axis=0, tiled=True).reshape(rows_all, model_width)
-    hidden = jax.nn.gelu(
-        jnp.dot(mlp_in, w_up, preferred_element_type=jnp.float32), approximate=True
-    ).astype(jnp.bfloat16)
-    mlp_part = jnp.dot(hidden, w_down, preferred_element_type=jnp.float32).astype(jnp.bfloat16)
-    mlp_grown = reduce_rows(mlp_part, parties).reshape(portion, requests, model_width)
+    arrived = [mlp_mine] + [shifted(mlp_mine, "tp", step) for step in range(1, parties)]
+    mlp_total = None
+    for step, block in enumerate(arrived):
+        hidden = jax.nn.gelu(
+            jnp.dot(
+                block.reshape(portion * requests, model_width),
+                w_up,
+                preferred_element_type=jnp.float32,
+            ),
+            approximate=True,
+        ).astype(jnp.bfloat16)
+        part = jnp.dot(hidden, w_down, preferred_element_type=jnp.float32).astype(jnp.bfloat16)
+        if step:
+            part = shifted(part, "tp", -step)
+        mlp_total = part.astype(jnp.float32) if mlp_total is None else mlp_total + part.astype(jnp.float32)
+    mlp_grown = mlp_total.reshape(portion, requests, model_width)
     after_mlp = after_attn + adaptive[:, 5] * mlp_grown
     head_in = modulate(after_mlp, adaptive[:, 8], adaptive[:, 9]).reshape(
         portion * requests, model_width

time: 153 us -> 149 us (0.974)
  blocking collectives: 66.2 us -> 52.2 us
  matrix products: 13.6 us -> 21.7 us
  starting transfers between devices: 9.63 us -> 14.4 us
  waiting for transfers between devices: 24 us -> 19.3 us
    all_gather x1 -> x0, blocking collectives: 14.1 us -> none  [shards(): lax.all_gather(mlp_mine, 'tp', axis=0, tiled=True)]
    all_to_all x2 -> x1, waiting for transfers between devices: 19.6 us -> 10.1 us  [reduce_rows(): got = lax.all_to_all(pieces, 'tp', split_axis=0, concat_axis=0, tiled=True)]
    ppermute x0 -> x6, starting transfers between devices: none -> 9.11 us  [shifted(): lax.ppermute(value, axis, [(i, (i + step) % size) for i in range(size)])]
    dot_general x1 -> x4, matrix products: 4.54 us -> 12.6 us  [shards(): jnp.dot(hidden, w_down, preferred_element_type=jnp.float32)]
    ppermute x0 -> x6, waiting for transfers between devices: none -> 4.81 us  [shifted(): lax.ppermute(value, axis, [(i, (i + step) % size) for i in range(size)])]
    all_to_all x2 -> x1, starting transfers between devices: 8.79 us -> 4.47 us  [reduce_rows(): got = lax.all_to_all(pieces, 'tp', split_axis=0, concat_axis=0, tiled=True)]
  transfers between devices with their start and end apart: 4 -> 9, of which waited for: 3 -> 4; matrix products, arithmetic and copies ran while one was open for 3% -> 12% of each run, Pallas kernels for 0% -> 0%
where the time goes in v12:
time: 149 us; the launch traced here: 147 us
  blocking collectives  52.2 us (35%)
  matrix products  21.7 us (15%)
  waiting for transfers between devices  19.3 us (13%)
  local copies, waits for them, and re-layouts  16.1 us (11%)
  other arithmetic  16.1 us (11%)
  starting transfers between devices  14.4 us (10%)
  Pallas kernels  6 us (4%)
  between operations  1.53 us (1%)
    all_to_all x1, blocking collectives, shards(): lax.all_to_all(payload, 'seq', split_axis=0, concat_axis=0, tiled=True)  35.2 us
    all_to_all x1, blocking collectives, shards(): lax.all_to_all(answer.reshape(senders, query_share, head_share), 'seq', s...  17 us
    dot_general x4, matrix products, shards(): jnp.dot(hidden, w_down, preferred_element_type=jnp.float32)  12.6 us
    all_to_all x1, waiting for transfers between devices, reduce_rows(): got = lax.all_to_all(pieces, 'tp', split_axis=0, concat_axis=0, tiled=True)  10.1 us
    ppermute x6, starting transfers between devices, shifted(): lax.ppermute(value, axis, [(i, (i + step) % size) for i in range(size)])  9.11 us
    pallas_call x1, Pallas kernels, attend_kernel(): pl.pallas_call(attention_kernel, out_shape=jax.ShapeDtypeStruct(queries.s...  6 us
    dot_general x3, matrix products, shards(): jnp.dot(normed, w_qkv[:, part], preferred_element_type=jnp.float32)  5.36 us
    ppermute x6, waiting for transfers between devices, shifted(): lax.ppermute(value, axis, [(i, (i + step) % size) for i in range(size)])  4.81 us
  transfers between devices with their start and end apart: 9, of which 4 were waited for; matrix products, arithmetic and copies ran while one was open for 12% of the time, Pallas kernels for 0%

profile of v12, /device:TPU:4, one launch (start us, length us, event | category | flops | bytes accessed | tf_op | source)
XLA Modules:
  0.0 147.3 jit_solution(7666997759765785971)
XLA Ops:
  0.7 1.1 bitcast_convert_fusion
  1.8 0.7 fusion.113
  2.5 0.2 convert_reduce_fusion.1
  2.7 0.3 multiply_reduce_fusion
  3.1 2.7 %fusion.16 = bf16[256,384]{1,0:T(8,128)(2,1)} fusion(bf16[1536,3,384]{2,0,1:T(8,128)(2,1)} %param.20, bf16[1,32,8,1536]{3,2,1,0:T(8,128)(2,1)S(1)} %copy-done.1, f32[8,1536]{1,0:T(8,128)S(1)} %get-tuple-element.19, f32[8,1536]{1,0:T(8,128)S(1)} %get-tuple-element.20, f32[32,8]{1,0:T(8,128)S(1)} %add_rsqrt_fusion, f32[32,8]{1,0:T(8,128)S(1)} %broadcast_multiply_fusion), kind=kOutput, calls=%fused_computation.22 | convolution fusion | flops 304447488 | bytes 2263040 | tf_op jit(solution)/shard_map/dot_general | solution.py:115
  5.8 1.3 fusion.13
  7.1 1.3 fusion.10
  8.4 0.4 copy-done.3
  8.9 0.5 copy.42
  9.4 0.4 copy-done.4
  9.8 0.1 convert_reduce_fusion.2
  9.9 0.2 fusion.25
  10.1 0.6 convolution_convert_fusion.5
  10.7 0.6 fusion.141
  11.3 0.1 concatenate.23
  11.4 1.1 concatenate.22
  12.5 0.8 concatenate.20
  13.3 1.8 %concatenate.19 = bf16[32,8,2,1,192]{4,2,1,0,3:T(2,128)(2,1)} reshape(bf16[256,384]{1,0:T(8,128)(2,1)} %fusion.13) | data formatting | bytes 393216 | tf_op jit(solution)/shard_map/concatenate | solution.py:138
  15.2 2.0 %maximum_bitcast_fusion = bf16[8,2,2,37,192]{4,1,0,3,2:T(2,128)(2,1)S(1)} fusion(bf16[5,8,2,1,192]{4,2,1,0,3:T(2,128)(2,1)S(1)} %concatenate.23, bf16[32,8,2,1,192]{4,2,1,0,3:T(2,128)(2,1)S(1)} %concatenate.22, bf16[5,8,2,1,192]{4,2,1,0,3:T(2,128)(2,1)S(1)} %concatenate.20, bf16[32,8,2,1,192]{4,2,1,0,3:T(2,128)(2,1)} %concatenate.19), kind=kLoop, calls=%fused_computation.28 | loop fusion | flops 681984 | bytes 909312 | tf_op jit(solution)/shard_map/transpose | solution.py:142
  17.2 1.0 copy.37
  18.2 1.1 reshape_reshape.3
  19.3 0.1 copy.36
  19.4 1.2 pad_maximum_fusion
  20.7 35.2 %all_to_all.15 = bf16[32,53,192]{2,1,0:T(8,128)(2,1)S(1)} all-to-all(bf16[32,53,192]{2,1,0:T(8,128)(2,1)S(1)} %pad_maximum_fusion), channel_id=1, replica_groups=mesh['cfg'=2,'seq'=32,'tp'=4] {'seq'}, dimensions={0} | all-to-all | bytes 1302528 | tf_op jit(solution)/shard_map/all_to_all | solution.py:146
  55.8 0.9 copy-done.2
  56.8 1.0 copy.38
  57.8 0.6 fusion.117
  59.1 0.6 compare_convert_fusion.valid_ref
  59.6 1.7 %slice.91 = bf16[32,16,192]{2,1,0:T(8,128)(2,1)} slice(bf16[32,53,192]{2,1,0:T(8,128)(2,1)} %copy-done.2), slice={[0:32], [0:16], [0:192]} | slice | bytes 393216 | tf_op jit(solution)/shard_map/slice | solution.py:147
  61.3 1.7 %broadcast_select_fusion = (bf16[32,37,192]{2,1,0:T(8,128)(2,1)S(1)}, bf16[32,37,192]{2,1,0:T(8,128)(2,1)S(1)}) fusion(pred[]{:T(512)S(6)} %eq.41, bf16[32,37,192]{2,0,1:T(8,128)(2,1)} %collective-permute-done, bf16[32,53,192]{2,1,0:T(8,128)(2,1)} %copy-done.2), kind=kLoop, calls=%fused_computation.26 | loop fusion | flops 454656 | bytes 1818625 | tf_op jit(solution)/shard_map/jit(_where)/select_n | solution.py:152
  63.0 0.9 slice.93
  63.9 0.9 slice.94
  64.9 0.7 pad.7.kt_ref
  65.5 0.7 pad.8.vt_ref
  66.2 6.0 %shard_map.140 = bf16[512,192]{1,0:T(8,128)(2,1)} custom-call(bf16[512,192]{1,0:T(8,128)(2,1)} %bitcast.154, bf16[1024,192]{1,0:T(8,128)(2,1)} %bitcast.152, bf16[1024,192]{1,0:T(8,128)(2,1)} %bitcast.153, bf16[256,192]{1,0:T(8,128)(2,1)} %pad.7.kt_ref, bf16[256,192]{1,0:T(8,128)(2,1)} %pad.8.vt_ref, f32[1,256]{1,0:T(1,128)} %compare_convert_fusion.valid_ref), custom_call_target="tpu_custom_call" | custom-call | tf_op jit(solution)/shard_map/pallas_call | solution.py:69
  72.2 17.0 %all_to_all.16 = bf16[32,16,192]{2,1,0:T(8,128)(2,1)S(1)} all-to-all(bf16[32,16,192]{2,1,0:T(8,128)(2,1)} %bitcast.155), channel_id=1, replica_groups=mesh['cfg'=2,'seq'=32,'tp'=4] {'seq'}, dimensions={0} | all-to-all | bytes 393216 | tf_op jit(solution)/shard_map/all_to_all | solution.py:175
  89.2 0.3 copy.41
  89.5 0.8 reshape.429
  90.3 2.8 %convolution_convert_fusion = bf16[256,1536]{1,0:T(8,128)(2,1)} fusion(bf16[256,384]{1,0:T(8,128)(2,1)} %reshape.429, bf16[384,1536]{1,0:T(8,128)(2,1)} %param.22), kind=kOutput, calls=%fused_computation | convolution fusion | flops 302383104 | bytes 2162688 | tf_op jit(solution)/shard_map/dot_general | solution.py:189
  93.2 4.5 %all-to-all-start.2 = ((bf16[4,64,1536]{2,1,0:T(8,128)(2,1)}), bf16[4,64,1536]{2,1,0:T(8,128)(2,1)}, u32[]{:S(2)}, u32[]{:S(2)}) async-start(bf16[4,64,1536]{2,1,0:T(8,128)(2,1)} %bitcast.149), calls=%async_computation.2 | async-start | bytes 1572864 | tf_op jit(solution)/shard_map/all_to_all | solution.py:82
  97.7 1.3 convert_element_type.149
  99.0 10.1 %all-to-all-done.2 = bf16[4,64,1536]{2,1,0:T(8,128)(2,1)} async-done(((bf16[4,64,1536]{2,1,0:T(8,128)(2,1)}), bf16[4,64,1536]{2,1,0:T(8,128)(2,1)}, u32[]{:S(2)}, u32[]{:S(2)}) %all-to-all-start.2) | async-done | bytes 786464 | tf_op jit(solution)/shard_map/all_to_all | solution.py:82
  109.1 1.3 convert_reduce_fusion
  110.4 1.1 fusion.139
  111.5 0.2 multiply_reduce_fusion.2
  111.8 0.1 add_convert_fusion.2
  111.9 1.2 collective-permute-start.5
  113.1 1.5 %collective-permute-start.3 = (bf16[8,8,1536]{2,1,0:T(8,128)(2,1)S(1)}, bf16[8,8,1536]{2,1,0:T(8,128)(2,1)S(1)}, u32[]{:S(2)}, u32[]{:S(2)}) collective-permute-start(bf16[8,8,1536]{2,1,0:T(8,128)(2,1)S(1)} %add_convert_fusion.2), channel_id=1, source_target_pairs={{0,2},{1,3},{2,0},{3,1},{4,6},{5,7},{6,4},{7,5},{8,10},{9,11},{10,... | collective-permute-start | bytes 589832 | tf_op jit(solution)/shard_map/ppermute | solution.py:77
  114.7 3.8 %collective-permute-done.5 = bf16[8,8,1536]{2,1,0:T(8,128)(2,1)} collective-permute-done((bf16[8,8,1536]{2,1,0:T(8,128)(2,1)S(1)}, bf16[8,8,1536]{2,1,0:T(8,128)(2,1)}, u32[]{:S(2)}, u32[]{:S(2)}) %collective-permute-start.5) | collective-permute-done | bytes 196640 | tf_op jit(solution)/shard_map/ppermute | solution.py:77
  118.5 2.9 %convolution_convert_fusion.1 = bf16[64,1536]{1,0:T(8,128)(2,1)S(1)} fusion(bf16[768,1536]{1,0:T(8,128)(2,1)S(1)} %copy-done, bf16[1536,768]{1,0:T(8,128)(2,1)} %param.23, bf16[8,8,1536]{2,1,0:T(8,128)(2,1)} %collective-permute-done.5), kind=kOutput, calls=%fused_computation.1 | convolution fusion | flops 302530560 | bytes 5111808 | tf_op jit(solution)/shard_map/dot_general | solution.py:204
  121.4 3.6 %collective-permute-start.6 = (bf16[64,1536]{1,0:T(8,128)(2,1)S(1)}, bf16[64,1536]{1,0:T(8,128)(2,1)}, u32[]{:S(2)}, u32[]{:S(2)}) collective-permute-start(bf16[64,1536]{1,0:T(8,128)(2,1)S(1)} %convolution_convert_fusion.1), channel_id=1, source_target_pairs={{0,1},{1,2},{2,3},{3,0},{4,5},{5,6},{6,7},{7,4},{8,9},{9,10},{10,1... | collective-permute-start | bytes 589832 | tf_op jit(solution)/shard_map/ppermute | solution.py:77
  125.0 3.5 %convolution_convert_fusion.2 = bf16[64,1536]{1,0:T(8,128)(2,1)} fusion(bf16[768,1536]{1,0:T(8,128)(2,1)S(1)} %copy-done, bf16[1536,768]{1,0:T(8,128)(2,1)} %param.23, bf16[8,8,1536]{2,1,0:T(8,128)(2,1)S(1)} %collective-permute-done.3), kind=kOutput, calls=%fused_computation.2 | convolution fusion | flops 302530560 | bytes 5111808 | tf_op jit(solution)/shard_map/dot_general | solution.py:204
  128.5 0.6 collective-permute-start.4
  129.1 3.5 %convolution_convert_fusion.3 = bf16[64,1536]{1,0:T(8,128)(2,1)} fusion(bf16[768,1536]{1,0:T(8,128)(2,1)S(1)} %copy-done, bf16[1536,768]{1,0:T(8,128)(2,1)} %param.23, bf16[8,8,1536]{2,1,0:T(8,128)(2,1)S(1)} %collective-permute-done.1), kind=kOutput, calls=%fused_computation.3 | convolution fusion | flops 302530560 | bytes 5111808 | tf_op jit(solution)/shard_map/dot_general | solution.py:204
  132.5 2.1 %collective-permute-start.2 = (bf16[64,1536]{1,0:T(8,128)(2,1)}, bf16[64,1536]{1,0:T(8,128)(2,1)}, u32[]{:S(2)}, u32[]{:S(2)}) collective-permute-start(bf16[64,1536]{1,0:T(8,128)(2,1)} %convolution_convert_fusion.3), channel_id=1, source_target_pairs={{0,3},{1,0},{2,1},{3,2},{4,7},{5,4},{6,5},{7,6},{8,11},{9,8},{10,9... | collective-permute-start | bytes 589832 | tf_op jit(solution)/shard_map/ppermute | solution.py:77
  134.7 2.8 %fusion = f32[64,1536]{1,0:T(8,128)S(1)} fusion(bf16[768,1536]{1,0:T(8,128)(2,1)S(1)} %copy-done, bf16[1536,768]{1,0:T(8,128)(2,1)} %param.23, bf16[8,8,1536]{2,1,0:T(8,128)(2,1)S(1)} %add_convert_fusion.2), kind=kOutput, calls=%fused_computation.5 | convolution fusion | flops 302628864 | bytes 5308416 | tf_op jit(solution)/shard_map/dot_general | solution.py:204
  137.5 1.0 collective-permute-done.2
  138.5 1.3 fusion.137
  139.9 0.2 multiply_reduce_fusion.1
  140.1 0.3 fusion.61
  140.4 0.8 collective-permute-start.7
  141.3 0.2 select_reduce_fusion
  141.5 4.4 %collective-permute-done.7 = f32[8,8,32]{2,1,0:T(8,128)S(1)} collective-permute-done((f32[8,8,32]{2,1,0:T(8,128)S(1)}, f32[8,8,32]{2,1,0:T(8,128)S(1)}, u32[]{:S(2)}, u32[]{:S(2)}) %collective-permute-start.7) | collective-permute-done | bytes 8224 | tf_op jit(solution)/shard_map/ppermute | solution.py:17
  145.9 1.5 multiply_add_fusion
  (48 shorter events, 0.4 us)
Async XLA Ops:
  0.6 117.8 %copy-start = (bf16[768,1536]{1,0:T(8,128)(2,1)S(1)}, bf16[768,1536]{1,0:T(8,128)(2,1)}, u32[]{:S(2)}) copy-start(bf16[768,1536]{1,0:T(8,128)(2,1)} %param.24) | copy-start | bytes 7077892
  0.6 1.9 %copy-start.1 = (bf16[1,32,8,1536]{3,2,1,0:T(8,128)(2,1)S(1)}, bf16[1,32,8,1536]{3,2,1,0:T(8,128)(2,1)}, u32[]{:S(2)}) copy-start(bf16[1,32,8,1536]{3,2,1,0:T(8,128)(2,1)} %param.13) | copy-start | bytes 2359300
  3.1 2.8 %copy-start.12 = (bf16[1536,3,384]{2,0,1:T(8,128)(2,1)S(1)}, bf16[1536,3,384]{2,0,1:T(8,128)(2,1)}, u32[]{:S(2)}) copy-start(bf16[1536,3,384]{2,0,1:T(8,128)(2,1)} %param.20) | copy-start | bytes 10616836
  7.1 1.7 %copy-start.3 = (bf16[1536,2,384]{2,1,0:T(2,128)(2,1)S(1)}, bf16[1536,2,384]{2,1,0:T(2,128)(2,1)}, u32[]{:S(2)}) copy-start(bf16[1536,2,384]{2,1,0:T(2,128)(2,1)} %param.21) | copy-start | bytes 7077892
  8.9 0.9 copy-start.4
  55.8 0.9 copy-start.2
  56.8 1.0 copy-start.13
  57.8 3.6 %collective-permute-start = (bf16[32,37,192]{2,0,1:T(8,128)(2,1)}, bf16[32,37,192]{2,0,1:T(8,128)(2,1)}, u32[]{:S(2)}, u32[]{:S(2)}) collective-permute-start(bf16[32,37,192]{2,0,1:T(8,128)(2,1)} %copy.38), channel_id=1, source_target_pairs={{0,4},{4,0},{8,12},{12,8},{16,20},{20,16},{24,28},{28,24},{32,36},... | collective-permute-start | bytes 1363976 | tf_op jit(solution)/shard_map/ppermute | solution.py:17
  93.2 15.9 %all-to-all-start.2 = ((bf16[4,64,1536]{2,1,0:T(8,128)(2,1)}), bf16[4,64,1536]{2,1,0:T(8,128)(2,1)}, u32[]{:S(2)}, u32[]{:S(2)}) async-start(bf16[4,64,1536]{2,1,0:T(8,128)(2,1)} %bitcast.149), calls=%async_computation.2 | async-start | bytes 1572864 | tf_op jit(solution)/shard_map/all_to_all | solution.py:82
  99.0 12.8 %copy-start.8 = (f32[8,1536]{1,0:T(8,128)S(1)}, f32[8,1536]{1,0:T(8,128)}, u32[]{:S(2)}) copy-start(f32[8,1536]{1,0:T(8,128)} %get-tuple-element.14) | copy-start | bytes 147460
  99.0 12.8 %copy-start.9 = (f32[8,1536]{1,0:T(8,128)S(1)}, f32[8,1536]{1,0:T(8,128)}, u32[]{:S(2)}) copy-start(f32[8,1536]{1,0:T(8,128)} %get-tuple-element.15) | copy-start | bytes 147460
  99.0 14.1 %copy-start.10 = (s32[8]{0:T(128)S(1)}, s32[8]{0:T(128)}, u32[]{:S(2)}) copy-start(s32[8]{0:T(128)} %param.17) | copy-start | bytes 100
  111.9 6.6 %collective-permute-start.5 = (bf16[8,8,1536]{2,1,0:T(8,128)(2,1)S(1)}, bf16[8,8,1536]{2,1,0:T(8,128)(2,1)}, u32[]{:S(2)}, u32[]{:S(2)}) collective-permute-start(bf16[8,8,1536]{2,1,0:T(8,128)(2,1)S(1)} %add_convert_fusion.2), channel_id=1, source_target_pairs={{0,3},{1,0},{2,1},{3,2},{4,7},{5,4},{6,5},{7,6},{8,11},{9,8},{10,9... | collective-permute-start | bytes 589832 | tf_op jit(solution)/shard_map/ppermute | solution.py:77
  113.1 11.9 %collective-permute-start.3 = (bf16[8,8,1536]{2,1,0:T(8,128)(2,1)S(1)}, bf16[8,8,1536]{2,1,0:T(8,128)(2,1)S(1)}, u32[]{:S(2)}, u32[]{:S(2)}) collective-permute-start(bf16[8,8,1536]{2,1,0:T(8,128)(2,1)S(1)} %add_convert_fusion.2), channel_id=1, source_target_pairs={{0,2},{1,3},{2,0},{3,1},{4,6},{5,7},{6,4},{7,5},{8,10},{9,11},{10,... | collective-permute-start | bytes 589832 | tf_op jit(solution)/shard_map/ppermute | solution.py:77
  114.7 14.4 %collective-permute-start.1 = (bf16[8,8,1536]{2,1,0:T(8,128)(2,1)S(1)}, bf16[8,8,1536]{2,1,0:T(8,128)(2,1)S(1)}, u32[]{:S(2)}, u32[]{:S(2)}) collective-permute-start(bf16[8,8,1536]{2,1,0:T(8,128)(2,1)S(1)} %add_convert_fusion.2), channel_id=1, source_target_pairs={{0,1},{1,2},{2,3},{3,0},{4,5},{5,6},{6,7},{7,4},{8,9},{9,10},{10,1... | collective-permute-start | bytes 589832 | tf_op jit(solution)/shard_map/ppermute | solution.py:77
  121.4 16.1 %collective-permute-start.6 = (bf16[64,1536]{1,0:T(8,128)(2,1)S(1)}, bf16[64,1536]{1,0:T(8,128)(2,1)}, u32[]{:S(2)}, u32[]{:S(2)}) collective-permute-start(bf16[64,1536]{1,0:T(8,128)(2,1)S(1)} %convolution_convert_fusion.1), channel_id=1, source_target_pairs={{0,1},{1,2},{2,3},{3,0},{4,5},{5,6},{6,7},{7,4},{8,9},{9,10},{10,1... | collective-permute-start | bytes 589832 | tf_op jit(solution)/shard_map/ppermute | solution.py:77
  128.5 9.0 %collective-permute-start.4 = (bf16[64,1536]{1,0:T(8,128)(2,1)}, bf16[64,1536]{1,0:T(8,128)(2,1)}, u32[]{:S(2)}, u32[]{:S(2)}) collective-permute-start(bf16[64,1536]{1,0:T(8,128)(2,1)} %convolution_convert_fusion.2), channel_id=1, source_target_pairs={{0,2},{1,3},{2,0},{3,1},{4,6},{5,7},{6,4},{7,5},{8,10},{9,11},{10,... | collective-permute-start | bytes 589832 | tf_op jit(solution)/shard_map/ppermute | solution.py:77
  132.5 6.0 %collective-permute-start.2 = (bf16[64,1536]{1,0:T(8,128)(2,1)}, bf16[64,1536]{1,0:T(8,128)(2,1)}, u32[]{:S(2)}, u32[]{:S(2)}) collective-permute-start(bf16[64,1536]{1,0:T(8,128)(2,1)} %convolution_convert_fusion.3), channel_id=1, source_target_pairs={{0,3},{1,0},{2,1},{3,2},{4,7},{5,4},{6,5},{7,6},{8,11},{9,8},{10,9... | collective-permute-start | bytes 589832 | tf_op jit(solution)/shard_map/ppermute | solution.py:77
  137.5 2.6 %copy-start.5 = (bf16[1536,64]{0,1:T(8,128)(2,1)S(1)}, bf16[1536,64]{0,1:T(8,128)(2,1)}, u32[]{:S(2)}) copy-start(bf16[1536,64]{0,1:T(8,128)(2,1)} %param.25) | copy-start | bytes 589828
  137.5 2.6 %copy-start.6 = (f32[8,1536]{1,0:T(8,128)S(1)}, f32[8,1536]{1,0:T(8,128)}, u32[]{:S(2)}) copy-start(f32[8,1536]{1,0:T(8,128)} %get-tuple-element.12) | copy-start | bytes 147460
  137.5 2.6 %copy-start.7 = (f32[8,1536]{1,0:T(8,128)S(1)}, f32[8,1536]{1,0:T(8,128)}, u32[]{:S(2)}) copy-start(f32[8,1536]{1,0:T(8,128)} %get-tuple-element.13) | copy-start | bytes 147460
  137.5 3.8 %copy-start.11 = (f32[9]{0:T(128)S(1)}, f32[9]{0:T(128)}, u32[]{:S(2)}) copy-start(f32[9]{0:T(128)} %param.18) | copy-start | bytes 112
  140.4 5.5 %collective-permute-start.7 = (f32[8,8,32]{2,1,0:T(8,128)S(1)}, f32[8,8,32]{2,1,0:T(8,128)S(1)}, u32[]{:S(2)}, u32[]{:S(2)}) collective-permute-start(f32[8,8,32]{2,1,0:T(8,128)S(1)} %constant_dynamic-slice_fusion), channel_id=1, source_target_pairs={{0,128},{128,0},{1,129},{129,1},{2,130},{130,2},{3,131},{131,3},{4... | collective-permute-start | bytes 24584 | tf_op jit(solution)/shard_map/ppermute | solution.py:17

commit v13 on v12

--- a/solution.py
+++ b/solution.py
@@ -75,12 +75,6 @@
 def shifted(value, axis, step):
     size = lax.axis_size(axis)
     return lax.ppermute(value, axis, [(i, (i + step) % size) for i in range(size)])
-
-
-def reduce_rows(partial, parties):
-    pieces = partial.reshape(parties, partial.shape[0] // parties, partial.shape[1])
-    got = lax.all_to_all(pieces, "tp", split_axis=0, concat_axis=0, tiled=True)
-    return jnp.sum(got.astype(jnp.float32), 0)
 
 
 def shards(
@@ -186,8 +180,19 @@
     )
     tp_index = lax.axis_index("tp")
     resident_mine = lax.dynamic_slice_in_dim(resident, tp_index * portion, portion, 0)
-    attn_part = jnp.dot(attn_rows, w_out, preferred_element_type=jnp.float32).astype(jnp.bfloat16)
-    attn_mixed = reduce_rows(attn_part, parties).reshape(portion, requests, model_width)
+    block_rows = portion * requests
+    attn_total = None
+    for step in range(parties):
+        rows_for = lax.dynamic_slice_in_dim(
+            attn_rows, ((tp_index + step) % parties) * block_rows, block_rows, 0
+        )
+        part = jnp.dot(rows_for, w_out, preferred_element_type=jnp.float32).astype(jnp.bfloat16)
+        if step:
+            part = shifted(part, "tp", step)
+        attn_total = (
+            part.astype(jnp.float32) if attn_total is None else attn_total + part.astype(jnp.float32)
+        )
+    attn_mixed = attn_total.reshape(portion, requests, model_width)
     after_attn = resident_mine + adaptive[:, 2] * attn_mixed
     mlp_mine = modulate(after_attn, adaptive[:, 3], adaptive[:, 4])
     arrived = [mlp_mine] + [shifted(mlp_mine, "tp", step) for step in range(1, parties)]

time: 149 us -> 139 us (0.933)
  blocking collectives: 52.2 us -> 35.2 us
  waiting for transfers between devices: 19.3 us -> 30.5 us
  other arithmetic: 16.1 us -> 11.8 us
  local copies, waits for them, and re-layouts: 16.1 us -> 12.6 us
  matrix products: 21.7 us -> 23.9 us
  starting transfers between devices: 14.4 us -> 16.1 us
    all_to_all x1 -> x0, blocking collectives: 17 us -> none  [shards(): lax.all_to_all(answer.reshape(senders, query_share, head_share), 'seq', s...]
    ppermute x6 -> x9, waiting for transfers between devices: 4.81 us -> 13.2 us  [shifted(): lax.ppermute(value, axis, [(i, (i + step) % size) for i in range(size)])]
    dot_general x1 -> x4, matrix products: 2.85 us -> 7.19 us  [shards(): jnp.dot(rows_for, w_out, preferred_element_type=jnp.float32)]
    all_to_all x1, waiting for transfers between devices: 10.1 us -> 12.9 us  [shards(): lax.all_to_all(answer.reshape(senders, query_share, head_share), 'seq', s...]
    concatenate x2, local copies, waits for them, and re-layouts: 2.66 us -> 0.26 us  [shards(): jnp.concatenate([keys_img, keys_txt], 0)]
    dot_general x3, matrix products: 5.36 us -> 3.3 us  [shards(): jnp.dot(normed, w_qkv[:, part], preferred_element_type=jnp.float32)]
    transpose x1, local copies, waits for them, and re-layouts: 0.27 us -> 1.92 us  [shards(): attn_rows = answer_back.reshape(requests, 2, halves, query_share, head_sh...]
    ppermute x6 -> x9, starting transfers between devices: 9.11 us -> 10.5 us  [shifted(): lax.ppermute(value, axis, [(i, (i + step) % size) for i in range(size)])]
  transfers between devices with their start and end apart: 9 -> 12, of which waited for: 4 -> 7; matrix products, arithmetic and copies ran while one was open for 12% -> 15% of each run, Pallas kernels for 0% -> 0%
where the time goes in v13:
time: 139 us; the launch traced here: 138 us
  blocking collectives  35.2 us (25%)
  waiting for transfers between devices  30.5 us (22%)
  matrix products  23.9 us (17%)
  starting transfers between devices  16.1 us (12%)
  local copies, waits for them, and re-layouts  12.6 us (9%)
  other arithmetic  11.8 us (8%)
  Pallas kernels  6.09 us (4%)
  between operations  1.67 us (1%)
    all_to_all x1, blocking collectives, shards(): lax.all_to_all(payload, 'seq', split_axis=0, concat_axis=0, tiled=True)  35.2 us
    ppermute x9, waiting for transfers between devices, shifted(): lax.ppermute(value, axis, [(i, (i + step) % size) for i in range(size)])  13.2 us
    all_to_all x1, waiting for transfers between devices, shards(): lax.all_to_all(answer.reshape(senders, query_share, head_share), 'seq', s...  12.9 us
    dot_general x4, matrix products, shards(): jnp.dot(hidden, w_down, preferred_element_type=jnp.float32)  12.5 us
    ppermute x9, starting transfers between devices, shifted(): lax.ppermute(value, axis, [(i, (i + step) % size) for i in range(size)])  10.5 us
    dot_general x4, matrix products, shards(): jnp.dot(rows_for, w_out, preferred_element_type=jnp.float32)  7.19 us
    pallas_call x1, Pallas kernels, attend_kernel(): pl.pallas_call(attention_kernel, out_shape=jax.ShapeDtypeStruct(queries.s...  6.09 us
    all_to_all x1, starting transfers between devices, shards(): lax.all_to_all(answer.reshape(senders, query_share, head_share), 'seq', s...  4.77 us
  transfers between devices with their start and end apart: 12, of which 7 were waited for; matrix products, arithmetic and copies ran while one was open for 15% of the time, Pallas kernels for 0%

profile of v13, /device:TPU:4, one launch (start us, length us, event | category | flops | bytes accessed | tf_op | source)
XLA Modules:
  0.0 137.7 jit_solution(15335888595317133261)
XLA Ops:
  0.7 1.1 bitcast_convert_fusion
  1.8 0.7 fusion.114
  2.5 0.2 convert_reduce_fusion
  2.7 0.3 multiply_reduce_fusion
  3.1 2.0 %fusion.17 = bf16[256,384]{1,0:T(8,128)(2,1)S(1)} fusion(bf16[1536,3,384]{2,0,1:T(8,128)(2,1)} %param.20, bf16[1,32,8,1536]{3,2,1,0:T(8,128)(2,1)S(1)} %copy-done.2, f32[8,1536]{1,0:T(8,128)S(1)} %get-tuple-element.17, f32[8,1536]{1,0:T(8,128)S(1)} %get-tuple-element.18, f32[32,8]{1,0:T(8,128)S(1)} %add_rsqrt_fusion, f32[32,8]{1,0:T(8,128)S(1)} %broadcast_multiply_fusion), kind=kOutput, calls=%fused_computation.25 | convolution fusion | flops 304447488 | bytes 2263040 | tf_op jit(solution)/shard_map/dot_general | solution.py:109
  5.2 0.3 copy-done.15
  5.4 0.6 fusion.14
  6.1 0.6 fusion.11
  6.7 1.0 copy-done.5
  7.7 0.5 copy.42
  8.2 0.4 copy-done.6
  8.8 0.2 fusion.26
  8.9 0.6 convolution_convert_fusion.8
  9.6 0.2 concatenate.22
  9.9 0.2 concatenate.19
  10.1 1.0 maximum_bitcast_fusion
  11.1 0.2 copy.37
  11.3 0.2 reshape_reshape.3
  11.6 0.2 pad_maximum_fusion
  11.8 35.2 %all_to_all.10 = bf16[32,53,192]{2,1,0:T(8,128)(2,1)S(1)} all-to-all(bf16[32,53,192]{2,1,0:T(8,128)(2,1)S(1)} %pad_maximum_fusion), channel_id=1, replica_groups=mesh['cfg'=2,'seq'=32,'tp'=4] {'seq'}, dimensions={0} | all-to-all | bytes 1302528 | tf_op jit(solution)/shard_map/all_to_all | solution.py:140
  47.0 1.0 copy.38
  48.0 0.6 fusion.128
  49.2 0.6 compare_convert_fusion.valid_ref
  49.8 0.7 slice.91
  50.5 1.4 %broadcast_select_fusion = (bf16[32,37,192]{2,1,0:T(8,128)(2,1)S(1)}, bf16[32,37,192]{2,1,0:T(8,128)(2,1)S(1)}) fusion(pred[]{:T(512)S(6)} %eq.45, bf16[32,37,192]{2,0,1:T(8,128)(2,1)} %collective-permute-done, bf16[32,53,192]{2,1,0:T(8,128)(2,1)S(1)} %all_to_all.10), kind=kLoop, calls=%fused_computation.29 | loop fusion | flops 454656 | bytes 1818625 | tf_op jit(solution)/shard_map/jit(_where)/select_n | solution.py:146
  52.0 0.9 slice.93
  52.9 0.9 slice.94
  53.9 0.7 pad.7.kt_ref
  54.6 0.7 pad.8.vt_ref
  55.2 6.1 %shard_map.140 = bf16[512,192]{1,0:T(8,128)(2,1)} custom-call(bf16[512,192]{1,0:T(8,128)(2,1)} %bitcast.153, bf16[1024,192]{1,0:T(8,128)(2,1)} %bitcast.150, bf16[1024,192]{1,0:T(8,128)(2,1)} %bitcast.151, bf16[256,192]{1,0:T(8,128)(2,1)} %pad.7.kt_ref, bf16[256,192]{1,0:T(8,128)(2,1)} %pad.8.vt_ref, f32[1,256]{1,0:T(1,128)} %compare_convert_fusion.valid_ref), custom_call_target="tpu_custom_call" | custom-call | tf_op jit(solution)/shard_map/pallas_call | solution.py:69
  61.3 4.8 %all-to-all-start.1 = ((bf16[32,16,192]{2,1,0:T(8,128)(2,1)}), bf16[32,16,192]{2,1,0:T(8,128)(2,1)}, u32[]{:S(2)}, u32[]{:S(2)}) async-start(bf16[32,16,192]{2,1,0:T(8,128)(2,1)} %bitcast.152), calls=%async_computation.1 | async-start | bytes 524288 | tf_op jit(solution)/shard_map/all_to_all | solution.py:169
  66.1 12.9 %all-to-all-done.1 = bf16[32,16,192]{2,1,0:T(8,128)(2,1)} async-done(((bf16[32,16,192]{2,1,0:T(8,128)(2,1)}), bf16[32,16,192]{2,1,0:T(8,128)(2,1)}, u32[]{:S(2)}, u32[]{:S(2)}) %all-to-all-start.1) | async-done | bytes 196640 | tf_op jit(solution)/shard_map/all_to_all | solution.py:169
  79.0 1.9 %copy.41 = bf16[2,16,8,2,192]{4,3,2,1,0:T(2,128)(2,1)} copy(bf16[2,16,8,2,192]{4,1,0,3,2:T(8,128)(2,1)} %bitcast.25) | data formatting | bytes 393216 | tf_op jit(solution)/shard_map/transpose | solution.py:178
  81.0 1.8 %reshape.426 = bf16[256,384]{1,0:T(8,128)(2,1)} reshape(bf16[2,16,8,2,192]{4,3,2,1,0:T(2,128)(2,1)} %copy.41) | data formatting | bytes 393216 | tf_op jit(solution)/shard_map/reshape | solution.py:179
  82.8 1.8 %convolution_convert_fusion.4 = bf16[64,1536]{1,0:T(8,128)(2,1)} fusion(bf16[384,1536]{1,0:T(8,128)(2,1)S(1)} %copy-done.1, bf16[256,384]{1,0:T(8,128)(2,1)} %reshape.426, s32[]{:T(128)S(6)} %select_n.98), kind=kOutput, calls=%fused_computation.5 | convolution fusion | flops 75595776 | bytes 1425412 | tf_op jit(solution)/shard_map/dot_general | solution.py:189
  84.6 3.0 %collective-permute-start.3 = (bf16[64,1536]{1,0:T(8,128)(2,1)}, bf16[64,1536]{1,0:T(8,128)(2,1)}, u32[]{:S(2)}, u32[]{:S(2)}) collective-permute-start(bf16[64,1536]{1,0:T(8,128)(2,1)} %convolution_convert_fusion.4), channel_id=1, source_target_pairs={{0,3},{1,0},{2,1},{3,2},{4,7},{5,4},{6,5},{7,6},{8,11},{9,8},{10,9... | collective-permute-start | bytes 589832 | tf_op jit(solution)/shard_map/ppermute | solution.py:77
  87.6 1.8 %convolution_convert_fusion.5 = bf16[64,1536]{1,0:T(8,128)(2,1)} fusion(bf16[384,1536]{1,0:T(8,128)(2,1)S(1)} %copy-done.1, bf16[256,384]{1,0:T(8,128)(2,1)} %reshape.426, s32[]{:T(128)S(6)} %select_n.96), kind=kOutput, calls=%fused_computation.6 | convolution fusion | flops 75595776 | bytes 1425412 | tf_op jit(solution)/shard_map/dot_general | solution.py:189
  89.4 0.6 collective-permute-start.2
  90.0 1.8 %convolution_convert_fusion.6 = bf16[64,1536]{1,0:T(8,128)(2,1)} fusion(bf16[384,1536]{1,0:T(8,128)(2,1)S(1)} %copy-done.1, bf16[256,384]{1,0:T(8,128)(2,1)} %reshape.426, s32[]{:T(128)S(6)} %select_n.94), kind=kOutput, calls=%fused_computation.7 | convolution fusion | flops 75595776 | bytes 1425412 | tf_op jit(solution)/shard_map/dot_general | solution.py:189
  91.9 1.0 collective-permute-start.1
  92.8 2.5 %convert_element_type.167 = f32[1,32,8,1536]{3,2,1,0:T(8,128)} convert(bf16[1,32,8,1536]{3,2,1,0:T(8,128)(2,1)} %param.13) | non-fusion elementwise | flops 393216 | bytes 2359296 | tf_op jit(solution)/shard_map/convert_element_type | solution.py:105
  95.4 3.4 %collective-permute-done.2 = bf16[64,1536]{1,0:T(8,128)(2,1)} collective-permute-done((bf16[64,1536]{1,0:T(8,128)(2,1)}, bf16[64,1536]{1,0:T(8,128)(2,1)}, u32[]{:S(2)}, u32[]{:S(2)}) %collective-permute-start.2) | collective-permute-done | bytes 196640 | tf_op jit(solution)/shard_map/ppermute | solution.py:77
  98.8 2.1 %collective-permute-done.1 = bf16[64,1536]{1,0:T(8,128)(2,1)} collective-permute-done((bf16[64,1536]{1,0:T(8,128)(2,1)}, bf16[64,1536]{1,0:T(8,128)(2,1)}, u32[]{:S(2)}, u32[]{:S(2)}) %collective-permute-start.1) | collective-permute-done | bytes 196640 | tf_op jit(solution)/shard_map/ppermute | solution.py:77
  100.9 1.8 %fusion.151 = (f32[8,8]{1,0:T(8,128)S(1)}, f32[8,8,1536]{2,1,0:T(8,128)S(1)}) fusion(bf16[64,1536]{1,0:T(8,128)(2,1)} %collective-permute-done.3, bf16[64,1536]{1,0:T(8,128)(2,1)} %collective-permute-done.2, bf16[64,1536]{1,0:T(8,128)(2,1)} %collective-permute-done.1, bf16[384,1536]{1,0:T(8,128)(2,1)S(1)} %copy-done.1, bf16[256,384]{1,0:T(8,128)(2,1)} %reshape.426, ...), kind=kOutput, calls=%fused_computation.180 | convolution fusion | flops 76578752 | bytes 2654472 | tf_op jit(solution)/shard_map/dot_general | solution.py:189
  102.7 0.2 multiply_reduce_fusion.2
  102.9 0.5 copy-done.3
  103.6 0.6 collective-permute-start.8
  104.2 0.8 collective-permute-start.6
  105.1 1.1 collective-permute-start.4
  106.1 5.2 %collective-permute-done.8 = bf16[8,8,1536]{2,1,0:T(8,128)(2,1)S(1)} collective-permute-done((bf16[8,8,1536]{2,1,0:T(8,128)(2,1)S(1)}, bf16[8,8,1536]{2,1,0:T(8,128)(2,1)S(1)}, u32[]{:S(2)}, u32[]{:S(2)}) %collective-permute-start.8) | collective-permute-done | bytes 196640 | tf_op jit(solution)/shard_map/ppermute | solution.py:77
  111.4 2.8 %convolution_convert_fusion = bf16[64,1536]{1,0:T(8,128)(2,1)S(1)} fusion(bf16[768,1536]{1,0:T(8,128)(2,1)S(1)} %copy-done, bf16[1536,768]{1,0:T(8,128)(2,1)} %param.23, bf16[8,8,1536]{2,1,0:T(8,128)(2,1)S(1)} %collective-permute-done.8), kind=kOutput, calls=%fused_computation | convolution fusion | flops 302530560 | bytes 5111808 | tf_op jit(solution)/shard_map/dot_general | solution.py:209
  114.3 3.5 %convolution_convert_fusion.1 = bf16[64,1536]{1,0:T(8,128)(2,1)} fusion(bf16[768,1536]{1,0:T(8,128)(2,1)S(1)} %copy-done, bf16[1536,768]{1,0:T(8,128)(2,1)} %param.23, bf16[8,8,1536]{2,1,0:T(8,128)(2,1)S(1)} %collective-permute-done.6), kind=kOutput, calls=%fused_computation.1 | convolution fusion | flops 302530560 | bytes 5111808 | tf_op jit(solution)/shard_map/dot_general | solution.py:209
  117.8 2.5 %collective-permute-start.7 = (bf16[64,1536]{1,0:T(8,128)(2,1)}, bf16[64,1536]{1,0:T(8,128)(2,1)}, u32[]{:S(2)}, u32[]{:S(2)}) collective-permute-start(bf16[64,1536]{1,0:T(8,128)(2,1)} %convolution_convert_fusion.1), channel_id=1, source_target_pairs={{0,2},{1,3},{2,0},{3,1},{4,6},{5,7},{6,4},{7,5},{8,10},{9,11},{10,... | collective-permute-start | bytes 589832 | tf_op jit(solution)/shard_map/ppermute | solution.py:77
  120.2 3.5 %convolution_convert_fusion.2 = bf16[64,1536]{1,0:T(8,128)(2,1)} fusion(bf16[768,1536]{1,0:T(8,128)(2,1)S(1)} %copy-done, bf16[1536,768]{1,0:T(8,128)(2,1)} %param.23, bf16[8,8,1536]{2,1,0:T(8,128)(2,1)S(1)} %collective-permute-done.4), kind=kOutput, calls=%fused_computation.2 | convolution fusion | flops 302530560 | bytes 5111808 | tf_op jit(solution)/shard_map/dot_general | solution.py:209
  123.7 0.8 collective-permute-start.5
  124.5 2.8 %fusion = f32[64,1536]{1,0:T(8,128)S(1)} fusion(bf16[768,1536]{1,0:T(8,128)(2,1)S(1)} %copy-done, bf16[1536,768]{1,0:T(8,128)(2,1)} %param.23, bf16[8,8,1536]{2,1,0:T(8,128)(2,1)S(1)} %add_convert_fusion.2), kind=kOutput, calls=%fused_computation.4 | convolution fusion | flops 302628864 | bytes 5308416 | tf_op jit(solution)/shard_map/dot_general | solution.py:209
  127.3 2.4 %collective-permute-done.5 = bf16[64,1536]{1,0:T(8,128)(2,1)} collective-permute-done((bf16[64,1536]{1,0:T(8,128)(2,1)}, bf16[64,1536]{1,0:T(8,128)(2,1)}, u32[]{:S(2)}, u32[]{:S(2)}) %collective-permute-start.5) | collective-permute-done | bytes 196640 | tf_op jit(solution)/shard_map/ppermute | solution.py:77
  129.7 1.3 fusion.148
  131.0 0.2 multiply_reduce_fusion.1
  131.2 0.3 fusion.62
  131.6 0.8 collective-permute-start.10
  132.4 0.2 select_reduce_fusion
  132.6 4.4 %collective-permute-done.10 = f32[8,8,32]{2,1,0:T(8,128)S(1)} collective-permute-done((f32[8,8,32]{2,1,0:T(8,128)S(1)}, f32[8,8,32]{2,1,0:T(8,128)S(1)}, u32[]{:S(2)}, u32[]{:S(2)}) %collective-permute-start.10) | collective-permute-done | bytes 8224 | tf_op jit(solution)/shard_map/ppermute | solution.py:17
  137.0 0.7 multiply_add_fusion
  (60 shorter events, 1.1 us)
Async XLA Ops:
  0.6 110.7 %copy-start = (bf16[768,1536]{1,0:T(8,128)(2,1)S(1)}, bf16[768,1536]{1,0:T(8,128)(2,1)}, u32[]{:S(2)}) copy-start(bf16[768,1536]{1,0:T(8,128)(2,1)} %param.24) | copy-start | bytes 7077892
  0.6 1.9 %copy-start.2 = (bf16[1,32,8,1536]{3,2,1,0:T(8,128)(2,1)S(1)}, bf16[1,32,8,1536]{3,2,1,0:T(8,128)(2,1)}, u32[]{:S(2)}) copy-start(bf16[1,32,8,1536]{3,2,1,0:T(8,128)(2,1)} %param.13) | copy-start | bytes 2359300
  3.1 2.4 %copy-start.15 = (bf16[1536,3,384]{2,0,1:T(8,128)(2,1)S(1)}, bf16[1536,3,384]{2,0,1:T(8,128)(2,1)}, u32[]{:S(2)}) copy-start(bf16[1536,3,384]{2,0,1:T(8,128)(2,1)} %param.20) | copy-start | bytes 10616836
  6.1 1.7 %copy-start.5 = (bf16[1536,2,384]{2,1,0:T(2,128)(2,1)S(1)}, bf16[1536,2,384]{2,1,0:T(2,128)(2,1)}, u32[]{:S(2)}) copy-start(bf16[1536,2,384]{2,1,0:T(2,128)(2,1)} %param.21) | copy-start | bytes 7077892
  7.7 0.9 copy-start.6
  46.9 1.0 copy-start.16
  47.9 2.6 %collective-permute-start = (bf16[32,37,192]{2,0,1:T(8,128)(2,1)}, bf16[32,37,192]{2,0,1:T(8,128)(2,1)}, u32[]{:S(2)}, u32[]{:S(2)}) collective-permute-start(bf16[32,37,192]{2,0,1:T(8,128)(2,1)} %copy.38), channel_id=1, source_target_pairs={{0,4},{4,0},{8,12},{12,8},{16,20},{20,16},{24,28},{28,24},{32,36},... | collective-permute-start | bytes 1363976 | tf_op jit(solution)/shard_map/ppermute | solution.py:17
  55.2 27.6 %copy-start.1 = (bf16[384,1536]{1,0:T(8,128)(2,1)S(1)}, bf16[384,1536]{1,0:T(8,128)(2,1)}, u32[]{:S(2)}) copy-start(bf16[384,1536]{1,0:T(8,128)(2,1)} %param.22) | copy-start | bytes 3538948
  61.3 17.7 %all-to-all-start.1 = ((bf16[32,16,192]{2,1,0:T(8,128)(2,1)}), bf16[32,16,192]{2,1,0:T(8,128)(2,1)}, u32[]{:S(2)}, u32[]{:S(2)}) async-start(bf16[32,16,192]{2,1,0:T(8,128)(2,1)} %bitcast.152), calls=%async_computation.1 | async-start | bytes 524288 | tf_op jit(solution)/shard_map/all_to_all | solution.py:169
  84.6 10.8 %collective-permute-start.3 = (bf16[64,1536]{1,0:T(8,128)(2,1)}, bf16[64,1536]{1,0:T(8,128)(2,1)}, u32[]{:S(2)}, u32[]{:S(2)}) collective-permute-start(bf16[64,1536]{1,0:T(8,128)(2,1)} %convolution_convert_fusion.4), channel_id=1, source_target_pairs={{0,3},{1,0},{2,1},{3,2},{4,7},{5,4},{6,5},{7,6},{8,11},{9,8},{10,9... | collective-permute-start | bytes 589832 | tf_op jit(solution)/shard_map/ppermute | solution.py:77
  89.4 9.4 %collective-permute-start.2 = (bf16[64,1536]{1,0:T(8,128)(2,1)}, bf16[64,1536]{1,0:T(8,128)(2,1)}, u32[]{:S(2)}, u32[]{:S(2)}) collective-permute-start(bf16[64,1536]{1,0:T(8,128)(2,1)} %convolution_convert_fusion.5), channel_id=1, source_target_pairs={{0,2},{1,3},{2,0},{3,1},{4,6},{5,7},{6,4},{7,5},{8,10},{9,11},{10,... | collective-permute-start | bytes 589832 | tf_op jit(solution)/shard_map/ppermute | solution.py:77
  91.9 9.0 %collective-permute-start.1 = (bf16[64,1536]{1,0:T(8,128)(2,1)}, bf16[64,1536]{1,0:T(8,128)(2,1)}, u32[]{:S(2)}, u32[]{:S(2)}) collective-permute-start(bf16[64,1536]{1,0:T(8,128)(2,1)} %convolution_convert_fusion.6), channel_id=1, source_target_pairs={{0,1},{1,2},{2,3},{3,0},{4,5},{5,6},{6,7},{7,4},{8,9},{9,10},{10,1... | collective-permute-start | bytes 589832 | tf_op jit(solution)/shard_map/ppermute | solution.py:77
  95.3 8.1 %copy-start.10 = (f32[8,1536]{1,0:T(8,128)S(1)}, f32[8,1536]{1,0:T(8,128)}, u32[]{:S(2)}) copy-start(f32[8,1536]{1,0:T(8,128)} %get-tuple-element.12) | copy-start | bytes 147460
  95.3 8.1 %copy-start.11 = (f32[8,1536]{1,0:T(8,128)S(1)}, f32[8,1536]{1,0:T(8,128)}, u32[]{:S(2)}) copy-start(f32[8,1536]{1,0:T(8,128)} %get-tuple-element.13) | copy-start | bytes 147460
  100.9 3.3 %copy-start.13 = (s32[8]{0:T(128)S(1)}, s32[8]{0:T(128)}, u32[]{:S(2)}) copy-start(s32[8]{0:T(128)} %param.17) | copy-start | bytes 100
  102.7 0.8 copy-start.3
  103.6 7.8 %collective-permute-start.8 = (bf16[8,8,1536]{2,1,0:T(8,128)(2,1)S(1)}, bf16[8,8,1536]{2,1,0:T(8,128)(2,1)S(1)}, u32[]{:S(2)}, u32[]{:S(2)}) collective-permute-start(bf16[8,8,1536]{2,1,0:T(8,128)(2,1)S(1)} %add_convert_fusion.2), channel_id=1, source_target_pairs={{0,3},{1,0},{2,1},{3,2},{4,7},{5,4},{6,5},{7,6},{8,11},{9,8},{10,9... | collective-permute-start | bytes 589832 | tf_op jit(solution)/shard_map/ppermute | solution.py:77
  104.2 10.1 %collective-permute-start.6 = (bf16[8,8,1536]{2,1,0:T(8,128)(2,1)S(1)}, bf16[8,8,1536]{2,1,0:T(8,128)(2,1)S(1)}, u32[]{:S(2)}, u32[]{:S(2)}) collective-permute-start(bf16[8,8,1536]{2,1,0:T(8,128)(2,1)S(1)} %add_convert_fusion.2), channel_id=1, source_target_pairs={{0,2},{1,3},{2,0},{3,1},{4,6},{5,7},{6,4},{7,5},{8,10},{9,11},{10,... | collective-permute-start | bytes 589832 | tf_op jit(solution)/shard_map/ppermute | solution.py:77
  105.1 15.2 %collective-permute-start.4 = (bf16[8,8,1536]{2,1,0:T(8,128)(2,1)S(1)}, bf16[8,8,1536]{2,1,0:T(8,128)(2,1)S(1)}, u32[]{:S(2)}, u32[]{:S(2)}) collective-permute-start(bf16[8,8,1536]{2,1,0:T(8,128)(2,1)S(1)} %add_convert_fusion.2), channel_id=1, source_target_pairs={{0,1},{1,2},{2,3},{3,0},{4,5},{5,6},{6,7},{7,4},{8,9},{9,10},{10,1... | collective-permute-start | bytes 589832 | tf_op jit(solution)/shard_map/ppermute | solution.py:77
  114.2 13.1 %collective-permute-start.9 = (bf16[64,1536]{1,0:T(8,128)(2,1)S(1)}, bf16[64,1536]{1,0:T(8,128)(2,1)}, u32[]{:S(2)}, u32[]{:S(2)}) collective-permute-start(bf16[64,1536]{1,0:T(8,128)(2,1)S(1)} %convolution_convert_fusion), channel_id=1, source_target_pairs={{0,1},{1,2},{2,3},{3,0},{4,5},{5,6},{6,7},{7,4},{8,9},{9,10},{10,1... | collective-permute-start | bytes 589832 | tf_op jit(solution)/shard_map/ppermute | solution.py:77
  117.8 9.6 %collective-permute-start.7 = (bf16[64,1536]{1,0:T(8,128)(2,1)}, bf16[64,1536]{1,0:T(8,128)(2,1)}, u32[]{:S(2)}, u32[]{:S(2)}) collective-permute-start(bf16[64,1536]{1,0:T(8,128)(2,1)} %convolution_convert_fusion.1), channel_id=1, source_target_pairs={{0,2},{1,3},{2,0},{3,1},{4,6},{5,7},{6,4},{7,5},{8,10},{9,11},{10,... | collective-permute-start | bytes 589832 | tf_op jit(solution)/shard_map/ppermute | solution.py:77
  123.7 6.0 %copy-start.4 = (f32[8,8,1536]{2,1,0:T(8,128)S(1)}, f32[8,8,1536]{2,1,0:T(8,128)}, u32[]{:S(2)}) copy-start(f32[8,8,1536]{2,1,0:T(8,128)} %copy-done.3) | copy-start | bytes 1179652
  123.7 6.0 %collective-permute-start.5 = (bf16[64,1536]{1,0:T(8,128)(2,1)}, bf16[64,1536]{1,0:T(8,128)(2,1)}, u32[]{:S(2)}, u32[]{:S(2)}) collective-permute-start(bf16[64,1536]{1,0:T(8,128)(2,1)} %convolution_convert_fusion.2), channel_id=1, source_target_pairs={{0,3},{1,0},{2,1},{3,2},{4,7},{5,4},{6,5},{7,6},{8,11},{9,8},{10,9... | collective-permute-start | bytes 589832 | tf_op jit(solution)/shard_map/ppermute | solution.py:77
  127.3 4.0 %copy-start.7 = (bf16[1536,64]{0,1:T(8,128)(2,1)S(1)}, bf16[1536,64]{0,1:T(8,128)(2,1)}, u32[]{:S(2)}) copy-start(bf16[1536,64]{0,1:T(8,128)(2,1)} %param.25) | copy-start | bytes 589828
  127.3 3.9 %copy-start.8 = (f32[8,1536]{1,0:T(8,128)S(1)}, f32[8,1536]{1,0:T(8,128)}, u32[]{:S(2)}) copy-start(f32[8,1536]{1,0:T(8,128)} %get-tuple-element.10) | copy-start | bytes 147460
  127.3 3.9 %copy-start.9 = (f32[8,1536]{1,0:T(8,128)S(1)}, f32[8,1536]{1,0:T(8,128)}, u32[]{:S(2)}) copy-start(f32[8,1536]{1,0:T(8,128)} %get-tuple-element.11) | copy-start | bytes 147460
  127.3 5.1 %copy-start.14 = (f32[9]{0:T(128)S(1)}, f32[9]{0:T(128)}, u32[]{:S(2)}) copy-start(f32[9]{0:T(128)} %param.18) | copy-start | bytes 112
  127.3 9.7 %copy-start.12 = (f32[8,8,32]{2,1,0:T(8,128)S(1)}, f32[8,8,32]{2,1,0:T(8,128)}, u32[]{:S(2)}) copy-start(f32[8,8,32]{2,1,0:T(8,128)} %param.19) | copy-start | bytes 24580
  131.6 5.5 %collective-permute-start.10 = (f32[8,8,32]{2,1,0:T(8,128)S(1)}, f32[8,8,32]{2,1,0:T(8,128)S(1)}, u32[]{:S(2)}, u32[]{:S(2)}) collective-permute-start(f32[8,8,32]{2,1,0:T(8,128)S(1)} %constant_dynamic-slice_fusion), channel_id=1, source_target_pairs={{0,128},{128,0},{1,129},{129,1},{2,130},{130,2},{3,131},{131,3},{4... | collective-permute-start | bytes 24584 | tf_op jit(solution)/shard_map/ppermute | solution.py:17

commit v14 on v13

--- a/solution.py
+++ b/solution.py
@@ -179,7 +179,9 @@
         .reshape(rows_all, features)
     )
     tp_index = lax.axis_index("tp")
-    resident_mine = lax.dynamic_slice_in_dim(resident, tp_index * portion, portion, 0)
+    resident_mine = lax.dynamic_slice_in_dim(img_hidden[0], tp_index * portion, portion, 0).astype(
+        jnp.float32
+    )
     block_rows = portion * requests
     attn_total = None
     for step in range(parties):

time: 139 us -> 147 us (1.058)
  waiting for transfers between devices: 30.5 us -> 34.6 us
  matrix products: 23.9 us -> 27.7 us
    ppermute x9, waiting for transfers between devices: 13.2 us -> 18 us  [shifted(): lax.ppermute(value, axis, [(i, (i + step) % size) for i in range(size)])]
    convert_element_type x1 -> x0, other arithmetic: 2.48 us -> none  [shards(): resident = img_hidden[0].astype(jnp.float32)]
    dot_general x4, matrix products: 12.5 us -> 14.5 us  [shards(): jnp.dot(hidden, w_down, preferred_element_type=jnp.float32)]
  transfers between devices with their start and end apart: 12 -> 12, of which waited for: 7 -> 7; matrix products, arithmetic and copies ran while one was open for 15% -> 12% of each run, Pallas kernels for 0% -> 0%
where the time goes in v14:
time: 147 us; the launch traced here: 146 us
  blocking collectives  35.2 us (24%)
  waiting for transfers between devices  34.6 us (24%)
  matrix products  27.7 us (19%)
  starting transfers between devices  16 us (11%)
  local copies, waits for them, and re-layouts  12.9 us (9%)
  other arithmetic  11.6 us (8%)
  Pallas kernels  6.08 us (4%)
  between operations  1.57 us (1%)
    all_to_all x1, blocking collectives, shards(): lax.all_to_all(payload, 'seq', split_axis=0, concat_axis=0, tiled=True)  35.2 us
    ppermute x9, waiting for transfers between devices, shifted(): lax.ppermute(value, axis, [(i, (i + step) % size) for i in range(size)])  18 us
    dot_general x4, matrix products, shards(): jnp.dot(hidden, w_down, preferred_element_type=jnp.float32)  14.5 us
    all_to_all x1, waiting for transfers between devices, shards(): lax.all_to_all(answer.reshape(senders, query_share, head_share), 'seq', s...  12.9 us
    ppermute x9, starting transfers between devices, shifted(): lax.ppermute(value, axis, [(i, (i + step) % size) for i in range(size)])  10.4 us
    dot_general x4, matrix products, shards(): jnp.dot(rows_for, w_out, preferred_element_type=jnp.float32)  7.8 us
    pallas_call x1, Pallas kernels, attend_kernel(): pl.pallas_call(attention_kernel, out_shape=jax.ShapeDtypeStruct(queries.s...  6.08 us
    all_to_all x1, starting transfers between devices, shards(): lax.all_to_all(answer.reshape(senders, query_share, head_share), 'seq', s...  4.77 us
  transfers between devices with their start and end apart: 12, of which 7 were waited for; matrix products, arithmetic and copies ran while one was open for 12% of the time, Pallas kernels for 0%

profile of v14, /device:TPU:4, one launch (start us, length us, event | category | flops | bytes accessed | tf_op | source)
XLA Modules:
  0.0 145.7 jit_solution(16885287577618364180)
XLA Ops:
  0.7 1.1 bitcast_convert_fusion
  1.8 0.7 slice_bitcast_fusion.2
  2.5 0.2 convert_reduce_fusion
  2.7 0.3 fusion.5
  3.1 2.1 %fusion.24 = bf16[256,384]{1,0:T(8,128)(2,1)S(1)} fusion(bf16[1536,3,384]{2,0,1:T(8,128)(2,1)} %param.20, bf16[1,32,8,1536]{3,2,1,0:T(8,128)(2,1)S(1)} %copy-done.4, f32[8,1536]{1,0:T(8,128)S(1)} %get-tuple-element.17, f32[8,1536]{1,0:T(8,128)S(1)} %get-tuple-element.18, f32[32,8]{1,0:T(8,128)S(1)} %add_rsqrt_fusion, f32[32,8]{1,0:T(8,128)S(1)} %broadcast_multiply_fusion), kind=kOutput, calls=%fused_computation.30 | convolution fusion | flops 304447488 | bytes 2263040 | tf_op jit(solution)/shard_map/dot_general | solution.py:109
  5.2 0.3 copy-done.13
  5.5 0.6 fusion.21
  6.1 0.6 fusion.18
  6.8 1.0 copy-done.6
  7.8 0.5 copy.42
  8.3 0.4 copy-done.7
  8.8 0.2 fusion.39
  9.0 0.6 convolution_convert_fusion.8
  9.7 0.2 concatenate.22
  9.9 0.2 concatenate.19
  10.1 1.0 maximum_bitcast_fusion
  11.1 0.2 copy.37
  11.4 0.2 reshape_reshape.3
  11.8 35.2 %all_to_all.10 = bf16[32,53,192]{2,1,0:T(8,128)(2,1)S(1)} all-to-all(bf16[32,53,192]{2,1,0:T(8,128)(2,1)S(1)} %pad_maximum_fusion), channel_id=1, replica_groups=mesh['cfg'=2,'seq'=32,'tp'=4] {'seq'}, dimensions={0} | all-to-all | bytes 1302528 | tf_op jit(solution)/shard_map/all_to_all | solution.py:140
  47.0 1.0 copy.38
  48.0 0.6 fusion.163
  49.2 0.6 compare_convert_fusion.valid_ref
  49.8 0.7 slice.91
  50.6 1.4 broadcast_select_fusion
  52.0 0.9 slice.93
  52.9 0.9 slice.94
  53.9 0.7 pad.7.kt_ref
  54.6 0.7 pad.8.vt_ref
  55.2 6.1 %shard_map.140 = bf16[512,192]{1,0:T(8,128)(2,1)} custom-call(bf16[512,192]{1,0:T(8,128)(2,1)} %bitcast.259, bf16[1024,192]{1,0:T(8,128)(2,1)} %bitcast.256, bf16[1024,192]{1,0:T(8,128)(2,1)} %bitcast.257, bf16[256,192]{1,0:T(8,128)(2,1)} %pad.7.kt_ref, bf16[256,192]{1,0:T(8,128)(2,1)} %pad.8.vt_ref, f32[1,256]{1,0:T(1,128)} %compare_convert_fusion.valid_ref), custom_call_target="tpu_custom_call" | custom-call | tf_op jit(solution)/shard_map/pallas_call | solution.py:69
  61.3 4.8 %all-to-all-start.1 = ((bf16[32,16,192]{2,1,0:T(8,128)(2,1)}), bf16[32,16,192]{2,1,0:T(8,128)(2,1)}, u32[]{:S(2)}, u32[]{:S(2)}) async-start(bf16[32,16,192]{2,1,0:T(8,128)(2,1)} %bitcast.258), calls=%async_computation.1 | async-start | bytes 524288 | tf_op jit(solution)/shard_map/all_to_all | solution.py:169
  66.1 12.9 %all-to-all-done.1 = bf16[32,16,192]{2,1,0:T(8,128)(2,1)} async-done(((bf16[32,16,192]{2,1,0:T(8,128)(2,1)}), bf16[32,16,192]{2,1,0:T(8,128)(2,1)}, u32[]{:S(2)}, u32[]{:S(2)}) %all-to-all-start.1) | async-done | bytes 196640 | tf_op jit(solution)/shard_map/all_to_all | solution.py:169
  79.0 1.9 %copy.41 = bf16[2,16,8,2,192]{4,3,2,1,0:T(2,128)(2,1)} copy(bf16[2,16,8,2,192]{4,1,0,3,2:T(8,128)(2,1)} %bitcast.26) | data formatting | bytes 393216 | tf_op jit(solution)/shard_map/transpose | solution.py:178
  81.0 1.8 %reshape.462 = bf16[256,384]{1,0:T(8,128)(2,1)} reshape(bf16[2,16,8,2,192]{4,3,2,1,0:T(2,128)(2,1)} %copy.41) | data formatting | bytes 393216 | tf_op jit(solution)/shard_map/reshape | solution.py:179
  82.8 1.8 %convolution_convert_fusion.4 = bf16[64,1536]{1,0:T(8,128)(2,1)} fusion(bf16[384,1536]{1,0:T(8,128)(2,1)S(1)} %copy-done.1, bf16[256,384]{1,0:T(8,128)(2,1)} %reshape.462, s32[]{:T(128)S(6)} %select_n.98), kind=kOutput, calls=%fused_computation.5 | convolution fusion | flops 75595776 | bytes 1425412 | tf_op jit(solution)/shard_map/dot_general | solution.py:191
  84.6 3.0 %collective-permute-start.3 = (bf16[64,1536]{1,0:T(8,128)(2,1)}, bf16[64,1536]{1,0:T(8,128)(2,1)}, u32[]{:S(2)}, u32[]{:S(2)}) collective-permute-start(bf16[64,1536]{1,0:T(8,128)(2,1)} %convolution_convert_fusion.4), channel_id=1, source_target_pairs={{0,3},{1,0},{2,1},{3,2},{4,7},{5,4},{6,5},{7,6},{8,11},{9,8},{10,9... | collective-permute-start | bytes 589832 | tf_op jit(solution)/shard_map/ppermute | solution.py:77
  87.6 1.8 %convolution_convert_fusion.5 = bf16[64,1536]{1,0:T(8,128)(2,1)} fusion(bf16[384,1536]{1,0:T(8,128)(2,1)S(1)} %copy-done.1, bf16[256,384]{1,0:T(8,128)(2,1)} %reshape.462, s32[]{:T(128)S(6)} %select_n.96), kind=kOutput, calls=%fused_computation.6 | convolution fusion | flops 75595776 | bytes 1425412 | tf_op jit(solution)/shard_map/dot_general | solution.py:191
  89.4 0.6 collective-permute-start.2
  90.0 1.8 %convolution_convert_fusion.6 = bf16[64,1536]{1,0:T(8,128)(2,1)} fusion(bf16[384,1536]{1,0:T(8,128)(2,1)S(1)} %copy-done.1, bf16[256,384]{1,0:T(8,128)(2,1)} %reshape.462, s32[]{:T(128)S(6)} %select_n.94), kind=kOutput, calls=%fused_computation.7 | convolution fusion | flops 75595776 | bytes 1425412 | tf_op jit(solution)/shard_map/dot_general | solution.py:191
  91.8 1.0 collective-permute-start.1
  92.8 2.5 %collective-permute-done.3 = bf16[64,1536]{1,0:T(8,128)(2,1)} collective-permute-done((bf16[64,1536]{1,0:T(8,128)(2,1)}, bf16[64,1536]{1,0:T(8,128)(2,1)}, u32[]{:S(2)}, u32[]{:S(2)}) %collective-permute-start.3) | collective-permute-done | bytes 196640 | tf_op jit(solution)/shard_map/ppermute | solution.py:77
  95.4 3.4 %collective-permute-done.2 = bf16[64,1536]{1,0:T(8,128)(2,1)} collective-permute-done((bf16[64,1536]{1,0:T(8,128)(2,1)}, bf16[64,1536]{1,0:T(8,128)(2,1)}, u32[]{:S(2)}, u32[]{:S(2)}) %collective-permute-start.2) | collective-permute-done | bytes 196640 | tf_op jit(solution)/shard_map/ppermute | solution.py:77
  98.8 2.1 %collective-permute-done.1 = bf16[64,1536]{1,0:T(8,128)(2,1)} collective-permute-done((bf16[64,1536]{1,0:T(8,128)(2,1)}, bf16[64,1536]{1,0:T(8,128)(2,1)}, u32[]{:S(2)}, u32[]{:S(2)}) %collective-permute-start.1) | collective-permute-done | bytes 196640 | tf_op jit(solution)/shard_map/ppermute | solution.py:77
  100.9 2.4 %fusion.183 = (f32[8,8]{1,0:T(8,128)S(1)}, f32[8,8,1536]{2,1,0:T(8,128)S(1)}, f32[64,1536]{1,0:T(8,128)}) fusion(f32[8,1536]{1,0:T(8,128)} %get-tuple-element.19, bf16[1,32,8,1536]{3,2,1,0:T(8,128)(2,1)} %param.13, s32[]{:T(128)S(6)} %select_n.84, bf16[64,1536]{1,0:T(8,128)(2,1)} %collective-permute-done.3, bf16[64,1536]{1,0:T(8,128)(2,1)} %collective-permute-done.2, ...), kind=kOutput, calls=%fused_computation.209 | convolution fusion | flops 76677056 | bytes 2851080 | tf_op jit(solution)/shard_map/dot_general | solution.py:191
  103.3 0.2 multiply_reduce_fusion.1
  103.5 0.5 copy-done.2
  104.0 0.8 add_convert_fusion
  104.8 0.6 collective-permute-start.8
  105.4 0.9 collective-permute-start.6
  106.3 1.1 collective-permute-start.4
  107.3 5.4 %collective-permute-done.8 = bf16[8,8,1536]{2,1,0:T(8,128)(2,1)S(1)} collective-permute-done((bf16[8,8,1536]{2,1,0:T(8,128)(2,1)}, bf16[8,8,1536]{2,1,0:T(8,128)(2,1)S(1)}, u32[]{:S(2)}, u32[]{:S(2)}) %collective-permute-start.8) | collective-permute-done | bytes 196640 | tf_op jit(solution)/shard_map/ppermute | solution.py:77
  112.8 3.5 %convolution_convert_fusion = bf16[64,1536]{1,0:T(8,128)(2,1)} fusion(bf16[768,1536]{1,0:T(8,128)(2,1)S(1)} %copy-done, bf16[1536,768]{1,0:T(8,128)(2,1)} %param.23, bf16[8,8,1536]{2,1,0:T(8,128)(2,1)S(1)} %collective-permute-done.8), kind=kOutput, calls=%fused_computation | convolution fusion | flops 302530560 | bytes 5111808 | tf_op jit(solution)/shard_map/dot_general | solution.py:211
  116.2 3.5 %convolution_convert_fusion.1 = bf16[64,1536]{1,0:T(8,128)(2,1)} fusion(bf16[768,1536]{1,0:T(8,128)(2,1)S(1)} %copy-done, bf16[1536,768]{1,0:T(8,128)(2,1)} %param.23, bf16[8,8,1536]{2,1,0:T(8,128)(2,1)S(1)} %collective-permute-done.6), kind=kOutput, calls=%fused_computation.1 | convolution fusion | flops 302530560 | bytes 5111808 | tf_op jit(solution)/shard_map/dot_general | solution.py:211
  119.7 2.5 %collective-permute-start.7 = (bf16[64,1536]{1,0:T(8,128)(2,1)}, bf16[64,1536]{1,0:T(8,128)(2,1)}, u32[]{:S(2)}, u32[]{:S(2)}) collective-permute-start(bf16[64,1536]{1,0:T(8,128)(2,1)} %convolution_convert_fusion.1), channel_id=1, source_target_pairs={{0,2},{1,3},{2,0},{3,1},{4,6},{5,7},{6,4},{7,5},{8,10},{9,11},{10,... | collective-permute-start | bytes 589832 | tf_op jit(solution)/shard_map/ppermute | solution.py:77
  122.3 3.6 %convolution_convert_fusion.2 = bf16[64,1536]{1,0:T(8,128)(2,1)} fusion(bf16[768,1536]{1,0:T(8,128)(2,1)S(1)} %copy-done, bf16[1536,768]{1,0:T(8,128)(2,1)} %param.23, bf16[8,8,1536]{2,1,0:T(8,128)(2,1)} %collective-permute-done.4), kind=kOutput, calls=%fused_computation.2 | convolution fusion | flops 302530560 | bytes 5111808 | tf_op jit(solution)/shard_map/dot_general | solution.py:211
  125.8 0.8 collective-permute-start.5
  126.7 0.5 broadcast_add_fusion
  127.4 4.5 %collective-permute-done.5 = bf16[64,1536]{1,0:T(8,128)(2,1)} collective-permute-done((bf16[64,1536]{1,0:T(8,128)(2,1)}, bf16[64,1536]{1,0:T(8,128)(2,1)}, u32[]{:S(2)}, u32[]{:S(2)}) %collective-permute-start.5) | collective-permute-done | bytes 196640 | tf_op jit(solution)/shard_map/ppermute | solution.py:77
  131.8 4.0 %fusion.123 = (f32[8,8]{1,0:T(8,128)S(1)}, f32[64,1536]{1,0:T(8,128)}) fusion(f32[8,8,1536]{2,1,0:T(8,128)S(1)} %copy-done.3, f32[8,1536]{1,0:T(8,128)} %get-tuple-element.10, bf16[64,1536]{1,0:T(8,128)(2,1)} %collective-permute-done.9, bf16[64,1536]{1,0:T(8,128)(2,1)} %collective-permute-done.7, bf16[64,1536]{1,0:T(8,128)(2,1)} %collective-permute-done.5, ...), kind=kOutput, calls=%fused_computation.128 | convolution fusion | flops 304299968 | bytes 6882564 | tf_op jit(solution)/shard_map/dot_general | solution.py:211
  135.9 1.2 multiply_reduce_fusion
  137.2 1.5 %fusion.84 = f32[8,8,64]{2,1,0:T(8,128)S(1)} fusion(bf16[1536,64]{0,1:T(8,128)(2,1)} %param.25, f32[64,1536]{1,0:T(8,128)} %get-tuple-element.24, f32[64,1536]{1,0:T(8,128)} %get-tuple-element.22, f32[8,1536]{1,0:T(8,128)} %get-tuple-element.11, f32[8,1536]{1,0:T(8,128)} %get-tuple-element.12, f32[64]{0:T(128)S(1)} %rsqrt.44, f32[64]{0:T(128)S(1)} %div.47, ...), kind=kOutput, calls=%fused_computation.108 | convolution fusion | flops 13565952 | bytes 1393668 | tf_op jit(solution)/shard_map/dot_general | solution.py:220
  138.8 0.8 collective-permute-start.10
  139.6 0.9 select_reduce_fusion
  140.5 3.8 %collective-permute-done.10 = f32[8,8,32]{2,1,0:T(8,128)S(1)} collective-permute-done((f32[8,8,32]{2,1,0:T(8,128)S(1)}, f32[8,8,32]{2,1,0:T(8,128)S(1)}, u32[]{:S(2)}, u32[]{:S(2)}) %collective-permute-start.10) | collective-permute-done | bytes 8224 | tf_op jit(solution)/shard_map/ppermute | solution.py:17
  144.2 1.5 %multiply_add_fusion = (f32[8,8,32]{2,1,0:T(8,128)}, f32[8,8,32]{2,1,0:T(8,128)}) fusion(f32[8,8,32]{2,1,0:T(8,128)} %param.19, f32[8]{0:T(128)S(1)} %sub.98, f32[8,8,32]{2,1,0:T(8,128)S(1)} %collective-permute-done.10, f32[8,8,64]{2,1,0:T(8,128)S(1)} %fusion.84, s32[]{:T(128)S(6)} %select_n.100, pred[]{:T(512)S(6)} %eq.44), kind=kLoop, calls=%fused_computation.168 | loop fusion | flops 14336 | bytes 40997 | tf_op jit(solution)/shard_map/add | solution.py:239
  (58 shorter events, 1.3 us)
Async XLA Ops:
  0.6 112.1 %copy-start = (bf16[768,1536]{1,0:T(8,128)(2,1)S(1)}, bf16[768,1536]{1,0:T(8,128)(2,1)}, u32[]{:S(2)}) copy-start(bf16[768,1536]{1,0:T(8,128)(2,1)} %param.24) | copy-start | bytes 7077892
  0.6 1.9 %copy-start.4 = (bf16[1,32,8,1536]{3,2,1,0:T(8,128)(2,1)S(1)}, bf16[1,32,8,1536]{3,2,1,0:T(8,128)(2,1)}, u32[]{:S(2)}) copy-start(bf16[1,32,8,1536]{3,2,1,0:T(8,128)(2,1)} %param.13) | copy-start | bytes 2359300
  3.1 2.4 %copy-start.13 = (bf16[1536,3,384]{2,0,1:T(8,128)(2,1)S(1)}, bf16[1536,3,384]{2,0,1:T(8,128)(2,1)}, u32[]{:S(2)}) copy-start(bf16[1536,3,384]{2,0,1:T(8,128)(2,1)} %param.20) | copy-start | bytes 10616836
  6.1 1.7 %copy-start.6 = (bf16[1536,2,384]{2,1,0:T(2,128)(2,1)S(1)}, bf16[1536,2,384]{2,1,0:T(2,128)(2,1)}, u32[]{:S(2)}) copy-start(bf16[1536,2,384]{2,1,0:T(2,128)(2,1)} %param.21) | copy-start | bytes 7077892
  7.8 0.9 copy-start.7
  46.9 1.0 copy-start.14
  48.0 2.6 %collective-permute-start = (bf16[32,37,192]{2,0,1:T(8,128)(2,1)}, bf16[32,37,192]{2,0,1:T(8,128)(2,1)}, u32[]{:S(2)}, u32[]{:S(2)}) collective-permute-start(bf16[32,37,192]{2,0,1:T(8,128)(2,1)} %copy.38), channel_id=1, source_target_pairs={{0,4},{4,0},{8,12},{12,8},{16,20},{20,16},{24,28},{28,24},{32,36},... | collective-permute-start | bytes 1363976 | tf_op jit(solution)/shard_map/ppermute | solution.py:17
  55.2 27.6 %copy-start.1 = (bf16[384,1536]{1,0:T(8,128)(2,1)S(1)}, bf16[384,1536]{1,0:T(8,128)(2,1)}, u32[]{:S(2)}) copy-start(bf16[384,1536]{1,0:T(8,128)(2,1)} %param.22) | copy-start | bytes 3538948
  61.3 17.7 %all-to-all-start.1 = ((bf16[32,16,192]{2,1,0:T(8,128)(2,1)}), bf16[32,16,192]{2,1,0:T(8,128)(2,1)}, u32[]{:S(2)}, u32[]{:S(2)}) async-start(bf16[32,16,192]{2,1,0:T(8,128)(2,1)} %bitcast.258), calls=%async_computation.1 | async-start | bytes 524288 | tf_op jit(solution)/shard_map/all_to_all | solution.py:169
  84.6 10.8 %collective-permute-start.3 = (bf16[64,1536]{1,0:T(8,128)(2,1)}, bf16[64,1536]{1,0:T(8,128)(2,1)}, u32[]{:S(2)}, u32[]{:S(2)}) collective-permute-start(bf16[64,1536]{1,0:T(8,128)(2,1)} %convolution_convert_fusion.4), channel_id=1, source_target_pairs={{0,3},{1,0},{2,1},{3,2},{4,7},{5,4},{6,5},{7,6},{8,11},{9,8},{10,9... | collective-permute-start | bytes 589832 | tf_op jit(solution)/shard_map/ppermute | solution.py:77
  89.4 9.4 %collective-permute-start.2 = (bf16[64,1536]{1,0:T(8,128)(2,1)}, bf16[64,1536]{1,0:T(8,128)(2,1)}, u32[]{:S(2)}, u32[]{:S(2)}) collective-permute-start(bf16[64,1536]{1,0:T(8,128)(2,1)} %convolution_convert_fusion.5), channel_id=1, source_target_pairs={{0,2},{1,3},{2,0},{3,1},{4,6},{5,7},{6,4},{7,5},{8,10},{9,11},{10,... | collective-permute-start | bytes 589832 | tf_op jit(solution)/shard_map/ppermute | solution.py:77
  91.8 9.0 %collective-permute-start.1 = (bf16[64,1536]{1,0:T(8,128)(2,1)}, bf16[64,1536]{1,0:T(8,128)(2,1)}, u32[]{:S(2)}, u32[]{:S(2)}) collective-permute-start(bf16[64,1536]{1,0:T(8,128)(2,1)} %convolution_convert_fusion.6), channel_id=1, source_target_pairs={{0,1},{1,2},{2,3},{3,0},{4,5},{5,6},{6,7},{7,4},{8,9},{9,10},{10,1... | collective-permute-start | bytes 589832 | tf_op jit(solution)/shard_map/ppermute | solution.py:77
  100.9 3.1 %copy-start.8 = (f32[8,1536]{1,0:T(8,128)S(1)}, f32[8,1536]{1,0:T(8,128)}, u32[]{:S(2)}) copy-start(f32[8,1536]{1,0:T(8,128)} %get-tuple-element.13) | copy-start | bytes 147460
  100.9 3.1 %copy-start.9 = (f32[8,1536]{1,0:T(8,128)S(1)}, f32[8,1536]{1,0:T(8,128)}, u32[]{:S(2)}) copy-start(f32[8,1536]{1,0:T(8,128)} %get-tuple-element.14) | copy-start | bytes 147460
  103.3 0.7 copy-start.2
  104.8 7.9 %collective-permute-start.8 = (bf16[8,8,1536]{2,1,0:T(8,128)(2,1)}, bf16[8,8,1536]{2,1,0:T(8,128)(2,1)S(1)}, u32[]{:S(2)}, u32[]{:S(2)}) collective-permute-start(bf16[8,8,1536]{2,1,0:T(8,128)(2,1)} %add_convert_fusion), channel_id=1, source_target_pairs={{0,3},{1,0},{2,1},{3,2},{4,7},{5,4},{6,5},{7,6},{8,11},{9,8},{10,9... | collective-permute-start | bytes 589832 | tf_op jit(solution)/shard_map/ppermute | solution.py:77
  105.4 10.9 %collective-permute-start.6 = (bf16[8,8,1536]{2,1,0:T(8,128)(2,1)}, bf16[8,8,1536]{2,1,0:T(8,128)(2,1)S(1)}, u32[]{:S(2)}, u32[]{:S(2)}) collective-permute-start(bf16[8,8,1536]{2,1,0:T(8,128)(2,1)} %add_convert_fusion), channel_id=1, source_target_pairs={{0,2},{1,3},{2,0},{3,1},{4,6},{5,7},{6,4},{7,5},{8,10},{9,11},{10,... | collective-permute-start | bytes 589832 | tf_op jit(solution)/shard_map/ppermute | solution.py:77
  106.3 16.0 %collective-permute-start.4 = (bf16[8,8,1536]{2,1,0:T(8,128)(2,1)}, bf16[8,8,1536]{2,1,0:T(8,128)(2,1)}, u32[]{:S(2)}, u32[]{:S(2)}) collective-permute-start(bf16[8,8,1536]{2,1,0:T(8,128)(2,1)} %add_convert_fusion), channel_id=1, source_target_pairs={{0,1},{1,2},{2,3},{3,0},{4,5},{5,6},{6,7},{7,4},{8,9},{9,10},{10,1... | collective-permute-start | bytes 589832 | tf_op jit(solution)/shard_map/ppermute | solution.py:77
  116.2 11.1 %collective-permute-start.9 = (bf16[64,1536]{1,0:T(8,128)(2,1)}, bf16[64,1536]{1,0:T(8,128)(2,1)}, u32[]{:S(2)}, u32[]{:S(2)}) collective-permute-start(bf16[64,1536]{1,0:T(8,128)(2,1)} %convolution_convert_fusion), channel_id=1, source_target_pairs={{0,1},{1,2},{2,3},{3,0},{4,5},{5,6},{6,7},{7,4},{8,9},{9,10},{10,1... | collective-permute-start | bytes 589832 | tf_op jit(solution)/shard_map/ppermute | solution.py:77
  119.7 6.9 %copy-start.10 = (s32[8]{0:T(128)S(1)}, s32[8]{0:T(128)}, u32[]{:S(2)}) copy-start(s32[8]{0:T(128)} %param.17) | copy-start | bytes 100
  119.7 12.1 %copy-start.3 = (f32[8,8,1536]{2,1,0:T(8,128)S(1)}, f32[8,8,1536]{2,1,0:T(8,128)}, u32[]{:S(2)}) copy-start(f32[8,8,1536]{2,1,0:T(8,128)} %copy-done.2) | copy-start | bytes 1179652
  119.7 12.1 %copy-start.5 = (bf16[1,32,8,1536]{3,2,1,0:T(8,128)(2,1)S(1)}, bf16[1,32,8,1536]{3,2,1,0:T(8,128)(2,1)}, u32[]{:S(2)}) copy-start(bf16[1,32,8,1536]{3,2,1,0:T(8,128)(2,1)} %param.13) | copy-start | bytes 2359300
  119.7 7.6 %collective-permute-start.7 = (bf16[64,1536]{1,0:T(8,128)(2,1)}, bf16[64,1536]{1,0:T(8,128)(2,1)}, u32[]{:S(2)}, u32[]{:S(2)}) collective-permute-start(bf16[64,1536]{1,0:T(8,128)(2,1)} %convolution_convert_fusion.1), channel_id=1, source_target_pairs={{0,2},{1,3},{2,0},{3,1},{4,6},{5,7},{6,4},{7,5},{8,10},{9,11},{10,... | collective-permute-start | bytes 589832 | tf_op jit(solution)/shard_map/ppermute | solution.py:77
  125.8 6.0 %collective-permute-start.5 = (bf16[64,1536]{1,0:T(8,128)(2,1)}, bf16[64,1536]{1,0:T(8,128)(2,1)}, u32[]{:S(2)}, u32[]{:S(2)}) collective-permute-start(bf16[64,1536]{1,0:T(8,128)(2,1)} %convolution_convert_fusion.2), channel_id=1, source_target_pairs={{0,3},{1,0},{2,1},{3,2},{4,7},{5,4},{6,5},{7,6},{8,11},{9,8},{10,9... | collective-permute-start | bytes 589832 | tf_op jit(solution)/shard_map/ppermute | solution.py:77
  135.8 3.8 %copy-start.11 = (s32[8]{0:T(128)S(1)}, s32[8]{0:T(128)}, u32[]{:S(2)}) copy-start(s32[8]{0:T(128)} %param.17) | copy-start | bytes 100
  135.8 3.8 %copy-start.12 = (f32[9]{0:T(128)S(1)}, f32[9]{0:T(128)}, u32[]{:S(2)}) copy-start(f32[9]{0:T(128)} %param.18) | copy-start | bytes 112
  138.8 5.5 %collective-permute-start.10 = (f32[8,8,32]{2,1,0:T(8,128)S(1)}, f32[8,8,32]{2,1,0:T(8,128)S(1)}, u32[]{:S(2)}, u32[]{:S(2)}) collective-permute-start(f32[8,8,32]{2,1,0:T(8,128)S(1)} %constant_dynamic-slice_fusion), channel_id=1, source_target_pairs={{0,128},{128,0},{1,129},{129,1},{2,130},{130,2},{3,131},{131,3},{4... | collective-permute-start | bytes 24584 | tf_op jit(solution)/shard_map/ppermute | solution.py:17

commit v15 on v13

--- a/solution.py
+++ b/solution.py
@@ -182,7 +182,7 @@
     resident_mine = lax.dynamic_slice_in_dim(resident, tp_index * portion, portion, 0)
     block_rows = portion * requests
     attn_total = None
-    for step in range(parties):
+    for step in list(range(1, parties)) + [0]:
         rows_for = lax.dynamic_slice_in_dim(
             attn_rows, ((tp_index + step) % parties) * block_rows, block_rows, 0
         )

time: 139 us -> 139 us (level)
  no operation moved by 1% of the time
where the time goes in v15:
time: 139 us; the launch traced here: 138 us
  blocking collectives  35.2 us (25%)
  waiting for transfers between devices  30.5 us (22%)
  matrix products  23.8 us (17%)
  starting transfers between devices  16.1 us (12%)
  local copies, waits for them, and re-layouts  12.6 us (9%)
  other arithmetic  11.8 us (8%)
  Pallas kernels  6.09 us (4%)
  between operations  1.67 us (1%)
    all_to_all x1, blocking collectives, shards(): lax.all_to_all(payload, 'seq', split_axis=0, concat_axis=0, tiled=True)  35.2 us
    ppermute x9, waiting for transfers between devices, shifted(): lax.ppermute(value, axis, [(i, (i + step) % size) for i in range(size)])  13.2 us
    all_to_all x1, waiting for transfers between devices, shards(): lax.all_to_all(answer.reshape(senders, query_share, head_share), 'seq', s...  12.9 us
    dot_general x4, matrix products, shards(): jnp.dot(hidden, w_down, preferred_element_type=jnp.float32)  12.5 us
    ppermute x9, starting transfers between devices, shifted(): lax.ppermute(value, axis, [(i, (i + step) % size) for i in range(size)])  10.5 us
    dot_general x4, matrix products, shards(): jnp.dot(rows_for, w_out, preferred_element_type=jnp.float32)  7.17 us
    pallas_call x1, Pallas kernels, attend_kernel(): pl.pallas_call(attention_kernel, out_shape=jax.ShapeDtypeStruct(queries.s...  6.09 us
    all_to_all x1, starting transfers between devices, shards(): lax.all_to_all(answer.reshape(senders, query_share, head_share), 'seq', s...  4.77 us
  transfers between devices with their start and end apart: 12, of which 7 were waited for; matrix products, arithmetic and copies ran while one was open for 15% of the time, Pallas kernels for 0%

profile of v15, /device:TPU:4, one launch (start us, length us, event | category | flops | bytes accessed | tf_op | source)
XLA Modules:
  0.0 137.7 jit_solution(14989224364950640829)
XLA Ops:
  0.7 1.1 bitcast_convert_fusion
  1.8 0.7 fusion.114
  2.5 0.2 convert_reduce_fusion
  2.7 0.3 multiply_reduce_fusion
  3.1 2.0 %fusion.17 = bf16[256,384]{1,0:T(8,128)(2,1)S(1)} fusion(bf16[1536,3,384]{2,0,1:T(8,128)(2,1)} %param.20, bf16[1,32,8,1536]{3,2,1,0:T(8,128)(2,1)S(1)} %copy-done.2, f32[8,1536]{1,0:T(8,128)S(1)} %get-tuple-element.17, f32[8,1536]{1,0:T(8,128)S(1)} %get-tuple-element.18, f32[32,8]{1,0:T(8,128)S(1)} %add_rsqrt_fusion, f32[32,8]{1,0:T(8,128)S(1)} %broadcast_multiply_fusion), kind=kOutput, calls=%fused_computation.25 | convolution fusion | flops 304447488 | bytes 2263040 | tf_op jit(solution)/shard_map/dot_general | solution.py:109
  5.2 0.3 copy-done.15
  5.4 0.6 fusion.14
  6.1 0.6 fusion.11
  6.7 1.0 copy-done.5
  7.7 0.5 copy.42
  8.2 0.4 copy-done.6
  8.8 0.2 fusion.26
  8.9 0.6 convolution_convert_fusion.8
  9.6 0.2 concatenate.22
  9.9 0.2 concatenate.19
  10.1 1.0 maximum_bitcast_fusion
  11.1 0.2 copy.37
  11.3 0.2 reshape_reshape.3
  11.6 0.2 pad_maximum_fusion
  11.8 35.2 %all_to_all.10 = bf16[32,53,192]{2,1,0:T(8,128)(2,1)S(1)} all-to-all(bf16[32,53,192]{2,1,0:T(8,128)(2,1)S(1)} %pad_maximum_fusion), channel_id=1, replica_groups=mesh['cfg'=2,'seq'=32,'tp'=4] {'seq'}, dimensions={0} | all-to-all | bytes 1302528 | tf_op jit(solution)/shard_map/all_to_all | solution.py:140
  47.0 1.0 copy.38
  48.0 0.6 fusion.128
  49.2 0.6 compare_convert_fusion.valid_ref
  49.8 0.7 slice.91
  50.5 1.4 %broadcast_select_fusion = (bf16[32,37,192]{2,1,0:T(8,128)(2,1)S(1)}, bf16[32,37,192]{2,1,0:T(8,128)(2,1)S(1)}) fusion(pred[]{:T(512)S(6)} %eq.45, bf16[32,37,192]{2,0,1:T(8,128)(2,1)} %collective-permute-done, bf16[32,53,192]{2,1,0:T(8,128)(2,1)S(1)} %all_to_all.10), kind=kLoop, calls=%fused_computation.29 | loop fusion | flops 454656 | bytes 1818625 | tf_op jit(solution)/shard_map/jit(_where)/select_n | solution.py:146
  52.0 0.9 slice.93
  52.9 0.9 slice.94
  53.9 0.7 pad.7.kt_ref
  54.6 0.7 pad.8.vt_ref
  55.2 6.1 %shard_map.140 = bf16[512,192]{1,0:T(8,128)(2,1)} custom-call(bf16[512,192]{1,0:T(8,128)(2,1)} %bitcast.153, bf16[1024,192]{1,0:T(8,128)(2,1)} %bitcast.150, bf16[1024,192]{1,0:T(8,128)(2,1)} %bitcast.151, bf16[256,192]{1,0:T(8,128)(2,1)} %pad.7.kt_ref, bf16[256,192]{1,0:T(8,128)(2,1)} %pad.8.vt_ref, f32[1,256]{1,0:T(1,128)} %compare_convert_fusion.valid_ref), custom_call_target="tpu_custom_call" | custom-call | tf_op jit(solution)/shard_map/pallas_call | solution.py:69
  61.3 4.8 %all-to-all-start.1 = ((bf16[32,16,192]{2,1,0:T(8,128)(2,1)}), bf16[32,16,192]{2,1,0:T(8,128)(2,1)}, u32[]{:S(2)}, u32[]{:S(2)}) async-start(bf16[32,16,192]{2,1,0:T(8,128)(2,1)} %bitcast.152), calls=%async_computation.1 | async-start | bytes 524288 | tf_op jit(solution)/shard_map/all_to_all | solution.py:169
  66.1 12.9 %all-to-all-done.1 = bf16[32,16,192]{2,1,0:T(8,128)(2,1)} async-done(((bf16[32,16,192]{2,1,0:T(8,128)(2,1)}), bf16[32,16,192]{2,1,0:T(8,128)(2,1)}, u32[]{:S(2)}, u32[]{:S(2)}) %all-to-all-start.1) | async-done | bytes 196640 | tf_op jit(solution)/shard_map/all_to_all | solution.py:169
  79.0 1.9 %copy.41 = bf16[2,16,8,2,192]{4,3,2,1,0:T(2,128)(2,1)} copy(bf16[2,16,8,2,192]{4,1,0,3,2:T(8,128)(2,1)} %bitcast.25) | data formatting | bytes 393216 | tf_op jit(solution)/shard_map/transpose | solution.py:178
  81.0 1.8 %reshape.426 = bf16[256,384]{1,0:T(8,128)(2,1)} reshape(bf16[2,16,8,2,192]{4,3,2,1,0:T(2,128)(2,1)} %copy.41) | data formatting | bytes 393216 | tf_op jit(solution)/shard_map/reshape | solution.py:179
  82.8 1.8 %convolution_convert_fusion.5 = bf16[64,1536]{1,0:T(8,128)(2,1)} fusion(bf16[384,1536]{1,0:T(8,128)(2,1)S(1)} %copy-done.1, bf16[256,384]{1,0:T(8,128)(2,1)} %reshape.426, s32[]{:T(128)S(6)} %select_n.96), kind=kOutput, calls=%fused_computation.7 | convolution fusion | flops 75595776 | bytes 1425412 | tf_op jit(solution)/shard_map/dot_general | solution.py:189
  84.6 3.0 %collective-permute-start.3 = (bf16[64,1536]{1,0:T(8,128)(2,1)}, bf16[64,1536]{1,0:T(8,128)(2,1)}, u32[]{:S(2)}, u32[]{:S(2)}) collective-permute-start(bf16[64,1536]{1,0:T(8,128)(2,1)} %convolution_convert_fusion.5), channel_id=1, source_target_pairs={{0,3},{1,0},{2,1},{3,2},{4,7},{5,4},{6,5},{7,6},{8,11},{9,8},{10,9... | collective-permute-start | bytes 589832 | tf_op jit(solution)/shard_map/ppermute | solution.py:77
  87.6 1.8 %convolution_convert_fusion.6 = bf16[64,1536]{1,0:T(8,128)(2,1)} fusion(bf16[384,1536]{1,0:T(8,128)(2,1)S(1)} %copy-done.1, bf16[256,384]{1,0:T(8,128)(2,1)} %reshape.426, s32[]{:T(128)S(6)} %select_n.94), kind=kOutput, calls=%fused_computation.8 | convolution fusion | flops 75595776 | bytes 1425412 | tf_op jit(solution)/shard_map/dot_general | solution.py:189
  89.4 0.6 collective-permute-start.2
  90.0 1.8 %convolution_convert_fusion.7 = bf16[64,1536]{1,0:T(8,128)(2,1)} fusion(bf16[384,1536]{1,0:T(8,128)(2,1)S(1)} %copy-done.1, bf16[256,384]{1,0:T(8,128)(2,1)} %reshape.426, s32[]{:T(128)S(6)} %select_n.92), kind=kOutput, calls=%fused_computation.9 | convolution fusion | flops 75595776 | bytes 1425412 | tf_op jit(solution)/shard_map/dot_general | solution.py:189
  91.9 1.0 collective-permute-start.1
  92.8 2.5 %convert_element_type.167 = f32[1,32,8,1536]{3,2,1,0:T(8,128)} convert(bf16[1,32,8,1536]{3,2,1,0:T(8,128)(2,1)} %param.13) | non-fusion elementwise | flops 393216 | bytes 2359296 | tf_op jit(solution)/shard_map/convert_element_type | solution.py:105
  95.4 3.4 %collective-permute-done.2 = bf16[64,1536]{1,0:T(8,128)(2,1)} collective-permute-done((bf16[64,1536]{1,0:T(8,128)(2,1)}, bf16[64,1536]{1,0:T(8,128)(2,1)}, u32[]{:S(2)}, u32[]{:S(2)}) %collective-permute-start.2) | collective-permute-done | bytes 196640 | tf_op jit(solution)/shard_map/ppermute | solution.py:77
  98.8 2.1 %collective-permute-done.1 = bf16[64,1536]{1,0:T(8,128)(2,1)} collective-permute-done((bf16[64,1536]{1,0:T(8,128)(2,1)}, bf16[64,1536]{1,0:T(8,128)(2,1)}, u32[]{:S(2)}, u32[]{:S(2)}) %collective-permute-start.1) | collective-permute-done | bytes 196640 | tf_op jit(solution)/shard_map/ppermute | solution.py:77
  100.9 1.7 %fusion.151 = (f32[8,8]{1,0:T(8,128)S(1)}, f32[8,8,1536]{2,1,0:T(8,128)S(1)}) fusion(bf16[384,1536]{1,0:T(8,128)(2,1)S(1)} %copy-done.1, bf16[256,384]{1,0:T(8,128)(2,1)} %reshape.426, s32[]{:T(128)S(6)} %select_n.98, bf16[64,1536]{1,0:T(8,128)(2,1)} %collective-permute-done.3, bf16[64,1536]{1,0:T(8,128)(2,1)} %collective-permute-done.2, ...), kind=kOutput, calls=%fused_computation.180 | convolution fusion | flops 76578752 | bytes 2654472 | tf_op jit(solution)/shard_map/dot_general | solution.py:189
  102.7 0.2 multiply_reduce_fusion.2
  102.9 0.5 copy-done.3
  103.5 0.6 collective-permute-start.8
  104.2 0.8 collective-permute-start.6
  105.0 1.1 collective-permute-start.4
  106.1 5.2 %collective-permute-done.8 = bf16[8,8,1536]{2,1,0:T(8,128)(2,1)S(1)} collective-permute-done((bf16[8,8,1536]{2,1,0:T(8,128)(2,1)S(1)}, bf16[8,8,1536]{2,1,0:T(8,128)(2,1)S(1)}, u32[]{:S(2)}, u32[]{:S(2)}) %collective-permute-start.8) | collective-permute-done | bytes 196640 | tf_op jit(solution)/shard_map/ppermute | solution.py:77
  111.4 2.8 %convolution_convert_fusion = bf16[64,1536]{1,0:T(8,128)(2,1)S(1)} fusion(bf16[768,1536]{1,0:T(8,128)(2,1)S(1)} %copy-done, bf16[1536,768]{1,0:T(8,128)(2,1)} %param.23, bf16[8,8,1536]{2,1,0:T(8,128)(2,1)S(1)} %collective-permute-done.8), kind=kOutput, calls=%fused_computation | convolution fusion | flops 302530560 | bytes 5111808 | tf_op jit(solution)/shard_map/dot_general | solution.py:209
  114.3 3.5 %convolution_convert_fusion.1 = bf16[64,1536]{1,0:T(8,128)(2,1)} fusion(bf16[768,1536]{1,0:T(8,128)(2,1)S(1)} %copy-done, bf16[1536,768]{1,0:T(8,128)(2,1)} %param.23, bf16[8,8,1536]{2,1,0:T(8,128)(2,1)S(1)} %collective-permute-done.6), kind=kOutput, calls=%fused_computation.1 | convolution fusion | flops 302530560 | bytes 5111808 | tf_op jit(solution)/shard_map/dot_general | solution.py:209
  117.7 2.5 %collective-permute-start.7 = (bf16[64,1536]{1,0:T(8,128)(2,1)}, bf16[64,1536]{1,0:T(8,128)(2,1)}, u32[]{:S(2)}, u32[]{:S(2)}) collective-permute-start(bf16[64,1536]{1,0:T(8,128)(2,1)} %convolution_convert_fusion.1), channel_id=1, source_target_pairs={{0,2},{1,3},{2,0},{3,1},{4,6},{5,7},{6,4},{7,5},{8,10},{9,11},{10,... | collective-permute-start | bytes 589832 | tf_op jit(solution)/shard_map/ppermute | solution.py:77
  120.2 3.5 %convolution_convert_fusion.2 = bf16[64,1536]{1,0:T(8,128)(2,1)} fusion(bf16[768,1536]{1,0:T(8,128)(2,1)S(1)} %copy-done, bf16[1536,768]{1,0:T(8,128)(2,1)} %param.23, bf16[8,8,1536]{2,1,0:T(8,128)(2,1)S(1)} %collective-permute-done.4), kind=kOutput, calls=%fused_computation.2 | convolution fusion | flops 302530560 | bytes 5111808 | tf_op jit(solution)/shard_map/dot_general | solution.py:209
  123.7 0.8 collective-permute-start.5
  124.4 2.8 %fusion = f32[64,1536]{1,0:T(8,128)S(1)} fusion(bf16[768,1536]{1,0:T(8,128)(2,1)S(1)} %copy-done, bf16[1536,768]{1,0:T(8,128)(2,1)} %param.23, bf16[8,8,1536]{2,1,0:T(8,128)(2,1)S(1)} %add_convert_fusion.2), kind=kOutput, calls=%fused_computation.4 | convolution fusion | flops 302628864 | bytes 5308416 | tf_op jit(solution)/shard_map/dot_general | solution.py:209
  127.3 2.3 %collective-permute-done.5 = bf16[64,1536]{1,0:T(8,128)(2,1)} collective-permute-done((bf16[64,1536]{1,0:T(8,128)(2,1)}, bf16[64,1536]{1,0:T(8,128)(2,1)}, u32[]{:S(2)}, u32[]{:S(2)}) %collective-permute-start.5) | collective-permute-done | bytes 196640 | tf_op jit(solution)/shard_map/ppermute | solution.py:77
  129.7 1.3 fusion.148
  131.0 0.2 multiply_reduce_fusion.1
  131.2 0.3 fusion.62
  131.5 0.8 collective-permute-start.10
  132.4 0.2 select_reduce_fusion
  132.6 4.4 %collective-permute-done.10 = f32[8,8,32]{2,1,0:T(8,128)S(1)} collective-permute-done((f32[8,8,32]{2,1,0:T(8,128)S(1)}, f32[8,8,32]{2,1,0:T(8,128)S(1)}, u32[]{:S(2)}, u32[]{:S(2)}) %collective-permute-start.10) | collective-permute-done | bytes 8224 | tf_op jit(solution)/shard_map/ppermute | solution.py:17
  137.0 0.7 multiply_add_fusion
  (60 shorter events, 1.1 us)
Async XLA Ops:
  0.6 110.7 %copy-start = (bf16[768,1536]{1,0:T(8,128)(2,1)S(1)}, bf16[768,1536]{1,0:T(8,128)(2,1)}, u32[]{:S(2)}) copy-start(bf16[768,1536]{1,0:T(8,128)(2,1)} %param.24) | copy-start | bytes 7077892
  0.6 1.9 %copy-start.2 = (bf16[1,32,8,1536]{3,2,1,0:T(8,128)(2,1)S(1)}, bf16[1,32,8,1536]{3,2,1,0:T(8,128)(2,1)}, u32[]{:S(2)}) copy-start(bf16[1,32,8,1536]{3,2,1,0:T(8,128)(2,1)} %param.13) | copy-start | bytes 2359300
  3.1 2.4 %copy-start.15 = (bf16[1536,3,384]{2,0,1:T(8,128)(2,1)S(1)}, bf16[1536,3,384]{2,0,1:T(8,128)(2,1)}, u32[]{:S(2)}) copy-start(bf16[1536,3,384]{2,0,1:T(8,128)(2,1)} %param.20) | copy-start | bytes 10616836
  6.1 1.7 %copy-start.5 = (bf16[1536,2,384]{2,1,0:T(2,128)(2,1)S(1)}, bf16[1536,2,384]{2,1,0:T(2,128)(2,1)}, u32[]{:S(2)}) copy-start(bf16[1536,2,384]{2,1,0:T(2,128)(2,1)} %param.21) | copy-start | bytes 7077892
  7.7 0.9 copy-start.6
  46.9 1.0 copy-start.16
  47.9 2.6 %collective-permute-start = (bf16[32,37,192]{2,0,1:T(8,128)(2,1)}, bf16[32,37,192]{2,0,1:T(8,128)(2,1)}, u32[]{:S(2)}, u32[]{:S(2)}) collective-permute-start(bf16[32,37,192]{2,0,1:T(8,128)(2,1)} %copy.38), channel_id=1, source_target_pairs={{0,4},{4,0},{8,12},{12,8},{16,20},{20,16},{24,28},{28,24},{32,36},... | collective-permute-start | bytes 1363976 | tf_op jit(solution)/shard_map/ppermute | solution.py:17
  55.2 27.6 %copy-start.1 = (bf16[384,1536]{1,0:T(8,128)(2,1)S(1)}, bf16[384,1536]{1,0:T(8,128)(2,1)}, u32[]{:S(2)}) copy-start(bf16[384,1536]{1,0:T(8,128)(2,1)} %param.22) | copy-start | bytes 3538948
  61.3 17.7 %all-to-all-start.1 = ((bf16[32,16,192]{2,1,0:T(8,128)(2,1)}), bf16[32,16,192]{2,1,0:T(8,128)(2,1)}, u32[]{:S(2)}, u32[]{:S(2)}) async-start(bf16[32,16,192]{2,1,0:T(8,128)(2,1)} %bitcast.152), calls=%async_computation.1 | async-start | bytes 524288 | tf_op jit(solution)/shard_map/all_to_all | solution.py:169
  84.6 10.8 %collective-permute-start.3 = (bf16[64,1536]{1,0:T(8,128)(2,1)}, bf16[64,1536]{1,0:T(8,128)(2,1)}, u32[]{:S(2)}, u32[]{:S(2)}) collective-permute-start(bf16[64,1536]{1,0:T(8,128)(2,1)} %convolution_convert_fusion.5), channel_id=1, source_target_pairs={{0,3},{1,0},{2,1},{3,2},{4,7},{5,4},{6,5},{7,6},{8,11},{9,8},{10,9... | collective-permute-start | bytes 589832 | tf_op jit(solution)/shard_map/ppermute | solution.py:77
  89.4 9.4 %collective-permute-start.2 = (bf16[64,1536]{1,0:T(8,128)(2,1)}, bf16[64,1536]{1,0:T(8,128)(2,1)}, u32[]{:S(2)}, u32[]{:S(2)}) collective-permute-start(bf16[64,1536]{1,0:T(8,128)(2,1)} %convolution_convert_fusion.6), channel_id=1, source_target_pairs={{0,2},{1,3},{2,0},{3,1},{4,6},{5,7},{6,4},{7,5},{8,10},{9,11},{10,... | collective-permute-start | bytes 589832 | tf_op jit(solution)/shard_map/ppermute | solution.py:77
  91.9 9.0 %collective-permute-start.1 = (bf16[64,1536]{1,0:T(8,128)(2,1)}, bf16[64,1536]{1,0:T(8,128)(2,1)}, u32[]{:S(2)}, u32[]{:S(2)}) collective-permute-start(bf16[64,1536]{1,0:T(8,128)(2,1)} %convolution_convert_fusion.7), channel_id=1, source_target_pairs={{0,1},{1,2},{2,3},{3,0},{4,5},{5,6},{6,7},{7,4},{8,9},{9,10},{10,1... | collective-permute-start | bytes 589832 | tf_op jit(solution)/shard_map/ppermute | solution.py:77
  95.3 8.1 %copy-start.10 = (f32[8,1536]{1,0:T(8,128)S(1)}, f32[8,1536]{1,0:T(8,128)}, u32[]{:S(2)}) copy-start(f32[8,1536]{1,0:T(8,128)} %get-tuple-element.12) | copy-start | bytes 147460
  95.3 8.1 %copy-start.11 = (f32[8,1536]{1,0:T(8,128)S(1)}, f32[8,1536]{1,0:T(8,128)}, u32[]{:S(2)}) copy-start(f32[8,1536]{1,0:T(8,128)} %get-tuple-element.13) | copy-start | bytes 147460
  100.9 3.3 %copy-start.13 = (s32[8]{0:T(128)S(1)}, s32[8]{0:T(128)}, u32[]{:S(2)}) copy-start(s32[8]{0:T(128)} %param.17) | copy-start | bytes 100
  102.7 0.7 copy-start.3
  103.5 7.8 %collective-permute-start.8 = (bf16[8,8,1536]{2,1,0:T(8,128)(2,1)S(1)}, bf16[8,8,1536]{2,1,0:T(8,128)(2,1)S(1)}, u32[]{:S(2)}, u32[]{:S(2)}) collective-permute-start(bf16[8,8,1536]{2,1,0:T(8,128)(2,1)S(1)} %add_convert_fusion.2), channel_id=1, source_target_pairs={{0,3},{1,0},{2,1},{3,2},{4,7},{5,4},{6,5},{7,6},{8,11},{9,8},{10,9... | collective-permute-start | bytes 589832 | tf_op jit(solution)/shard_map/ppermute | solution.py:77
  104.2 10.1 %collective-permute-start.6 = (bf16[8,8,1536]{2,1,0:T(8,128)(2,1)S(1)}, bf16[8,8,1536]{2,1,0:T(8,128)(2,1)S(1)}, u32[]{:S(2)}, u32[]{:S(2)}) collective-permute-start(bf16[8,8,1536]{2,1,0:T(8,128)(2,1)S(1)} %add_convert_fusion.2), channel_id=1, source_target_pairs={{0,2},{1,3},{2,0},{3,1},{4,6},{5,7},{6,4},{7,5},{8,10},{9,11},{10,... | collective-permute-start | bytes 589832 | tf_op jit(solution)/shard_map/ppermute | solution.py:77
  105.0 15.2 %collective-permute-start.4 = (bf16[8,8,1536]{2,1,0:T(8,128)(2,1)S(1)}, bf16[8,8,1536]{2,1,0:T(8,128)(2,1)S(1)}, u32[]{:S(2)}, u32[]{:S(2)}) collective-permute-start(bf16[8,8,1536]{2,1,0:T(8,128)(2,1)S(1)} %add_convert_fusion.2), channel_id=1, source_target_pairs={{0,1},{1,2},{2,3},{3,0},{4,5},{5,6},{6,7},{7,4},{8,9},{9,10},{10,1... | collective-permute-start | bytes 589832 | tf_op jit(solution)/shard_map/ppermute | solution.py:77
  114.2 13.1 %collective-permute-start.9 = (bf16[64,1536]{1,0:T(8,128)(2,1)S(1)}, bf16[64,1536]{1,0:T(8,128)(2,1)}, u32[]{:S(2)}, u32[]{:S(2)}) collective-permute-start(bf16[64,1536]{1,0:T(8,128)(2,1)S(1)} %convolution_convert_fusion), channel_id=1, source_target_pairs={{0,1},{1,2},{2,3},{3,0},{4,5},{5,6},{6,7},{7,4},{8,9},{9,10},{10,1... | collective-permute-start | bytes 589832 | tf_op jit(solution)/shard_map/ppermute | solution.py:77
  117.7 9.6 %collective-permute-start.7 = (bf16[64,1536]{1,0:T(8,128)(2,1)}, bf16[64,1536]{1,0:T(8,128)(2,1)}, u32[]{:S(2)}, u32[]{:S(2)}) collective-permute-start(bf16[64,1536]{1,0:T(8,128)(2,1)} %convolution_convert_fusion.1), channel_id=1, source_target_pairs={{0,2},{1,3},{2,0},{3,1},{4,6},{5,7},{6,4},{7,5},{8,10},{9,11},{10,... | collective-permute-start | bytes 589832 | tf_op jit(solution)/shard_map/ppermute | solution.py:77
  123.7 6.0 %copy-start.4 = (f32[8,8,1536]{2,1,0:T(8,128)S(1)}, f32[8,8,1536]{2,1,0:T(8,128)}, u32[]{:S(2)}) copy-start(f32[8,8,1536]{2,1,0:T(8,128)} %copy-done.3) | copy-start | bytes 1179652
  123.7 6.0 %collective-permute-start.5 = (bf16[64,1536]{1,0:T(8,128)(2,1)}, bf16[64,1536]{1,0:T(8,128)(2,1)}, u32[]{:S(2)}, u32[]{:S(2)}) collective-permute-start(bf16[64,1536]{1,0:T(8,128)(2,1)} %convolution_convert_fusion.2), channel_id=1, source_target_pairs={{0,3},{1,0},{2,1},{3,2},{4,7},{5,4},{6,5},{7,6},{8,11},{9,8},{10,9... | collective-permute-start | bytes 589832 | tf_op jit(solution)/shard_map/ppermute | solution.py:77
  127.2 3.9 %copy-start.7 = (bf16[1536,64]{0,1:T(8,128)(2,1)S(1)}, bf16[1536,64]{0,1:T(8,128)(2,1)}, u32[]{:S(2)}) copy-start(bf16[1536,64]{0,1:T(8,128)(2,1)} %param.25) | copy-start | bytes 589828
  127.3 3.9 %copy-start.8 = (f32[8,1536]{1,0:T(8,128)S(1)}, f32[8,1536]{1,0:T(8,128)}, u32[]{:S(2)}) copy-start(f32[8,1536]{1,0:T(8,128)} %get-tuple-element.10) | copy-start | bytes 147460
  127.3 3.9 %copy-start.9 = (f32[8,1536]{1,0:T(8,128)S(1)}, f32[8,1536]{1,0:T(8,128)}, u32[]{:S(2)}) copy-start(f32[8,1536]{1,0:T(8,128)} %get-tuple-element.11) | copy-start | bytes 147460
  127.3 5.1 %copy-start.14 = (f32[9]{0:T(128)S(1)}, f32[9]{0:T(128)}, u32[]{:S(2)}) copy-start(f32[9]{0:T(128)} %param.18) | copy-start | bytes 112
  127.3 9.7 %copy-start.12 = (f32[8,8,32]{2,1,0:T(8,128)S(1)}, f32[8,8,32]{2,1,0:T(8,128)}, u32[]{:S(2)}) copy-start(f32[8,8,32]{2,1,0:T(8,128)} %param.19) | copy-start | bytes 24580
  131.5 5.5 %collective-permute-start.10 = (f32[8,8,32]{2,1,0:T(8,128)S(1)}, f32[8,8,32]{2,1,0:T(8,128)S(1)}, u32[]{:S(2)}, u32[]{:S(2)}) collective-permute-start(f32[8,8,32]{2,1,0:T(8,128)S(1)} %constant_dynamic-slice_fusion), channel_id=1, source_target_pairs={{0,128},{128,0},{1,129},{129,1},{2,130},{130,2},{3,131},{131,3},{4... | collective-permute-start | bytes 24584 | tf_op jit(solution)/shard_map/ppermute | solution.py:17

commit v16 on v13

--- a/solution.py
+++ b/solution.py
@@ -215,14 +215,18 @@
     head_in = modulate(after_mlp, adaptive[:, 8], adaptive[:, 9]).reshape(
         portion * requests, model_width
     )
-    velocity_own = jnp.dot(head_in, w_final, preferred_element_type=jnp.float32).reshape(
-        portion, requests, w_final.shape[1]
-    )
     half_width = w_final.shape[1] // 2
     cfg_index = lax.axis_index("cfg")
-    own_kept = lax.dynamic_slice_in_dim(velocity_own, cfg_index * half_width, half_width, 2)
-    own_given = lax.dynamic_slice_in_dim(velocity_own, (1 - cfg_index) * half_width, half_width, 2)
+
+    def head_columns(start):
+        columns = lax.dynamic_slice_in_dim(w_final, start * half_width, half_width, 1)
+        return jnp.dot(head_in, columns, preferred_element_type=jnp.float32).reshape(
+            portion, requests, half_width
+        )
+
+    own_given = head_columns(1 - cfg_index)
     velocity_other = swapped(own_given, "cfg", 0)
+    own_kept = head_columns(cfg_index)
     is_first = cfg_index == 0
     guided_cond = jnp.where(is_first, own_kept, velocity_other)
     guided_free = jnp.where(is_first, velocity_other, own_kept)

time: 139 us -> 140 us (level)
  matrix products: 23.9 us -> 25.7 us
    dot_general x1 -> x2, matrix products: 0.26 us -> 2.1 us  [head_columns(): jnp.dot(head_in, columns, preferred_element_type=jnp.float32)]
    unnamed x35 -> x33, local copies, waits for them, and re-layouts: 2.82 us -> 2.82 us
where the time goes in v16:
time: 140 us; the launch traced here: 139 us
  blocking collectives  35.2 us (25%)
  waiting for transfers between devices  30.5 us (22%)
  matrix products  25.7 us (18%)
  starting transfers between devices  16.1 us (12%)
  local copies, waits for them, and re-layouts  12.5 us (9%)
  other arithmetic  11.1 us (8%)
  Pallas kernels  6.08 us (4%)
  between operations  1.66 us (1%)
    all_to_all x1, blocking collectives, shards(): lax.all_to_all(payload, 'seq', split_axis=0, concat_axis=0, tiled=True)  35.2 us
    ppermute x9, waiting for transfers between devices, shifted(): lax.ppermute(value, axis, [(i, (i + step) % size) for i in range(size)])  13.2 us
    all_to_all x1, waiting for transfers between devices, shards(): lax.all_to_all(answer.reshape(senders, query_share, head_share), 'seq', s...  12.9 us
    dot_general x4, matrix products, shards(): jnp.dot(hidden, w_down, preferred_element_type=jnp.float32)  12.5 us
    ppermute x9, starting transfers between devices, shifted(): lax.ppermute(value, axis, [(i, (i + step) % size) for i in range(size)])  10.5 us
    dot_general x4, matrix products, shards(): jnp.dot(rows_for, w_out, preferred_element_type=jnp.float32)  7.18 us
    pallas_call x1, Pallas kernels, attend_kernel(): pl.pallas_call(attention_kernel, out_shape=jax.ShapeDtypeStruct(queries.s...  6.08 us
    all_to_all x1, starting transfers between devices, shards(): lax.all_to_all(answer.reshape(senders, query_share, head_share), 'seq', s...  4.77 us
  transfers between devices with their start and end apart: 12, of which 7 were waited for; matrix products, arithmetic and copies ran while one was open for 15% of the time, Pallas kernels for 0%

profile of v16, /device:TPU:4, one launch (start us, length us, event | category | flops | bytes accessed | tf_op | source)
XLA Modules:
  0.0 138.8 jit_solution(15574595463465852252)
XLA Ops:
  0.7 1.1 bitcast_convert_fusion
  1.8 0.7 fusion.114
  2.5 0.2 convert_reduce_fusion
  2.7 0.3 multiply_reduce_fusion
  3.1 2.0 %fusion.17 = bf16[256,384]{1,0:T(8,128)(2,1)S(1)} fusion(bf16[1536,3,384]{2,0,1:T(8,128)(2,1)} %param.20, bf16[1,32,8,1536]{3,2,1,0:T(8,128)(2,1)S(1)} %copy-done.2, f32[8,1536]{1,0:T(8,128)S(1)} %get-tuple-element.15, f32[8,1536]{1,0:T(8,128)S(1)} %get-tuple-element.16, f32[32,8]{1,0:T(8,128)S(1)} %add_rsqrt_fusion, f32[32,8]{1,0:T(8,128)S(1)} %broadcast_multiply_fusion), kind=kOutput, calls=%fused_computation.25 | convolution fusion | flops 304447488 | bytes 2263040 | tf_op jit(solution)/shard_map/dot_general | solution.py:109
  5.2 0.3 copy-done.14
  5.4 0.6 fusion.14
  6.1 0.6 fusion.11
  6.7 1.0 copy-done.5
  7.7 0.5 copy.42
  8.2 0.4 copy-done.6
  8.8 0.2 fusion.26
  8.9 0.6 convolution_convert_fusion.8
  9.6 0.2 concatenate.22
  9.9 0.2 concatenate.19
  10.1 1.0 maximum_bitcast_fusion
  11.1 0.2 copy.37
  11.3 0.2 reshape_reshape.3
  11.6 0.2 pad_maximum_fusion
  11.8 35.2 %all_to_all.10 = bf16[32,53,192]{2,1,0:T(8,128)(2,1)S(1)} all-to-all(bf16[32,53,192]{2,1,0:T(8,128)(2,1)S(1)} %pad_maximum_fusion), channel_id=1, replica_groups=mesh['cfg'=2,'seq'=32,'tp'=4] {'seq'}, dimensions={0} | all-to-all | bytes 1302528 | tf_op jit(solution)/shard_map/all_to_all | solution.py:140
  47.0 1.0 copy.38
  48.0 0.6 fusion.132
  49.2 0.6 compare_convert_fusion.valid_ref
  49.8 0.7 slice.91
  50.5 1.4 %broadcast_select_fusion = (bf16[32,37,192]{2,1,0:T(8,128)(2,1)S(1)}, bf16[32,37,192]{2,1,0:T(8,128)(2,1)S(1)}) fusion(pred[]{:T(512)S(6)} %eq.45, bf16[32,37,192]{2,0,1:T(8,128)(2,1)} %collective-permute-done, bf16[32,53,192]{2,1,0:T(8,128)(2,1)S(1)} %all_to_all.10), kind=kLoop, calls=%fused_computation.29 | loop fusion | flops 454656 | bytes 1818625 | tf_op jit(solution)/shard_map/jit(_where)/select_n | solution.py:146
  52.0 0.9 slice.93
  52.9 0.9 slice.94
  53.9 0.7 pad.7.kt_ref
  54.5 0.7 pad.8.vt_ref
  55.2 6.1 %shard_map.140 = bf16[512,192]{1,0:T(8,128)(2,1)} custom-call(bf16[512,192]{1,0:T(8,128)(2,1)} %bitcast.160, bf16[1024,192]{1,0:T(8,128)(2,1)} %bitcast.157, bf16[1024,192]{1,0:T(8,128)(2,1)} %bitcast.158, bf16[256,192]{1,0:T(8,128)(2,1)} %pad.7.kt_ref, bf16[256,192]{1,0:T(8,128)(2,1)} %pad.8.vt_ref, f32[1,256]{1,0:T(1,128)} %compare_convert_fusion.valid_ref), custom_call_target="tpu_custom_call" | custom-call | tf_op jit(solution)/shard_map/pallas_call | solution.py:69
  61.3 4.8 %all-to-all-start.1 = ((bf16[32,16,192]{2,1,0:T(8,128)(2,1)}), bf16[32,16,192]{2,1,0:T(8,128)(2,1)}, u32[]{:S(2)}, u32[]{:S(2)}) async-start(bf16[32,16,192]{2,1,0:T(8,128)(2,1)} %bitcast.159), calls=%async_computation.1 | async-start | bytes 524288 | tf_op jit(solution)/shard_map/all_to_all | solution.py:169
  66.1 12.9 %all-to-all-done.1 = bf16[32,16,192]{2,1,0:T(8,128)(2,1)} async-done(((bf16[32,16,192]{2,1,0:T(8,128)(2,1)}), bf16[32,16,192]{2,1,0:T(8,128)(2,1)}, u32[]{:S(2)}, u32[]{:S(2)}) %all-to-all-start.1) | async-done | bytes 196640 | tf_op jit(solution)/shard_map/all_to_all | solution.py:169
  79.0 1.9 %copy.41 = bf16[2,16,8,2,192]{4,3,2,1,0:T(2,128)(2,1)} copy(bf16[2,16,8,2,192]{4,1,0,3,2:T(8,128)(2,1)} %bitcast.25) | data formatting | bytes 393216 | tf_op jit(solution)/shard_map/transpose | solution.py:178
  80.9 1.8 %reshape.429 = bf16[256,384]{1,0:T(8,128)(2,1)} reshape(bf16[2,16,8,2,192]{4,3,2,1,0:T(2,128)(2,1)} %copy.41) | data formatting | bytes 393216 | tf_op jit(solution)/shard_map/reshape | solution.py:179
  82.7 1.8 %convolution_convert_fusion.4 = bf16[64,1536]{1,0:T(8,128)(2,1)} fusion(bf16[384,1536]{1,0:T(8,128)(2,1)S(1)} %copy-done.1, bf16[256,384]{1,0:T(8,128)(2,1)} %reshape.429, s32[]{:T(128)S(6)} %select_n.98), kind=kOutput, calls=%fused_computation.5 | convolution fusion | flops 75595776 | bytes 1425412 | tf_op jit(solution)/shard_map/dot_general | solution.py:189
  84.5 3.0 %collective-permute-start.3 = (bf16[64,1536]{1,0:T(8,128)(2,1)}, bf16[64,1536]{1,0:T(8,128)(2,1)}, u32[]{:S(2)}, u32[]{:S(2)}) collective-permute-start(bf16[64,1536]{1,0:T(8,128)(2,1)} %convolution_convert_fusion.4), channel_id=1, source_target_pairs={{0,3},{1,0},{2,1},{3,2},{4,7},{5,4},{6,5},{7,6},{8,11},{9,8},{10,9... | collective-permute-start | bytes 589832 | tf_op jit(solution)/shard_map/ppermute | solution.py:77
  87.6 1.8 %convolution_convert_fusion.5 = bf16[64,1536]{1,0:T(8,128)(2,1)} fusion(bf16[384,1536]{1,0:T(8,128)(2,1)S(1)} %copy-done.1, bf16[256,384]{1,0:T(8,128)(2,1)} %reshape.429, s32[]{:T(128)S(6)} %select_n.96), kind=kOutput, calls=%fused_computation.6 | convolution fusion | flops 75595776 | bytes 1425412 | tf_op jit(solution)/shard_map/dot_general | solution.py:189
  89.4 0.6 collective-permute-start.2
  90.0 1.8 %convolution_convert_fusion.6 = bf16[64,1536]{1,0:T(8,128)(2,1)} fusion(bf16[384,1536]{1,0:T(8,128)(2,1)S(1)} %copy-done.1, bf16[256,384]{1,0:T(8,128)(2,1)} %reshape.429, s32[]{:T(128)S(6)} %select_n.94), kind=kOutput, calls=%fused_computation.7 | convolution fusion | flops 75595776 | bytes 1425412 | tf_op jit(solution)/shard_map/dot_general | solution.py:189
  91.8 1.0 collective-permute-start.1
  92.7 2.5 %convert_element_type.167 = f32[1,32,8,1536]{3,2,1,0:T(8,128)} convert(bf16[1,32,8,1536]{3,2,1,0:T(8,128)(2,1)} %param.13) | non-fusion elementwise | flops 393216 | bytes 2359296 | tf_op jit(solution)/shard_map/convert_element_type | solution.py:105
  95.3 3.4 %collective-permute-done.2 = bf16[64,1536]{1,0:T(8,128)(2,1)} collective-permute-done((bf16[64,1536]{1,0:T(8,128)(2,1)}, bf16[64,1536]{1,0:T(8,128)(2,1)}, u32[]{:S(2)}, u32[]{:S(2)}) %collective-permute-start.2) | collective-permute-done | bytes 196640 | tf_op jit(solution)/shard_map/ppermute | solution.py:77
  98.7 2.1 %collective-permute-done.1 = bf16[64,1536]{1,0:T(8,128)(2,1)} collective-permute-done((bf16[64,1536]{1,0:T(8,128)(2,1)}, bf16[64,1536]{1,0:T(8,128)(2,1)}, u32[]{:S(2)}, u32[]{:S(2)}) %collective-permute-start.1) | collective-permute-done | bytes 196640 | tf_op jit(solution)/shard_map/ppermute | solution.py:77
  100.8 1.8 %fusion.155 = (f32[8,8]{1,0:T(8,128)S(1)}, f32[8,8,1536]{2,1,0:T(8,128)S(1)}) fusion(bf16[64,1536]{1,0:T(8,128)(2,1)} %collective-permute-done.3, bf16[64,1536]{1,0:T(8,128)(2,1)} %collective-permute-done.2, bf16[64,1536]{1,0:T(8,128)(2,1)} %collective-permute-done.1, bf16[384,1536]{1,0:T(8,128)(2,1)S(1)} %copy-done.1, bf16[256,384]{1,0:T(8,128)(2,1)} %reshape.429, ...), kind=kOutput, calls=%fused_computation.181 | convolution fusion | flops 76578752 | bytes 2654472 | tf_op jit(solution)/shard_map/dot_general | solution.py:189
  102.6 0.2 multiply_reduce_fusion.2
  102.8 0.5 copy-done.3
  103.5 0.6 collective-permute-start.8
  104.1 0.9 collective-permute-start.6
  105.0 1.1 collective-permute-start.4
  106.1 5.2 %collective-permute-done.8 = bf16[8,8,1536]{2,1,0:T(8,128)(2,1)S(1)} collective-permute-done((bf16[8,8,1536]{2,1,0:T(8,128)(2,1)S(1)}, bf16[8,8,1536]{2,1,0:T(8,128)(2,1)S(1)}, u32[]{:S(2)}, u32[]{:S(2)}) %collective-permute-start.8) | collective-permute-done | bytes 196640 | tf_op jit(solution)/shard_map/ppermute | solution.py:77
  111.3 2.8 %convolution_convert_fusion = bf16[64,1536]{1,0:T(8,128)(2,1)S(1)} fusion(bf16[768,1536]{1,0:T(8,128)(2,1)S(1)} %copy-done, bf16[1536,768]{1,0:T(8,128)(2,1)} %param.23, bf16[8,8,1536]{2,1,0:T(8,128)(2,1)S(1)} %collective-permute-done.8), kind=kOutput, calls=%fused_computation | convolution fusion | flops 302530560 | bytes 5111808 | tf_op jit(solution)/shard_map/dot_general | solution.py:209
  114.2 3.5 %convolution_convert_fusion.1 = bf16[64,1536]{1,0:T(8,128)(2,1)} fusion(bf16[768,1536]{1,0:T(8,128)(2,1)S(1)} %copy-done, bf16[1536,768]{1,0:T(8,128)(2,1)} %param.23, bf16[8,8,1536]{2,1,0:T(8,128)(2,1)S(1)} %collective-permute-done.6), kind=kOutput, calls=%fused_computation.1 | convolution fusion | flops 302530560 | bytes 5111808 | tf_op jit(solution)/shard_map/dot_general | solution.py:209
  117.7 2.5 %collective-permute-start.7 = (bf16[64,1536]{1,0:T(8,128)(2,1)}, bf16[64,1536]{1,0:T(8,128)(2,1)}, u32[]{:S(2)}, u32[]{:S(2)}) collective-permute-start(bf16[64,1536]{1,0:T(8,128)(2,1)} %convolution_convert_fusion.1), channel_id=1, source_target_pairs={{0,2},{1,3},{2,0},{3,1},{4,6},{5,7},{6,4},{7,5},{8,10},{9,11},{10,... | collective-permute-start | bytes 589832 | tf_op jit(solution)/shard_map/ppermute | solution.py:77
  120.2 3.5 %convolution_convert_fusion.2 = bf16[64,1536]{1,0:T(8,128)(2,1)} fusion(bf16[768,1536]{1,0:T(8,128)(2,1)S(1)} %copy-done, bf16[1536,768]{1,0:T(8,128)(2,1)} %param.23, bf16[8,8,1536]{2,1,0:T(8,128)(2,1)S(1)} %collective-permute-done.4), kind=kOutput, calls=%fused_computation.2 | convolution fusion | flops 302530560 | bytes 5111808 | tf_op jit(solution)/shard_map/dot_general | solution.py:209
  123.6 0.8 collective-permute-start.5
  124.4 2.8 %fusion = f32[64,1536]{1,0:T(8,128)S(1)} fusion(bf16[768,1536]{1,0:T(8,128)(2,1)S(1)} %copy-done, bf16[1536,768]{1,0:T(8,128)(2,1)} %param.23, bf16[8,8,1536]{2,1,0:T(8,128)(2,1)S(1)} %add_convert_fusion.2), kind=kOutput, calls=%fused_computation.4 | convolution fusion | flops 302628864 | bytes 5308416 | tf_op jit(solution)/shard_map/dot_general | solution.py:209
  127.2 2.4 %collective-permute-done.5 = bf16[64,1536]{1,0:T(8,128)(2,1)} collective-permute-done((bf16[64,1536]{1,0:T(8,128)(2,1)}, bf16[64,1536]{1,0:T(8,128)(2,1)}, u32[]{:S(2)}, u32[]{:S(2)}) %collective-permute-start.5) | collective-permute-done | bytes 196640 | tf_op jit(solution)/shard_map/ppermute | solution.py:77
  129.6 1.3 fusion.152
  130.9 0.2 multiply_reduce_fusion.1
  131.1 0.3 fusion.94
  131.4 0.9 collective-permute-start.10
  132.3 0.2 select_reduce_fusion
  132.5 4.4 %collective-permute-done.10 = f32[8,8,32]{2,1,0:T(8,128)S(1)} collective-permute-done((f32[8,8,32]{2,1,0:T(8,128)S(1)}, f32[8,8,32]{2,1,0:T(8,128)S(1)}, u32[]{:S(2)}, u32[]{:S(2)}) %collective-permute-start.10) | collective-permute-done | bytes 8224 | tf_op jit(solution)/shard_map/ppermute | solution.py:17
  136.9 1.8 %multiply_add_fusion = (f32[8,8,32]{2,1,0:T(8,128)}, f32[8,8,32]{2,1,0:T(8,128)}) fusion(f32[8,8,32]{2,1,0:T(8,128)} %param.19, f32[8]{0:T(128)S(1)} %sub.84, f32[8,8,32]{2,1,0:T(8,128)S(1)} %collective-permute-done.10, bf16[1536,64]{0,1:T(8,128)(2,1)} %param.25, s32[]{:T(128)S(6)} %select_n.100, f32[8,8,1536]{2,1,0:T(8,128)S(1)} %get-tuple-element.5, ...), kind=kOutput, calls=%fused_computation.139 | convolution fusion | flops 6797312 | bytes 647717 | tf_op jit(solution)/shard_map/dot_general | solution.py:223
  (57 shorter events, 1.0 us)
Async XLA Ops:
  0.6 110.7 %copy-start = (bf16[768,1536]{1,0:T(8,128)(2,1)S(1)}, bf16[768,1536]{1,0:T(8,128)(2,1)}, u32[]{:S(2)}) copy-start(bf16[768,1536]{1,0:T(8,128)(2,1)} %param.24) | copy-start | bytes 7077892
  0.6 1.9 %copy-start.2 = (bf16[1,32,8,1536]{3,2,1,0:T(8,128)(2,1)S(1)}, bf16[1,32,8,1536]{3,2,1,0:T(8,128)(2,1)}, u32[]{:S(2)}) copy-start(bf16[1,32,8,1536]{3,2,1,0:T(8,128)(2,1)} %param.13) | copy-start | bytes 2359300
  3.1 2.4 %copy-start.14 = (bf16[1536,3,384]{2,0,1:T(8,128)(2,1)S(1)}, bf16[1536,3,384]{2,0,1:T(8,128)(2,1)}, u32[]{:S(2)}) copy-start(bf16[1536,3,384]{2,0,1:T(8,128)(2,1)} %param.20) | copy-start | bytes 10616836
  6.1 1.7 %copy-start.5 = (bf16[1536,2,384]{2,1,0:T(2,128)(2,1)S(1)}, bf16[1536,2,384]{2,1,0:T(2,128)(2,1)}, u32[]{:S(2)}) copy-start(bf16[1536,2,384]{2,1,0:T(2,128)(2,1)} %param.21) | copy-start | bytes 7077892
  7.7 0.9 copy-start.6
  46.9 1.0 copy-start.15
  48.0 2.6 %collective-permute-start = (bf16[32,37,192]{2,0,1:T(8,128)(2,1)}, bf16[32,37,192]{2,0,1:T(8,128)(2,1)}, u32[]{:S(2)}, u32[]{:S(2)}) collective-permute-start(bf16[32,37,192]{2,0,1:T(8,128)(2,1)} %copy.38), channel_id=1, source_target_pairs={{0,4},{4,0},{8,12},{12,8},{16,20},{20,16},{24,28},{28,24},{32,36},... | collective-permute-start | bytes 1363976 | tf_op jit(solution)/shard_map/ppermute | solution.py:17
  55.2 27.5 %copy-start.1 = (bf16[384,1536]{1,0:T(8,128)(2,1)S(1)}, bf16[384,1536]{1,0:T(8,128)(2,1)}, u32[]{:S(2)}) copy-start(bf16[384,1536]{1,0:T(8,128)(2,1)} %param.22) | copy-start | bytes 3538948
  61.3 17.7 %all-to-all-start.1 = ((bf16[32,16,192]{2,1,0:T(8,128)(2,1)}), bf16[32,16,192]{2,1,0:T(8,128)(2,1)}, u32[]{:S(2)}, u32[]{:S(2)}) async-start(bf16[32,16,192]{2,1,0:T(8,128)(2,1)} %bitcast.159), calls=%async_computation.1 | async-start | bytes 524288 | tf_op jit(solution)/shard_map/all_to_all | solution.py:169
  84.5 10.8 %collective-permute-start.3 = (bf16[64,1536]{1,0:T(8,128)(2,1)}, bf16[64,1536]{1,0:T(8,128)(2,1)}, u32[]{:S(2)}, u32[]{:S(2)}) collective-permute-start(bf16[64,1536]{1,0:T(8,128)(2,1)} %convolution_convert_fusion.4), channel_id=1, source_target_pairs={{0,3},{1,0},{2,1},{3,2},{4,7},{5,4},{6,5},{7,6},{8,11},{9,8},{10,9... | collective-permute-start | bytes 589832 | tf_op jit(solution)/shard_map/ppermute | solution.py:77
  89.4 9.4 %collective-permute-start.2 = (bf16[64,1536]{1,0:T(8,128)(2,1)}, bf16[64,1536]{1,0:T(8,128)(2,1)}, u32[]{:S(2)}, u32[]{:S(2)}) collective-permute-start(bf16[64,1536]{1,0:T(8,128)(2,1)} %convolution_convert_fusion.5), channel_id=1, source_target_pairs={{0,2},{1,3},{2,0},{3,1},{4,6},{5,7},{6,4},{7,5},{8,10},{9,11},{10,... | collective-permute-start | bytes 589832 | tf_op jit(solution)/shard_map/ppermute | solution.py:77
  91.8 9.0 %collective-permute-start.1 = (bf16[64,1536]{1,0:T(8,128)(2,1)}, bf16[64,1536]{1,0:T(8,128)(2,1)}, u32[]{:S(2)}, u32[]{:S(2)}) collective-permute-start(bf16[64,1536]{1,0:T(8,128)(2,1)} %convolution_convert_fusion.6), channel_id=1, source_target_pairs={{0,1},{1,2},{2,3},{3,0},{4,5},{5,6},{6,7},{7,4},{8,9},{9,10},{10,1... | collective-permute-start | bytes 589832 | tf_op jit(solution)/shard_map/ppermute | solution.py:77
  95.2 8.1 %copy-start.10 = (f32[8,1536]{1,0:T(8,128)S(1)}, f32[8,1536]{1,0:T(8,128)}, u32[]{:S(2)}) copy-start(f32[8,1536]{1,0:T(8,128)} %get-tuple-element.10) | copy-start | bytes 147460
  95.2 8.1 %copy-start.11 = (f32[8,1536]{1,0:T(8,128)S(1)}, f32[8,1536]{1,0:T(8,128)}, u32[]{:S(2)}) copy-start(f32[8,1536]{1,0:T(8,128)} %get-tuple-element.11) | copy-start | bytes 147460
  100.8 3.3 %copy-start.12 = (s32[8]{0:T(128)S(1)}, s32[8]{0:T(128)}, u32[]{:S(2)}) copy-start(s32[8]{0:T(128)} %param.17) | copy-start | bytes 100
  102.6 0.8 copy-start.3
  103.5 7.8 %collective-permute-start.8 = (bf16[8,8,1536]{2,1,0:T(8,128)(2,1)S(1)}, bf16[8,8,1536]{2,1,0:T(8,128)(2,1)S(1)}, u32[]{:S(2)}, u32[]{:S(2)}) collective-permute-start(bf16[8,8,1536]{2,1,0:T(8,128)(2,1)S(1)} %add_convert_fusion.2), channel_id=1, source_target_pairs={{0,3},{1,0},{2,1},{3,2},{4,7},{5,4},{6,5},{7,6},{8,11},{9,8},{10,9... | collective-permute-start | bytes 589832 | tf_op jit(solution)/shard_map/ppermute | solution.py:77
  104.1 10.1 %collective-permute-start.6 = (bf16[8,8,1536]{2,1,0:T(8,128)(2,1)S(1)}, bf16[8,8,1536]{2,1,0:T(8,128)(2,1)S(1)}, u32[]{:S(2)}, u32[]{:S(2)}) collective-permute-start(bf16[8,8,1536]{2,1,0:T(8,128)(2,1)S(1)} %add_convert_fusion.2), channel_id=1, source_target_pairs={{0,2},{1,3},{2,0},{3,1},{4,6},{5,7},{6,4},{7,5},{8,10},{9,11},{10,... | collective-permute-start | bytes 589832 | tf_op jit(solution)/shard_map/ppermute | solution.py:77
  105.0 15.2 %collective-permute-start.4 = (bf16[8,8,1536]{2,1,0:T(8,128)(2,1)S(1)}, bf16[8,8,1536]{2,1,0:T(8,128)(2,1)S(1)}, u32[]{:S(2)}, u32[]{:S(2)}) collective-permute-start(bf16[8,8,1536]{2,1,0:T(8,128)(2,1)S(1)} %add_convert_fusion.2), channel_id=1, source_target_pairs={{0,1},{1,2},{2,3},{3,0},{4,5},{5,6},{6,7},{7,4},{8,9},{9,10},{10,1... | collective-permute-start | bytes 589832 | tf_op jit(solution)/shard_map/ppermute | solution.py:77
  114.1 13.1 %collective-permute-start.9 = (bf16[64,1536]{1,0:T(8,128)(2,1)S(1)}, bf16[64,1536]{1,0:T(8,128)(2,1)}, u32[]{:S(2)}, u32[]{:S(2)}) collective-permute-start(bf16[64,1536]{1,0:T(8,128)(2,1)S(1)} %convolution_convert_fusion), channel_id=1, source_target_pairs={{0,1},{1,2},{2,3},{3,0},{4,5},{5,6},{6,7},{7,4},{8,9},{9,10},{10,1... | collective-permute-start | bytes 589832 | tf_op jit(solution)/shard_map/ppermute | solution.py:77
  117.7 9.5 %collective-permute-start.7 = (bf16[64,1536]{1,0:T(8,128)(2,1)}, bf16[64,1536]{1,0:T(8,128)(2,1)}, u32[]{:S(2)}, u32[]{:S(2)}) collective-permute-start(bf16[64,1536]{1,0:T(8,128)(2,1)} %convolution_convert_fusion.1), channel_id=1, source_target_pairs={{0,2},{1,3},{2,0},{3,1},{4,6},{5,7},{6,4},{7,5},{8,10},{9,11},{10,... | collective-permute-start | bytes 589832 | tf_op jit(solution)/shard_map/ppermute | solution.py:77
  123.6 6.0 %copy-start.4 = (f32[8,8,1536]{2,1,0:T(8,128)S(1)}, f32[8,8,1536]{2,1,0:T(8,128)}, u32[]{:S(2)}) copy-start(f32[8,8,1536]{2,1,0:T(8,128)} %copy-done.3) | copy-start | bytes 1179652
  123.6 6.0 %collective-permute-start.5 = (bf16[64,1536]{1,0:T(8,128)(2,1)}, bf16[64,1536]{1,0:T(8,128)(2,1)}, u32[]{:S(2)}, u32[]{:S(2)}) collective-permute-start(bf16[64,1536]{1,0:T(8,128)(2,1)} %convolution_convert_fusion.2), channel_id=1, source_target_pairs={{0,3},{1,0},{2,1},{3,2},{4,7},{5,4},{6,5},{7,6},{8,11},{9,8},{10,9... | collective-permute-start | bytes 589832 | tf_op jit(solution)/shard_map/ppermute | solution.py:77
  127.2 4.0 %copy-start.7 = (f32[8,1536]{1,0:T(8,128)S(1)}, f32[8,1536]{1,0:T(8,128)}, u32[]{:S(2)}) copy-start(f32[8,1536]{1,0:T(8,128)} %get-tuple-element.8) | copy-start | bytes 147460
  127.2 4.0 %copy-start.8 = (f32[8,1536]{1,0:T(8,128)S(1)}, f32[8,1536]{1,0:T(8,128)}, u32[]{:S(2)}) copy-start(f32[8,1536]{1,0:T(8,128)} %get-tuple-element.9) | copy-start | bytes 147460
  127.2 4.0 %copy-start.9 = (bf16[1536,64]{0,1:T(8,128)(2,1)S(1)}, bf16[1536,64]{0,1:T(8,128)(2,1)}, u32[]{:S(2)}) copy-start(bf16[1536,64]{0,1:T(8,128)(2,1)} %param.25) | copy-start | bytes 589828
  127.2 5.1 %copy-start.13 = (f32[9]{0:T(128)S(1)}, f32[9]{0:T(128)}, u32[]{:S(2)}) copy-start(f32[9]{0:T(128)} %param.18) | copy-start | bytes 112
  131.4 5.5 %collective-permute-start.10 = (f32[8,8,32]{2,1,0:T(8,128)S(1)}, f32[8,8,32]{2,1,0:T(8,128)S(1)}, u32[]{:S(2)}, u32[]{:S(2)}) collective-permute-start(f32[8,8,32]{2,1,0:T(8,128)S(1)} %fusion.94), channel_id=1, source_target_pairs={{0,128},{128,0},{1,129},{129,1},{2,130},{130,2},{3,131},{131,3},{4... | collective-permute-start | bytes 24584 | tf_op jit(solution)/shard_map/ppermute | solution.py:17

commit v17 on v13

--- a/solution.py
+++ b/solution.py
@@ -182,11 +182,11 @@
     resident_mine = lax.dynamic_slice_in_dim(resident, tp_index * portion, portion, 0)
     block_rows = portion * requests
     attn_total = None
+    attn_whole = jnp.dot(attn_rows, w_out, preferred_element_type=jnp.float32).astype(jnp.bfloat16)
     for step in range(parties):
-        rows_for = lax.dynamic_slice_in_dim(
-            attn_rows, ((tp_index + step) % parties) * block_rows, block_rows, 0
-        )
-        part = jnp.dot(rows_for, w_out, preferred_element_type=jnp.float32).astype(jnp.bfloat16)
+        part = lax.dynamic_slice_in_dim(
+            attn_whole, ((tp_index + step) % parties) * block_rows, block_rows, 0
+        )
         if step:
             part = shifted(part, "tp", step)
         attn_total = (

time: 139 us -> 147 us (1.058)
  local copies, waits for them, and re-layouts: 12.6 us -> 18 us
  waiting for transfers between devices: 30.5 us -> 34.1 us
  other arithmetic: 11.8 us -> 15.3 us
  matrix products: 23.9 us -> 20.8 us
    dot_general x4 -> x1, matrix products: 7.19 us -> 1.95 us  [shards(): jnp.dot(attn_rows, w_out, preferred_element_type=jnp.float32)]
    ppermute x9, waiting for transfers between devices: 13.2 us -> 16.8 us  [shifted(): lax.ppermute(value, axis, [(i, (i + step) % size) for i in range(size)])]
    dot_general x3, matrix products: 3.3 us -> 5.36 us  [shards(): jnp.dot(normed, w_qkv[:, part], preferred_element_type=jnp.float32)]
    concatenate x2, local copies, waits for them, and re-layouts: 0.26 us -> 1.91 us  [shards(): jnp.concatenate([keys_img, keys_txt], 0)]
    reduce_sum x3 -> x4, other arithmetic: 1.59 us -> 3.16 us  [layer_norm(): center = values - jnp.mean(values, -1, keepdims=True)]
    unnamed x35 -> x33, local copies, waits for them, and re-layouts: 2.82 us -> 3.89 us
  transfers between devices with their start and end apart: 12 -> 12, of which waited for: 7 -> 7; matrix products, arithmetic and copies ran while one was open for 15% -> 12% of each run, Pallas kernels for 0% -> 0%
where the time goes in v17:
time: 147 us; the launch traced here: 146 us
  blocking collectives  35.2 us (24%)
  waiting for transfers between devices  34.1 us (23%)
  matrix products  20.8 us (14%)
  local copies, waits for them, and re-layouts  18 us (12%)
  other arithmetic  15.3 us (10%)
  starting transfers between devices  15 us (10%)
  Pallas kernels  5.98 us (4%)
  between operations  1.62 us (1%)
    all_to_all x1, blocking collectives, shards(): lax.all_to_all(payload, 'seq', split_axis=0, concat_axis=0, tiled=True)  35.2 us
    ppermute x9, waiting for transfers between devices, shifted(): lax.ppermute(value, axis, [(i, (i + step) % size) for i in range(size)])  16.8 us
    all_to_all x1, waiting for transfers between devices, shards(): lax.all_to_all(answer.reshape(senders, query_share, head_share), 'seq', s...  12.9 us
    dot_general x4, matrix products, shards(): jnp.dot(hidden, w_down, preferred_element_type=jnp.float32)  12.6 us
    ppermute x9, starting transfers between devices, shifted(): lax.ppermute(value, axis, [(i, (i + step) % size) for i in range(size)])  10.1 us
    pallas_call x1, Pallas kernels, attend_kernel(): pl.pallas_call(attention_kernel, out_shape=jax.ShapeDtypeStruct(queries.s...  5.98 us
    dot_general x3, matrix products, shards(): jnp.dot(normed, w_qkv[:, part], preferred_element_type=jnp.float32)  5.36 us
    ppermute x2, waiting for transfers between devices, swapped(): lax.ppermute(value, axis, [(i, i ^ 1 << apart) for i in range(lax.axis_si...  4.39 us
  transfers between devices with their start and end apart: 12, of which 7 were waited for; matrix products, arithmetic and copies ran while one was open for 12% of the time, Pallas kernels for 0%

profile of v17, /device:TPU:4, one launch (start us, length us, event | category | flops | bytes accessed | tf_op | source)
XLA Modules:
  0.0 145.9 jit_solution(15351924213751777582)
XLA Ops:
  0.7 1.1 bitcast_convert_fusion
  1.8 0.7 fusion.113
  2.7 0.3 multiply_reduce_fusion
  3.1 2.7 %fusion.16 = bf16[256,384]{1,0:T(8,128)(2,1)} fusion(bf16[1536,3,384]{2,0,1:T(8,128)(2,1)} %param.20, bf16[1,32,8,1536]{3,2,1,0:T(8,128)(2,1)S(1)} %copy-done.1, f32[8,1536]{1,0:T(8,128)S(1)} %get-tuple-element.22, f32[8,1536]{1,0:T(8,128)S(1)} %get-tuple-element.23, f32[32,8]{1,0:T(8,128)S(1)} %add_rsqrt_fusion, f32[32,8]{1,0:T(8,128)S(1)} %broadcast_multiply_fusion), kind=kOutput, calls=%fused_computation.21 | convolution fusion | flops 304447488 | bytes 2263040 | tf_op jit(solution)/shard_map/dot_general | solution.py:109
  5.8 1.3 fusion.13
  7.1 1.3 fusion.10
  8.5 0.4 copy-done.4
  8.9 0.5 copy.42
  9.4 0.4 copy-done.5
  9.9 0.2 fusion.25
  10.1 0.6 convolution_convert_fusion.5
  10.8 1.1 concatenate.22
  12.0 1.8 %concatenate.19 = bf16[32,8,2,1,192]{4,2,1,0,3:T(2,128)(2,1)} reshape(bf16[256,384]{1,0:T(8,128)(2,1)} %fusion.13) | data formatting | bytes 393216 | tf_op jit(solution)/shard_map/concatenate | solution.py:132
  13.8 2.0 %maximum_bitcast_fusion = bf16[8,2,2,37,192]{4,1,0,3,2:T(2,128)(2,1)S(1)} fusion(bf16[5,8,2,1,192]{4,2,1,0,3:T(2,128)(2,1)S(1)} %concatenate.23, bf16[32,8,2,1,192]{4,2,1,0,3:T(2,128)(2,1)S(1)} %concatenate.22, bf16[5,8,2,1,192]{4,2,1,0,3:T(2,128)(2,1)S(1)} %concatenate.20, bf16[32,8,2,1,192]{4,2,1,0,3:T(2,128)(2,1)} %concatenate.19), kind=kLoop, calls=%fused_computation.27 | loop fusion | flops 681984 | bytes 909312 | tf_op jit(solution)/shard_map/transpose | solution.py:136
  15.8 1.0 copy.37
  16.9 1.1 reshape_reshape.3
  18.1 1.2 pad_maximum_fusion
  19.3 35.2 %all_to_all.10 = bf16[32,53,192]{2,1,0:T(8,128)(2,1)S(1)} all-to-all(bf16[32,53,192]{2,1,0:T(8,128)(2,1)S(1)} %pad_maximum_fusion), channel_id=1, replica_groups=mesh['cfg'=2,'seq'=32,'tp'=4] {'seq'}, dimensions={0} | all-to-all | bytes 1302528 | tf_op jit(solution)/shard_map/all_to_all | solution.py:140
  54.5 0.9 copy-done.2
  55.5 1.0 copy.38
  56.5 0.6 fusion.117
  57.7 0.6 compare_convert_fusion.valid_ref
  58.3 1.7 %slice.91 = bf16[32,16,192]{2,1,0:T(8,128)(2,1)} slice(bf16[32,53,192]{2,1,0:T(8,128)(2,1)} %copy-done.2), slice={[0:32], [0:16], [0:192]} | slice | bytes 393216 | tf_op jit(solution)/shard_map/slice | solution.py:141
  60.0 1.7 %broadcast_select_fusion = (bf16[32,37,192]{2,1,0:T(8,128)(2,1)S(1)}, bf16[32,37,192]{2,1,0:T(8,128)(2,1)S(1)}) fusion(pred[]{:T(512)S(6)} %eq.45, bf16[32,37,192]{2,0,1:T(8,128)(2,1)} %collective-permute-done, bf16[32,53,192]{2,1,0:T(8,128)(2,1)} %copy-done.2), kind=kLoop, calls=%fused_computation.25 | loop fusion | flops 454656 | bytes 1818625 | tf_op jit(solution)/shard_map/jit(_where)/select_n | solution.py:146
  61.6 0.9 slice.93
  62.5 0.9 slice.94
  63.5 0.7 pad.7.kt_ref
  64.2 0.7 pad.8.vt_ref
  64.9 6.0 %shard_map.140 = bf16[512,192]{1,0:T(8,128)(2,1)} custom-call(bf16[512,192]{1,0:T(8,128)(2,1)} %bitcast.153, bf16[1024,192]{1,0:T(8,128)(2,1)} %bitcast.150, bf16[1024,192]{1,0:T(8,128)(2,1)} %bitcast.151, bf16[256,192]{1,0:T(8,128)(2,1)} %pad.7.kt_ref, bf16[256,192]{1,0:T(8,128)(2,1)} %pad.8.vt_ref, f32[1,256]{1,0:T(1,128)} %compare_convert_fusion.valid_ref), custom_call_target="tpu_custom_call" | custom-call | tf_op jit(solution)/shard_map/pallas_call | solution.py:69
  70.8 4.0 %all-to-all-start.1 = ((bf16[32,16,192]{2,1,0:T(8,128)(2,1)}), bf16[32,16,192]{2,1,0:T(8,128)(2,1)S(1)}, u32[]{:S(2)}, u32[]{:S(2)}) async-start(bf16[32,16,192]{2,1,0:T(8,128)(2,1)} %bitcast.152), calls=%async_computation.1 | async-start | bytes 524288 | tf_op jit(solution)/shard_map/all_to_all | solution.py:169
  74.9 12.9 %all-to-all-done.1 = bf16[32,16,192]{2,1,0:T(8,128)(2,1)S(1)} async-done(((bf16[32,16,192]{2,1,0:T(8,128)(2,1)}), bf16[32,16,192]{2,1,0:T(8,128)(2,1)S(1)}, u32[]{:S(2)}, u32[]{:S(2)}) %all-to-all-start.1) | async-done | bytes 196640 | tf_op jit(solution)/shard_map/all_to_all | solution.py:169
  87.9 0.7 copy-done.6
  88.6 1.2 copy.41
  89.8 0.8 reshape.426
  90.6 2.0 %convolution_convert_fusion = bf16[256,1536]{1,0:T(8,128)(2,1)S(1)} fusion(bf16[256,384]{1,0:T(8,128)(2,1)} %reshape.426, bf16[384,1536]{1,0:T(8,128)(2,1)} %param.22), kind=kOutput, calls=%fused_computation | convolution fusion | flops 302383104 | bytes 2162688 | tf_op jit(solution)/shard_map/dot_general | solution.py:185
  92.6 0.9 copy-done.3
  93.5 0.7 constant_dynamic-slice_fusion.3
  94.2 3.0 %collective-permute-start.3 = (bf16[64,1536]{1,0:T(8,128)(2,1)}, bf16[64,1536]{1,0:T(8,128)(2,1)}, u32[]{:S(2)}, u32[]{:S(2)}) collective-permute-start(bf16[64,1536]{1,0:T(8,128)(2,1)} %get-tuple-element.13), channel_id=1, source_target_pairs={{0,3},{1,0},{2,1},{3,2},{4,7},{5,4},{6,5},{7,6},{8,11},{9,8},{10,9... | collective-permute-start | bytes 589832 | tf_op jit(solution)/shard_map/ppermute | solution.py:77
  97.2 0.6 collective-permute-start.2
  97.9 1.0 collective-permute-start.1
  98.8 1.3 convert_element_type.158
  100.2 4.8 %collective-permute-done.3 = bf16[64,1536]{1,0:T(8,128)(2,1)} collective-permute-done((bf16[64,1536]{1,0:T(8,128)(2,1)}, bf16[64,1536]{1,0:T(8,128)(2,1)}, u32[]{:S(2)}, u32[]{:S(2)}) %collective-permute-start.3) | collective-permute-done | bytes 196640 | tf_op jit(solution)/shard_map/ppermute | solution.py:77
  105.0 1.4 collective-permute-done.2
  106.4 2.1 %collective-permute-done.1 = bf16[64,1536]{1,0:T(8,128)(2,1)} collective-permute-done((bf16[64,1536]{1,0:T(8,128)(2,1)S(1)}, bf16[64,1536]{1,0:T(8,128)(2,1)}, u32[]{:S(2)}, u32[]{:S(2)}) %collective-permute-start.1) | collective-permute-done | bytes 196640 | tf_op jit(solution)/shard_map/ppermute | solution.py:77
  108.5 1.6 %fusion.139 = (f32[8,8]{1,0:T(8,128)S(1)}, f32[8,8,1536]{2,1,0:T(8,128)S(1)}) fusion(bf16[64,1536]{1,0:T(8,128)(2,1)} %collective-permute-done.3, bf16[64,1536]{1,0:T(8,128)(2,1)} %collective-permute-done.2, bf16[64,1536]{1,0:T(8,128)(2,1)} %collective-permute-done.1, bf16[256,1536]{1,0:T(8,128)(2,1)} %copy-done.3, s32[]{:T(128)S(6)} %select_n.92, ...), kind=kLoop, calls=%fused_computation.170 | loop fusion | flops 982976 | bytes 1622280 | tf_op jit(solution)/shard_map/reduce_sum | solution.py:21
  110.1 0.2 multiply_reduce_fusion.2
  110.4 0.7 collective-permute-start.8
  111.1 0.6 collective-permute-start.6
  111.7 0.9 collective-permute-start.4
  112.6 5.8 %collective-permute-done.8 = bf16[8,8,1536]{2,1,0:T(8,128)(2,1)} collective-permute-done((bf16[8,8,1536]{2,1,0:T(8,128)(2,1)S(1)}, bf16[8,8,1536]{2,1,0:T(8,128)(2,1)}, u32[]{:S(2)}, u32[]{:S(2)}) %collective-permute-start.8) | collective-permute-done | bytes 196640 | tf_op jit(solution)/shard_map/ppermute | solution.py:77
  118.4 2.9 %convolution_convert_fusion.1 = bf16[64,1536]{1,0:T(8,128)(2,1)S(1)} fusion(bf16[768,1536]{1,0:T(8,128)(2,1)S(1)} %copy-done, bf16[1536,768]{1,0:T(8,128)(2,1)} %param.23, bf16[8,8,1536]{2,1,0:T(8,128)(2,1)} %collective-permute-done.8), kind=kOutput, calls=%fused_computation.1 | convolution fusion | flops 302530560 | bytes 5111808 | tf_op jit(solution)/shard_map/dot_general | solution.py:209
  121.4 3.5 %convolution_convert_fusion.2 = bf16[64,1536]{1,0:T(8,128)(2,1)} fusion(bf16[768,1536]{1,0:T(8,128)(2,1)S(1)} %copy-done, bf16[1536,768]{1,0:T(8,128)(2,1)} %param.23, bf16[8,8,1536]{2,1,0:T(8,128)(2,1)S(1)} %collective-permute-done.6), kind=kOutput, calls=%fused_computation.2 | convolution fusion | flops 302530560 | bytes 5111808 | tf_op jit(solution)/shard_map/dot_general | solution.py:209
  124.9 1.8 %collective-permute-start.7 = (bf16[64,1536]{1,0:T(8,128)(2,1)}, bf16[64,1536]{1,0:T(8,128)(2,1)}, u32[]{:S(2)}, u32[]{:S(2)}) collective-permute-start(bf16[64,1536]{1,0:T(8,128)(2,1)} %convolution_convert_fusion.2), channel_id=1, source_target_pairs={{0,2},{1,3},{2,0},{3,1},{4,6},{5,7},{6,4},{7,5},{8,10},{9,11},{10,... | collective-permute-start | bytes 589832 | tf_op jit(solution)/shard_map/ppermute | solution.py:77
  126.6 3.5 %convolution_convert_fusion.3 = bf16[64,1536]{1,0:T(8,128)(2,1)} fusion(bf16[768,1536]{1,0:T(8,128)(2,1)S(1)} %copy-done, bf16[1536,768]{1,0:T(8,128)(2,1)} %param.23, bf16[8,8,1536]{2,1,0:T(8,128)(2,1)S(1)} %collective-permute-done.4), kind=kOutput, calls=%fused_computation.3 | convolution fusion | flops 302530560 | bytes 5111808 | tf_op jit(solution)/shard_map/dot_general | solution.py:209
  130.1 1.5 %collective-permute-start.5 = (bf16[64,1536]{1,0:T(8,128)(2,1)}, bf16[64,1536]{1,0:T(8,128)(2,1)}, u32[]{:S(2)}, u32[]{:S(2)}) collective-permute-start(bf16[64,1536]{1,0:T(8,128)(2,1)} %convolution_convert_fusion.3), channel_id=1, source_target_pairs={{0,3},{1,0},{2,1},{3,2},{4,7},{5,4},{6,5},{7,6},{8,11},{9,8},{10,9... | collective-permute-start | bytes 589832 | tf_op jit(solution)/shard_map/ppermute | solution.py:77
  131.6 2.8 %fusion = f32[64,1536]{1,0:T(8,128)S(1)} fusion(bf16[768,1536]{1,0:T(8,128)(2,1)S(1)} %copy-done, bf16[1536,768]{1,0:T(8,128)(2,1)} %param.23, bf16[8,8,1536]{2,1,0:T(8,128)(2,1)S(1)} %add_convert_fusion.2), kind=kOutput, calls=%fused_computation.5 | convolution fusion | flops 302628864 | bytes 5308416 | tf_op jit(solution)/shard_map/dot_general | solution.py:209
  134.4 2.7 %collective-permute-done.5 = bf16[64,1536]{1,0:T(8,128)(2,1)} collective-permute-done((bf16[64,1536]{1,0:T(8,128)(2,1)}, bf16[64,1536]{1,0:T(8,128)(2,1)}, u32[]{:S(2)}, u32[]{:S(2)}) %collective-permute-start.5) | collective-permute-done | bytes 196640 | tf_op jit(solution)/shard_map/ppermute | solution.py:77
  137.1 1.3 fusion.137
  138.4 0.2 multiply_reduce_fusion.1
  138.7 0.3 fusion.61
  139.0 0.8 collective-permute-start.10
  139.8 0.2 select_reduce_fusion
  140.1 4.4 %collective-permute-done.10 = f32[8,8,32]{2,1,0:T(8,128)S(1)} collective-permute-done((f32[8,8,32]{2,1,0:T(8,128)S(1)}, f32[8,8,32]{2,1,0:T(8,128)S(1)}, u32[]{:S(2)}, u32[]{:S(2)}) %collective-permute-start.10) | collective-permute-done | bytes 8224 | tf_op jit(solution)/shard_map/ppermute | solution.py:17
  144.5 1.5 %multiply_add_fusion = (f32[8,8,32]{2,1,0:T(8,128)}, f32[8,8,32]{2,1,0:T(8,128)}) fusion(f32[8,8,32]{2,1,0:T(8,128)} %param.19, f32[8]{0:T(128)S(1)} %sub.84, f32[8,8,32]{2,1,0:T(8,128)S(1)} %collective-permute-done.10, f32[8,8,64]{2,1,0:T(8,128)S(1)} %fusion.61, s32[]{:T(128)S(6)} %select_n.100, pred[]{:T(512)S(6)} %eq.44), kind=kLoop, calls=%fused_computation.131 | loop fusion | flops 14336 | bytes 40997 | tf_op jit(solution)/shard_map/add | solution.py:237
  (57 shorter events, 1.2 us)
Async XLA Ops:
  0.6 117.8 %copy-start = (bf16[768,1536]{1,0:T(8,128)(2,1)S(1)}, bf16[768,1536]{1,0:T(8,128)(2,1)}, u32[]{:S(2)}) copy-start(bf16[768,1536]{1,0:T(8,128)(2,1)} %param.24) | copy-start | bytes 7077892
  0.6 1.9 %copy-start.1 = (bf16[1,32,8,1536]{3,2,1,0:T(8,128)(2,1)S(1)}, bf16[1,32,8,1536]{3,2,1,0:T(8,128)(2,1)}, u32[]{:S(2)}) copy-start(bf16[1,32,8,1536]{3,2,1,0:T(8,128)(2,1)} %param.13) | copy-start | bytes 2359300
  3.1 2.8 %copy-start.14 = (bf16[1536,3,384]{2,0,1:T(8,128)(2,1)S(1)}, bf16[1536,3,384]{2,0,1:T(8,128)(2,1)}, u32[]{:S(2)}) copy-start(bf16[1536,3,384]{2,0,1:T(8,128)(2,1)} %param.20) | copy-start | bytes 10616836
  7.1 1.7 %copy-start.4 = (bf16[1536,2,384]{2,1,0:T(2,128)(2,1)S(1)}, bf16[1536,2,384]{2,1,0:T(2,128)(2,1)}, u32[]{:S(2)}) copy-start(bf16[1536,2,384]{2,1,0:T(2,128)(2,1)} %param.21) | copy-start | bytes 7077892
  8.9 0.9 copy-start.5
  19.3 37.1 %copy-start.15 = (s32[1,8]{1,0:T(1,128)S(1)}, s32[1,8]{1,0:T(1,128)}, u32[]{:S(2)}) copy-start(s32[1,8]{1,0:T(1,128)} %param.16) | copy-start | bytes 100
  54.5 0.9 copy-start.2
  56.5 3.5 %collective-permute-start = (bf16[32,37,192]{2,0,1:T(8,128)(2,1)}, bf16[32,37,192]{2,0,1:T(8,128)(2,1)}, u32[]{:S(2)}, u32[]{:S(2)}) collective-permute-start(bf16[32,37,192]{2,0,1:T(8,128)(2,1)} %copy.38), channel_id=1, source_target_pairs={{0,4},{4,0},{8,12},{12,8},{16,20},{20,16},{24,28},{28,24},{32,36},... | collective-permute-start | bytes 1363976 | tf_op jit(solution)/shard_map/ppermute | solution.py:17
  70.8 17.0 %all-to-all-start.1 = ((bf16[32,16,192]{2,1,0:T(8,128)(2,1)}), bf16[32,16,192]{2,1,0:T(8,128)(2,1)S(1)}, u32[]{:S(2)}, u32[]{:S(2)}) async-start(bf16[32,16,192]{2,1,0:T(8,128)(2,1)} %bitcast.152), calls=%async_computation.1 | async-start | bytes 524288 | tf_op jit(solution)/shard_map/all_to_all | solution.py:169
  87.9 0.7 copy-start.6
  92.6 0.9 copy-start.3
  94.2 10.8 %collective-permute-start.3 = (bf16[64,1536]{1,0:T(8,128)(2,1)}, bf16[64,1536]{1,0:T(8,128)(2,1)}, u32[]{:S(2)}, u32[]{:S(2)}) collective-permute-start(bf16[64,1536]{1,0:T(8,128)(2,1)} %get-tuple-element.13), channel_id=1, source_target_pairs={{0,3},{1,0},{2,1},{3,2},{4,7},{5,4},{6,5},{7,6},{8,11},{9,8},{10,9... | collective-permute-start | bytes 589832 | tf_op jit(solution)/shard_map/ppermute | solution.py:77
  97.2 9.2 %collective-permute-start.2 = (bf16[64,1536]{1,0:T(8,128)(2,1)S(1)}, bf16[64,1536]{1,0:T(8,128)(2,1)}, u32[]{:S(2)}, u32[]{:S(2)}) collective-permute-start(bf16[64,1536]{1,0:T(8,128)(2,1)S(1)} %get-tuple-element.14), channel_id=1, source_target_pairs={{0,2},{1,3},{2,0},{3,1},{4,6},{5,7},{6,4},{7,5},{8,10},{9,11},{10,... | collective-permute-start | bytes 589832 | tf_op jit(solution)/shard_map/ppermute | solution.py:77
  97.9 10.6 %collective-permute-start.1 = (bf16[64,1536]{1,0:T(8,128)(2,1)S(1)}, bf16[64,1536]{1,0:T(8,128)(2,1)}, u32[]{:S(2)}, u32[]{:S(2)}) collective-permute-start(bf16[64,1536]{1,0:T(8,128)(2,1)S(1)} %get-tuple-element.12), channel_id=1, source_target_pairs={{0,1},{1,2},{2,3},{3,0},{4,5},{5,6},{6,7},{7,4},{8,9},{9,10},{10,1... | collective-permute-start | bytes 589832 | tf_op jit(solution)/shard_map/ppermute | solution.py:77
  100.2 10.1 %copy-start.10 = (f32[8,1536]{1,0:T(8,128)S(1)}, f32[8,1536]{1,0:T(8,128)}, u32[]{:S(2)}) copy-start(f32[8,1536]{1,0:T(8,128)} %get-tuple-element.17) | copy-start | bytes 147460
  100.2 10.1 %copy-start.11 = (f32[8,1536]{1,0:T(8,128)S(1)}, f32[8,1536]{1,0:T(8,128)}, u32[]{:S(2)}) copy-start(f32[8,1536]{1,0:T(8,128)} %get-tuple-element.18) | copy-start | bytes 147460
  100.2 10.9 %copy-start.12 = (s32[8]{0:T(128)S(1)}, s32[8]{0:T(128)}, u32[]{:S(2)}) copy-start(s32[8]{0:T(128)} %param.17) | copy-start | bytes 100
  110.4 8.0 %collective-permute-start.8 = (bf16[8,8,1536]{2,1,0:T(8,128)(2,1)S(1)}, bf16[8,8,1536]{2,1,0:T(8,128)(2,1)}, u32[]{:S(2)}, u32[]{:S(2)}) collective-permute-start(bf16[8,8,1536]{2,1,0:T(8,128)(2,1)S(1)} %add_convert_fusion.2), channel_id=1, source_target_pairs={{0,3},{1,0},{2,1},{3,2},{4,7},{5,4},{6,5},{7,6},{8,11},{9,8},{10,9... | collective-permute-start | bytes 589832 | tf_op jit(solution)/shard_map/ppermute | solution.py:77
  111.1 10.3 %collective-permute-start.6 = (bf16[8,8,1536]{2,1,0:T(8,128)(2,1)S(1)}, bf16[8,8,1536]{2,1,0:T(8,128)(2,1)S(1)}, u32[]{:S(2)}, u32[]{:S(2)}) collective-permute-start(bf16[8,8,1536]{2,1,0:T(8,128)(2,1)S(1)} %add_convert_fusion.2), channel_id=1, source_target_pairs={{0,2},{1,3},{2,0},{3,1},{4,6},{5,7},{6,4},{7,5},{8,10},{9,11},{10,... | collective-permute-start | bytes 589832 | tf_op jit(solution)/shard_map/ppermute | solution.py:77
  111.7 14.9 %collective-permute-start.4 = (bf16[8,8,1536]{2,1,0:T(8,128)(2,1)S(1)}, bf16[8,8,1536]{2,1,0:T(8,128)(2,1)S(1)}, u32[]{:S(2)}, u32[]{:S(2)}) collective-permute-start(bf16[8,8,1536]{2,1,0:T(8,128)(2,1)S(1)} %add_convert_fusion.2), channel_id=1, source_target_pairs={{0,1},{1,2},{2,3},{3,0},{4,5},{5,6},{6,7},{7,4},{8,9},{9,10},{10,1... | collective-permute-start | bytes 589832 | tf_op jit(solution)/shard_map/ppermute | solution.py:77
  121.3 13.1 %collective-permute-start.9 = (bf16[64,1536]{1,0:T(8,128)(2,1)S(1)}, bf16[64,1536]{1,0:T(8,128)(2,1)}, u32[]{:S(2)}, u32[]{:S(2)}) collective-permute-start(bf16[64,1536]{1,0:T(8,128)(2,1)S(1)} %convolution_convert_fusion.1), channel_id=1, source_target_pairs={{0,1},{1,2},{2,3},{3,0},{4,5},{5,6},{6,7},{7,4},{8,9},{9,10},{10,1... | collective-permute-start | bytes 589832 | tf_op jit(solution)/shard_map/ppermute | solution.py:77
  124.9 9.5 %collective-permute-start.7 = (bf16[64,1536]{1,0:T(8,128)(2,1)}, bf16[64,1536]{1,0:T(8,128)(2,1)}, u32[]{:S(2)}, u32[]{:S(2)}) collective-permute-start(bf16[64,1536]{1,0:T(8,128)(2,1)} %convolution_convert_fusion.2), channel_id=1, source_target_pairs={{0,2},{1,3},{2,0},{3,1},{4,6},{5,7},{6,4},{7,5},{8,10},{9,11},{10,... | collective-permute-start | bytes 589832 | tf_op jit(solution)/shard_map/ppermute | solution.py:77
  130.1 7.0 %collective-permute-start.5 = (bf16[64,1536]{1,0:T(8,128)(2,1)}, bf16[64,1536]{1,0:T(8,128)(2,1)}, u32[]{:S(2)}, u32[]{:S(2)}) collective-permute-start(bf16[64,1536]{1,0:T(8,128)(2,1)} %convolution_convert_fusion.3), channel_id=1, source_target_pairs={{0,3},{1,0},{2,1},{3,2},{4,7},{5,4},{6,5},{7,6},{8,11},{9,8},{10,9... | collective-permute-start | bytes 589832 | tf_op jit(solution)/shard_map/ppermute | solution.py:77
  134.4 4.3 %copy-start.7 = (bf16[1536,64]{0,1:T(8,128)(2,1)S(1)}, bf16[1536,64]{0,1:T(8,128)(2,1)}, u32[]{:S(2)}) copy-start(bf16[1536,64]{0,1:T(8,128)(2,1)} %param.25) | copy-start | bytes 589828
  134.4 4.3 %copy-start.8 = (f32[8,1536]{1,0:T(8,128)S(1)}, f32[8,1536]{1,0:T(8,128)}, u32[]{:S(2)}) copy-start(f32[8,1536]{1,0:T(8,128)} %get-tuple-element.15) | copy-start | bytes 147460
  134.4 4.3 %copy-start.9 = (f32[8,1536]{1,0:T(8,128)S(1)}, f32[8,1536]{1,0:T(8,128)}, u32[]{:S(2)}) copy-start(f32[8,1536]{1,0:T(8,128)} %get-tuple-element.16) | copy-start | bytes 147460
  134.4 5.4 %copy-start.13 = (f32[9]{0:T(128)S(1)}, f32[9]{0:T(128)}, u32[]{:S(2)}) copy-start(f32[9]{0:T(128)} %param.18) | copy-start | bytes 112
  139.0 5.5 %collective-permute-start.10 = (f32[8,8,32]{2,1,0:T(8,128)S(1)}, f32[8,8,32]{2,1,0:T(8,128)S(1)}, u32[]{:S(2)}, u32[]{:S(2)}) collective-permute-start(f32[8,8,32]{2,1,0:T(8,128)S(1)} %constant_dynamic-slice_fusion), channel_id=1, source_target_pairs={{0,128},{128,0},{1,129},{129,1},{2,130},{130,2},{3,131},{131,3},{4... | collective-permute-start | bytes 24584 | tf_op jit(solution)/shard_map/ppermute | solution.py:17
